TPU v7x, 32 devices: a whole 2x2x4 slice. The times are simulated.
32 devices in a mesh: ens: 4 (over x, core), lat: 2 (over y), lon: 4 (over z).
Axes of the slice: x: 2, y: 2, z: 4, core: 2. Of those that a mesh axis runs over, the one named last changes fastest.
Arguments:
- state_field: bfloat16 [4, 256, 4, 512], P('ens', None, 'lat', 'lon'), may hold values from -6 to 6
- first_weight: bfloat16 [3, 256, 256], replicated, may hold values from -0.21875 to 0.21875
- second_weight: bfloat16 [3, 256, 256], replicated, may hold values from -0.21875 to 0.21875
- quadrature: float32 [4, 3, 12], P('lat'), may hold values from 0.05 to 0.4
- lat_offsets: int32 [4, 3, 12], P('lat'), may hold values from -1 to 1, as said below
- lon_offsets: int32 [4, 3, 12], P('lat'), may hold values from -4 to 4, as said below
- cotangent: bfloat16 [4, 256, 4, 512], P('ens', None, 'lat', 'lon'), may hold values from -6 to 6
Outputs:
- layer_output: bfloat16 [4, 256, 4, 512], P('ens', None, 'lat', 'lon')
- state_grad: bfloat16 [4, 256, 4, 512], P('ens', None, 'lat', 'lon')
- first_grad: float32 [3, 256, 256], replicated
- second_grad: float32 [3, 256, 256], replicated
Inputs may be any that keep to these rules, and one draw needn't show every extreme that they name: `lat_offsets`: for every row and basis function the first three support points have latitude offsets 0, -1 and 1. `lon_offsets`: in a row p rows from the nearer pole the longitude offsets lie within plus or minus max(2, 4 - p), and the first three support points have offsets 0, minus that bound and that bound.
All inputs are finite; a program needn't handle non-finite values.
Results may differ from a plain program's by a relative error of at most 0.013.
Values may be sent and summed in bfloat16 or wider, within the bound.
No kernel may reach another device: no remote copies, remote signals or barrier semaphores. Data moves between devices by JAX's collectives and lax.ppermute only.
A program may use at most 64 MiB of HBM per device.

v0:
```python
import math

import jax
import jax.numpy as jnp
from jax import lax
from jax.sharding import PartitionSpec as P

LAT_REACH = 1
LON_REACH = 4


def with_halo(block, sides, width, periodic):
    for axis, dim in sides:
        count = lax.axis_size(axis)
        forward = [(i, i + 1) for i in range(count - 1)]
        if periodic:
            forward.append((count - 1, 0))
        backward = [(target, source) for source, target in forward]
        low = lax.ppermute(
            lax.slice_in_dim(block, block.shape[dim] - width, None, axis=dim), axis, forward
        )
        high = lax.ppermute(lax.slice_in_dim(block, 0, width, axis=dim), axis, backward)
        block = jnp.concatenate([low, block, high], axis=dim)
    return block


def passed_along(value, axis, by):
    devices = lax.axis_size(axis)
    return lax.ppermute(value, axis, [(i, (i + by) % devices) for i in range(devices)])


def passed_along_2(value, axis, steps):
    count = lax.axis_size(axis)
    leading, last = (max(0, -steps), min(count, count - steps))
    return lax.ppermute(value, axis, [(source, source + steps) for source in range(leading, last)])


def coefficients(quadrature, lat_offsets, lon_offsets):
    lat_levels = jnp.arange(2 * LAT_REACH + 1, dtype=jnp.int32)
    lon_levels = jnp.arange(2 * LON_REACH + 1, dtype=jnp.int32)
    lat_onehot = (lat_offsets[..., None] + LAT_REACH == lat_levels).astype(jnp.float32)
    lon_onehot = (lon_offsets[..., None] + LON_REACH == lon_levels).astype(jnp.float32)
    stencil = jnp.einsum(
        "rks,rksa,rksd->krad", quadrature, lat_onehot, lon_onehot, precision=lax.Precision.HIGHEST
    )
    return stencil.astype(jnp.bfloat16)


def lon_picker(col_count):
    span_count = 2 * LON_REACH + 1
    wide_count = col_count + 2 * LON_REACH
    table_shape = (span_count, wide_count, col_count)
    offset_level = lax.broadcasted_iota(jnp.int32, table_shape, 0)
    source = lax.broadcasted_iota(jnp.int32, table_shape, 1)
    target = lax.broadcasted_iota(jnp.int32, table_shape, 2)
    matches = source - target == offset_level
    return matches.astype(jnp.bfloat16)


def widen(values):
    wide_lon = with_halo(values, (("lon", 2),), LON_REACH, True)
    return with_halo(wide_lon, (("lat", 1),), LAT_REACH, False)


def lon_pass(piece, steps):
    return passed_along(piece, "lon", steps)


def lat_pass(piece, steps):
    return passed_along_2(piece.astype(jnp.bfloat16), "lat", steps).astype(piece.dtype)


def mix_channels(weight, spreaded):
    return jnp.einsum("koc,cikj->oij", weight, spreaded, preferred_element_type=jnp.float32)


def filter_term(gradient, spreaded):
    return jnp.einsum("oij,cikj->koc", gradient, spreaded, preferred_element_type=jnp.float32)


def body(state_field, first_weight, second_weight, quadrature, lat_offsets, lon_offsets, cotangent):
    source = state_field[0]
    channels, row_count, col_count = source.shape
    lat_taps = 2 * LAT_REACH + 1
    wide_count = col_count + 2 * LON_REACH
    stencil = coefficients(quadrature, lat_offsets, lon_offsets)
    basis_count = stencil.shape[0]
    forward_band = jnp.einsum(
        "kiad,dpq->iapkq", stencil, lon_picker(col_count), preferred_element_type=jnp.float32
    )
    forward_band = forward_band.astype(jnp.bfloat16).reshape(
        row_count, lat_taps * wide_count, basis_count * col_count
    )

    def spread(values):
        extended = widen(values)
        stacked = jnp.stack(
            [extended[:, offset : offset + row_count] for offset in range(lat_taps)], axis=2
        )
        stacked = stacked.reshape(channels, row_count, lat_taps * wide_count)
        mixed = jnp.einsum(
            "cin,inm->cim", stacked, forward_band, preferred_element_type=jnp.float32
        )
        return mixed.reshape(channels, row_count, basis_count, col_count).astype(jnp.bfloat16)

    first_spread = spread(source)
    hidden = mix_channels(first_weight, first_spread)
    activation = jax.nn.gelu(hidden).astype(jnp.bfloat16)
    second_spread = spread(activation)
    layer_output = mix_channels(second_weight, second_spread).astype(jnp.bfloat16)
    gradient = cotangent[0]
    second_sum = filter_term(gradient, second_spread)

    def carry_back(weight, grad_rows):
        mixed_grad = jnp.einsum(
            "koc,oij->cikj", weight, grad_rows, preferred_element_type=jnp.float32
        ).astype(jnp.bfloat16)
        partial_rows = jnp.einsum(
            "cim,inm->cin",
            mixed_grad.reshape(channels, row_count, basis_count * col_count),
            forward_band,
            preferred_element_type=jnp.float32,
        )
        partial_rows = partial_rows.reshape(channels, row_count, lat_taps, wide_count)
        extended = jnp.zeros((channels, row_count + 2 * LAT_REACH, wide_count), jnp.float32)
        for offset in range(lat_taps):
            extended = extended + jnp.pad(
                partial_rows[:, :, offset], ((0, 0), (offset, lat_taps - 1 - offset), (0, 0))
            )
        left_rim = extended[:, :, :LON_REACH]
        right_rim = extended[:, :, LON_REACH + col_count :]
        core_block = extended[:, :, LON_REACH : LON_REACH + col_count]
        core_block = core_block.at[:, :, col_count - LON_REACH :].add(lon_pass(left_rim, -1))
        core_block = core_block.at[:, :, :LON_REACH].add(lon_pass(right_rim, 1))
        top_rows = core_block[:, :LAT_REACH]
        bottom_rows = core_block[:, LAT_REACH + row_count :]
        inner_rows = core_block[:, LAT_REACH : LAT_REACH + row_count]
        inner_rows = inner_rows.at[:, row_count - LAT_REACH :].add(lat_pass(top_rows, -1))
        inner_rows = inner_rows.at[:, :LAT_REACH].add(lat_pass(bottom_rows, 1))
        return inner_rows.astype(jnp.bfloat16)

    activation_grad = carry_back(second_weight, gradient)
    hidden_grad = jax.vjp(jax.nn.gelu, hidden)[1](activation_grad.astype(jnp.float32))[0].astype(
        jnp.bfloat16
    )
    first_sum = filter_term(hidden_grad, first_spread)
    state_grad = carry_back(first_weight, hidden_grad)
    first_sum, second_sum = lax.psum((first_sum, second_sum), ("ens", "lat", "lon"))
    member_total = state_field.shape[0] * lax.axis_size("ens")
    grad_scale = 1.0 / math.sqrt(
        member_total * row_count * lax.axis_size("lat") * col_count * lax.axis_size("lon")
    )
    return (layer_output[None], state_grad[None], first_sum * grad_scale, second_sum * grad_scale)


def solution(mesh):
    in_specs = (
        P("ens", None, "lat", "lon"),
        P(),
        P(),
        P("lat", None, None),
        P("lat", None, None),
        P("lat", None, None),
        P("ens", None, "lat", "lon"),
    )
    out_specs = (P("ens", None, "lat", "lon"), P("ens", None, "lat", "lon"), P(), P())
    return jax.shard_map(body, mesh=mesh, in_specs=in_specs, out_specs=out_specs, check_vma=False)
```

profile of v0, /device:TPU:0, one launch (start us, length us, event | category | flops | bytes accessed | tf_op | source)
XLA Modules:
  0.0 267.8 jit_solution(15908329832763771891)
XLA Ops:
  7.2 0.7 broadcast_add_fusion
  8.0 0.9 fusion.5
  8.9 0.6 fusion
  9.5 0.4 copy.50
  9.9 0.6 reshape.267
  10.4 0.4 copy-done.1
  10.9 0.3 convolution_convert_fusion.2
  11.2 0.4 fusion.48
  11.6 0.1 slice_bitcast_fusion.2
  11.7 5.1 %collective-permute-start.8 = (f32[256,4,4]{0,2,1:T(4,128)S(1)}, f32[256,4,4]{0,2,1:T(4,128)S(1)}, u32[]{:S(2)}, u32[]{:S(2)}) collective-permute-start(f32[256,4,4]{0,2,1:T(4,128)S(1)} %get-tuple-element.120), channel_id=1, source_target_pairs={{0,3},{1,0},{2,1},{3,2},{4,7},{5,4},{6,5},{7,6},{8,11},{9,8},{10,9... | collective-permute-start | bytes 49160 | tf_op jit(solution)/shard_map/ppermute | solution.py:29
  16.8 0.1 copy.51
  16.9 3.9 %collective-permute-start.1 = (bf16[256,2,4]{0,2,1:T(4,128)(2,1)S(1)}, bf16[256,2,4]{0,2,1:T(4,128)(2,1)S(1)}, u32[]{:S(2)}, u32[]{:S(2)}) collective-permute-start(bf16[256,2,4]{0,2,1:T(4,128)(2,1)S(1)} %get-tuple-element.143), channel_id=1, source_target_pairs={{1,0},{2,1},{3,2},{0,3},{5,4},{6,5},{7,6},{4,7},{9,8},{10,9},{11,1... | collective-permute-start | bytes 12296 | tf_op jit(solution)/shard_map/ppermute | solution.py:22
  20.8 0.1 pad_add_fusion.1
  20.9 1.2 collective-permute-done.1
  22.1 4.1 %collective-permute-done = bf16[256,2,4]{0,2,1:T(4,128)(2,1)S(1)} collective-permute-done((bf16[256,2,4]{0,2,1:T(4,128)(2,1)S(1)}, bf16[256,2,4]{0,2,1:T(4,128)(2,1)S(1)}, u32[]{:S(2)}, u32[]{:S(2)}) %collective-permute-start) | collective-permute-done | bytes 4128 | tf_op jit(solution)/shard_map/ppermute | solution.py:19
  26.3 3.4 %collective-permute-start.2 = (bf16[256,1,136]{0,2,1:T(8,128)(2,1)S(1)}, bf16[256,1,136]{0,2,1:T(8,128)(2,1)S(1)}, u32[]{:S(2)}, u32[]{:S(2)}) collective-permute-start(bf16[256,1,136]{0,2,1:T(8,128)(2,1)S(1)} %get-tuple-element.138), channel_id=1, source_target_pairs={{0,4},{1,5},{2,6},{3,7},{8,12},{9,13},{10,14},{11,15},{16,20},{17,... | collective-permute-start | bytes 208904 | tf_op jit(solution)/shard_map/ppermute | solution.py:19
  29.7 1.3 collective-permute-start.3
  31.1 1.3 collective-permute-start.10
  32.4 4.5 %collective-permute-start.11 = (bf16[256,1,128]{0,2,1:T(8,128)(2,1)S(1)}, bf16[256,1,128]{0,2,1:T(8,128)(2,1)S(1)}, u32[]{:S(2)}, u32[]{:S(2)}) collective-permute-start(bf16[256,1,128]{0,2,1:T(8,128)(2,1)S(1)} %get-tuple-element.128), channel_id=1, source_target_pairs={{0,4},{1,5},{2,6},{3,7},{8,12},{9,13},{10,14},{11,15},{16,20},{17,... | collective-permute-start | bytes 196616 | tf_op jit(solution)/shard_map/ppermute | solution.py:35
  37.2 0.4 convolution_convert_fusion.4
  37.6 1.3 collective-permute-done.11
  38.9 0.5 fusion.12
  39.4 0.1 collective-permute-start.5
  39.5 2.0 collective-permute-start.4
  41.5 0.3 convolution_convert_fusion.1
  41.8 0.4 fusion.49
  42.2 0.8 fusion.41
  43.0 0.2 copy.92
  43.2 0.2 copy.91
  43.4 1.2 copy.90
  44.6 0.7 pad_add_fusion
  45.4 1.1 fusion.40
  46.5 1.2 convolution_bitcast_fusion.1
  47.7 0.3 slice.353
  48.0 1.9 collective-permute-start.12
  49.9 0.2 collective-permute-start.13
  50.2 4.3 %collective-permute-start.6 = (bf16[256,1,136]{0,2,1:T(8,128)(2,1)S(1)}, bf16[256,1,136]{0,2,1:T(8,128)(2,1)S(1)}, u32[]{:S(2)}, u32[]{:S(2)}) collective-permute-start(bf16[256,1,136]{0,2,1:T(8,128)(2,1)S(1)} %get-tuple-element.133), channel_id=1, source_target_pairs={{0,4},{1,5},{2,6},{3,7},{8,12},{9,13},{10,14},{11,15},{16,20},{17,... | collective-permute-start | bytes 208904 | tf_op jit(solution)/shard_map/ppermute | solution.py:19
  54.5 1.3 collective-permute-start.7
  55.8 6.5 %collective-permute-done.12 = f32[256,4,4]{2,1,0:T(4,128)S(1)} collective-permute-done((f32[256,4,4]{2,1,0:T(4,128)S(1)}, f32[256,4,4]{2,1,0:T(4,128)S(1)}, u32[]{:S(2)}, u32[]{:S(2)}) %collective-permute-start.12) | collective-permute-done | bytes 16416 | tf_op jit(solution)/shard_map/ppermute | solution.py:29
  62.3 0.1 slice_add_fusion.1
  62.4 42.8 %scatter-add.34 = f32[256,4,128]{2,1,0:T(4,128)S(1)} dynamic-update-slice(f32[256,4,128]{2,1,0:T(4,128)S(1)} %slice.353, f32[256,4,4]{2,1,0:T(4,128)S(1)} %slice_add_fusion.1, s32[]{:T(128)} %constant.204.clone.1, s32[]{:T(128)} %constant.204.clone.1, s32[]{:T(128)} %constant.205.clone.1) | dynamic-update-slice | bytes 32772 | tf_op jit(solution)/shard_map/scatter-add | solution.py:133
  105.2 0.1 slice_add_fusion
  105.4 8.4 %scatter-add.35 = f32[256,4,128]{2,1,0:T(4,128)S(1)} dynamic-update-slice(f32[256,4,128]{2,1,0:T(4,128)S(1)} %scatter-add.34, f32[256,4,4]{2,1,0:T(4,128)S(1)} %slice_add_fusion, s32[]{:T(128)} %constant.204.clone.1, s32[]{:T(128)} %constant.204.clone.1, s32[]{:T(128)} %constant.204.clone.1) | dynamic-update-slice | bytes 32772 | tf_op jit(solution)/shard_map/scatter-add | solution.py:134
  113.7 0.1 convert.10
  113.8 0.2 fusion.42
  114.0 0.1 slice.358
  114.2 1.3 collective-permute-start.14
  115.5 4.7 %collective-permute-start.15 = (bf16[256,1,128]{2,1,0:T(2,128)(2,1)S(1)}, bf16[256,1,128]{2,1,0:T(2,128)(2,1)S(1)}, u32[]{:S(2)}, u32[]{:S(2)}) collective-permute-start(bf16[256,1,128]{2,1,0:T(2,128)(2,1)S(1)} %get-tuple-element.124), channel_id=1, source_target_pairs={{0,4},{1,5},{2,6},{3,7},{8,12},{9,13},{10,14},{11,15},{16,20},{17,... | collective-permute-start | bytes 196616 | tf_op jit(solution)/shard_map/ppermute | solution.py:35
  120.2 0.9 fusion.21
  121.3 0.4 convolution_convert_fusion.3
  121.7 0.4 copy-done.4
  122.1 1.2 convolution_bitcast_fusion
  123.4 0.3 fusion.2
  123.7 0.8 copy.67
  124.4 0.2 slice_add_fusion.3
  124.7 2.9 %scatter-add.36 = f32[256,2,128]{2,1,0:T(2,128)S(1)} dynamic-update-slice(f32[256,2,128]{2,1,0:T(2,128)S(1)} %slice.358, f32[256,1,128]{2,1,0:T(1,128)S(1)} %slice_add_fusion.3, s32[]{:T(128)} %constant.204.clone.1, s32[]{:T(128)} %constant.197.clone.1, s32[]{:T(128)} %constant.204.clone.1) | dynamic-update-slice | bytes 262148 | tf_op jit(solution)/shard_map/scatter-add | solution.py:138
  127.6 0.2 slice_add_fusion.2
  127.8 2.9 %scatter-add.39 = f32[256,2,128]{2,1,0:T(2,128)S(1)} dynamic-update-slice(f32[256,2,128]{2,1,0:T(2,128)S(1)} %scatter-add.36, f32[256,1,128]{2,1,0:T(1,128)S(1)} %slice_add_fusion.2, s32[]{:T(128)} %constant.204.clone.1, s32[]{:T(128)} %constant.204.clone.1, s32[]{:T(128)} %constant.204.clone.1) | dynamic-update-slice | bytes 262148 | tf_op jit(solution)/shard_map/scatter-add | solution.py:139
  130.7 0.7 convert_bitcast_fusion
  131.4 126.0 %all-reduce.9.cloned.1.call-done = (f32[3,256,256]{1,2,0:T(8,128)}, f32[3,256,256]{1,2,0:T(8,128)}) async-done(((f32[3,256,256]{1,2,0:T(8,128)}, f32[3,256,256]{1,2,0:T(8,128)}), (f32[3,256,256]{1,2,0:T(8,128)}, f32[3,256,256]{1,2,0:T(8,128)})) %all-reduce.9.cloned.1.call-update) | async-done | bytes 1572880 | tf_op jit(solution)/shard_map/psum | solution.py:148
  257.4 1.2 broadcast_multiply_fusion.1
  258.6 1.1 copy.68
  259.8 0.1 broadcast_multiply_fusion
  259.8 1.1 copy.69
  (50 shorter events, 0.7 us)
Async XLA Ops:
  7.2 31.8 %copy-start = (bf16[3,256,256]{2,1,0:T(8,128)(2,1)S(1)}, bf16[3,256,256]{2,1,0:T(8,128)(2,1)}, u32[]{:S(2)}) copy-start(bf16[3,256,256]{2,1,0:T(8,128)(2,1)} %param.24) | copy-start | bytes 1179652
  7.2 250.2 %all-reduce.9.cloned.1.call-start = ((), (), s32[]{:S(2)}) async-start(), calls=%async_computation | async-start | bytes 3145728 | tf_op jit(solution)/shard_map/psum | solution.py:148
  9.8 1.0 copy-start.1
  9.8 1.0 copy-start.3
  11.6 5.2 %copy-start.7 = (bf16[1,256,2,128]{3,2,1,0:T(2,128)(2,1)S(1)}, bf16[1,256,2,128]{3,2,1,0:T(2,128)(2,1)}, u32[]{:S(2)}) copy-start(bf16[1,256,2,128]{3,2,1,0:T(2,128)(2,1)} %param.23) | copy-start | bytes 393220
  11.7 19.3 %collective-permute-start.8 = (f32[256,4,4]{0,2,1:T(4,128)S(1)}, f32[256,4,4]{0,2,1:T(4,128)S(1)}, u32[]{:S(2)}, u32[]{:S(2)}) collective-permute-start(f32[256,4,4]{0,2,1:T(4,128)S(1)} %get-tuple-element.120), channel_id=1, source_target_pairs={{0,3},{1,0},{2,1},{3,2},{4,7},{5,4},{6,5},{7,6},{8,11},{9,8},{10,9... | collective-permute-start | bytes 49160 | tf_op jit(solution)/shard_map/ppermute | solution.py:29
  16.8 14.2 %collective-permute-start.9 = (f32[256,4,4]{0,2,1:T(4,128)S(1)}, f32[256,4,4]{0,2,1:T(4,128)S(1)}, u32[]{:S(2)}, u32[]{:S(2)}) collective-permute-start(f32[256,4,4]{0,2,1:T(4,128)S(1)} %get-tuple-element.119), channel_id=1, source_target_pairs={{0,1},{1,2},{2,3},{3,0},{4,5},{5,6},{6,7},{7,4},{8,9},{9,10},{10,1... | collective-permute-start | bytes 49160 | tf_op jit(solution)/shard_map/ppermute | solution.py:29
  16.9 5.2 %collective-permute-start.1 = (bf16[256,2,4]{0,2,1:T(4,128)(2,1)S(1)}, bf16[256,2,4]{0,2,1:T(4,128)(2,1)S(1)}, u32[]{:S(2)}, u32[]{:S(2)}) collective-permute-start(bf16[256,2,4]{0,2,1:T(4,128)(2,1)S(1)} %get-tuple-element.143), channel_id=1, source_target_pairs={{1,0},{2,1},{3,2},{0,3},{5,4},{6,5},{7,6},{4,7},{9,8},{10,9},{11,1... | collective-permute-start | bytes 12296 | tf_op jit(solution)/shard_map/ppermute | solution.py:22
  20.8 5.4 %collective-permute-start = (bf16[256,2,4]{0,2,1:T(4,128)(2,1)S(1)}, bf16[256,2,4]{0,2,1:T(4,128)(2,1)S(1)}, u32[]{:S(2)}, u32[]{:S(2)}) collective-permute-start(bf16[256,2,4]{0,2,1:T(4,128)(2,1)S(1)} %get-tuple-element.142), channel_id=1, source_target_pairs={{0,1},{1,2},{2,3},{3,0},{4,5},{5,6},{6,7},{7,4},{8,9},{9,10},{10,1... | collective-permute-start | bytes 12296 | tf_op jit(solution)/shard_map/ppermute | solution.py:19
  26.3 10.7 %collective-permute-start.2 = (bf16[256,1,136]{0,2,1:T(8,128)(2,1)S(1)}, bf16[256,1,136]{0,2,1:T(8,128)(2,1)S(1)}, u32[]{:S(2)}, u32[]{:S(2)}) collective-permute-start(bf16[256,1,136]{0,2,1:T(8,128)(2,1)S(1)} %get-tuple-element.138), channel_id=1, source_target_pairs={{0,4},{1,5},{2,6},{3,7},{8,12},{9,13},{10,14},{11,15},{16,20},{17,... | collective-permute-start | bytes 208904 | tf_op jit(solution)/shard_map/ppermute | solution.py:19
  29.7 7.3 %collective-permute-start.3 = (bf16[256,1,136]{0,2,1:T(8,128)(2,1)S(1)}, bf16[256,1,136]{0,2,1:T(8,128)(2,1)S(1)}, u32[]{:S(2)}, u32[]{:S(2)}) collective-permute-start(bf16[256,1,136]{0,2,1:T(8,128)(2,1)S(1)} %get-tuple-element.139), channel_id=1, source_target_pairs={{4,0},{5,1},{6,2},{7,3},{12,8},{13,9},{14,10},{15,11},{20,16},{21,... | collective-permute-start | bytes 208904 | tf_op jit(solution)/shard_map/ppermute | solution.py:22
  31.1 6.5 %collective-permute-start.10 = (bf16[256,1,128]{0,2,1:T(8,128)(2,1)S(1)}, bf16[256,1,128]{0,2,1:T(8,128)(2,1)S(1)}, u32[]{:S(2)}, u32[]{:S(2)}) collective-permute-start(bf16[256,1,128]{0,2,1:T(8,128)(2,1)S(1)} %get-tuple-element.129), channel_id=1, source_target_pairs={{4,0},{5,1},{6,2},{7,3},{12,8},{13,9},{14,10},{15,11},{20,16},{21,... | collective-permute-start | bytes 196616 | tf_op jit(solution)/shard_map/ppermute | solution.py:35
  32.4 6.4 %collective-permute-start.11 = (bf16[256,1,128]{0,2,1:T(8,128)(2,1)S(1)}, bf16[256,1,128]{0,2,1:T(8,128)(2,1)S(1)}, u32[]{:S(2)}, u32[]{:S(2)}) collective-permute-start(bf16[256,1,128]{0,2,1:T(8,128)(2,1)S(1)} %get-tuple-element.128), channel_id=1, source_target_pairs={{0,4},{1,5},{2,6},{3,7},{8,12},{9,13},{10,14},{11,15},{16,20},{17,... | collective-permute-start | bytes 196616 | tf_op jit(solution)/shard_map/ppermute | solution.py:35
  39.4 2.8 %copy-start.5 = (bf16[256,2,128]{0,2,1:T(8,128)(2,1)}, bf16[256,2,128]{0,2,1:T(8,128)(2,1)S(1)}, u32[]{:S(2)}) copy-start(bf16[256,2,128]{0,2,1:T(8,128)(2,1)S(1)} %get-tuple-element.126) | copy-start | bytes 393220
  39.4 10.7 %collective-permute-start.5 = (bf16[256,2,4]{0,2,1:T(4,128)(2,1)S(1)}, bf16[256,2,4]{0,2,1:T(4,128)(2,1)S(1)}, u32[]{:S(2)}, u32[]{:S(2)}) collective-permute-start(bf16[256,2,4]{0,2,1:T(4,128)(2,1)S(1)} %get-tuple-element.141), channel_id=1, source_target_pairs={{1,0},{2,1},{3,2},{0,3},{5,4},{6,5},{7,6},{4,7},{9,8},{10,9},{11,1... | collective-permute-start | bytes 12296 | tf_op jit(solution)/shard_map/ppermute | solution.py:22
  39.5 10.6 %collective-permute-start.4 = (bf16[256,2,4]{0,2,1:T(4,128)(2,1)S(1)}, bf16[256,2,4]{0,2,1:T(4,128)(2,1)S(1)}, u32[]{:S(2)}, u32[]{:S(2)}) collective-permute-start(bf16[256,2,4]{0,2,1:T(4,128)(2,1)S(1)} %get-tuple-element.140), channel_id=1, source_target_pairs={{0,1},{1,2},{2,3},{3,0},{4,5},{5,6},{6,7},{7,4},{8,9},{9,10},{10,1... | collective-permute-start | bytes 12296 | tf_op jit(solution)/shard_map/ppermute | solution.py:19
  45.4 1.2 copy-start.6
  48.0 14.2 %collective-permute-start.12 = (f32[256,4,4]{2,1,0:T(4,128)S(1)}, f32[256,4,4]{2,1,0:T(4,128)S(1)}, u32[]{:S(2)}, u32[]{:S(2)}) collective-permute-start(f32[256,4,4]{2,1,0:T(4,128)S(1)} %get-tuple-element.115), channel_id=1, source_target_pairs={{0,3},{1,0},{2,1},{3,2},{4,7},{5,4},{6,5},{7,6},{8,11},{9,8},{10,9... | collective-permute-start | bytes 49160 | tf_op jit(solution)/shard_map/ppermute | solution.py:29
  49.9 55.3 %collective-permute-start.13 = (f32[256,4,4]{2,1,0:T(4,128)}, f32[256,4,4]{2,1,0:T(4,128)S(1)}, u32[]{:S(2)}, u32[]{:S(2)}) collective-permute-start(f32[256,4,4]{2,1,0:T(4,128)} %get-tuple-element.114), channel_id=1, source_target_pairs={{0,1},{1,2},{2,3},{3,0},{4,5},{5,6},{6,7},{7,4},{8,9},{9,10},{10,1... | collective-permute-start | bytes 49160 | tf_op jit(solution)/shard_map/ppermute | solution.py:29
  50.2 70.1 %collective-permute-start.6 = (bf16[256,1,136]{0,2,1:T(8,128)(2,1)S(1)}, bf16[256,1,136]{0,2,1:T(8,128)(2,1)S(1)}, u32[]{:S(2)}, u32[]{:S(2)}) collective-permute-start(bf16[256,1,136]{0,2,1:T(8,128)(2,1)S(1)} %get-tuple-element.133), channel_id=1, source_target_pairs={{0,4},{1,5},{2,6},{3,7},{8,12},{9,13},{10,14},{11,15},{16,20},{17,... | collective-permute-start | bytes 208904 | tf_op jit(solution)/shard_map/ppermute | solution.py:19
  54.5 65.8 %collective-permute-start.7 = (bf16[256,1,136]{0,2,1:T(8,128)(2,1)S(1)}, bf16[256,1,136]{0,2,1:T(8,128)(2,1)}, u32[]{:S(2)}, u32[]{:S(2)}) collective-permute-start(bf16[256,1,136]{0,2,1:T(8,128)(2,1)S(1)} %get-tuple-element.134), channel_id=1, source_target_pairs={{4,0},{5,1},{6,2},{7,3},{12,8},{13,9},{14,10},{15,11},{20,16},{21,... | collective-permute-start | bytes 208904 | tf_op jit(solution)/shard_map/ppermute | solution.py:22
  114.2 10.3 %collective-permute-start.14 = (bf16[256,1,128]{2,1,0:T(2,128)(2,1)S(1)}, bf16[256,1,128]{2,1,0:T(2,128)(2,1)S(1)}, u32[]{:S(2)}, u32[]{:S(2)}) collective-permute-start(bf16[256,1,128]{2,1,0:T(2,128)(2,1)S(1)} %get-tuple-element.125), channel_id=1, source_target_pairs={{4,0},{5,1},{6,2},{7,3},{12,8},{13,9},{14,10},{15,11},{20,16},{21,... | collective-permute-start | bytes 196616 | tf_op jit(solution)/shard_map/ppermute | solution.py:35
  115.5 12.1 %collective-permute-start.15 = (bf16[256,1,128]{2,1,0:T(2,128)(2,1)S(1)}, bf16[256,1,128]{2,1,0:T(2,128)(2,1)S(1)}, u32[]{:S(2)}, u32[]{:S(2)}) collective-permute-start(bf16[256,1,128]{2,1,0:T(2,128)(2,1)S(1)} %get-tuple-element.124), channel_id=1, source_target_pairs={{0,4},{1,5},{2,6},{3,7},{8,12},{9,13},{10,14},{11,15},{16,20},{17,... | collective-permute-start | bytes 196616 | tf_op jit(solution)/shard_map/ppermute | solution.py:35
  121.2 0.9 copy-start.4
  258.6 1.2 copy-start.2
Sparse Core Ops, SparseCore 0:
  123.5 133.8 all-reduce.8
where the time goes:
time: 268 us
  waiting for transfers between devices  139 us (52%)
  local copies, waits for them, and re-layouts  66.4 us (25%)
  starting transfers between devices  35.3 us (13%)
  between operations  14.6 us (5%)
  matrix products  6.81 us (3%)
  other arithmetic  5.61 us (2%)
    psum x1, waiting for transfers between devices, body(): lax.psum((first_sum, second_sum), ('ens', 'lat', 'lon'))  126 us
    scatter-add x1, local copies, waits for them, and re-layouts, carry_back(): core_block.at[:, :, col_count - LON_REACH:].add(lon_pass(left_rim, -1))  42.8 us
    ppermute x4, starting transfers between devices, passed_along_2(): lax.ppermute(value, axis, [(source, source + steps) for source in range(l...  11.9 us
    ppermute x4, starting transfers between devices, with_halo(): lax.ppermute(lax.slice_in_dim(block, block.shape[dim] - width, None, axis...  9.71 us
    scatter-add x1, local copies, waits for them, and re-layouts, carry_back(): core_block = core_block.at[:, :, :LON_REACH].add(lon_pass(right_rim, 1))  8.38 us
    ppermute x4, starting transfers between devices, passed_along(): lax.ppermute(value, axis, [(i, (i + by) % devices) for i in range(devices)])  7.21 us
    ppermute x4, starting transfers between devices, with_halo(): lax.ppermute(lax.slice_in_dim(block, 0, width, axis=dim), axis, backward)  6.52 us
    ppermute x4, waiting for transfers between devices, passed_along(): lax.ppermute(value, axis, [(i, (i + by) % devices) for i in range(devices)])  6.51 us
  transfers between devices with their start and end apart: 17, of which 5 were waited for; matrix products, arithmetic and copies ran while one was open for 26% of the time, Pallas kernels for 0%

commit v1 on v0

--- a/solution.py
+++ b/solution.py
@@ -35,6 +35,31 @@
     return lax.ppermute(value, axis, [(source, source + steps) for source in range(leading, last)])
 
 
+def halving_sum(value, axes):
+    stages = []
+    for axis in axes:
+        bit = 1
+        while bit < lax.axis_size(axis):
+            stages.append((axis, bit))
+            bit *= 2
+    flat = value.reshape(-1)
+    for axis, bit in stages:
+        pairs = [(i, i ^ bit) for i in range(lax.axis_size(axis))]
+        upper = (lax.axis_index(axis) // bit) % 2
+        half = flat.shape[0] // 2
+        keep = lax.dynamic_slice_in_dim(flat, upper * half, half)
+        send = lax.dynamic_slice_in_dim(flat, (1 - upper) * half, half)
+        flat = keep + lax.ppermute(send, axis, pairs)
+    for axis, bit in reversed(stages):
+        pairs = [(i, i ^ bit) for i in range(lax.axis_size(axis))]
+        upper = (lax.axis_index(axis) // bit) % 2
+        other = lax.ppermute(flat, axis, pairs)
+        flat = jnp.where(
+            upper == 1, jnp.concatenate([other, flat]), jnp.concatenate([flat, other])
+        )
+    return flat.reshape(value.shape)
+
+
 def coefficients(quadrature, lat_offsets, lon_offsets):
     lat_levels = jnp.arange(2 * LAT_REACH + 1, dtype=jnp.int32)
     lon_levels = jnp.arange(2 * LON_REACH + 1, dtype=jnp.int32)
@@ -130,13 +155,19 @@
         left_rim = extended[:, :, :LON_REACH]
         right_rim = extended[:, :, LON_REACH + col_count :]
         core_block = extended[:, :, LON_REACH : LON_REACH + col_count]
-        core_block = core_block.at[:, :, col_count - LON_REACH :].add(lon_pass(left_rim, -1))
-        core_block = core_block.at[:, :, :LON_REACH].add(lon_pass(right_rim, 1))
+        core_block = (
+            core_block
+            + jnp.pad(lon_pass(left_rim, -1), ((0, 0), (0, 0), (col_count - LON_REACH, 0)))
+            + jnp.pad(lon_pass(right_rim, 1), ((0, 0), (0, 0), (0, col_count - LON_REACH)))
+        )
         top_rows = core_block[:, :LAT_REACH]
         bottom_rows = core_block[:, LAT_REACH + row_count :]
         inner_rows = core_block[:, LAT_REACH : LAT_REACH + row_count]
-        inner_rows = inner_rows.at[:, row_count - LAT_REACH :].add(lat_pass(top_rows, -1))
-        inner_rows = inner_rows.at[:, :LAT_REACH].add(lat_pass(bottom_rows, 1))
+        inner_rows = (
+            inner_rows
+            + jnp.pad(lat_pass(top_rows, -1), ((0, 0), (row_count - LAT_REACH, 0), (0, 0)))
+            + jnp.pad(lat_pass(bottom_rows, 1), ((0, 0), (0, row_count - LAT_REACH), (0, 0)))
+        )
         return inner_rows.astype(jnp.bfloat16)
 
     activation_grad = carry_back(second_weight, gradient)
@@ -145,7 +176,9 @@
     )
     first_sum = filter_term(hidden_grad, first_spread)
     state_grad = carry_back(first_weight, hidden_grad)
-    first_sum, second_sum = lax.psum((first_sum, second_sum), ("ens", "lat", "lon"))
+    first_sum, second_sum = jnp.split(
+        halving_sum(jnp.concatenate([first_sum, second_sum]), ("ens", "lat", "lon")), 2
+    )
     member_total = state_field.shape[0] * lax.axis_size("ens")
     grad_scale = 1.0 / math.sqrt(
         member_total * row_count * lax.axis_size("lat") * col_count * lax.axis_size("lon")

time: 268 us -> 140 us (0.52)
  waiting for transfers between devices: 139 us -> 78.9 us
  local copies, waits for them, and re-layouts: 66.4 us -> 10.7 us
  between operations: 14.6 us -> 1.26 us
  other arithmetic: 5.61 us -> 9.46 us
    psum x1 -> x0, waiting for transfers between devices: 126 us -> none  [body(): lax.psum((first_sum, second_sum), ('ens', 'lat', 'lon'))]
    scatter-add x4 -> x0, local copies, waits for them, and re-layouts: 56.9 us -> none  [the longest x1 42.8 us: carry_back(): core_block.at[:, :, col_count - LON_REACH:].add(lon_pass(left_rim, -1))]
    ppermute x0 -> x10, waiting for transfers between devices: none -> 44.1 us  [the longest x5 28.9 us: halving_sum(): flat = keep + lax.ppermute(send, axis, pairs)]
    ppermute x4, waiting for transfers between devices: 1.26 us -> 8.72 us  [passed_along_2(): lax.ppermute(value, axis, [(source, source + steps) for source in range(l...]
    ppermute x4, waiting for transfers between devices: 6.51 us -> 12.7 us  [passed_along(): lax.ppermute(value, axis, [(i, (i + by) % devices) for i in range(devices)])]
    ppermute x4, waiting for transfers between devices: 1.23 us -> 7.39 us  [with_halo(): lax.ppermute(lax.slice_in_dim(block, 0, width, axis=dim), axis, backward)]
    ppermute x0 -> x10, starting transfers between devices: none -> 3.9 us  [the longest x5 1.97 us: halving_sum(): other = lax.ppermute(flat, axis, pairs)]
    concatenate x0 -> x2, local copies, waits for them, and re-layouts: none -> 3.02 us  [the longest x1 1.65 us: body(): jnp.concatenate([first_sum, second_sum])]
  transfers between devices with their start and end apart: 17 -> 26, of which waited for: 5 -> 20; matrix products, arithmetic and copies ran while one was open for 26% -> 5% of each run, Pallas kernels for 0% -> 0%
where the time goes in v1:
time: 140 us; the launch traced here: 139 us
  waiting for transfers between devices  78.9 us (56%)
  starting transfers between devices  34 us (24%)
  local copies, waits for them, and re-layouts  10.7 us (8%)
  other arithmetic  9.46 us (7%)
  matrix products  5.08 us (4%)
    ppermute x5, waiting for transfers between devices, halving_sum(): flat = keep + lax.ppermute(send, axis, pairs)  28.9 us
    ppermute x5, waiting for transfers between devices, halving_sum(): other = lax.ppermute(flat, axis, pairs)  15.2 us
    ppermute x4, waiting for transfers between devices, passed_along(): lax.ppermute(value, axis, [(i, (i + by) % devices) for i in range(devices)])  12.7 us
    ppermute x4, starting transfers between devices, passed_along_2(): lax.ppermute(value, axis, [(source, source + steps) for source in range(l...  9.33 us
    ppermute x4, starting transfers between devices, passed_along(): lax.ppermute(value, axis, [(i, (i + by) % devices) for i in range(devices)])  9.07 us
    ppermute x4, waiting for transfers between devices, passed_along_2(): lax.ppermute(value, axis, [(source, source + steps) for source in range(l...  8.72 us
    ppermute x4, waiting for transfers between devices, with_halo(): lax.ppermute(lax.slice_in_dim(block, 0, width, axis=dim), axis, backward)  7.39 us
    ppermute x4, starting transfers between devices, with_halo(): lax.ppermute(lax.slice_in_dim(block, block.shape[dim] - width, None, axis...  7.08 us
  transfers between devices with their start and end apart: 26, of which 20 were waited for; matrix products, arithmetic and copies ran while one was open for 5% of the time, Pallas kernels for 0%

profile of v1, /device:TPU:0, one launch (start us, length us, event | category | flops | bytes accessed | tf_op | source)
XLA Modules:
  0.0 139.4 jit_solution(16114874764465652594)
XLA Ops:
  0.6 0.8 broadcast_add_fusion
  1.4 0.9 fusion.5
  2.3 0.6 fusion
  2.9 0.4 copy.47
  3.3 0.6 reshape.58
  3.9 0.3 convolution_convert_fusion.2
  4.2 0.4 fusion.55
  4.7 3.1 %collective-permute-start.9 = (f32[256,4,4]{0,2,1:T(4,128)S(1)}, f32[256,4,4]{0,2,1:T(4,128)S(1)}, u32[]{:S(2)}, u32[]{:S(2)}) collective-permute-start(f32[256,4,4]{0,2,1:T(4,128)S(1)} %get-tuple-element.28), channel_id=1, source_target_pairs={{0,1},{1,2},{2,3},{3,0},{4,5},{5,6},{6,7},{7,4},{8,9},{9,10},{10,1... | collective-permute-start | bytes 49160 | tf_op jit(solution)/shard_map/ppermute | solution.py:29
  7.8 2.1 %collective-permute-start.8 = (f32[256,4,4]{0,2,1:T(4,128)S(1)}, f32[256,4,4]{0,2,1:T(4,128)S(1)}, u32[]{:S(2)}, u32[]{:S(2)}) collective-permute-start(f32[256,4,4]{0,2,1:T(4,128)S(1)} %get-tuple-element.27), channel_id=1, source_target_pairs={{0,3},{1,0},{2,1},{3,2},{4,7},{5,4},{6,5},{7,6},{8,11},{9,8},{10,9... | collective-permute-start | bytes 49160 | tf_op jit(solution)/shard_map/ppermute | solution.py:29
  10.1 2.0 %collective-permute-start.1 = (bf16[256,2,4]{0,2,1:T(4,128)(2,1)S(1)}, bf16[256,2,4]{0,2,1:T(4,128)(2,1)S(1)}, u32[]{:S(2)}, u32[]{:S(2)}) collective-permute-start(bf16[256,2,4]{0,2,1:T(4,128)(2,1)S(1)} %get-tuple-element.51), channel_id=1, source_target_pairs={{1,0},{2,1},{3,2},{0,3},{5,4},{6,5},{7,6},{4,7},{9,8},{10,9},{11,1... | collective-permute-start | bytes 12296 | tf_op jit(solution)/shard_map/ppermute | solution.py:22
  12.2 1.5 %collective-permute-done.1 = bf16[256,2,4]{0,2,1:T(4,128)(2,1)S(1)} collective-permute-done((bf16[256,2,4]{0,2,1:T(4,128)(2,1)S(1)}, bf16[256,2,4]{0,2,1:T(4,128)(2,1)S(1)}, u32[]{:S(2)}, u32[]{:S(2)}) %collective-permute-start.1) | collective-permute-done | bytes 4128 | tf_op jit(solution)/shard_map/ppermute | solution.py:22
  13.7 3.8 %collective-permute-done = bf16[256,2,4]{0,2,1:T(4,128)(2,1)S(1)} collective-permute-done((bf16[256,2,4]{0,2,1:T(4,128)(2,1)S(1)}, bf16[256,2,4]{0,2,1:T(4,128)(2,1)S(1)}, u32[]{:S(2)}, u32[]{:S(2)}) %collective-permute-start) | collective-permute-done | bytes 4128 | tf_op jit(solution)/shard_map/ppermute | solution.py:19
  17.6 3.4 %collective-permute-start.2 = (bf16[256,1,136]{0,2,1:T(8,128)(2,1)S(1)}, bf16[256,1,136]{0,2,1:T(8,128)(2,1)S(1)}, u32[]{:S(2)}, u32[]{:S(2)}) collective-permute-start(bf16[256,1,136]{0,2,1:T(8,128)(2,1)S(1)} %get-tuple-element.46), channel_id=1, source_target_pairs={{0,4},{1,5},{2,6},{3,7},{8,12},{9,13},{10,14},{11,15},{16,20},{17,... | collective-permute-start | bytes 208904 | tf_op jit(solution)/shard_map/ppermute | solution.py:19
  21.0 1.3 collective-permute-start.3
  22.4 4.5 %collective-permute-start.11 = (bf16[256,1,128]{0,2,1:T(8,128)(2,1)S(1)}, bf16[256,1,128]{0,2,1:T(8,128)(2,1)S(1)}, u32[]{:S(2)}, u32[]{:S(2)}) collective-permute-start(bf16[256,1,128]{0,2,1:T(8,128)(2,1)S(1)} %get-tuple-element.37), channel_id=1, source_target_pairs={{0,4},{1,5},{2,6},{3,7},{8,12},{9,13},{10,14},{11,15},{16,20},{17,... | collective-permute-start | bytes 196616 | tf_op jit(solution)/shard_map/ppermute | solution.py:35
  27.0 1.3 collective-permute-start.10
  28.4 0.4 convolution_convert_fusion.4
  28.9 4.2 %collective-permute-done.10 = bf16[256,1,128]{0,2,1:T(8,128)(2,1)S(1)} collective-permute-done((bf16[256,1,128]{0,2,1:T(8,128)(2,1)S(1)}, bf16[256,1,128]{0,2,1:T(8,128)(2,1)S(1)}, u32[]{:S(2)}, u32[]{:S(2)}) %collective-permute-start.10) | collective-permute-done | bytes 65568 | tf_op jit(solution)/shard_map/ppermute | solution.py:35
  33.1 0.5 fusion.14
  33.7 2.0 %collective-permute-start.4 = (bf16[256,2,4]{0,2,1:T(4,128)(2,1)S(1)}, bf16[256,2,4]{0,2,1:T(4,128)(2,1)S(1)}, u32[]{:S(2)}, u32[]{:S(2)}) collective-permute-start(bf16[256,2,4]{0,2,1:T(4,128)(2,1)S(1)} %get-tuple-element.48), channel_id=1, source_target_pairs={{0,1},{1,2},{2,3},{3,0},{4,5},{5,6},{6,7},{7,4},{8,9},{9,10},{10,1... | collective-permute-start | bytes 12296 | tf_op jit(solution)/shard_map/ppermute | solution.py:19
  35.7 1.6 %collective-permute-done.5 = bf16[256,2,4]{0,2,1:T(4,128)(2,1)S(1)} collective-permute-done((bf16[256,2,4]{0,2,1:T(4,128)(2,1)S(1)}, bf16[256,2,4]{0,2,1:T(4,128)(2,1)S(1)}, u32[]{:S(2)}, u32[]{:S(2)}) %collective-permute-start.5) | collective-permute-done | bytes 4128 | tf_op jit(solution)/shard_map/ppermute | solution.py:22
  37.3 1.9 %collective-permute-done.4 = bf16[256,2,4]{0,2,1:T(4,128)(2,1)S(1)} collective-permute-done((bf16[256,2,4]{0,2,1:T(4,128)(2,1)S(1)}, bf16[256,2,4]{0,2,1:T(4,128)(2,1)S(1)}, u32[]{:S(2)}, u32[]{:S(2)}) %collective-permute-start.4) | collective-permute-done | bytes 4128 | tf_op jit(solution)/shard_map/ppermute | solution.py:19
  39.2 1.6 %collective-permute-start.6 = (bf16[256,1,136]{0,2,1:T(8,128)(2,1)S(1)}, bf16[256,1,136]{0,2,1:T(8,128)(2,1)S(1)}, u32[]{:S(2)}, u32[]{:S(2)}) collective-permute-start(bf16[256,1,136]{0,2,1:T(8,128)(2,1)S(1)} %get-tuple-element.41), channel_id=1, source_target_pairs={{0,4},{1,5},{2,6},{3,7},{8,12},{9,13},{10,14},{11,15},{16,20},{17,... | collective-permute-start | bytes 208904 | tf_op jit(solution)/shard_map/ppermute | solution.py:19
  40.8 1.3 collective-permute-start.7
  42.1 0.3 convolution_bitcast_fusion.1
  42.4 0.3 collective-permute-done.6
  42.7 4.3 %collective-permute-done.7 = bf16[256,1,136]{0,2,1:T(8,128)(2,1)S(1)} collective-permute-done((bf16[256,1,136]{0,2,1:T(8,128)(2,1)S(1)}, bf16[256,1,136]{0,2,1:T(8,128)(2,1)S(1)}, u32[]{:S(2)}, u32[]{:S(2)}) %collective-permute-start.7) | collective-permute-done | bytes 69664 | tf_op jit(solution)/shard_map/ppermute | solution.py:22
  47.2 0.4 convolution_convert_fusion.3
  47.6 0.3 convolution_bitcast_fusion
  48.0 1.7 %copy.64 = f32[6,256,256]{2,1,0:T(8,128)} copy(f32[6,256,256]{1,2,0:T(8,128)S(1)} %pad_maximum_fusion) | data formatting | bytes 3145728 | tf_op jit(solution)/shard_map/concatenate | solution.py:180
  49.7 2.2 %copy.89 = f32[192,2,8,128]{3,1,2,0:T(2,128)S(1)} copy(f32[192,2,8,128]{3,2,1,0:T(8,128)} %bitcast.126) | data formatting | bytes 3145728
  51.9 0.9 dynamic_slice.31
  52.8 2.6 %collective-permute-done.16 = f32[196608]{0:T(1024)} collective-permute-done((f32[196608]{0:T(1024)}, f32[196608]{0:T(1024)}, u32[]{:S(2)}, u32[]{:S(2)}) %collective-permute-start.16) | collective-permute-done | bytes 786464 | tf_op jit(solution)/shard_map/ppermute | solution.py:52
  55.4 1.2 dynamic-slice_add_fusion
  56.7 0.9 copy-done.1
  57.6 1.6 %collective-permute-start.17 = (f32[98304]{0:T(1024)S(1)}, f32[98304]{0:T(1024)S(1)}, u32[]{:S(2)}, u32[]{:S(2)}) collective-permute-start(f32[98304]{0:T(1024)S(1)} %dynamic_slice.33), channel_id=1, source_target_pairs={{0,16},{8,24},{16,0},{24,8},{1,17},{9,25},{17,1},{25,9},{2,18},{10... | collective-permute-start | bytes 1179656 | tf_op jit(solution)/shard_map/ppermute | solution.py:52
  59.1 9.7 %collective-permute-done.17 = f32[98304]{0:T(1024)S(1)} collective-permute-done((f32[98304]{0:T(1024)S(1)}, f32[98304]{0:T(1024)S(1)}, u32[]{:S(2)}, u32[]{:S(2)}) %collective-permute-start.17) | collective-permute-done | bytes 393248 | tf_op jit(solution)/shard_map/ppermute | solution.py:52
  68.8 1.1 dynamic-slice_add_fusion.1
  70.0 6.0 %collective-permute-done.18 = f32[49152]{0:T(1024)S(1)} collective-permute-done((f32[49152]{0:T(1024)S(1)}, f32[49152]{0:T(1024)S(1)}, u32[]{:S(2)}, u32[]{:S(2)}) %collective-permute-start.18) | collective-permute-done | bytes 196640 | tf_op jit(solution)/shard_map/ppermute | solution.py:52
  76.3 4.5 %collective-permute-done.19 = f32[24576]{0:T(1024)S(1)} collective-permute-done((f32[24576]{0:T(1024)S(1)}, f32[24576]{0:T(1024)S(1)}, u32[]{:S(2)}, u32[]{:S(2)}) %collective-permute-start.19) | collective-permute-done | bytes 98336 | tf_op jit(solution)/shard_map/ppermute | solution.py:52
  80.9 6.1 %collective-permute-done.20 = f32[12288]{0:T(1024)S(1)} collective-permute-done((f32[12288]{0:T(1024)S(1)}, f32[12288]{0:T(1024)S(1)}, u32[]{:S(2)}, u32[]{:S(2)}) %collective-permute-start.20) | collective-permute-done | bytes 49184 | tf_op jit(solution)/shard_map/ppermute | solution.py:52
  87.1 0.3 convolution_convert_fusion.1
  87.4 4.7 %collective-permute-done.21 = f32[12288]{0:T(1024)S(1)} collective-permute-done((f32[12288]{0:T(1024)S(1)}, f32[12288]{0:T(1024)S(1)}, u32[]{:S(2)}, u32[]{:S(2)}) %collective-permute-start.21) | collective-permute-done | bytes 49184 | tf_op jit(solution)/shard_map/ppermute | solution.py:56
  92.2 0.4 fusion.56
  92.6 4.2 %collective-permute-done.22 = f32[24576]{0:T(1024)S(1)} collective-permute-done((f32[24576]{0:T(1024)S(1)}, f32[24576]{0:T(1024)S(1)}, u32[]{:S(2)}, u32[]{:S(2)}) %collective-permute-start.22) | collective-permute-done | bytes 98336 | tf_op jit(solution)/shard_map/ppermute | solution.py:56
  96.8 0.7 maximum_select_fusion.3
  98.5 5.0 %collective-permute-done.23 = f32[49152]{0:T(1024)} collective-permute-done((f32[49152]{0:T(1024)}, f32[49152]{0:T(1024)}, u32[]{:S(2)}, u32[]{:S(2)}) %collective-permute-start.23) | collective-permute-done | bytes 196640 | tf_op jit(solution)/shard_map/ppermute | solution.py:56
  103.5 1.3 maximum_select_fusion.2
  104.7 1.6 %collective-permute-start.24 = (f32[98304]{0:T(1024)S(1)}, f32[98304]{0:T(1024)S(1)}, u32[]{:S(2)}, u32[]{:S(2)}) collective-permute-start(f32[98304]{0:T(1024)S(1)} %maximum_select_fusion.2), channel_id=1, source_target_pairs={{0,16},{8,24},{16,0},{24,8},{1,17},{9,25},{17,1},{25,9},{2,18},{10... | collective-permute-start | bytes 1179656 | tf_op jit(solution)/shard_map/ppermute | solution.py:56
  106.3 0.7 pad_add_fusion
  107.0 0.3 fusion.47
  107.4 3.8 %collective-permute-start.12 = (f32[256,4,4]{2,1,0:T(4,128)S(1)}, f32[256,4,4]{2,1,0:T(4,128)S(1)}, u32[]{:S(2)}, u32[]{:S(2)}) collective-permute-start(f32[256,4,4]{2,1,0:T(4,128)S(1)} %get-tuple-element.22), channel_id=1, source_target_pairs={{0,3},{1,0},{2,1},{3,2},{4,7},{5,4},{6,5},{7,6},{8,11},{9,8},{10,9... | collective-permute-start | bytes 49160 | tf_op jit(solution)/shard_map/ppermute | solution.py:29
  111.3 1.3 collective-permute-done.24
  112.7 8.8 %collective-permute-done.13 = f32[256,4,4]{2,1,0:T(4,128)S(1)} collective-permute-done((f32[256,4,4]{2,1,0:T(4,128)S(1)}, f32[256,4,4]{2,1,0:T(4,128)S(1)}, u32[]{:S(2)}, u32[]{:S(2)}) %collective-permute-start.13) | collective-permute-done | bytes 16416 | tf_op jit(solution)/shard_map/ppermute | solution.py:29
  121.5 4.0 %collective-permute-done.12 = f32[256,4,4]{2,1,0:T(4,128)S(1)} collective-permute-done((f32[256,4,4]{2,1,0:T(4,128)S(1)}, f32[256,4,4]{2,1,0:T(4,128)S(1)}, u32[]{:S(2)}, u32[]{:S(2)}) %collective-permute-start.12) | collective-permute-done | bytes 16416 | tf_op jit(solution)/shard_map/ppermute | solution.py:29
  125.5 0.6 fusion.43
  126.3 2.2 %collective-permute-start.15 = (bf16[256,1,128]{2,1,0:T(2,128)(2,1)S(1)}, bf16[256,1,128]{2,1,0:T(2,128)(2,1)S(1)}, u32[]{:S(2)}, u32[]{:S(2)}) collective-permute-start(bf16[256,1,128]{2,1,0:T(2,128)(2,1)S(1)} %get-tuple-element.33), channel_id=1, source_target_pairs={{0,4},{1,5},{2,6},{3,7},{8,12},{9,13},{10,14},{11,15},{16,20},{17,... | collective-permute-start | bytes 196616 | tf_op jit(solution)/shard_map/ppermute | solution.py:35
  128.5 1.3 collective-permute-start.14
  129.8 0.3 fusion.2
  130.1 0.8 copy.65
  131.0 4.4 %collective-permute-done.14 = bf16[256,1,128]{2,1,0:T(2,128)(2,1)S(1)} collective-permute-done((bf16[256,1,128]{2,1,0:T(2,128)(2,1)S(1)}, bf16[256,1,128]{2,1,0:T(2,128)(2,1)S(1)}, u32[]{:S(2)}, u32[]{:S(2)}) %collective-permute-start.14) | collective-permute-done | bytes 65568 | tf_op jit(solution)/shard_map/ppermute | solution.py:35
  135.3 1.0 fusion.32
  136.6 1.4 concatenate.74
  138.1 1.3 slice_multiply_fusion
  (62 shorter events, 3.5 us)
Async XLA Ops:
  0.6 32.5 %copy-start = (bf16[3,256,256]{2,1,0:T(8,128)(2,1)S(1)}, bf16[3,256,256]{2,1,0:T(8,128)(2,1)}, u32[]{:S(2)}) copy-start(bf16[3,256,256]{2,1,0:T(8,128)(2,1)} %param.8) | copy-start | bytes 1179652
  2.9 1.0 copy-start.2
  2.9 1.0 copy-start.3
  4.6 5.3 %copy-start.4 = (bf16[1,256,2,128]{3,2,1,0:T(2,128)(2,1)S(1)}, bf16[1,256,2,128]{3,2,1,0:T(2,128)(2,1)}, u32[]{:S(2)}) copy-start(bf16[1,256,2,128]{3,2,1,0:T(2,128)(2,1)} %param.7) | copy-start | bytes 393220
  4.7 17.6 %collective-permute-start.9 = (f32[256,4,4]{0,2,1:T(4,128)S(1)}, f32[256,4,4]{0,2,1:T(4,128)S(1)}, u32[]{:S(2)}, u32[]{:S(2)}) collective-permute-start(f32[256,4,4]{0,2,1:T(4,128)S(1)} %get-tuple-element.28), channel_id=1, source_target_pairs={{0,1},{1,2},{2,3},{3,0},{4,5},{5,6},{6,7},{7,4},{8,9},{9,10},{10,1... | collective-permute-start | bytes 49160 | tf_op jit(solution)/shard_map/ppermute | solution.py:29
  7.8 14.5 %collective-permute-start.8 = (f32[256,4,4]{0,2,1:T(4,128)S(1)}, f32[256,4,4]{0,2,1:T(4,128)S(1)}, u32[]{:S(2)}, u32[]{:S(2)}) collective-permute-start(f32[256,4,4]{0,2,1:T(4,128)S(1)} %get-tuple-element.27), channel_id=1, source_target_pairs={{0,3},{1,0},{2,1},{3,2},{4,7},{5,4},{6,5},{7,6},{8,11},{9,8},{10,9... | collective-permute-start | bytes 49160 | tf_op jit(solution)/shard_map/ppermute | solution.py:29
  10.1 3.7 %collective-permute-start.1 = (bf16[256,2,4]{0,2,1:T(4,128)(2,1)S(1)}, bf16[256,2,4]{0,2,1:T(4,128)(2,1)S(1)}, u32[]{:S(2)}, u32[]{:S(2)}) collective-permute-start(bf16[256,2,4]{0,2,1:T(4,128)(2,1)S(1)} %get-tuple-element.51), channel_id=1, source_target_pairs={{1,0},{2,1},{3,2},{0,3},{5,4},{6,5},{7,6},{4,7},{9,8},{10,9},{11,1... | collective-permute-start | bytes 12296 | tf_op jit(solution)/shard_map/ppermute | solution.py:22
  12.1 5.4 %collective-permute-start = (bf16[256,2,4]{0,2,1:T(4,128)(2,1)S(1)}, bf16[256,2,4]{0,2,1:T(4,128)(2,1)S(1)}, u32[]{:S(2)}, u32[]{:S(2)}) collective-permute-start(bf16[256,2,4]{0,2,1:T(4,128)(2,1)S(1)} %get-tuple-element.50), channel_id=1, source_target_pairs={{0,1},{1,2},{2,3},{3,0},{4,5},{5,6},{6,7},{7,4},{8,9},{9,10},{10,1... | collective-permute-start | bytes 12296 | tf_op jit(solution)/shard_map/ppermute | solution.py:19
  17.6 10.7 %collective-permute-start.2 = (bf16[256,1,136]{0,2,1:T(8,128)(2,1)S(1)}, bf16[256,1,136]{0,2,1:T(8,128)(2,1)S(1)}, u32[]{:S(2)}, u32[]{:S(2)}) collective-permute-start(bf16[256,1,136]{0,2,1:T(8,128)(2,1)S(1)} %get-tuple-element.46), channel_id=1, source_target_pairs={{0,4},{1,5},{2,6},{3,7},{8,12},{9,13},{10,14},{11,15},{16,20},{17,... | collective-permute-start | bytes 208904 | tf_op jit(solution)/shard_map/ppermute | solution.py:19
  21.0 7.3 %collective-permute-start.3 = (bf16[256,1,136]{0,2,1:T(8,128)(2,1)S(1)}, bf16[256,1,136]{0,2,1:T(8,128)(2,1)S(1)}, u32[]{:S(2)}, u32[]{:S(2)}) collective-permute-start(bf16[256,1,136]{0,2,1:T(8,128)(2,1)S(1)} %get-tuple-element.47), channel_id=1, source_target_pairs={{4,0},{5,1},{6,2},{7,3},{12,8},{13,9},{14,10},{15,11},{20,16},{21,... | collective-permute-start | bytes 208904 | tf_op jit(solution)/shard_map/ppermute | solution.py:22
  22.4 6.5 %collective-permute-start.11 = (bf16[256,1,128]{0,2,1:T(8,128)(2,1)S(1)}, bf16[256,1,128]{0,2,1:T(8,128)(2,1)S(1)}, u32[]{:S(2)}, u32[]{:S(2)}) collective-permute-start(bf16[256,1,128]{0,2,1:T(8,128)(2,1)S(1)} %get-tuple-element.37), channel_id=1, source_target_pairs={{0,4},{1,5},{2,6},{3,7},{8,12},{9,13},{10,14},{11,15},{16,20},{17,... | collective-permute-start | bytes 196616 | tf_op jit(solution)/shard_map/ppermute | solution.py:35
  27.0 6.2 %collective-permute-start.10 = (bf16[256,1,128]{0,2,1:T(8,128)(2,1)S(1)}, bf16[256,1,128]{0,2,1:T(8,128)(2,1)S(1)}, u32[]{:S(2)}, u32[]{:S(2)}) collective-permute-start(bf16[256,1,128]{0,2,1:T(8,128)(2,1)S(1)} %get-tuple-element.36), channel_id=1, source_target_pairs={{4,0},{5,1},{6,2},{7,3},{12,8},{13,9},{14,10},{15,11},{20,16},{21,... | collective-permute-start | bytes 196616 | tf_op jit(solution)/shard_map/ppermute | solution.py:35
  33.6 3.7 %collective-permute-start.5 = (bf16[256,2,4]{0,2,1:T(4,128)(2,1)S(1)}, bf16[256,2,4]{0,2,1:T(4,128)(2,1)S(1)}, u32[]{:S(2)}, u32[]{:S(2)}) collective-permute-start(bf16[256,2,4]{0,2,1:T(4,128)(2,1)S(1)} %get-tuple-element.49), channel_id=1, source_target_pairs={{1,0},{2,1},{3,2},{0,3},{5,4},{6,5},{7,6},{4,7},{9,8},{10,9},{11,1... | collective-permute-start | bytes 12296 | tf_op jit(solution)/shard_map/ppermute | solution.py:22
  33.7 5.5 %collective-permute-start.4 = (bf16[256,2,4]{0,2,1:T(4,128)(2,1)S(1)}, bf16[256,2,4]{0,2,1:T(4,128)(2,1)S(1)}, u32[]{:S(2)}, u32[]{:S(2)}) collective-permute-start(bf16[256,2,4]{0,2,1:T(4,128)(2,1)S(1)} %get-tuple-element.48), channel_id=1, source_target_pairs={{0,1},{1,2},{2,3},{3,0},{4,5},{5,6},{6,7},{7,4},{8,9},{9,10},{10,1... | collective-permute-start | bytes 12296 | tf_op jit(solution)/shard_map/ppermute | solution.py:19
  39.2 3.5 %collective-permute-start.6 = (bf16[256,1,136]{0,2,1:T(8,128)(2,1)S(1)}, bf16[256,1,136]{0,2,1:T(8,128)(2,1)S(1)}, u32[]{:S(2)}, u32[]{:S(2)}) collective-permute-start(bf16[256,1,136]{0,2,1:T(8,128)(2,1)S(1)} %get-tuple-element.41), channel_id=1, source_target_pairs={{0,4},{1,5},{2,6},{3,7},{8,12},{9,13},{10,14},{11,15},{16,20},{17,... | collective-permute-start | bytes 208904 | tf_op jit(solution)/shard_map/ppermute | solution.py:19
  40.8 6.2 %collective-permute-start.7 = (bf16[256,1,136]{0,2,1:T(8,128)(2,1)S(1)}, bf16[256,1,136]{0,2,1:T(8,128)(2,1)S(1)}, u32[]{:S(2)}, u32[]{:S(2)}) collective-permute-start(bf16[256,1,136]{0,2,1:T(8,128)(2,1)S(1)} %get-tuple-element.42), channel_id=1, source_target_pairs={{4,0},{5,1},{6,2},{7,3},{12,8},{13,9},{14,10},{15,11},{20,16},{21,... | collective-permute-start | bytes 208904 | tf_op jit(solution)/shard_map/ppermute | solution.py:22
  52.8 2.6 %collective-permute-start.16 = (f32[196608]{0:T(1024)}, f32[196608]{0:T(1024)}, u32[]{:S(2)}, u32[]{:S(2)}) collective-permute-start(f32[196608]{0:T(1024)} %dynamic_slice.31), channel_id=1, source_target_pairs={{0,8},{8,0},{16,24},{24,16},{1,9},{9,1},{17,25},{25,17},{2,10},{10... | collective-permute-start | bytes 2359304 | tf_op jit(solution)/shard_map/ppermute | solution.py:52
  56.7 0.9 copy-start.1
  57.6 11.2 %collective-permute-start.17 = (f32[98304]{0:T(1024)S(1)}, f32[98304]{0:T(1024)S(1)}, u32[]{:S(2)}, u32[]{:S(2)}) collective-permute-start(f32[98304]{0:T(1024)S(1)} %dynamic_slice.33), channel_id=1, source_target_pairs={{0,16},{8,24},{16,0},{24,8},{1,17},{9,25},{17,1},{25,9},{2,18},{10... | collective-permute-start | bytes 1179656 | tf_op jit(solution)/shard_map/ppermute | solution.py:52
  69.9 6.2 %collective-permute-start.18 = (f32[49152]{0:T(1024)S(1)}, f32[49152]{0:T(1024)S(1)}, u32[]{:S(2)}, u32[]{:S(2)}) collective-permute-start(f32[49152]{0:T(1024)S(1)} %dynamic_slice.35), channel_id=1, source_target_pairs={{0,4},{4,0},{1,5},{5,1},{2,6},{6,2},{3,7},{7,3},{8,12},{12,8},{9,1... | collective-permute-start | bytes 589832 | tf_op jit(solution)/shard_map/ppermute | solution.py:52
  76.1 4.7 %collective-permute-start.19 = (f32[24576]{0:T(1024)S(1)}, f32[24576]{0:T(1024)S(1)}, u32[]{:S(2)}, u32[]{:S(2)}) collective-permute-start(f32[24576]{0:T(1024)S(1)} %dynamic_slice.37), channel_id=1, source_target_pairs={{0,1},{1,0},{2,3},{3,2},{4,5},{5,4},{6,7},{7,6},{8,9},{9,8},{10,11... | collective-permute-start | bytes 294920 | tf_op jit(solution)/shard_map/ppermute | solution.py:52
  80.8 6.2 %collective-permute-start.20 = (f32[12288]{0:T(1024)S(1)}, f32[12288]{0:T(1024)S(1)}, u32[]{:S(2)}, u32[]{:S(2)}) collective-permute-start(f32[12288]{0:T(1024)S(1)} %dynamic_slice.39), channel_id=1, source_target_pairs={{0,2},{1,3},{2,0},{3,1},{4,6},{5,7},{6,4},{7,5},{8,10},{9,11},{10,... | collective-permute-start | bytes 147464 | tf_op jit(solution)/shard_map/ppermute | solution.py:52
  87.0 5.1 %collective-permute-start.21 = (f32[12288]{0:T(1024)S(1)}, f32[12288]{0:T(1024)S(1)}, u32[]{:S(2)}, u32[]{:S(2)}) collective-permute-start(f32[12288]{0:T(1024)S(1)} %dynamic-slice_add_fusion.4), channel_id=1, source_target_pairs={{0,2},{1,3},{2,0},{3,1},{4,6},{5,7},{6,4},{7,5},{8,10},{9,11},{10,... | collective-permute-start | bytes 147464 | tf_op jit(solution)/shard_map/ppermute | solution.py:56
  92.1 4.7 %collective-permute-start.22 = (f32[24576]{0:T(1024)S(1)}, f32[24576]{0:T(1024)S(1)}, u32[]{:S(2)}, u32[]{:S(2)}) collective-permute-start(f32[24576]{0:T(1024)S(1)} %maximum_select_fusion.4), channel_id=1, source_target_pairs={{0,1},{1,0},{2,3},{3,2},{4,5},{5,4},{6,7},{7,6},{8,9},{9,8},{10,11... | collective-permute-start | bytes 294920 | tf_op jit(solution)/shard_map/ppermute | solution.py:56
  97.5 6.0 %collective-permute-start.23 = (f32[49152]{0:T(1024)}, f32[49152]{0:T(1024)}, u32[]{:S(2)}, u32[]{:S(2)}) collective-permute-start(f32[49152]{0:T(1024)} %maximum_select_fusion.3), channel_id=1, source_target_pairs={{0,4},{4,0},{1,5},{5,1},{2,6},{6,2},{3,7},{7,3},{8,12},{12,8},{9,1... | collective-permute-start | bytes 589832 | tf_op jit(solution)/shard_map/ppermute | solution.py:56
  104.7 7.8 %collective-permute-start.24 = (f32[98304]{0:T(1024)S(1)}, f32[98304]{0:T(1024)S(1)}, u32[]{:S(2)}, u32[]{:S(2)}) collective-permute-start(f32[98304]{0:T(1024)S(1)} %maximum_select_fusion.2), channel_id=1, source_target_pairs={{0,16},{8,24},{16,0},{24,8},{1,17},{9,25},{17,1},{25,9},{2,18},{10... | collective-permute-start | bytes 1179656 | tf_op jit(solution)/shard_map/ppermute | solution.py:56
  107.4 14.1 %collective-permute-start.13 = (f32[256,4,4]{2,1,0:T(4,128)S(1)}, f32[256,4,4]{2,1,0:T(4,128)S(1)}, u32[]{:S(2)}, u32[]{:S(2)}) collective-permute-start(f32[256,4,4]{2,1,0:T(4,128)S(1)} %get-tuple-element.23), channel_id=1, source_target_pairs={{0,1},{1,2},{2,3},{3,0},{4,5},{5,6},{6,7},{7,4},{8,9},{9,10},{10,1... | collective-permute-start | bytes 49160 | tf_op jit(solution)/shard_map/ppermute | solution.py:29
  107.4 18.0 %collective-permute-start.12 = (f32[256,4,4]{2,1,0:T(4,128)S(1)}, f32[256,4,4]{2,1,0:T(4,128)S(1)}, u32[]{:S(2)}, u32[]{:S(2)}) collective-permute-start(f32[256,4,4]{2,1,0:T(4,128)S(1)} %get-tuple-element.22), channel_id=1, source_target_pairs={{0,3},{1,0},{2,1},{3,2},{4,7},{5,4},{6,5},{7,6},{8,11},{9,8},{10,9... | collective-permute-start | bytes 49160 | tf_op jit(solution)/shard_map/ppermute | solution.py:29
  112.6 24.0 %collective-permute-start.25 = (f32[196608]{0:T(1024)S(1)}, f32[196608]{0:T(1024)}, u32[]{:S(2)}, u32[]{:S(2)}) collective-permute-start(f32[196608]{0:T(1024)S(1)} %maximum_select_fusion.1), channel_id=1, source_target_pairs={{0,8},{8,0},{16,24},{24,16},{1,9},{9,1},{17,25},{25,17},{2,10},{10... | collective-permute-start | bytes 2359304 | tf_op jit(solution)/shard_map/ppermute | solution.py:56
  126.3 4.7 %collective-permute-start.15 = (bf16[256,1,128]{2,1,0:T(2,128)(2,1)S(1)}, bf16[256,1,128]{2,1,0:T(2,128)(2,1)S(1)}, u32[]{:S(2)}, u32[]{:S(2)}) collective-permute-start(bf16[256,1,128]{2,1,0:T(2,128)(2,1)S(1)} %get-tuple-element.33), channel_id=1, source_target_pairs={{0,4},{1,5},{2,6},{3,7},{8,12},{9,13},{10,14},{11,15},{16,20},{17,... | collective-permute-start | bytes 196616 | tf_op jit(solution)/shard_map/ppermute | solution.py:35
  128.5 6.9 %collective-permute-start.14 = (bf16[256,1,128]{2,1,0:T(2,128)(2,1)S(1)}, bf16[256,1,128]{2,1,0:T(2,128)(2,1)S(1)}, u32[]{:S(2)}, u32[]{:S(2)}) collective-permute-start(bf16[256,1,128]{2,1,0:T(2,128)(2,1)S(1)} %get-tuple-element.32), channel_id=1, source_target_pairs={{4,0},{5,1},{6,2},{7,3},{12,8},{13,9},{14,10},{15,11},{20,16},{21,... | collective-permute-start | bytes 196616 | tf_op jit(solution)/shard_map/ppermute | solution.py:35

commit v2 on v1

v2 whole, which is shorter than its diff:
```python
import math

import jax
import jax.numpy as jnp
from jax import lax
from jax.sharding import PartitionSpec as P

LAT_REACH = 1
LON_REACH = 4
LAT_HALO = 2 * LAT_REACH
LON_HALO = 2 * LON_REACH


def halving_sum(value, axes):
    stages = []
    for axis in axes:
        bit = 1
        while bit < lax.axis_size(axis):
            stages.append((axis, bit))
            bit *= 2
    flat = value.reshape(-1)
    for axis, bit in stages:
        pairs = [(i, i ^ bit) for i in range(lax.axis_size(axis))]
        upper = (lax.axis_index(axis) // bit) % 2
        half = flat.shape[0] // 2
        keep = lax.dynamic_slice_in_dim(flat, upper * half, half)
        send = lax.dynamic_slice_in_dim(flat, (1 - upper) * half, half)
        flat = keep + lax.ppermute(send, axis, pairs)
    for axis, bit in reversed(stages):
        pairs = [(i, i ^ bit) for i in range(lax.axis_size(axis))]
        upper = (lax.axis_index(axis) // bit) % 2
        other = lax.ppermute(flat, axis, pairs)
        flat = jnp.where(
            upper == 1, jnp.concatenate([other, flat]), jnp.concatenate([flat, other])
        )
    return flat.reshape(value.shape)


def lat_halo(block, dim, width):
    count = lax.axis_size("lat")
    rows = block.shape[dim]
    above = lax.ppermute(
        lax.slice_in_dim(block, rows - width, rows, axis=dim),
        "lat",
        [(i, i + 1) for i in range(count - 1)],
    )
    below = lax.ppermute(
        lax.slice_in_dim(block, 0, width, axis=dim), "lat", [(i + 1, i) for i in range(count - 1)]
    )
    return jnp.concatenate([above, block, below], axis=dim)


def lon_halo(block, width):
    count = lax.axis_size("lon")
    cols = block.shape[-1]
    left = lax.ppermute(block[..., cols - width :], "lon", [(i, (i + 1) % count) for i in range(count)])
    right = lax.ppermute(block[..., :width], "lon", [(i, (i - 1) % count) for i in range(count)])
    return jnp.concatenate([left, block, right], axis=-1)


def coefficients(quadrature, lat_offsets, lon_offsets):
    lat_levels = jnp.arange(2 * LAT_REACH + 1, dtype=jnp.int32)
    lon_levels = jnp.arange(2 * LON_REACH + 1, dtype=jnp.int32)
    lat_onehot = (lat_offsets[..., None] + LAT_REACH == lat_levels).astype(jnp.float32)
    lon_onehot = (lon_offsets[..., None] + LON_REACH == lon_levels).astype(jnp.float32)
    stencil = jnp.einsum(
        "rks,rksa,rksd->krad", quadrature, lat_onehot, lon_onehot, precision=lax.Precision.HIGHEST
    )
    return stencil.astype(jnp.bfloat16)


def lon_picker(col_count):
    span_count = 2 * LON_REACH + 1
    wide_count = col_count + 2 * LON_REACH
    table_shape = (span_count, wide_count, col_count)
    offset_level = lax.broadcasted_iota(jnp.int32, table_shape, 0)
    source = lax.broadcasted_iota(jnp.int32, table_shape, 1)
    target = lax.broadcasted_iota(jnp.int32, table_shape, 2)
    matches = source - target == offset_level
    return matches.astype(jnp.bfloat16)


def band_of(stencil, col_count):
    row_count = stencil.shape[1]
    basis_count = stencil.shape[0]
    lat_taps = 2 * LAT_REACH + 1
    band = jnp.einsum(
        "kiad,dpq->iapkq", stencil, lon_picker(col_count), preferred_element_type=jnp.float32
    )
    return band.astype(jnp.bfloat16).reshape(
        row_count, lat_taps * (col_count + 2 * LON_REACH), basis_count * col_count
    )


def spread(values, band, basis_count):
    channels = values.shape[0]
    row_count = values.shape[1] - 2 * LAT_REACH
    col_count = values.shape[2] - 2 * LON_REACH
    lat_taps = 2 * LAT_REACH + 1
    stacked = jnp.stack(
        [values[:, offset : offset + row_count] for offset in range(lat_taps)], axis=2
    )
    stacked = stacked.reshape(channels, row_count, lat_taps * values.shape[2])
    mixed = jnp.einsum("cin,inm->cim", stacked, band, preferred_element_type=jnp.float32)
    return mixed.reshape(channels, row_count, basis_count, col_count)


def spread_adjoint(mixed, band):
    channels, row_count, basis_count, col_count = mixed.shape
    lat_taps = 2 * LAT_REACH + 1
    partial = jnp.einsum(
        "cim,inm->cin",
        mixed.reshape(channels, row_count, basis_count * col_count),
        band,
        preferred_element_type=jnp.float32,
    )
    partial = partial.reshape(channels, row_count, lat_taps, col_count + 2 * LON_REACH)
    partial = partial[:, :, :, LON_HALO : col_count]
    out_rows = row_count - LAT_HALO
    total = partial[:, LAT_HALO : LAT_HALO + out_rows, 0]
    for offset in range(1, lat_taps):
        start = LAT_HALO - offset
        total = total + partial[:, start : start + out_rows, offset]
    return total


def mix_channels(weight, spreaded):
    return jnp.einsum("koc,cikj->oij", weight, spreaded, preferred_element_type=jnp.float32)


def unmix(weight, grad_rows):
    return jnp.einsum(
        "koc,oij->cikj", weight, grad_rows, preferred_element_type=jnp.float32
    ).astype(jnp.bfloat16)


def filter_term(gradient, spreaded):
    return jnp.einsum("oij,cikj->koc", gradient, spreaded, preferred_element_type=jnp.float32)


def body(state_field, first_weight, second_weight, quadrature, lat_offsets, lon_offsets, cotangent):
    source = state_field[0]
    gradient = cotangent[0]
    channels, row_count, col_count = source.shape
    stencil = coefficients(quadrature, lat_offsets, lon_offsets)
    basis_count = stencil.shape[0]

    packed = jnp.concatenate([source, gradient], axis=0)
    framed = lat_halo(lon_halo(packed, LON_HALO), 1, LAT_HALO)
    source_wide, gradient_wide = framed[:channels], framed[channels:]
    stencil_wide = lat_halo(stencil, 1, LAT_HALO)

    total_rows = row_count * lax.axis_size("lat")
    first_row = lax.axis_index("lat") * row_count
    near_rows = first_row - LAT_REACH + jnp.arange(row_count + 2 * LAT_REACH)
    near_valid = ((near_rows >= 0) & (near_rows < total_rows))[None, :, None]

    near_band = band_of(stencil_wide[:, LAT_REACH : LAT_REACH + row_count + 2 * LAT_REACH], col_count + LON_HALO)
    own_band = band_of(stencil, col_count)
    wide_band = band_of(stencil_wide, col_count + 2 * LON_HALO)

    first_near = spread(source_wide, near_band, basis_count).astype(jnp.bfloat16)
    hidden = mix_channels(first_weight, first_near)
    activation = jnp.where(near_valid, jax.nn.gelu(hidden), 0.0).astype(jnp.bfloat16)
    second_spread = spread(activation, own_band, basis_count).astype(jnp.bfloat16)
    layer_output = mix_channels(second_weight, second_spread).astype(jnp.bfloat16)
    own_gradient = gradient_wide[:, LAT_HALO : LAT_HALO + row_count, LON_HALO : LON_HALO + col_count]
    second_sum = filter_term(own_gradient, second_spread)

    second_mixed = unmix(second_weight, gradient_wide)
    activation_grad = spread_adjoint(second_mixed, wide_band).astype(jnp.bfloat16)
    hidden_grad = jax.vjp(jax.nn.gelu, hidden)[1](activation_grad.astype(jnp.float32))[0]
    hidden_grad = jnp.where(near_valid, hidden_grad, 0.0).astype(jnp.bfloat16)
    own_hidden_grad = hidden_grad[:, LAT_REACH : LAT_REACH + row_count, LON_REACH : LON_REACH + col_count]
    own_first = first_near[:, LAT_REACH : LAT_REACH + row_count, :, LON_REACH : LON_REACH + col_count]
    first_sum = filter_term(own_hidden_grad, own_first)
    first_mixed = unmix(first_weight, hidden_grad)
    state_grad = spread_adjoint(first_mixed, near_band).astype(jnp.bfloat16)

    first_sum, second_sum = jnp.split(
        halving_sum(jnp.concatenate([first_sum, second_sum]), ("ens", "lat", "lon")), 2
    )
    member_total = state_field.shape[0] * lax.axis_size("ens")
    grad_scale = 1.0 / math.sqrt(
        member_total * row_count * lax.axis_size("lat") * col_count * lax.axis_size("lon")
    )
    return (layer_output[None], state_grad[None], first_sum * grad_scale, second_sum * grad_scale)


def solution(mesh):
    in_specs = (
        P("ens", None, "lat", "lon"),
        P(),
        P(),
        P("lat", None, None),
        P("lat", None, None),
        P("lat", None, None),
        P("ens", None, "lat", "lon"),
    )
    out_specs = (P("ens", None, "lat", "lon"), P("ens", None, "lat", "lon"), P(), P())
    return jax.shard_map(body, mesh=mesh, in_specs=in_specs, out_specs=out_specs, check_vma=False)
```

time: 140 us -> 128 us (0.914)
  waiting for transfers between devices: 78.9 us -> 51.8 us
  local copies, waits for them, and re-layouts: 10.7 us -> 34.8 us
  starting transfers between devices: 34 us -> 21.9 us
  matrix products: 5.08 us -> 11.1 us
  other arithmetic: 9.46 us -> 6.61 us
    ppermute x16 -> x6, waiting for transfers between devices: 34.8 us -> 3.22 us  [the longest x1 3.21 us: lon_halo(): lax.ppermute(block[..., cols - width:], 'lon', [(i, (i + 1) % count) for...]
    reshape x1 -> x3, local copies, waits for them, and re-layouts: 0.58 us -> 17.8 us  [band_of(): band.astype(jnp.bfloat16)]
    ppermute x16 -> x6, starting transfers between devices: 30.1 us -> 18.2 us  [the longest x2 10.9 us: lat_halo(): lax.ppermute(lax.slice_in_dim(block, rows - width, rows, axis=dim), 'lat'...]
    convert_element_type x1 -> x3, local copies, waits for them, and re-layouts: 0.36 us -> 8.42 us  [band_of(): band.astype(jnp.bfloat16)]
    dot_general x7 -> x9, matrix products: 2.8 us -> 8.52 us  [the longest x3 3.67 us: band_of(): jnp.einsum('kiad,dpq->iapkq', stencil, lon_picker(col_count), preferred_e...]
    ppermute x5, waiting for transfers between devices: 15.2 us -> 20.1 us  [halving_sum(): other = lax.ppermute(flat, axis, pairs)]
    add x5, other arithmetic: 2.35 us -> 0.17 us  [halving_sum(): flat = keep + lax.ppermute(send, axis, pairs)]
    unnamed x16 -> x31, local copies, waits for them, and re-layouts: 4.75 us -> 6.24 us
  transfers between devices with their start and end apart: 26 -> 16, of which waited for: 20 -> 10; matrix products, arithmetic and copies ran while one was open for 5% -> 28% of each run, Pallas kernels for 0% -> 0%
where the time goes in v2:
time: 128 us
  waiting for transfers between devices  51.8 us (40%)
  local copies, waits for them, and re-layouts  34.8 us (27%)
  starting transfers between devices  21.9 us (17%)
  matrix products  11.1 us (9%)
  other arithmetic  6.61 us (5%)
  between operations  1.37 us (1%)
    ppermute x5, waiting for transfers between devices, halving_sum(): flat = keep + lax.ppermute(send, axis, pairs)  28.4 us
    ppermute x5, waiting for transfers between devices, halving_sum(): other = lax.ppermute(flat, axis, pairs)  20.1 us
    reshape x3, local copies, waits for them, and re-layouts, band_of(): band.astype(jnp.bfloat16)  17.8 us
    ppermute x2, starting transfers between devices, lat_halo(): lax.ppermute(lax.slice_in_dim(block, rows - width, rows, axis=dim), 'lat'...  10.9 us
    convert_element_type x3, local copies, waits for them, and re-layouts, band_of(): band.astype(jnp.bfloat16)  8.42 us
    unnamed x31, local copies, waits for them, and re-layouts  6.24 us
    ppermute x1, starting transfers between devices, lon_halo(): lax.ppermute(block[..., :width], 'lon', [(i, (i - 1) % count) for i in ra...  4.77 us
    dot_general x3, matrix products, band_of(): jnp.einsum('kiad,dpq->iapkq', stencil, lon_picker(col_count), preferred_e...  3.67 us
  transfers between devices with their start and end apart: 16, of which 10 were waited for; matrix products, arithmetic and copies ran while one was open for 28% of the time, Pallas kernels for 0%

profile of v2, /device:TPU:0, one launch (start us, length us, event | category | flops | bytes accessed | tf_op | source)
XLA Modules:
  0.0 127.6 jit_solution(15661245246103855769)
XLA Ops:
  0.6 0.8 broadcast_add_fusion
  1.4 0.9 convolution_convert_fusion.5
  2.3 1.3 %collective-permute-start.1 = (bf16[3,2,3,9]{3,2,1,0:T(4,128)(2,1)S(1)}, bf16[3,2,3,9]{3,2,1,0:T(4,128)(2,1)S(1)}, u32[]{:S(2)}, u32[]{:S(2)}) collective-permute-start(bf16[3,2,3,9]{3,2,1,0:T(4,128)(2,1)S(1)} %convolution_convert_fusion.5), channel_id=1, source_target_pairs={{4,0},{5,1},{6,2},{7,3},{12,8},{13,9},{14,10},{15,11},{20,16},{21,... | collective-permute-start | bytes 980 | tf_op jit(solution)/shard_map/ppermute | solution.py:47
  3.6 4.9 %collective-permute-start = (bf16[3,2,3,9]{3,2,1,0:T(4,128)(2,1)S(1)}, bf16[3,2,3,9]{3,2,1,0:T(4,128)(2,1)S(1)}, u32[]{:S(2)}, u32[]{:S(2)}) collective-permute-start(bf16[3,2,3,9]{3,2,1,0:T(4,128)(2,1)S(1)} %convolution_convert_fusion.5), channel_id=1, source_target_pairs={{0,4},{1,5},{2,6},{3,7},{8,12},{9,13},{10,14},{11,15},{16,20},{17,... | collective-permute-start | bytes 980 | tf_op jit(solution)/shard_map/ppermute | solution.py:42
  8.5 1.0 copy.28
  9.5 1.0 copy.27
  10.6 4.8 %collective-permute-start.3 = (bf16[512,2,8]{0,2,1:T(8,128)(2,1)S(1)}, bf16[512,2,8]{0,2,1:T(8,128)(2,1)S(1)}, u32[]{:S(2)}, u32[]{:S(2)}) collective-permute-start(bf16[512,2,8]{0,2,1:T(8,128)(2,1)S(1)} %get-tuple-element.26), channel_id=1, source_target_pairs={{0,3},{1,0},{2,1},{3,2},{4,7},{5,4},{6,5},{7,6},{8,11},{9,8},{10,9... | collective-permute-start | bytes 49160 | tf_op jit(solution)/shard_map/ppermute | solution.py:57
  15.3 0.6 fusion.7
  15.9 0.4 copy.24
  16.3 1.3 %reshape.109 = bf16[2,408,384]{2,1,0:T(8,128)(2,1)} reshape(bf16[2,3,136,3,128]{4,3,2,1,0:T(4,128)(2,1)S(1)} %copy.24) | data formatting | bytes 1253376 | tf_op jit(solution)/shard_map/reshape | solution.py:90
  17.7 3.2 %collective-permute-done.2 = bf16[512,2,8]{0,2,1:T(8,128)(2,1)S(1)} collective-permute-done((bf16[512,2,8]{0,2,1:T(8,128)(2,1)S(1)}, bf16[512,2,8]{0,2,1:T(8,128)(2,1)S(1)}, u32[]{:S(2)}, u32[]{:S(2)}) %collective-permute-start.2) | collective-permute-done | bytes 16416 | tf_op jit(solution)/shard_map/ppermute | solution.py:56
  20.9 0.7 pad_maximum_fusion.20
  21.6 1.3 %collective-permute-start.5 = (bf16[512,2,144]{0,2,1:T(8,128)(2,1)}, bf16[512,2,144]{0,2,1:T(8,128)(2,1)}, u32[]{:S(2)}, u32[]{:S(2)}) collective-permute-start(bf16[512,2,144]{0,2,1:T(8,128)(2,1)} %pad_maximum_fusion.20), channel_id=1, source_target_pairs={{4,0},{5,1},{6,2},{7,3},{12,8},{13,9},{14,10},{15,11},{20,16},{21,... | collective-permute-start | bytes 884744 | tf_op jit(solution)/shard_map/ppermute | solution.py:47
  22.9 6.0 %collective-permute-start.4 = (bf16[512,2,144]{0,2,1:T(8,128)(2,1)}, bf16[512,2,144]{0,2,1:T(8,128)(2,1)}, u32[]{:S(2)}, u32[]{:S(2)}) collective-permute-start(bf16[512,2,144]{0,2,1:T(8,128)(2,1)} %pad_maximum_fusion.20), channel_id=1, source_target_pairs={{0,4},{1,5},{2,6},{3,7},{8,12},{9,13},{10,14},{11,15},{16,20},{17,... | collective-permute-start | bytes 884744 | tf_op jit(solution)/shard_map/ppermute | solution.py:42
  28.9 1.6 %convert_bitcast_fusion = bf16[6,3,152,3,144]{2,0,1,3,4:T(8,128)(2,1)S(1)} fusion(bf16[3,6,3,9]{3,2,1,0:T(4,128)(2,1)S(1)} %pad_maximum_fusion.21), kind=kOutput, calls=%fused_computation | convolution fusion | flops 22851072 | bytes 2364876 | tf_op jit(solution)/shard_map/kiad,dpq->iapkq/dot_general | solution.py:87
  30.5 4.9 %copy.32 = bf16[6,3,152,3,144]{2,1,4,3,0:T(4,128)(2,1)} copy(bf16[6,3,152,3,144]{2,0,1,3,4:T(8,128)(2,1)S(1)} %convert_bitcast_fusion) | data formatting | bytes 4727808 | tf_op jit(solution)/shard_map/convert_element_type | solution.py:90
  35.4 9.4 %reshape.113 = bf16[6,456,432]{1,2,0:T(8,128)(2,1)S(1)} reshape(bf16[6,3,152,3,144]{2,1,4,3,0:T(4,128)(2,1)} %copy.32) | data formatting | bytes 4727808 | tf_op jit(solution)/shard_map/reshape | solution.py:90
  44.9 1.5 %convert_bitcast_fusion.1 = bf16[4,3,144,3,136]{2,0,1,3,4:T(4,128)(2,1)S(1)} fusion(bf16[3,4,3,9]{3,2,1,0:T(4,128)(2,1)S(1)} %slice-done), kind=kOutput, calls=%fused_computation.1 | convolution fusion | flops 13747968 | bytes 1410696 | tf_op jit(solution)/shard_map/kiad,dpq->iapkq/dot_general | solution.py:87
  46.4 3.1 %copy.26 = bf16[4,3,144,3,136]{2,1,4,3,0:T(4,128)(2,1)} copy(bf16[4,3,144,3,136]{2,0,1,3,4:T(4,128)(2,1)S(1)} %convert_bitcast_fusion.1) | data formatting | bytes 2820096 | tf_op jit(solution)/shard_map/convert_element_type | solution.py:90
  49.5 7.0 %reshape.110 = bf16[4,432,408]{1,2,0:T(8,128)(2,1)} reshape(bf16[4,3,144,3,136]{2,1,4,3,0:T(4,128)(2,1)} %copy.26) | data formatting | bytes 2820096 | tf_op jit(solution)/shard_map/reshape | solution.py:90
  56.6 1.1 fusion.35
  57.7 0.1 pad_maximum_fusion.1
  57.9 1.5 %convolution_convert_fusion = bf16[6,144,3,256]{3,1,2,0:T(8,128)(2,1)S(1)} fusion(bf16[512,2,144]{0,2,1:T(8,128)(2,1)} %collective-permute-done.5, bf16[512,2,144]{0,2,1:T(8,128)(2,1)} %collective-permute-done.4, bf16[512,2,8]{0,2,1:T(8,128)(2,1)S(1)} %collective-permute-done.3, bf16[512,2,8]{0,2,1:T(8,128)(2,1)S(1)} %collective-permute-done.2, ...), kind=kOutput, calls=%fused_computation.7 | convolution fusion | flops 343056384 | bytes 2605056 | tf_op jit(solution)/shard_map/koc,oij->cikj/dot_general | solution.py:132
  59.4 1.1 fusion.54
  60.5 0.3 copy-done.1
  60.8 0.6 convolution_convert_fusion.3
  61.4 0.4 copy-done.7
  61.8 0.8 fusion.15
  62.8 1.0 copy-done.5
  63.8 0.4 convolution_convert_fusion.4
  64.2 0.3 convolution_bitcast_fusion.1
  64.6 0.4 copy-done.3
  65.0 0.3 convolution_bitcast_fusion
  65.3 0.1 pad_maximum_fusion
  65.4 0.5 copy.43
  65.9 0.8 copy.65
  66.9 2.2 %collective-permute-done.6 = f32[196608]{0:T(1024)S(1)} collective-permute-done((f32[196608]{0:T(1024)S(1)}, f32[196608]{0:T(1024)S(1)}, u32[]{:S(2)}, u32[]{:S(2)}) %collective-permute-start.6) | collective-permute-done | bytes 786464 | tf_op jit(solution)/shard_map/ppermute | solution.py:28
  69.1 0.1 dynamic-slice_add_fusion
  69.3 1.6 %collective-permute-start.7 = (f32[98304]{0:T(1024)S(1)}, f32[98304]{0:T(1024)S(1)}, u32[]{:S(2)}, u32[]{:S(2)}) collective-permute-start(f32[98304]{0:T(1024)S(1)} %dynamic_slice.33), channel_id=1, source_target_pairs={{0,16},{8,24},{16,0},{24,8},{1,17},{9,25},{17,1},{25,9},{2,18},{10... | collective-permute-start | bytes 1179656 | tf_op jit(solution)/shard_map/ppermute | solution.py:28
  70.8 9.7 %collective-permute-done.7 = f32[98304]{0:T(1024)S(1)} collective-permute-done((f32[98304]{0:T(1024)S(1)}, f32[98304]{0:T(1024)S(1)}, u32[]{:S(2)}, u32[]{:S(2)}) %collective-permute-start.7) | collective-permute-done | bytes 393248 | tf_op jit(solution)/shard_map/ppermute | solution.py:28
  80.6 0.1 collective-permute-start.8
  80.7 6.0 %collective-permute-done.8 = f32[49152]{0:T(1024)S(1)} collective-permute-done((f32[49152]{0:T(1024)S(1)}, f32[49152]{0:T(1024)S(1)}, u32[]{:S(2)}, u32[]{:S(2)}) %collective-permute-start.8) | collective-permute-done | bytes 196640 | tf_op jit(solution)/shard_map/ppermute | solution.py:28
  86.9 4.6 %collective-permute-done.9 = f32[24576]{0:T(1024)S(1)} collective-permute-done((f32[24576]{0:T(1024)S(1)}, f32[24576]{0:T(1024)S(1)}, u32[]{:S(2)}, u32[]{:S(2)}) %collective-permute-start.9) | collective-permute-done | bytes 98336 | tf_op jit(solution)/shard_map/ppermute | solution.py:28
  91.6 5.9 %collective-permute-done.10 = f32[12288]{0:T(1024)S(1)} collective-permute-done((f32[12288]{0:T(1024)S(1)}, f32[12288]{0:T(1024)S(1)}, u32[]{:S(2)}, u32[]{:S(2)}) %collective-permute-start.10) | collective-permute-done | bytes 49184 | tf_op jit(solution)/shard_map/ppermute | solution.py:28
  97.6 5.0 %collective-permute-done.11 = f32[12288]{0:T(1024)S(1)} collective-permute-done((f32[12288]{0:T(1024)S(1)}, f32[12288]{0:T(1024)S(1)}, u32[]{:S(2)}, u32[]{:S(2)}) %collective-permute-start.11) | collective-permute-done | bytes 49184 | tf_op jit(solution)/shard_map/ppermute | solution.py:32
  102.7 4.6 %collective-permute-done.12 = f32[24576]{0:T(1024)S(1)} collective-permute-done((f32[24576]{0:T(1024)S(1)}, f32[24576]{0:T(1024)S(1)}, u32[]{:S(2)}, u32[]{:S(2)}) %collective-permute-start.12) | collective-permute-done | bytes 98336 | tf_op jit(solution)/shard_map/ppermute | solution.py:32
  107.3 0.1 collective-permute-start.13
  107.4 5.6 %collective-permute-done.13 = f32[49152]{0:T(1024)S(1)} collective-permute-done((f32[49152]{0:T(1024)S(1)}, f32[49152]{0:T(1024)S(1)}, u32[]{:S(2)}, u32[]{:S(2)}) %collective-permute-start.13) | collective-permute-done | bytes 196640 | tf_op jit(solution)/shard_map/ppermute | solution.py:32
  113.1 1.6 %collective-permute-start.14 = (f32[98304]{0:T(1024)S(1)}, f32[98304]{0:T(1024)}, u32[]{:S(2)}, u32[]{:S(2)}) collective-permute-start(f32[98304]{0:T(1024)S(1)} %maximum_select_fusion.2), channel_id=1, source_target_pairs={{0,16},{8,24},{16,0},{24,8},{1,17},{9,25},{17,1},{25,9},{2,18},{10... | collective-permute-start | bytes 1179656 | tf_op jit(solution)/shard_map/ppermute | solution.py:32
  114.7 0.3 fusion.9
  115.0 0.8 copy.44
  115.8 0.4 convolution_convert_fusion.2
  116.2 4.9 %collective-permute-done.14 = f32[98304]{0:T(1024)} collective-permute-done((f32[98304]{0:T(1024)S(1)}, f32[98304]{0:T(1024)}, u32[]{:S(2)}, u32[]{:S(2)}) %collective-permute-start.14) | collective-permute-done | bytes 393248 | tf_op jit(solution)/shard_map/ppermute | solution.py:32
  121.0 1.2 maximum_select_fusion.1
  122.2 0.1 collective-permute-start.15
  122.3 0.8 fusion.55
  123.2 0.1 copy.63
  123.4 0.1 copy.61
  123.5 0.1 copy.62
  123.7 0.8 fusion.38
  124.5 0.2 select_n.159
  124.8 1.4 %concatenate.72 = f32[3,256,256]{2,1,0:T(8,128)S(1)} reshape(f32[196608]{0:T(1024)} %collective-permute-done.15) | data formatting | bytes 1572864 | tf_op jit(solution)/shard_map/concatenate | solution.py:34
  126.1 0.2 maximum_select_fusion
  126.3 1.3 %slice_multiply_fusion = (f32[3,256,256]{2,1,0:T(8,128)}, f32[3,256,256]{2,1,0:T(8,128)}) fusion(f32[6,256,256]{2,1,0:T(8,128)S(1)} %maximum_select_fusion), kind=kLoop, calls=%fused_computation.27 | loop fusion | flops 393216 | bytes 3145728 | tf_op jit(solution)/shard_map/mul | solution.py:187
  (54 shorter events, 1.0 us)
Async XLA Ops:
  0.6 57.2 %copy-start = (bf16[3,256,256]{2,1,0:T(8,128)(2,1)S(1)}, bf16[3,256,256]{2,1,0:T(8,128)(2,1)}, u32[]{:S(2)}) copy-start(bf16[3,256,256]{2,1,0:T(8,128)(2,1)} %param.9) | copy-start | bytes 1179652
  2.3 15.3 %collective-permute-start.1 = (bf16[3,2,3,9]{3,2,1,0:T(4,128)(2,1)S(1)}, bf16[3,2,3,9]{3,2,1,0:T(4,128)(2,1)S(1)}, u32[]{:S(2)}, u32[]{:S(2)}) collective-permute-start(bf16[3,2,3,9]{3,2,1,0:T(4,128)(2,1)S(1)} %convolution_convert_fusion.5), channel_id=1, source_target_pairs={{4,0},{5,1},{6,2},{7,3},{12,8},{13,9},{14,10},{15,11},{20,16},{21,... | collective-permute-start | bytes 980 | tf_op jit(solution)/shard_map/ppermute | solution.py:47
  3.6 14.0 %collective-permute-start = (bf16[3,2,3,9]{3,2,1,0:T(4,128)(2,1)S(1)}, bf16[3,2,3,9]{3,2,1,0:T(4,128)(2,1)S(1)}, u32[]{:S(2)}, u32[]{:S(2)}) collective-permute-start(bf16[3,2,3,9]{3,2,1,0:T(4,128)(2,1)S(1)} %convolution_convert_fusion.5), channel_id=1, source_target_pairs={{0,4},{1,5},{2,6},{3,7},{8,12},{9,13},{10,14},{11,15},{16,20},{17,... | collective-permute-start | bytes 980 | tf_op jit(solution)/shard_map/ppermute | solution.py:42
  10.6 7.1 %collective-permute-start.3 = (bf16[512,2,8]{0,2,1:T(8,128)(2,1)S(1)}, bf16[512,2,8]{0,2,1:T(8,128)(2,1)S(1)}, u32[]{:S(2)}, u32[]{:S(2)}) collective-permute-start(bf16[512,2,8]{0,2,1:T(8,128)(2,1)S(1)} %get-tuple-element.26), channel_id=1, source_target_pairs={{0,3},{1,0},{2,1},{3,2},{4,7},{5,4},{6,5},{7,6},{8,11},{9,8},{10,9... | collective-permute-start | bytes 49160 | tf_op jit(solution)/shard_map/ppermute | solution.py:57
  15.3 5.5 %collective-permute-start.2 = (bf16[512,2,8]{0,2,1:T(8,128)(2,1)S(1)}, bf16[512,2,8]{0,2,1:T(8,128)(2,1)S(1)}, u32[]{:S(2)}, u32[]{:S(2)}) collective-permute-start(bf16[512,2,8]{0,2,1:T(8,128)(2,1)S(1)} %get-tuple-element.25), channel_id=1, source_target_pairs={{0,1},{1,2},{2,3},{3,0},{4,5},{5,6},{6,7},{7,4},{8,9},{9,10},{10,1... | collective-permute-start | bytes 49160 | tf_op jit(solution)/shard_map/ppermute | solution.py:56
  17.6 12.8 %copy-start.11 = (bf16[3,6,3,9]{3,2,1,0:T(4,128)(2,1)}, bf16[3,6,3,9]{3,2,1,0:T(4,128)(2,1)S(1)}, u32[]{:S(2)}) copy-start(bf16[3,6,3,9]{3,2,1,0:T(4,128)(2,1)S(1)} %pad_maximum_fusion.21) | copy-start | bytes 2920
  21.6 34.9 %collective-permute-start.5 = (bf16[512,2,144]{0,2,1:T(8,128)(2,1)}, bf16[512,2,144]{0,2,1:T(8,128)(2,1)}, u32[]{:S(2)}, u32[]{:S(2)}) collective-permute-start(bf16[512,2,144]{0,2,1:T(8,128)(2,1)} %pad_maximum_fusion.20), channel_id=1, source_target_pairs={{4,0},{5,1},{6,2},{7,3},{12,8},{13,9},{14,10},{15,11},{20,16},{21,... | collective-permute-start | bytes 884744 | tf_op jit(solution)/shard_map/ppermute | solution.py:47
  22.9 33.7 %collective-permute-start.4 = (bf16[512,2,144]{0,2,1:T(8,128)(2,1)}, bf16[512,2,144]{0,2,1:T(8,128)(2,1)}, u32[]{:S(2)}, u32[]{:S(2)}) collective-permute-start(bf16[512,2,144]{0,2,1:T(8,128)(2,1)} %pad_maximum_fusion.20), channel_id=1, source_target_pairs={{0,4},{1,5},{2,6},{3,7},{8,12},{9,13},{10,14},{11,15},{16,20},{17,... | collective-permute-start | bytes 884744 | tf_op jit(solution)/shard_map/ppermute | solution.py:42
  35.4 9.5 %slice-start = ((bf16[3,6,3,9]{3,2,1,0:T(4,128)(2,1)}), bf16[3,4,3,9]{3,2,1,0:T(4,128)(2,1)S(1)}, s32[]{:S(2)}) async-start(bf16[3,6,3,9]{3,2,1,0:T(4,128)(2,1)} %copy-done.11), calls=%async_computation | async-start | bytes 24576 | tf_op jit(solution)/shard_map/slice | solution.py:158
  59.4 1.4 %copy-start.1 = (bf16[4,432,408]{1,2,0:T(8,128)(2,1)S(1)}, bf16[4,432,408]{1,2,0:T(8,128)(2,1)}, u32[]{:S(2)}) copy-start(bf16[4,432,408]{1,2,0:T(8,128)(2,1)} %reshape.110) | copy-start | bytes 4230148
  60.8 1.0 copy-start.7
  62.6 2.0 %copy-start.9 = (bf16[256,4,136]{0,2,1:T(8,128)(2,1)}, bf16[256,4,136]{0,2,1:T(8,128)(2,1)S(1)}, u32[]{:S(2)}) copy-start(bf16[256,4,136]{0,2,1:T(8,128)(2,1)S(1)} %get-tuple-element.20) | copy-start | bytes 835588
  62.6 1.2 copy-start.5
  62.6 1.6 %copy-start.6 = (bf16[1,256,2,128]{3,2,1,0:T(2,128)(2,1)S(1)}, bf16[1,256,2,128]{3,2,1,0:T(2,128)(2,1)}, u32[]{:S(2)}) copy-start(bf16[1,256,2,128]{3,2,1,0:T(2,128)(2,1)} %param.13) | copy-start | bytes 393220
  64.2 0.7 copy-start.3
  66.8 2.4 %collective-permute-start.6 = (f32[196608]{0:T(1024)S(1)}, f32[196608]{0:T(1024)S(1)}, u32[]{:S(2)}, u32[]{:S(2)}) collective-permute-start(f32[196608]{0:T(1024)S(1)} %dynamic_slice.31), channel_id=1, source_target_pairs={{0,8},{8,0},{16,24},{24,16},{1,9},{9,1},{17,25},{25,17},{2,10},{10... | collective-permute-start | bytes 2359304 | tf_op jit(solution)/shard_map/ppermute | solution.py:28
  69.3 11.2 %collective-permute-start.7 = (f32[98304]{0:T(1024)S(1)}, f32[98304]{0:T(1024)S(1)}, u32[]{:S(2)}, u32[]{:S(2)}) collective-permute-start(f32[98304]{0:T(1024)S(1)} %dynamic_slice.33), channel_id=1, source_target_pairs={{0,16},{8,24},{16,0},{24,8},{1,17},{9,25},{17,1},{25,9},{2,18},{10... | collective-permute-start | bytes 1179656 | tf_op jit(solution)/shard_map/ppermute | solution.py:28
  80.5 34.1 %copy-start.4 = (bf16[2,384,256]{2,1,0:T(8,128)(2,1)S(1)}, bf16[2,384,256]{2,1,0:T(8,128)(2,1)}, u32[]{:S(2)}) copy-start(bf16[2,384,256]{2,1,0:T(8,128)(2,1)} %copy-done.3) | copy-start | bytes 1179652
  80.6 6.2 %collective-permute-start.8 = (f32[49152]{0:T(1024)S(1)}, f32[49152]{0:T(1024)S(1)}, u32[]{:S(2)}, u32[]{:S(2)}) collective-permute-start(f32[49152]{0:T(1024)S(1)} %dynamic_slice.35), channel_id=1, source_target_pairs={{0,4},{4,0},{1,5},{5,1},{2,6},{6,2},{3,7},{7,3},{8,12},{12,8},{9,1... | collective-permute-start | bytes 589832 | tf_op jit(solution)/shard_map/ppermute | solution.py:28
  86.7 29.0 %copy-start.8 = (bf16[3,256,256]{2,1,0:T(8,128)(2,1)S(1)}, bf16[3,256,256]{2,1,0:T(8,128)(2,1)}, u32[]{:S(2)}) copy-start(bf16[3,256,256]{2,1,0:T(8,128)(2,1)} %param.8) | copy-start | bytes 1179652
  86.8 29.0 %copy-start.10 = (bf16[256,4,136]{0,2,1:T(8,128)(2,1)S(1)}, bf16[256,4,136]{0,2,1:T(8,128)(2,1)}, u32[]{:S(2)}) copy-start(bf16[256,4,136]{0,2,1:T(8,128)(2,1)} %copy-done.9) | copy-start | bytes 835588
  86.8 4.7 %collective-permute-start.9 = (f32[24576]{0:T(1024)S(1)}, f32[24576]{0:T(1024)S(1)}, u32[]{:S(2)}, u32[]{:S(2)}) collective-permute-start(f32[24576]{0:T(1024)S(1)} %dynamic_slice.37), channel_id=1, source_target_pairs={{0,1},{1,0},{2,3},{3,2},{4,5},{5,4},{6,7},{7,6},{8,9},{9,8},{10,11... | collective-permute-start | bytes 294920 | tf_op jit(solution)/shard_map/ppermute | solution.py:28
  91.5 6.0 %collective-permute-start.10 = (f32[12288]{0:T(1024)S(1)}, f32[12288]{0:T(1024)S(1)}, u32[]{:S(2)}, u32[]{:S(2)}) collective-permute-start(f32[12288]{0:T(1024)S(1)} %dynamic_slice.39), channel_id=1, source_target_pairs={{0,2},{1,3},{2,0},{3,1},{4,6},{5,7},{6,4},{7,5},{8,10},{9,11},{10,... | collective-permute-start | bytes 147464 | tf_op jit(solution)/shard_map/ppermute | solution.py:28
  97.6 5.1 %collective-permute-start.11 = (f32[12288]{0:T(1024)S(1)}, f32[12288]{0:T(1024)S(1)}, u32[]{:S(2)}, u32[]{:S(2)}) collective-permute-start(f32[12288]{0:T(1024)S(1)} %dynamic-slice_add_fusion.4), channel_id=1, source_target_pairs={{0,2},{1,3},{2,0},{3,1},{4,6},{5,7},{6,4},{7,5},{8,10},{9,11},{10,... | collective-permute-start | bytes 147464 | tf_op jit(solution)/shard_map/ppermute | solution.py:32
  102.6 4.7 %collective-permute-start.12 = (f32[24576]{0:T(1024)S(1)}, f32[24576]{0:T(1024)S(1)}, u32[]{:S(2)}, u32[]{:S(2)}) collective-permute-start(f32[24576]{0:T(1024)S(1)} %maximum_select_fusion.4), channel_id=1, source_target_pairs={{0,1},{1,0},{2,3},{3,2},{4,5},{5,4},{6,7},{7,6},{8,9},{9,8},{10,11... | collective-permute-start | bytes 294920 | tf_op jit(solution)/shard_map/ppermute | solution.py:32
  107.3 5.7 %collective-permute-start.13 = (f32[49152]{0:T(1024)S(1)}, f32[49152]{0:T(1024)S(1)}, u32[]{:S(2)}, u32[]{:S(2)}) collective-permute-start(f32[49152]{0:T(1024)S(1)} %maximum_select_fusion.3), channel_id=1, source_target_pairs={{0,4},{4,0},{1,5},{5,1},{2,6},{6,2},{3,7},{7,3},{8,12},{12,8},{9,1... | collective-permute-start | bytes 589832 | tf_op jit(solution)/shard_map/ppermute | solution.py:32
  113.1 7.9 %collective-permute-start.14 = (f32[98304]{0:T(1024)S(1)}, f32[98304]{0:T(1024)}, u32[]{:S(2)}, u32[]{:S(2)}) collective-permute-start(f32[98304]{0:T(1024)S(1)} %maximum_select_fusion.2), channel_id=1, source_target_pairs={{0,16},{8,24},{16,0},{24,8},{1,17},{9,25},{17,1},{25,9},{2,18},{10... | collective-permute-start | bytes 1179656 | tf_op jit(solution)/shard_map/ppermute | solution.py:32
  115.0 7.4 %copy-start.2 = (bf16[4,432,408]{1,2,0:T(8,128)(2,1)S(1)}, bf16[4,432,408]{1,2,0:T(8,128)(2,1)}, u32[]{:S(2)}) copy-start(bf16[4,432,408]{1,2,0:T(8,128)(2,1)} %reshape.110) | copy-start | bytes 4230148
  122.2 2.5 %collective-permute-start.15 = (f32[196608]{0:T(1024)S(1)}, f32[196608]{0:T(1024)}, u32[]{:S(2)}, u32[]{:S(2)}) collective-permute-start(f32[196608]{0:T(1024)S(1)} %maximum_select_fusion.1), channel_id=1, source_target_pairs={{0,8},{8,0},{16,24},{24,16},{1,9},{9,1},{17,25},{25,17},{2,10},{10... | collective-permute-start | bytes 2359304 | tf_op jit(solution)/shard_map/ppermute | solution.py:32

commit v3 on v2

--- a/solution.py
+++ b/solution.py
@@ -81,40 +81,24 @@
 
 
 def band_of(stencil, col_count):
-    row_count = stencil.shape[1]
-    basis_count = stencil.shape[0]
-    lat_taps = 2 * LAT_REACH + 1
-    band = jnp.einsum(
+    return jnp.einsum(
         "kiad,dpq->iapkq", stencil, lon_picker(col_count), preferred_element_type=jnp.float32
-    )
-    return band.astype(jnp.bfloat16).reshape(
-        row_count, lat_taps * (col_count + 2 * LON_REACH), basis_count * col_count
-    )
+    ).astype(jnp.bfloat16)
 
 
 def spread(values, band, basis_count):
-    channels = values.shape[0]
     row_count = values.shape[1] - 2 * LAT_REACH
-    col_count = values.shape[2] - 2 * LON_REACH
     lat_taps = 2 * LAT_REACH + 1
     stacked = jnp.stack(
         [values[:, offset : offset + row_count] for offset in range(lat_taps)], axis=2
     )
-    stacked = stacked.reshape(channels, row_count, lat_taps * values.shape[2])
-    mixed = jnp.einsum("cin,inm->cim", stacked, band, preferred_element_type=jnp.float32)
-    return mixed.reshape(channels, row_count, basis_count, col_count)
+    return jnp.einsum("ciap,iapkq->cikq", stacked, band, preferred_element_type=jnp.float32)
 
 
 def spread_adjoint(mixed, band):
-    channels, row_count, basis_count, col_count = mixed.shape
+    row_count, col_count = mixed.shape[1], mixed.shape[3]
     lat_taps = 2 * LAT_REACH + 1
-    partial = jnp.einsum(
-        "cim,inm->cin",
-        mixed.reshape(channels, row_count, basis_count * col_count),
-        band,
-        preferred_element_type=jnp.float32,
-    )
-    partial = partial.reshape(channels, row_count, lat_taps, col_count + 2 * LON_REACH)
+    partial = jnp.einsum("cikq,iapkq->ciap", mixed, band, preferred_element_type=jnp.float32)
     partial = partial[:, :, :, LON_HALO : col_count]
     out_rows = row_count - LAT_HALO
     total = partial[:, LAT_HALO : LAT_HALO + out_rows, 0]

time: 128 us -> 110 us (0.86)
  local copies, waits for them, and re-layouts: 34.8 us -> 8.24 us
  matrix products: 11.1 us -> 21.7 us
  starting transfers between devices: 21.9 us -> 31.8 us
  waiting for transfers between devices: 51.8 us -> 42.6 us
  other arithmetic: 6.61 us -> 4.08 us
    reshape x3 -> x0, local copies, waits for them, and re-layouts: 17.8 us -> none  [band_of(): band.astype(jnp.bfloat16)]
    convert_element_type x3 -> x0, local copies, waits for them, and re-layouts: 8.42 us -> none  [band_of(): band.astype(jnp.bfloat16)]
    ppermute x5, starting transfers between devices: 1.86 us -> 8.43 us  [halving_sum(): other = lax.ppermute(flat, axis, pairs)]
    dot_general x6 -> x4, matrix products: 4.85 us -> 11 us  [the longest x2 9.81 us: spread_adjoint(): jnp.einsum('cikq,iapkq->ciap', mixed, band, preferred_element_type=jnp.fl...]
    ppermute x5, waiting for transfers between devices: 28.4 us -> 23.7 us  [halving_sum(): flat = keep + lax.ppermute(send, axis, pairs)]
    ppermute x5, waiting for transfers between devices: 20.1 us -> 15.5 us  [halving_sum(): other = lax.ppermute(flat, axis, pairs)]
    ppermute x5, starting transfers between devices: 1.85 us -> 6.4 us  [halving_sum(): flat = keep + lax.ppermute(send, axis, pairs)]
    ppermute x1, waiting for transfers between devices: 3.21 us -> 0.01 us  [lon_halo(): lax.ppermute(block[..., cols - width:], 'lon', [(i, (i + 1) % count) for...]
  transfers between devices with their start and end apart: 16 -> 16, of which waited for: 10 -> 11; matrix products, arithmetic and copies ran while one was open for 28% -> 16% of each run, Pallas kernels for 0% -> 0%
where the time goes in v3:
time: 110 us
  waiting for transfers between devices  42.6 us (39%)
  starting transfers between devices  31.8 us (29%)
  matrix products  21.7 us (20%)
  local copies, waits for them, and re-layouts  8.24 us (7%)
  other arithmetic  4.08 us (4%)
  between operations  1.2 us (1%)
    ppermute x5, waiting for transfers between devices, halving_sum(): flat = keep + lax.ppermute(send, axis, pairs)  23.7 us
    ppermute x5, waiting for transfers between devices, halving_sum(): other = lax.ppermute(flat, axis, pairs)  15.5 us
    dot_general x2, matrix products, spread_adjoint(): jnp.einsum('cikq,iapkq->ciap', mixed, band, preferred_element_type=jnp.fl...  9.81 us
    ppermute x2, starting transfers between devices, lat_halo(): lax.ppermute(lax.slice_in_dim(block, rows - width, rows, axis=dim), 'lat'...  9.66 us
    ppermute x5, starting transfers between devices, halving_sum(): other = lax.ppermute(flat, axis, pairs)  8.43 us
    dot_general x3, matrix products, band_of(): jnp.einsum('kiad,dpq->iapkq', stencil, lon_picker(col_count), preferred_e...  6.73 us
    ppermute x5, starting transfers between devices, halving_sum(): flat = keep + lax.ppermute(send, axis, pairs)  6.4 us
    unnamed x23, local copies, waits for them, and re-layouts  5.4 us
  transfers between devices with their start and end apart: 16, of which 11 were waited for; matrix products, arithmetic and copies ran while one was open for 16% of the time, Pallas kernels for 0%

profile of v3, /device:TPU:0, one launch (start us, length us, event | category | flops | bytes accessed | tf_op | source)
XLA Modules:
  0.0 109.6 jit_solution(13476648376419108963)
XLA Ops:
  0.6 0.0 copy-start
  0.6 0.8 broadcast_add_fusion
  1.4 0.9 convolution_convert_fusion.2
  2.3 1.3 %collective-permute-start.1 = (bf16[3,2,3,9]{3,2,1,0:T(4,128)(2,1)S(1)}, bf16[3,2,3,9]{3,2,1,0:T(4,128)(2,1)S(1)}, u32[]{:S(2)}, u32[]{:S(2)}) collective-permute-start(bf16[3,2,3,9]{3,2,1,0:T(4,128)(2,1)S(1)} %convolution_convert_fusion.2), channel_id=1, source_target_pairs={{4,0},{5,1},{6,2},{7,3},{12,8},{13,9},{14,10},{15,11},{20,16},{21,... | collective-permute-start | bytes 980 | tf_op jit(solution)/shard_map/ppermute | solution.py:47
  3.6 4.9 %collective-permute-start = (bf16[3,2,3,9]{3,2,1,0:T(4,128)(2,1)S(1)}, bf16[3,2,3,9]{3,2,1,0:T(4,128)(2,1)S(1)}, u32[]{:S(2)}, u32[]{:S(2)}) collective-permute-start(bf16[3,2,3,9]{3,2,1,0:T(4,128)(2,1)S(1)} %convolution_convert_fusion.2), channel_id=1, source_target_pairs={{0,4},{1,5},{2,6},{3,7},{8,12},{9,13},{10,14},{11,15},{16,20},{17,... | collective-permute-start | bytes 980 | tf_op jit(solution)/shard_map/ppermute | solution.py:42
  8.5 1.0 copy.28
  9.5 1.0 copy.27
  10.6 4.8 %collective-permute-start.3 = (bf16[512,2,8]{0,2,1:T(8,128)(2,1)S(1)}, bf16[512,2,8]{0,2,1:T(8,128)(2,1)S(1)}, u32[]{:S(2)}, u32[]{:S(2)}) collective-permute-start(bf16[512,2,8]{0,2,1:T(8,128)(2,1)S(1)} %get-tuple-element.23), channel_id=1, source_target_pairs={{0,3},{1,0},{2,1},{3,2},{4,7},{5,4},{6,5},{7,6},{8,11},{9,8},{10,9... | collective-permute-start | bytes 49160 | tf_op jit(solution)/shard_map/ppermute | solution.py:57
  15.3 0.1 fusion.38
  15.4 0.1 fusion.21
  15.6 0.6 fusion.30
  16.2 1.8 %copy.51 = pred[9,152,144,1,1]{1,0,4,3,2:T(8,128)(4,1)S(1)} copy(pred[9,152,144,1,1]{2,1,0,3,4:T(8,128)(4,1)S(1)} %fusion.21) | data formatting | bytes 393984 | tf_op jit(solution)/shard_map/eq | solution.py:79
  18.0 4.6 %fusion.74 = bf16[152,144,3,6,3]{0,4,3,2,1:T(4,128)(2,1)} fusion(pred[9,152,144,1,1]{1,0,4,3,2:T(8,128)(4,1)S(1)} %copy.51, bf16[3,2,3,9]{3,2,1,0:T(4,128)(2,1)S(1)} %collective-permute-done.1, bf16[3,2,3,9]{3,2,1,0:T(4,128)(2,1)S(1)} %convolution_convert_fusion.2, bf16[3,2,3,9]{3,2,1,0:T(4,128)(2,1)S(1)} %collective-permute-done), kind=kOutput, calls=%fused_computation.116 | convolution fusion | flops 21278052 | bytes 2561868 | tf_op jit(solution)/shard_map/kiad,dpq->iapkq/dot_general | solution.py:84
  22.7 1.3 %collective-permute-start.5 = (bf16[512,2,144]{0,2,1:T(8,128)(2,1)S(1)}, bf16[512,2,144]{0,2,1:T(8,128)(2,1)S(1)}, u32[]{:S(2)}, u32[]{:S(2)}) collective-permute-start(bf16[512,2,144]{0,2,1:T(8,128)(2,1)S(1)} %pad_maximum_fusion.22), channel_id=1, source_target_pairs={{4,0},{5,1},{6,2},{7,3},{12,8},{13,9},{14,10},{15,11},{20,16},{21,... | collective-permute-start | bytes 884744 | tf_op jit(solution)/shard_map/ppermute | solution.py:47
  24.0 4.8 %collective-permute-start.4 = (bf16[512,2,144]{0,2,1:T(8,128)(2,1)S(1)}, bf16[512,2,144]{0,2,1:T(8,128)(2,1)S(1)}, u32[]{:S(2)}, u32[]{:S(2)}) collective-permute-start(bf16[512,2,144]{0,2,1:T(8,128)(2,1)S(1)} %pad_maximum_fusion.22), channel_id=1, source_target_pairs={{0,4},{1,5},{2,6},{3,7},{8,12},{9,13},{10,14},{11,15},{16,20},{17,... | collective-permute-start | bytes 884744 | tf_op jit(solution)/shard_map/ppermute | solution.py:42
  28.8 1.5 %convert_bitcast_fusion = bf16[4,3,144,3,136]{2,0,1,3,4:T(4,128)(2,1)S(1)} fusion(bf16[3,4,3,9]{3,2,1,0:T(4,128)(2,1)S(1)} %slice.94), kind=kOutput, calls=%fused_computation.8 | convolution fusion | flops 13747968 | bytes 1410696 | tf_op jit(solution)/shard_map/kiad,dpq->iapkq/dot_general | solution.py:84
  30.3 2.2 %collective-permute-done.5 = bf16[512,2,144]{0,2,1:T(8,128)(2,1)S(1)} collective-permute-done((bf16[512,2,144]{0,2,1:T(8,128)(2,1)S(1)}, bf16[512,2,144]{0,2,1:T(8,128)(2,1)S(1)}, u32[]{:S(2)}, u32[]{:S(2)}) %collective-permute-start.5) | collective-permute-done | bytes 294944 | tf_op jit(solution)/shard_map/ppermute | solution.py:47
  32.5 1.2 %collective-permute-done.4 = bf16[512,2,144]{0,2,1:T(8,128)(2,1)S(1)} collective-permute-done((bf16[512,2,144]{0,2,1:T(8,128)(2,1)S(1)}, bf16[512,2,144]{0,2,1:T(8,128)(2,1)S(1)}, u32[]{:S(2)}, u32[]{:S(2)}) %collective-permute-start.4) | collective-permute-done | bytes 294944 | tf_op jit(solution)/shard_map/ppermute | solution.py:42
  33.7 0.1 fusion.65
  33.7 0.8 fusion.23
  34.5 5.8 %fusion.12 = f32[256,6,3,152]{0,3,1,2:T(8,128)} fusion(bf16[512,2,144]{0,2,1:T(8,128)(2,1)S(1)} %collective-permute-done.5, bf16[512,2,144]{0,2,1:T(8,128)(2,1)S(1)} %collective-permute-done.4, bf16[512,2,8]{0,2,1:T(8,128)(2,1)S(1)} %collective-permute-done.3, bf16[512,2,8]{0,2,1:T(8,128)(2,1)S(1)} %collective-permute-done.2, ...), kind=kOutput, calls=%fused_computation.12 | convolution fusion | flops 948215808 | bytes 6443520 | tf_op jit(solution)/shard_map/cikq,iapkq->ciap/dot_general | solution.py:101
  40.4 2.2 %fusion.42 = (bf16[256,4,136]{0,2,1:T(8,128)(2,1)S(1)}, bf16[256,4,136]{0,2,1:T(8,128)(2,1)S(1)}) fusion(f32[256,6,3,152]{0,3,1,2:T(8,128)} %fusion.12, pred[4]{0:T(512)(128)(4,1)S(1)} %compare_and_fusion, bf16[256,4,3,136]{0,3,2,1:T(8,128)(2,1)S(1)} %fusion.23, bf16[3,256,256]{2,1,0:T(8,128)(2,1)S(1)} %copy-done.5), kind=kOutput, calls=%fused_computation.56 | convolution fusion | flops 217808896 | bytes 3457028 | tf_op jit(solution)/shard_map/koc,cikj->oij/dot_general | solution.py:112
  42.6 0.4 fusion.27
  43.0 0.5 copy-done.4
  43.5 0.3 convolution_bitcast_fusion.1
  43.9 0.4 copy-done.2
  44.3 0.3 convolution_bitcast_fusion.2
  44.6 0.1 pad_maximum_fusion
  44.7 0.5 copy.39
  45.2 0.8 copy.69
  46.0 0.1 dynamic_slice.31
  46.1 0.1 collective-permute-start.6
  46.2 2.2 %collective-permute-done.6 = f32[196608]{0:T(1024)S(1)} collective-permute-done((f32[196608]{0:T(1024)S(1)}, f32[196608]{0:T(1024)S(1)}, u32[]{:S(2)}, u32[]{:S(2)}) %collective-permute-start.6) | collective-permute-done | bytes 786464 | tf_op jit(solution)/shard_map/ppermute | solution.py:28
  48.4 0.1 dynamic-slice_add_fusion
  48.6 1.6 %collective-permute-start.7 = (f32[98304]{0:T(1024)S(1)}, f32[98304]{0:T(1024)S(1)}, u32[]{:S(2)}, u32[]{:S(2)}) collective-permute-start(f32[98304]{0:T(1024)S(1)} %dynamic_slice.33), channel_id=1, source_target_pairs={{0,16},{8,24},{16,0},{24,8},{1,17},{9,25},{17,1},{25,9},{2,18},{10... | collective-permute-start | bytes 1179656 | tf_op jit(solution)/shard_map/ppermute | solution.py:28
  50.1 9.7 %collective-permute-done.7 = f32[98304]{0:T(1024)S(1)} collective-permute-done((f32[98304]{0:T(1024)S(1)}, f32[98304]{0:T(1024)S(1)}, u32[]{:S(2)}, u32[]{:S(2)}) %collective-permute-start.7) | collective-permute-done | bytes 393248 | tf_op jit(solution)/shard_map/ppermute | solution.py:28
  59.9 0.0 copy-start.3
  59.9 2.5 %collective-permute-start.8 = (f32[49152]{0:T(1024)S(1)}, f32[49152]{0:T(1024)S(1)}, u32[]{:S(2)}, u32[]{:S(2)}) collective-permute-start(f32[49152]{0:T(1024)S(1)} %dynamic_slice.35), channel_id=1, source_target_pairs={{0,4},{4,0},{1,5},{5,1},{2,6},{6,2},{3,7},{7,3},{8,12},{12,8},{9,1... | collective-permute-start | bytes 589832 | tf_op jit(solution)/shard_map/ppermute | solution.py:28
  62.4 4.3 %collective-permute-done.8 = f32[49152]{0:T(1024)S(1)} collective-permute-done((f32[49152]{0:T(1024)S(1)}, f32[49152]{0:T(1024)S(1)}, u32[]{:S(2)}, u32[]{:S(2)}) %collective-permute-start.8) | collective-permute-done | bytes 196640 | tf_op jit(solution)/shard_map/ppermute | solution.py:28
  66.8 0.1 collective-permute-start.9
  66.9 4.6 %collective-permute-done.9 = f32[24576]{0:T(1024)S(1)} collective-permute-done((f32[24576]{0:T(1024)S(1)}, f32[24576]{0:T(1024)S(1)}, u32[]{:S(2)}, u32[]{:S(2)}) %collective-permute-start.9) | collective-permute-done | bytes 98336 | tf_op jit(solution)/shard_map/ppermute | solution.py:28
  71.5 0.0 copy-start.6
  71.5 0.0 copy-start.8
  71.6 2.2 %collective-permute-start.10 = (f32[12288]{0:T(1024)S(1)}, f32[12288]{0:T(1024)S(1)}, u32[]{:S(2)}, u32[]{:S(2)}) collective-permute-start(f32[12288]{0:T(1024)S(1)} %dynamic_slice.39), channel_id=1, source_target_pairs={{0,2},{1,3},{2,0},{3,1},{4,6},{5,7},{6,4},{7,5},{8,10},{9,11},{10,... | collective-permute-start | bytes 147464 | tf_op jit(solution)/shard_map/ppermute | solution.py:28
  73.7 2.9 %collective-permute-done.10 = f32[12288]{0:T(1024)S(1)} collective-permute-done((f32[12288]{0:T(1024)S(1)}, f32[12288]{0:T(1024)S(1)}, u32[]{:S(2)}, u32[]{:S(2)}) %collective-permute-start.10) | collective-permute-done | bytes 49184 | tf_op jit(solution)/shard_map/ppermute | solution.py:28
  76.6 2.1 %collective-permute-start.11 = (f32[12288]{0:T(1024)S(1)}, f32[12288]{0:T(1024)S(1)}, u32[]{:S(2)}, u32[]{:S(2)}) collective-permute-start(f32[12288]{0:T(1024)S(1)} %dynamic-slice_add_fusion.4), channel_id=1, source_target_pairs={{0,2},{1,3},{2,0},{3,1},{4,6},{5,7},{6,4},{7,5},{8,10},{9,11},{10,... | collective-permute-start | bytes 147464 | tf_op jit(solution)/shard_map/ppermute | solution.py:32
  78.8 2.9 %collective-permute-done.11 = f32[12288]{0:T(1024)S(1)} collective-permute-done((f32[12288]{0:T(1024)S(1)}, f32[12288]{0:T(1024)S(1)}, u32[]{:S(2)}, u32[]{:S(2)}) %collective-permute-start.11) | collective-permute-done | bytes 49184 | tf_op jit(solution)/shard_map/ppermute | solution.py:32
  81.8 2.4 %collective-permute-start.12 = (f32[24576]{0:T(1024)S(1)}, f32[24576]{0:T(1024)S(1)}, u32[]{:S(2)}, u32[]{:S(2)}) collective-permute-start(f32[24576]{0:T(1024)S(1)} %maximum_select_fusion.4), channel_id=1, source_target_pairs={{0,1},{1,0},{2,3},{3,2},{4,5},{5,4},{6,7},{7,6},{8,9},{9,8},{10,11... | collective-permute-start | bytes 294920 | tf_op jit(solution)/shard_map/ppermute | solution.py:32
  84.2 2.6 %collective-permute-done.12 = f32[24576]{0:T(1024)S(1)} collective-permute-done((f32[24576]{0:T(1024)S(1)}, f32[24576]{0:T(1024)S(1)}, u32[]{:S(2)}, u32[]{:S(2)}) %collective-permute-start.12) | collective-permute-done | bytes 98336 | tf_op jit(solution)/shard_map/ppermute | solution.py:32
  86.8 2.2 %collective-permute-start.13 = (f32[49152]{0:T(1024)S(1)}, f32[49152]{0:T(1024)S(1)}, u32[]{:S(2)}, u32[]{:S(2)}) collective-permute-start(f32[49152]{0:T(1024)S(1)} %maximum_select_fusion.3), channel_id=1, source_target_pairs={{0,4},{4,0},{1,5},{5,1},{2,6},{6,2},{3,7},{7,3},{8,12},{12,8},{9,1... | collective-permute-start | bytes 589832 | tf_op jit(solution)/shard_map/ppermute | solution.py:32
  89.0 3.6 %collective-permute-done.13 = f32[49152]{0:T(1024)S(1)} collective-permute-done((f32[49152]{0:T(1024)S(1)}, f32[49152]{0:T(1024)S(1)}, u32[]{:S(2)}, u32[]{:S(2)}) %collective-permute-start.13) | collective-permute-done | bytes 196640 | tf_op jit(solution)/shard_map/ppermute | solution.py:32
  92.7 1.6 %collective-permute-start.14 = (f32[98304]{0:T(1024)S(1)}, f32[98304]{0:T(1024)S(1)}, u32[]{:S(2)}, u32[]{:S(2)}) collective-permute-start(f32[98304]{0:T(1024)S(1)} %maximum_select_fusion.2), channel_id=1, source_target_pairs={{0,16},{8,24},{16,0},{24,8},{1,17},{9,25},{17,1},{25,9},{2,18},{10... | collective-permute-start | bytes 1179656 | tf_op jit(solution)/shard_map/ppermute | solution.py:32
  94.3 6.3 %collective-permute-done.14 = f32[98304]{0:T(1024)S(1)} collective-permute-done((f32[98304]{0:T(1024)S(1)}, f32[98304]{0:T(1024)S(1)}, u32[]{:S(2)}, u32[]{:S(2)}) %collective-permute-start.14) | collective-permute-done | bytes 393248 | tf_op jit(solution)/shard_map/ppermute | solution.py:32
  100.6 0.1 maximum_select_fusion.1
  100.6 0.1 collective-permute-start.15
  100.7 0.3 fusion.29
  101.0 0.8 copy.40
  101.8 4.0 %fusion.15 = f32[256,4,3,144]{0,3,2,1:T(8,128)} fusion(bf16[4,3,144,3,136]{2,0,1,3,4:T(4,128)(2,1)} %copy-done.1, bf16[3,256,256]{2,1,0:T(8,128)(2,1)S(1)} %copy-done.6, bf16[256,4,136]{0,2,1:T(8,128)(2,1)S(1)} %copy-done.8), kind=kOutput, calls=%fused_computation.17 | convolution fusion | flops 575299584 | bytes 3851264 | tf_op jit(solution)/shard_map/cikq,iapkq->ciap/dot_general | solution.py:101
  105.8 1.1 %fusion.70 = bf16[1,256,2,128]{1,3,2,0:T(8,128)(2,1)S(1)} fusion(f32[256,4,3,144]{0,3,2,1:T(8,128)} %fusion.15), kind=kLoop, calls=%fused_computation.106 | loop fusion | flops 196608 | bytes 917504 | tf_op jit(solution)/shard_map/convert_element_type | solution.py:162
  106.9 0.8 copy.41
  107.7 0.2 select_n.159
  107.9 0.2 concatenate.72
  108.2 0.2 maximum_select_fusion
  108.3 1.3 %slice_multiply_fusion = (f32[3,256,256]{2,1,0:T(8,128)}, f32[3,256,256]{2,1,0:T(8,128)}) fusion(f32[6,256,256]{2,1,0:T(8,128)S(1)} %maximum_select_fusion), kind=kLoop, calls=%fused_computation.44 | loop fusion | flops 393216 | bytes 3145728 | tf_op jit(solution)/shard_map/mul | solution.py:171
  (35 shorter events, 0.4 us)
Async XLA Ops:
  0.6 33.9 %copy-start = (bf16[3,256,256]{2,1,0:T(8,128)(2,1)S(1)}, bf16[3,256,256]{2,1,0:T(8,128)(2,1)}, u32[]{:S(2)}) copy-start(bf16[3,256,256]{2,1,0:T(8,128)(2,1)} %param.9) | copy-start | bytes 1179652
  2.3 15.7 %collective-permute-start.1 = (bf16[3,2,3,9]{3,2,1,0:T(4,128)(2,1)S(1)}, bf16[3,2,3,9]{3,2,1,0:T(4,128)(2,1)S(1)}, u32[]{:S(2)}, u32[]{:S(2)}) collective-permute-start(bf16[3,2,3,9]{3,2,1,0:T(4,128)(2,1)S(1)} %convolution_convert_fusion.2), channel_id=1, source_target_pairs={{4,0},{5,1},{6,2},{7,3},{12,8},{13,9},{14,10},{15,11},{20,16},{21,... | collective-permute-start | bytes 980 | tf_op jit(solution)/shard_map/ppermute | solution.py:47
  3.6 14.4 %collective-permute-start = (bf16[3,2,3,9]{3,2,1,0:T(4,128)(2,1)S(1)}, bf16[3,2,3,9]{3,2,1,0:T(4,128)(2,1)S(1)}, u32[]{:S(2)}, u32[]{:S(2)}) collective-permute-start(bf16[3,2,3,9]{3,2,1,0:T(4,128)(2,1)S(1)} %convolution_convert_fusion.2), channel_id=1, source_target_pairs={{0,4},{1,5},{2,6},{3,7},{8,12},{9,13},{10,14},{11,15},{16,20},{17,... | collective-permute-start | bytes 980 | tf_op jit(solution)/shard_map/ppermute | solution.py:42
  10.6 12.1 %collective-permute-start.3 = (bf16[512,2,8]{0,2,1:T(8,128)(2,1)S(1)}, bf16[512,2,8]{0,2,1:T(8,128)(2,1)S(1)}, u32[]{:S(2)}, u32[]{:S(2)}) collective-permute-start(bf16[512,2,8]{0,2,1:T(8,128)(2,1)S(1)} %get-tuple-element.23), channel_id=1, source_target_pairs={{0,3},{1,0},{2,1},{3,2},{4,7},{5,4},{6,5},{7,6},{8,11},{9,8},{10,9... | collective-permute-start | bytes 49160 | tf_op jit(solution)/shard_map/ppermute | solution.py:57
  15.3 7.3 %collective-permute-start.2 = (bf16[512,2,8]{0,2,1:T(8,128)(2,1)S(1)}, bf16[512,2,8]{0,2,1:T(8,128)(2,1)S(1)}, u32[]{:S(2)}, u32[]{:S(2)}) collective-permute-start(bf16[512,2,8]{0,2,1:T(8,128)(2,1)S(1)} %get-tuple-element.22), channel_id=1, source_target_pairs={{0,1},{1,2},{2,3},{3,0},{4,5},{5,6},{6,7},{7,4},{8,9},{9,10},{10,1... | collective-permute-start | bytes 49160 | tf_op jit(solution)/shard_map/ppermute | solution.py:56
  22.7 9.8 %collective-permute-start.5 = (bf16[512,2,144]{0,2,1:T(8,128)(2,1)S(1)}, bf16[512,2,144]{0,2,1:T(8,128)(2,1)S(1)}, u32[]{:S(2)}, u32[]{:S(2)}) collective-permute-start(bf16[512,2,144]{0,2,1:T(8,128)(2,1)S(1)} %pad_maximum_fusion.22), channel_id=1, source_target_pairs={{4,0},{5,1},{6,2},{7,3},{12,8},{13,9},{14,10},{15,11},{20,16},{21,... | collective-permute-start | bytes 884744 | tf_op jit(solution)/shard_map/ppermute | solution.py:47
  24.0 9.7 %collective-permute-start.4 = (bf16[512,2,144]{0,2,1:T(8,128)(2,1)S(1)}, bf16[512,2,144]{0,2,1:T(8,128)(2,1)S(1)}, u32[]{:S(2)}, u32[]{:S(2)}) collective-permute-start(bf16[512,2,144]{0,2,1:T(8,128)(2,1)S(1)} %pad_maximum_fusion.22), channel_id=1, source_target_pairs={{0,4},{1,5},{2,6},{3,7},{8,12},{9,13},{10,14},{11,15},{16,20},{17,... | collective-permute-start | bytes 884744 | tf_op jit(solution)/shard_map/ppermute | solution.py:42
  30.3 3.4 %copy-start.1 = (bf16[4,3,144,3,136]{2,0,1,3,4:T(4,128)(2,1)}, bf16[4,3,144,3,136]{2,0,1,3,4:T(4,128)(2,1)S(1)}, u32[]{:S(2)}) copy-start(bf16[4,3,144,3,136]{2,0,1,3,4:T(4,128)(2,1)S(1)} %convert_bitcast_fusion) | copy-start | bytes 4230148
  34.5 5.8 %copy-start.5 = (bf16[3,256,256]{2,1,0:T(8,128)(2,1)S(1)}, bf16[3,256,256]{2,1,0:T(8,128)(2,1)}, u32[]{:S(2)}) copy-start(bf16[3,256,256]{2,1,0:T(8,128)(2,1)} %param.8) | copy-start | bytes 1179652
  42.5 1.3 %copy-start.7 = (bf16[256,4,136]{0,2,1:T(8,128)(2,1)}, bf16[256,4,136]{0,2,1:T(8,128)(2,1)S(1)}, u32[]{:S(2)}) copy-start(bf16[256,4,136]{0,2,1:T(8,128)(2,1)S(1)} %get-tuple-element.17) | copy-start | bytes 835588
  42.5 1.0 copy-start.4
  43.5 0.7 copy-start.2
  46.1 2.4 %collective-permute-start.6 = (f32[196608]{0:T(1024)S(1)}, f32[196608]{0:T(1024)S(1)}, u32[]{:S(2)}, u32[]{:S(2)}) collective-permute-start(f32[196608]{0:T(1024)S(1)} %dynamic_slice.31), channel_id=1, source_target_pairs={{0,8},{8,0},{16,24},{24,16},{1,9},{9,1},{17,25},{25,17},{2,10},{10... | collective-permute-start | bytes 2359304 | tf_op jit(solution)/shard_map/ppermute | solution.py:28
  48.6 11.2 %collective-permute-start.7 = (f32[98304]{0:T(1024)S(1)}, f32[98304]{0:T(1024)S(1)}, u32[]{:S(2)}, u32[]{:S(2)}) collective-permute-start(f32[98304]{0:T(1024)S(1)} %dynamic_slice.33), channel_id=1, source_target_pairs={{0,16},{8,24},{16,0},{24,8},{1,17},{9,25},{17,1},{25,9},{2,18},{10... | collective-permute-start | bytes 1179656 | tf_op jit(solution)/shard_map/ppermute | solution.py:28
  59.9 40.8 %copy-start.3 = (bf16[256,2,3,128]{0,3,2,1:T(8,128)(2,1)S(1)}, bf16[256,2,3,128]{0,3,2,1:T(8,128)(2,1)}, u32[]{:S(2)}) copy-start(bf16[256,2,3,128]{0,3,2,1:T(8,128)(2,1)} %copy-done.2) | copy-start | bytes 1179652
  59.9 6.9 %collective-permute-start.8 = (f32[49152]{0:T(1024)S(1)}, f32[49152]{0:T(1024)S(1)}, u32[]{:S(2)}, u32[]{:S(2)}) collective-permute-start(f32[49152]{0:T(1024)S(1)} %dynamic_slice.35), channel_id=1, source_target_pairs={{0,4},{4,0},{1,5},{5,1},{2,6},{6,2},{3,7},{7,3},{8,12},{12,8},{9,1... | collective-permute-start | bytes 589832 | tf_op jit(solution)/shard_map/ppermute | solution.py:28
  66.8 4.7 %collective-permute-start.9 = (f32[24576]{0:T(1024)S(1)}, f32[24576]{0:T(1024)S(1)}, u32[]{:S(2)}, u32[]{:S(2)}) collective-permute-start(f32[24576]{0:T(1024)S(1)} %dynamic_slice.37), channel_id=1, source_target_pairs={{0,1},{1,0},{2,3},{3,2},{4,5},{5,4},{6,7},{7,6},{8,9},{9,8},{10,11... | collective-permute-start | bytes 294920 | tf_op jit(solution)/shard_map/ppermute | solution.py:28
  71.5 30.3 %copy-start.6 = (bf16[3,256,256]{2,1,0:T(8,128)(2,1)S(1)}, bf16[3,256,256]{2,1,0:T(8,128)(2,1)}, u32[]{:S(2)}) copy-start(bf16[3,256,256]{2,1,0:T(8,128)(2,1)} %param.8) | copy-start | bytes 1179652
  71.5 30.3 %copy-start.8 = (bf16[256,4,136]{0,2,1:T(8,128)(2,1)S(1)}, bf16[256,4,136]{0,2,1:T(8,128)(2,1)}, u32[]{:S(2)}) copy-start(bf16[256,4,136]{0,2,1:T(8,128)(2,1)} %copy-done.7) | copy-start | bytes 835588
  71.6 5.1 %collective-permute-start.10 = (f32[12288]{0:T(1024)S(1)}, f32[12288]{0:T(1024)S(1)}, u32[]{:S(2)}, u32[]{:S(2)}) collective-permute-start(f32[12288]{0:T(1024)S(1)} %dynamic_slice.39), channel_id=1, source_target_pairs={{0,2},{1,3},{2,0},{3,1},{4,6},{5,7},{6,4},{7,5},{8,10},{9,11},{10,... | collective-permute-start | bytes 147464 | tf_op jit(solution)/shard_map/ppermute | solution.py:28
  76.6 5.1 %collective-permute-start.11 = (f32[12288]{0:T(1024)S(1)}, f32[12288]{0:T(1024)S(1)}, u32[]{:S(2)}, u32[]{:S(2)}) collective-permute-start(f32[12288]{0:T(1024)S(1)} %dynamic-slice_add_fusion.4), channel_id=1, source_target_pairs={{0,2},{1,3},{2,0},{3,1},{4,6},{5,7},{6,4},{7,5},{8,10},{9,11},{10,... | collective-permute-start | bytes 147464 | tf_op jit(solution)/shard_map/ppermute | solution.py:32
  81.8 5.0 %collective-permute-start.12 = (f32[24576]{0:T(1024)S(1)}, f32[24576]{0:T(1024)S(1)}, u32[]{:S(2)}, u32[]{:S(2)}) collective-permute-start(f32[24576]{0:T(1024)S(1)} %maximum_select_fusion.4), channel_id=1, source_target_pairs={{0,1},{1,0},{2,3},{3,2},{4,5},{5,4},{6,7},{7,6},{8,9},{9,8},{10,11... | collective-permute-start | bytes 294920 | tf_op jit(solution)/shard_map/ppermute | solution.py:32
  86.8 5.9 %collective-permute-start.13 = (f32[49152]{0:T(1024)S(1)}, f32[49152]{0:T(1024)S(1)}, u32[]{:S(2)}, u32[]{:S(2)}) collective-permute-start(f32[49152]{0:T(1024)S(1)} %maximum_select_fusion.3), channel_id=1, source_target_pairs={{0,4},{4,0},{1,5},{5,1},{2,6},{6,2},{3,7},{7,3},{8,12},{12,8},{9,1... | collective-permute-start | bytes 589832 | tf_op jit(solution)/shard_map/ppermute | solution.py:32
  92.7 7.8 %collective-permute-start.14 = (f32[98304]{0:T(1024)S(1)}, f32[98304]{0:T(1024)S(1)}, u32[]{:S(2)}, u32[]{:S(2)}) collective-permute-start(f32[98304]{0:T(1024)S(1)} %maximum_select_fusion.2), channel_id=1, source_target_pairs={{0,16},{8,24},{16,0},{24,8},{1,17},{9,25},{17,1},{25,9},{2,18},{10... | collective-permute-start | bytes 1179656 | tf_op jit(solution)/shard_map/ppermute | solution.py:32
  100.6 7.3 %collective-permute-start.15 = (f32[196608]{0:T(1024)S(1)}, f32[196608]{0:T(1024)S(1)}, u32[]{:S(2)}, u32[]{:S(2)}) collective-permute-start(f32[196608]{0:T(1024)S(1)} %maximum_select_fusion.1), channel_id=1, source_target_pairs={{0,8},{8,0},{16,24},{24,16},{1,9},{9,1},{17,25},{25,17},{2,10},{10... | collective-permute-start | bytes 2359304 | tf_op jit(solution)/shard_map/ppermute | solution.py:32

commit v4 on v3

--- a/solution.py
+++ b/solution.py
@@ -11,29 +11,35 @@
 LON_HALO = 2 * LON_REACH
 
 
-def halving_sum(value, axes):
+def halving_sum(value, axes, exchanged=2):
     stages = []
     for axis in axes:
         bit = 1
         while bit < lax.axis_size(axis):
             stages.append((axis, bit))
             bit *= 2
+    exchanged = min(exchanged, len(stages))
+    halved = stages[: len(stages) - exchanged]
     flat = value.reshape(-1)
-    for axis, bit in stages:
+    for axis, bit in halved:
         pairs = [(i, i ^ bit) for i in range(lax.axis_size(axis))]
         upper = (lax.axis_index(axis) // bit) % 2
         half = flat.shape[0] // 2
         keep = lax.dynamic_slice_in_dim(flat, upper * half, half)
         send = lax.dynamic_slice_in_dim(flat, (1 - upper) * half, half)
         flat = keep + lax.ppermute(send, axis, pairs)
-    for axis, bit in reversed(stages):
+    for axis, bit in stages[len(halved) :]:
+        pairs = [(i, i ^ bit) for i in range(lax.axis_size(axis))]
+        flat = flat + lax.ppermute(flat, axis, pairs)
+    flat = flat.astype(jnp.bfloat16)
+    for axis, bit in reversed(halved):
         pairs = [(i, i ^ bit) for i in range(lax.axis_size(axis))]
         upper = (lax.axis_index(axis) // bit) % 2
         other = lax.ppermute(flat, axis, pairs)
         flat = jnp.where(
             upper == 1, jnp.concatenate([other, flat]), jnp.concatenate([flat, other])
         )
-    return flat.reshape(value.shape)
+    return flat.astype(jnp.float32).reshape(value.shape)
 
 
 def lat_halo(block, dim, width):
@@ -129,10 +135,16 @@
     stencil = coefficients(quadrature, lat_offsets, lon_offsets)
     basis_count = stencil.shape[0]
 
-    packed = jnp.concatenate([source, gradient], axis=0)
-    framed = lat_halo(lon_halo(packed, LON_HALO), 1, LAT_HALO)
-    source_wide, gradient_wide = framed[:channels], framed[channels:]
-    stencil_wide = lat_halo(stencil, 1, LAT_HALO)
+    packed = lon_halo(jnp.concatenate([source, gradient], axis=0), LON_HALO)
+    taps_per_row = stencil.size // row_count
+    stencil_rows = jnp.transpose(stencil, (1, 0, 2, 3)).reshape(row_count, taps_per_row)
+    stencil_rows = jnp.pad(stencil_rows, ((0, 0), (0, packed.shape[2] - taps_per_row)))
+    framed = lat_halo(jnp.concatenate([packed, stencil_rows[None]], axis=0), 1, LAT_HALO)
+    source_wide, gradient_wide = framed[:channels], framed[channels : 2 * channels]
+    stencil_wide = framed[2 * channels, :, :taps_per_row].reshape(
+        row_count + 2 * LAT_HALO, stencil.shape[0], stencil.shape[2], stencil.shape[3]
+    )
+    stencil_wide = jnp.transpose(stencil_wide, (1, 0, 2, 3))
 
     total_rows = row_count * lax.axis_size("lat")
     first_row = lax.axis_index("lat") * row_count

time: 110 us -> 107 us (0.973)
  starting transfers between devices: 31.8 us -> 18.1 us
  local copies, waits for them, and re-layouts: 8.24 us -> 11.8 us
  waiting for transfers between devices: 42.6 us -> 45.3 us
  matrix products: 21.7 us -> 24 us
  other arithmetic: 4.08 us -> 5.87 us
    ppermute x0 -> x2, waiting for transfers between devices: none -> 15.1 us  [halving_sum(): flat = flat + lax.ppermute(flat, axis, pairs)]
    ppermute x5 -> x3, waiting for transfers between devices: 15.5 us -> 7.63 us  [halving_sum(): other = lax.ppermute(flat, axis, pairs)]
    ppermute x5 -> x3, waiting for transfers between devices: 23.7 us -> 16.3 us  [halving_sum(): flat = keep + lax.ppermute(send, axis, pairs)]
    ppermute x5 -> x3, starting transfers between devices: 8.43 us -> 2.79 us  [halving_sum(): other = lax.ppermute(flat, axis, pairs)]
    ppermute x2 -> x1, starting transfers between devices: 9.66 us -> 4.59 us  [lat_halo(): lax.ppermute(lax.slice_in_dim(block, rows - width, rows, axis=dim), 'lat'...]
    ppermute x1, waiting for transfers between devices: 0.01 us -> 3.41 us  [lon_halo(): lax.ppermute(block[..., cols - width:], 'lon', [(i, (i + 1) % count) for...]
    ppermute x5 -> x3, starting transfers between devices: 6.4 us -> 4.19 us  [halving_sum(): flat = keep + lax.ppermute(send, axis, pairs)]
    unnamed x23, local copies, waits for them, and re-layouts: 5.4 us -> 6.86 us
  transfers between devices with their start and end apart: 16 -> 12, of which waited for: 11 -> 10; matrix products, arithmetic and copies ran while one was open for 16% -> 12% of each run, Pallas kernels for 0% -> 0%
where the time goes in v4:
time: 107 us; the launch traced here: 106 us
  waiting for transfers between devices  45.3 us (42%)
  matrix products  24 us (22%)
  starting transfers between devices  18.1 us (17%)
  local copies, waits for them, and re-layouts  11.8 us (11%)
  other arithmetic  5.87 us (5%)
    ppermute x3, waiting for transfers between devices, halving_sum(): flat = keep + lax.ppermute(send, axis, pairs)  16.3 us
    ppermute x2, waiting for transfers between devices, halving_sum(): flat = flat + lax.ppermute(flat, axis, pairs)  15.1 us
    dot_general x2, matrix products, spread_adjoint(): jnp.einsum('cikq,iapkq->ciap', mixed, band, preferred_element_type=jnp.fl...  9.67 us
    ppermute x3, waiting for transfers between devices, halving_sum(): other = lax.ppermute(flat, axis, pairs)  7.63 us
    dot_general x3, matrix products, band_of(): jnp.einsum('kiad,dpq->iapkq', stencil, lon_picker(col_count), preferred_e...  6.86 us
    unnamed x23, local copies, waits for them, and re-layouts  6.86 us
    ppermute x1, starting transfers between devices, lon_halo(): lax.ppermute(block[..., :width], 'lon', [(i, (i - 1) % count) for i in ra...  5.13 us
    ppermute x1, starting transfers between devices, lat_halo(): lax.ppermute(lax.slice_in_dim(block, rows - width, rows, axis=dim), 'lat'...  4.59 us
  transfers between devices with their start and end apart: 12, of which 10 were waited for; matrix products, arithmetic and copies ran while one was open for 12% of the time, Pallas kernels for 0%

profile of v4, /device:TPU:0, one launch (start us, length us, event | category | flops | bytes accessed | tf_op | source)
XLA Modules:
  0.0 106.2 jit_solution(15619190067575008547)
XLA Ops:
  0.6 0.0 copy-start
  0.6 1.1 %copy.26 = bf16[1,256,2,128]{1,3,2,0:T(8,128)(2,1)S(1)} copy(bf16[1,256,2,128]{3,2,1,0:T(2,128)(2,1)} %param.13) | data formatting | bytes 262144 | tf_op args[6]
  1.7 1.0 copy.25
  2.8 5.1 %collective-permute-start.1 = (bf16[512,2,8]{0,2,1:T(8,128)(2,1)S(1)}, bf16[512,2,8]{0,2,1:T(8,128)(2,1)S(1)}, u32[]{:S(2)}, u32[]{:S(2)}) collective-permute-start(bf16[512,2,8]{0,2,1:T(8,128)(2,1)S(1)} %get-tuple-element.23), channel_id=1, source_target_pairs={{0,3},{1,0},{2,1},{3,2},{4,7},{5,4},{6,5},{7,6},{8,11},{9,8},{10,9... | collective-permute-start | bytes 49160 | tf_op jit(solution)/shard_map/ppermute | solution.py:63
  7.9 0.0 collective-permute-start
  7.9 0.1 fusion.39
  8.0 0.1 fusion.21
  8.1 0.7 broadcast_add_fusion
  8.8 0.9 convolution_convert_fusion.2
  9.7 0.1 reshape.80
  9.8 0.2 copy.28
  10.0 0.0 collective-permute-done.1
  10.0 3.4 %collective-permute-done = bf16[512,2,8]{0,2,1:T(8,128)(2,1)S(1)} collective-permute-done((bf16[512,2,8]{0,2,1:T(8,128)(2,1)S(1)}, bf16[512,2,8]{0,2,1:T(8,128)(2,1)S(1)}, u32[]{:S(2)}, u32[]{:S(2)}) %collective-permute-start) | collective-permute-done | bytes 16416 | tf_op jit(solution)/shard_map/ppermute | solution.py:62
  13.5 1.3 %collective-permute-start.3 = (bf16[513,2,144]{0,2,1:T(8,128)(2,1)S(1)}, bf16[513,2,144]{0,2,1:T(8,128)(2,1)S(1)}, u32[]{:S(2)}, u32[]{:S(2)}) collective-permute-start(bf16[513,2,144]{0,2,1:T(8,128)(2,1)S(1)} %pad_maximum_fusion.17), channel_id=1, source_target_pairs={{4,0},{5,1},{6,2},{7,3},{12,8},{13,9},{14,10},{15,11},{20,16},{21,... | collective-permute-start | bytes 886472 | tf_op jit(solution)/shard_map/ppermute | solution.py:53
  14.8 4.6 %collective-permute-start.2 = (bf16[513,2,144]{0,2,1:T(8,128)(2,1)S(1)}, bf16[513,2,144]{0,2,1:T(8,128)(2,1)S(1)}, u32[]{:S(2)}, u32[]{:S(2)}) collective-permute-start(bf16[513,2,144]{0,2,1:T(8,128)(2,1)S(1)} %pad_maximum_fusion.17), channel_id=1, source_target_pairs={{0,4},{1,5},{2,6},{3,7},{8,12},{9,13},{10,14},{11,15},{16,20},{17,... | collective-permute-start | bytes 886472 | tf_op jit(solution)/shard_map/ppermute | solution.py:48
  19.4 1.8 %copy.52 = pred[9,152,144,1,1]{1,0,4,3,2:T(8,128)(4,1)S(1)} copy(pred[9,152,144,1,1]{2,1,0,3,4:T(8,128)(4,1)S(1)} %fusion.21) | data formatting | bytes 393984 | tf_op jit(solution)/shard_map/eq | solution.py:85
  21.2 1.5 %fusion.30 = bf16[136,128,3,2,3]{1,4,3,2,0:T(4,128)(2,1)} fusion(pred[9,136,128,1,1]{2,1,0,3,4:T(8,128)(4,1)S(1)} %fusion.39, bf16[3,2,3,9]{3,2,1,0:T(4,128)(2,1)S(1)} %convolution_convert_fusion.2), kind=kOutput, calls=%fused_computation.33 | convolution fusion | flops 5640192 | bytes 783684 | tf_op jit(solution)/shard_map/kiad,dpq->iapkq/dot_general | solution.py:90
  22.6 1.6 %collective-permute-done.3 = bf16[513,2,144]{0,2,1:T(8,128)(2,1)S(1)} collective-permute-done((bf16[513,2,144]{0,2,1:T(8,128)(2,1)S(1)}, bf16[513,2,144]{0,2,1:T(8,128)(2,1)S(1)}, u32[]{:S(2)}, u32[]{:S(2)}) %collective-permute-start.3) | collective-permute-done | bytes 295520 | tf_op jit(solution)/shard_map/ppermute | solution.py:53
  24.2 1.2 %collective-permute-done.2 = bf16[513,2,144]{0,2,1:T(8,128)(2,1)S(1)} collective-permute-done((bf16[513,2,144]{0,2,1:T(8,128)(2,1)S(1)}, bf16[513,2,144]{0,2,1:T(8,128)(2,1)S(1)}, u32[]{:S(2)}, u32[]{:S(2)}) %collective-permute-start.2) | collective-permute-done | bytes 295520 | tf_op jit(solution)/shard_map/ppermute | solution.py:48
  25.4 0.1 maximum_reduce_fusion
  25.6 0.1 reshape_squeeze.3
  25.7 3.9 %fusion.75 = bf16[152,144,3,6,3]{0,3,4,2,1:T(8,128)(2,1)} fusion(pred[9,152,144,1,1]{1,0,4,3,2:T(8,128)(4,1)S(1)} %copy.52, bf16[6,3,3,9]{3,2,1,0:T(4,128)(2,1)S(1)} %reshape_squeeze.3), kind=kOutput, calls=%fused_computation.117 | convolution fusion | flops 21275136 | bytes 2561868 | tf_op jit(solution)/shard_map/kiad,dpq->iapkq/dot_general | solution.py:90
  29.6 1.5 %convert_bitcast_fusion = bf16[4,3,144,3,136]{2,0,1,3,4:T(4,128)(2,1)S(1)} fusion(bf16[3,6,3,9]{3,1,2,0:T(8,128)(2,1)S(1)} %bitcast.189), kind=kOutput, calls=%fused_computation.8 | convolution fusion | flops 13747968 | bytes 1419264 | tf_op jit(solution)/shard_map/kiad,dpq->iapkq/dot_general | solution.py:90
  31.1 0.1 fusion.66
  31.2 1.4 %copy-done.1 = bf16[4,3,144,3,136]{2,0,1,3,4:T(4,128)(2,1)} copy-done((bf16[4,3,144,3,136]{2,0,1,3,4:T(4,128)(2,1)}, bf16[4,3,144,3,136]{2,0,1,3,4:T(4,128)(2,1)S(1)}, u32[]{:S(2)}) %copy-start.1) | copy-done | bytes 1410072
  32.6 1.7 %fusion.23 = bf16[256,4,3,136]{0,3,2,1:T(8,128)(2,1)} fusion(bf16[4,3,144,3,136]{2,0,1,3,4:T(4,128)(2,1)S(1)} %convert_bitcast_fusion, bf16[256,4,1,144]{0,3,2,1:T(8,128)(2,1)S(1)} %get-tuple-element.16, bf16[256,4,1,144]{0,3,2,1:T(8,128)(2,1)S(1)} %get-tuple-element.15, bf16[256,4,1,144]{0,3,2,1:T(8,128)(2,1)S(1)} %get-tuple-element.14), kind=kOutput, calls=%fused_computation.22 | convolution fusion | flops 362274816 | bytes 3130368 | tf_op jit(solution)/shard_map/ciap,iapkq->cikq/dot_general | solution.py:101
  34.3 6.3 %fusion.12 = f32[256,6,3,152]{0,3,1,2:T(8,128)} fusion(bf16[513,2,144]{0,2,1:T(8,128)(2,1)S(1)} %collective-permute-done.3, bf16[513,2,144]{0,2,1:T(8,128)(2,1)S(1)} %collective-permute-done.2, bf16[1,2,144]{0,2,1:T(8,128)(2,1)S(1)} %copy.28, bf16[512,2,8]{0,2,1:T(8,128)(2,1)S(1)} %collective-permute-done.1, ...), kind=kOutput, calls=%fused_computation.12 | convolution fusion | flops 948658176 | bytes 6445248 | tf_op jit(solution)/shard_map/cikq,iapkq->ciap/dot_general | solution.py:107
  40.6 2.5 %fusion.43 = (bf16[256,4,136]{0,2,1:T(8,128)(2,1)S(1)}, bf16[256,4,136]{0,2,1:T(8,128)(2,1)S(1)}) fusion(f32[256,6,3,152]{0,3,1,2:T(8,128)} %fusion.12, pred[4]{0:T(512)(128)(4,1)S(1)} %compare_and_fusion, bf16[256,4,3,136]{0,3,2,1:T(8,128)(2,1)} %fusion.23, bf16[3,256,256]{2,1,0:T(8,128)(2,1)S(1)} %copy-done.6), kind=kOutput, calls=%fused_computation.56 | convolution fusion | flops 217808896 | bytes 3457028 | tf_op jit(solution)/shard_map/koc,cikj->oij/dot_general | solution.py:118
  43.1 0.0 copy-start.5
  43.2 0.4 fusion.27
  43.6 0.5 copy-done.5
  44.1 0.3 convolution_bitcast_fusion.1
  44.4 0.4 copy-done.3
  44.9 1.3 %convolution_bitcast_fusion.2 = f32[3,256,256]{1,2,0:T(8,128)S(1)} fusion(bf16[256,4,3,136]{0,3,2,1:T(8,128)(2,1)} %fusion.23, bf16[256,4,136]{0,2,1:T(8,128)(2,1)S(1)} %get-tuple-element.17), kind=kOutput, calls=%fused_computation.25 | convolution fusion | flops 100663296 | bytes 1310720 | tf_op jit(solution)/shard_map/oij,cikj->koc/dot_general | solution.py:128
  46.2 0.1 pad_maximum_fusion
  46.3 0.5 copy.40
  46.8 0.8 copy.70
  47.6 0.1 dynamic_slice.19
  47.7 0.1 collective-permute-start.4
  47.8 2.2 %collective-permute-done.4 = f32[196608]{0:T(1024)S(1)} collective-permute-done((f32[196608]{0:T(1024)S(1)}, f32[196608]{0:T(1024)S(1)}, u32[]{:S(2)}, u32[]{:S(2)}) %collective-permute-start.4) | collective-permute-done | bytes 786464 | tf_op jit(solution)/shard_map/ppermute | solution.py:30
  50.0 0.1 dynamic-slice_add_fusion
  50.2 1.6 %collective-permute-start.5 = (f32[98304]{0:T(1024)S(1)}, f32[98304]{0:T(1024)S(1)}, u32[]{:S(2)}, u32[]{:S(2)}) collective-permute-start(f32[98304]{0:T(1024)S(1)} %dynamic_slice.21), channel_id=1, source_target_pairs={{0,16},{8,24},{16,0},{24,8},{1,17},{9,25},{17,1},{25,9},{2,18},{10... | collective-permute-start | bytes 1179656 | tf_op jit(solution)/shard_map/ppermute | solution.py:30
  51.7 9.7 %collective-permute-done.5 = f32[98304]{0:T(1024)S(1)} collective-permute-done((f32[98304]{0:T(1024)S(1)}, f32[98304]{0:T(1024)S(1)}, u32[]{:S(2)}, u32[]{:S(2)}) %collective-permute-start.5) | collective-permute-done | bytes 393248 | tf_op jit(solution)/shard_map/ppermute | solution.py:30
  61.5 2.6 %collective-permute-start.6 = (f32[49152]{0:T(1024)S(1)}, f32[49152]{0:T(1024)}, u32[]{:S(2)}, u32[]{:S(2)}) collective-permute-start(f32[49152]{0:T(1024)S(1)} %dynamic_slice.23), channel_id=1, source_target_pairs={{0,4},{4,0},{1,5},{5,1},{2,6},{6,2},{3,7},{7,3},{8,12},{12,8},{9,1... | collective-permute-start | bytes 589832 | tf_op jit(solution)/shard_map/ppermute | solution.py:30
  64.0 4.5 %collective-permute-done.6 = f32[49152]{0:T(1024)} collective-permute-done((f32[49152]{0:T(1024)S(1)}, f32[49152]{0:T(1024)}, u32[]{:S(2)}, u32[]{:S(2)}) %collective-permute-start.6) | collective-permute-done | bytes 196640 | tf_op jit(solution)/shard_map/ppermute | solution.py:30
  68.5 0.9 dynamic-slice_add_fusion.2
  69.4 0.1 collective-permute-start.7
  69.5 5.7 %collective-permute-done.7 = f32[49152]{0:T(1024)S(1)} collective-permute-done((f32[49152]{0:T(1024)S(1)}, f32[49152]{0:T(1024)S(1)}, u32[]{:S(2)}, u32[]{:S(2)}) %collective-permute-start.7) | collective-permute-done | bytes 196640 | tf_op jit(solution)/shard_map/ppermute | solution.py:33
  75.2 0.1 collective-permute-start.8
  75.3 9.5 %collective-permute-done.8 = f32[49152]{0:T(1024)S(1)} collective-permute-done((f32[49152]{0:T(1024)S(1)}, f32[49152]{0:T(1024)S(1)}, u32[]{:S(2)}, u32[]{:S(2)}) %collective-permute-start.8) | collective-permute-done | bytes 196640 | tf_op jit(solution)/shard_map/ppermute | solution.py:33
  84.8 1.2 %collective-permute-start.9 = (bf16[49152]{0:T(1024)(128)(2,1)S(1)}, bf16[49152]{0:T(1024)(128)(2,1)S(1)}, u32[]{:S(2)}, u32[]{:S(2)}) collective-permute-start(bf16[49152]{0:T(1024)(128)(2,1)S(1)} %add_convert_fusion), channel_id=1, source_target_pairs={{0,4},{4,0},{1,5},{5,1},{2,6},{6,2},{3,7},{7,3},{8,12},{12,8},{9,1... | collective-permute-start | bytes 294920 | tf_op jit(solution)/shard_map/ppermute | solution.py:38
  86.0 3.4 %collective-permute-done.9 = bf16[49152]{0:T(1024)(128)(2,1)S(1)} collective-permute-done((bf16[49152]{0:T(1024)(128)(2,1)S(1)}, bf16[49152]{0:T(1024)(128)(2,1)S(1)}, u32[]{:S(2)}, u32[]{:S(2)}) %collective-permute-start.9) | collective-permute-done | bytes 98336 | tf_op jit(solution)/shard_map/ppermute | solution.py:38
  89.5 1.5 %collective-permute-start.10 = (bf16[98304]{0:T(1024)(128)(2,1)S(1)}, bf16[98304]{0:T(1024)(128)(2,1)S(1)}, u32[]{:S(2)}, u32[]{:S(2)}) collective-permute-start(bf16[98304]{0:T(1024)(128)(2,1)S(1)} %maximum_select_fusion.2), channel_id=1, source_target_pairs={{0,16},{8,24},{16,0},{24,8},{1,17},{9,25},{17,1},{25,9},{2,18},{10... | collective-permute-start | bytes 589832 | tf_op jit(solution)/shard_map/ppermute | solution.py:38
  91.0 4.2 %collective-permute-done.10 = bf16[98304]{0:T(1024)(128)(2,1)S(1)} collective-permute-done((bf16[98304]{0:T(1024)(128)(2,1)S(1)}, bf16[98304]{0:T(1024)(128)(2,1)S(1)}, u32[]{:S(2)}, u32[]{:S(2)}) %collective-permute-start.10) | collective-permute-done | bytes 196640 | tf_op jit(solution)/shard_map/ppermute | solution.py:38
  95.2 0.8 maximum_select_fusion.1
  96.1 3.4 %fusion.15 = f32[256,4,3,144]{0,3,2,1:T(8,128)} fusion(bf16[4,3,144,3,136]{2,0,1,3,4:T(4,128)(2,1)S(1)} %copy-done.2, bf16[3,256,256]{2,1,0:T(8,128)(2,1)} %param.8, bf16[256,4,136]{0,2,1:T(8,128)(2,1)} %copy-done.8), kind=kOutput, calls=%fused_computation.16 | convolution fusion | flops 575299584 | bytes 3851264 | tf_op jit(solution)/shard_map/cikq,iapkq->ciap/dot_general | solution.py:107
  99.5 0.3 fusion.29
  99.8 0.8 copy.41
  100.6 1.1 %fusion.71 = bf16[1,256,2,128]{1,3,2,0:T(8,128)(2,1)S(1)} fusion(f32[256,4,3,144]{0,3,2,1:T(8,128)} %fusion.15), kind=kLoop, calls=%fused_computation.111 | loop fusion | flops 196608 | bytes 917504 | tf_op jit(solution)/shard_map/convert_element_type | solution.py:174
  101.7 0.8 copy.42
  102.5 1.1 %select_n.102 = bf16[3,256,256]{2,1,0:T(8,128)(2,1)S(1)} reshape(bf16[196608]{0:T(1024)(128)(2,1)} %maximum_select_fusion.1) | data formatting | bytes 786432 | tf_op jit(solution)/shard_map/jit(_where)/select_n | solution.py:39
  103.6 1.1 %concatenate.56 = bf16[3,256,256]{2,1,0:T(8,128)(2,1)S(1)} reshape(bf16[196608]{0:T(1024)(128)(2,1)} %collective-permute-done.11) | data formatting | bytes 786432 | tf_op jit(solution)/shard_map/concatenate | solution.py:40
  104.8 0.1 fusion.36
  104.9 1.3 %slice_multiply_fusion = (f32[3,256,256]{2,1,0:T(8,128)}, f32[3,256,256]{2,1,0:T(8,128)}) fusion(f32[6,256,256]{2,1,0:T(8,128)S(1)} %fusion.36), kind=kLoop, calls=%fused_computation.43 | loop fusion | flops 393216 | bytes 3145728 | tf_op jit(solution)/shard_map/mul | solution.py:183
  (28 shorter events, 0.3 us)
Async XLA Ops:
  0.6 33.7 %copy-start = (bf16[3,256,256]{2,1,0:T(8,128)(2,1)S(1)}, bf16[3,256,256]{2,1,0:T(8,128)(2,1)}, u32[]{:S(2)}) copy-start(bf16[3,256,256]{2,1,0:T(8,128)(2,1)} %param.9) | copy-start | bytes 1179652
  2.8 7.3 %collective-permute-start.1 = (bf16[512,2,8]{0,2,1:T(8,128)(2,1)S(1)}, bf16[512,2,8]{0,2,1:T(8,128)(2,1)S(1)}, u32[]{:S(2)}, u32[]{:S(2)}) collective-permute-start(bf16[512,2,8]{0,2,1:T(8,128)(2,1)S(1)} %get-tuple-element.23), channel_id=1, source_target_pairs={{0,3},{1,0},{2,1},{3,2},{4,7},{5,4},{6,5},{7,6},{8,11},{9,8},{10,9... | collective-permute-start | bytes 49160 | tf_op jit(solution)/shard_map/ppermute | solution.py:63
  7.9 5.5 %collective-permute-start = (bf16[512,2,8]{0,2,1:T(8,128)(2,1)S(1)}, bf16[512,2,8]{0,2,1:T(8,128)(2,1)S(1)}, u32[]{:S(2)}, u32[]{:S(2)}) collective-permute-start(bf16[512,2,8]{0,2,1:T(8,128)(2,1)S(1)} %get-tuple-element.22), channel_id=1, source_target_pairs={{0,1},{1,2},{2,3},{3,0},{4,5},{5,6},{6,7},{7,4},{8,9},{9,10},{10,1... | collective-permute-start | bytes 49160 | tf_op jit(solution)/shard_map/ppermute | solution.py:62
  13.5 10.8 %collective-permute-start.3 = (bf16[513,2,144]{0,2,1:T(8,128)(2,1)S(1)}, bf16[513,2,144]{0,2,1:T(8,128)(2,1)S(1)}, u32[]{:S(2)}, u32[]{:S(2)}) collective-permute-start(bf16[513,2,144]{0,2,1:T(8,128)(2,1)S(1)} %pad_maximum_fusion.17), channel_id=1, source_target_pairs={{4,0},{5,1},{6,2},{7,3},{12,8},{13,9},{14,10},{15,11},{20,16},{21,... | collective-permute-start | bytes 886472 | tf_op jit(solution)/shard_map/ppermute | solution.py:53
  14.8 10.7 %collective-permute-start.2 = (bf16[513,2,144]{0,2,1:T(8,128)(2,1)S(1)}, bf16[513,2,144]{0,2,1:T(8,128)(2,1)S(1)}, u32[]{:S(2)}, u32[]{:S(2)}) collective-permute-start(bf16[513,2,144]{0,2,1:T(8,128)(2,1)S(1)} %pad_maximum_fusion.17), channel_id=1, source_target_pairs={{0,4},{1,5},{2,6},{3,7},{8,12},{9,13},{10,14},{11,15},{16,20},{17,... | collective-permute-start | bytes 886472 | tf_op jit(solution)/shard_map/ppermute | solution.py:48
  31.1 1.5 %copy-start.1 = (bf16[4,3,144,3,136]{2,0,1,3,4:T(4,128)(2,1)}, bf16[4,3,144,3,136]{2,0,1,3,4:T(4,128)(2,1)S(1)}, u32[]{:S(2)}) copy-start(bf16[4,3,144,3,136]{2,0,1,3,4:T(4,128)(2,1)S(1)} %convert_bitcast_fusion) | copy-start | bytes 4230148
  34.3 6.3 %copy-start.6 = (bf16[3,256,256]{2,1,0:T(8,128)(2,1)S(1)}, bf16[3,256,256]{2,1,0:T(8,128)(2,1)}, u32[]{:S(2)}) copy-start(bf16[3,256,256]{2,1,0:T(8,128)(2,1)} %param.8) | copy-start | bytes 1179652
  40.6 2.6 %copy-start.7 = (bf16[136,128,3,2,3]{1,4,3,2,0:T(4,128)(2,1)S(1)}, bf16[136,128,3,2,3]{1,4,3,2,0:T(4,128)(2,1)}, u32[]{:S(2)}) copy-start(bf16[136,128,3,2,3]{1,4,3,2,0:T(4,128)(2,1)} %fusion.30) | copy-start | bytes 1880068
  43.1 1.3 %copy-start.8 = (bf16[256,4,136]{0,2,1:T(8,128)(2,1)}, bf16[256,4,136]{0,2,1:T(8,128)(2,1)S(1)}, u32[]{:S(2)}) copy-start(bf16[256,4,136]{0,2,1:T(8,128)(2,1)S(1)} %get-tuple-element.17) | copy-start | bytes 835588
  43.1 1.0 copy-start.5
  44.1 0.7 copy-start.3
  47.7 2.4 %collective-permute-start.4 = (f32[196608]{0:T(1024)S(1)}, f32[196608]{0:T(1024)S(1)}, u32[]{:S(2)}, u32[]{:S(2)}) collective-permute-start(f32[196608]{0:T(1024)S(1)} %dynamic_slice.19), channel_id=1, source_target_pairs={{0,8},{8,0},{16,24},{24,16},{1,9},{9,1},{17,25},{25,17},{2,10},{10... | collective-permute-start | bytes 2359304 | tf_op jit(solution)/shard_map/ppermute | solution.py:30
  50.2 11.2 %collective-permute-start.5 = (f32[98304]{0:T(1024)S(1)}, f32[98304]{0:T(1024)S(1)}, u32[]{:S(2)}, u32[]{:S(2)}) collective-permute-start(f32[98304]{0:T(1024)S(1)} %dynamic_slice.21), channel_id=1, source_target_pairs={{0,16},{8,24},{16,0},{24,8},{1,17},{9,25},{17,1},{25,9},{2,18},{10... | collective-permute-start | bytes 1179656 | tf_op jit(solution)/shard_map/ppermute | solution.py:30
  61.4 34.6 %copy-start.2 = (bf16[4,3,144,3,136]{2,0,1,3,4:T(4,128)(2,1)S(1)}, bf16[4,3,144,3,136]{2,0,1,3,4:T(4,128)(2,1)}, u32[]{:S(2)}) copy-start(bf16[4,3,144,3,136]{2,0,1,3,4:T(4,128)(2,1)} %copy-done.1) | copy-start | bytes 4230148
  61.5 7.0 %collective-permute-start.6 = (f32[49152]{0:T(1024)S(1)}, f32[49152]{0:T(1024)}, u32[]{:S(2)}, u32[]{:S(2)}) collective-permute-start(f32[49152]{0:T(1024)S(1)} %dynamic_slice.23), channel_id=1, source_target_pairs={{0,4},{4,0},{1,5},{5,1},{2,6},{6,2},{3,7},{7,3},{8,12},{12,8},{9,1... | collective-permute-start | bytes 589832 | tf_op jit(solution)/shard_map/ppermute | solution.py:30
  69.4 5.7 %collective-permute-start.7 = (f32[49152]{0:T(1024)S(1)}, f32[49152]{0:T(1024)S(1)}, u32[]{:S(2)}, u32[]{:S(2)}) collective-permute-start(f32[49152]{0:T(1024)S(1)} %dynamic-slice_add_fusion.2), channel_id=1, source_target_pairs={{0,1},{1,0},{2,3},{3,2},{4,5},{5,4},{6,7},{7,6},{8,9},{9,8},{10,11... | collective-permute-start | bytes 589832 | tf_op jit(solution)/shard_map/ppermute | solution.py:33
  75.2 9.5 %collective-permute-start.8 = (f32[49152]{0:T(1024)S(1)}, f32[49152]{0:T(1024)S(1)}, u32[]{:S(2)}, u32[]{:S(2)}) collective-permute-start(f32[49152]{0:T(1024)S(1)} %add.139), channel_id=1, source_target_pairs={{0,2},{1,3},{2,0},{3,1},{4,6},{5,7},{6,4},{7,5},{8,10},{9,11},{10,... | collective-permute-start | bytes 589832 | tf_op jit(solution)/shard_map/ppermute | solution.py:33
  84.8 4.7 %collective-permute-start.9 = (bf16[49152]{0:T(1024)(128)(2,1)S(1)}, bf16[49152]{0:T(1024)(128)(2,1)S(1)}, u32[]{:S(2)}, u32[]{:S(2)}) collective-permute-start(bf16[49152]{0:T(1024)(128)(2,1)S(1)} %add_convert_fusion), channel_id=1, source_target_pairs={{0,4},{4,0},{1,5},{5,1},{2,6},{6,2},{3,7},{7,3},{8,12},{12,8},{9,1... | collective-permute-start | bytes 294920 | tf_op jit(solution)/shard_map/ppermute | solution.py:38
  89.5 5.7 %collective-permute-start.10 = (bf16[98304]{0:T(1024)(128)(2,1)S(1)}, bf16[98304]{0:T(1024)(128)(2,1)S(1)}, u32[]{:S(2)}, u32[]{:S(2)}) collective-permute-start(bf16[98304]{0:T(1024)(128)(2,1)S(1)} %maximum_select_fusion.2), channel_id=1, source_target_pairs={{0,16},{8,24},{16,0},{24,8},{1,17},{9,25},{17,1},{25,9},{2,18},{10... | collective-permute-start | bytes 589832 | tf_op jit(solution)/shard_map/ppermute | solution.py:38
  96.1 3.4 %copy-start.4 = (bf16[256,2,3,128]{0,3,2,1:T(8,128)(2,1)S(1)}, bf16[256,2,3,128]{0,3,2,1:T(8,128)(2,1)}, u32[]{:S(2)}) copy-start(bf16[256,2,3,128]{0,3,2,1:T(8,128)(2,1)} %copy-done.3) | copy-start | bytes 1179652
  96.1 7.6 %collective-permute-start.11 = (bf16[196608]{0:T(1024)(128)(2,1)}, bf16[196608]{0:T(1024)(128)(2,1)}, u32[]{:S(2)}, u32[]{:S(2)}) collective-permute-start(bf16[196608]{0:T(1024)(128)(2,1)} %maximum_select_fusion.1), channel_id=1, source_target_pairs={{0,8},{8,0},{16,24},{24,16},{1,9},{9,1},{17,25},{25,17},{2,10},{10... | collective-permute-start | bytes 1179656 | tf_op jit(solution)/shard_map/ppermute | solution.py:38

commit v5 on v4

--- a/solution.py
+++ b/solution.py
@@ -173,14 +173,13 @@
     first_mixed = unmix(first_weight, hidden_grad)
     state_grad = spread_adjoint(first_mixed, near_band).astype(jnp.bfloat16)
 
-    first_sum, second_sum = jnp.split(
-        halving_sum(jnp.concatenate([first_sum, second_sum]), ("ens", "lat", "lon")), 2
-    )
     member_total = state_field.shape[0] * lax.axis_size("ens")
     grad_scale = 1.0 / math.sqrt(
         member_total * row_count * lax.axis_size("lat") * col_count * lax.axis_size("lon")
     )
-    return (layer_output[None], state_grad[None], first_sum * grad_scale, second_sum * grad_scale)
+    first_grad = halving_sum(first_sum * grad_scale, ("ens", "lat", "lon"))
+    second_grad = halving_sum(second_sum * grad_scale, ("ens", "lat", "lon"))
+    return (layer_output[None], state_grad[None], first_grad, second_grad)
 
 
 def solution(mesh):

time: 107 us -> 97.1 us (0.907)
  waiting for transfers between devices: 45.3 us -> 26 us
  starting transfers between devices: 18.1 us -> 27.8 us
  other arithmetic: 5.87 us -> 3.85 us
  matrix products: 24 us -> 25.8 us
    ppermute x2 -> x4, waiting for transfers between devices: 15.1 us -> 7.01 us  [halving_sum(): flat = flat + lax.ppermute(flat, axis, pairs)]
    ppermute x3 -> x6, waiting for transfers between devices: 16.3 us -> 8.76 us  [halving_sum(): flat = keep + lax.ppermute(send, axis, pairs)]
    ppermute x3 -> x6, starting transfers between devices: 2.79 us -> 6.51 us  [halving_sum(): other = lax.ppermute(flat, axis, pairs)]
    ppermute x3 -> x6, starting transfers between devices: 4.19 us -> 7.83 us  [halving_sum(): flat = keep + lax.ppermute(send, axis, pairs)]
    ppermute x3 -> x6, waiting for transfers between devices: 7.63 us -> 4.18 us  [halving_sum(): other = lax.ppermute(flat, axis, pairs)]
    ppermute x2 -> x4, starting transfers between devices: 0.14 us -> 2.47 us  [halving_sum(): flat = flat + lax.ppermute(flat, axis, pairs)]
    convert_element_type x0 -> x2, local copies, waits for them, and re-layouts: none -> 2.2 us  [halving_sum(): return flat.astype(jnp.float32).reshape(value.shape)]
    unnamed x23 -> x24, local copies, waits for them, and re-layouts: 6.86 us -> 5.2 us
  transfers between devices with their start and end apart: 12 -> 20, of which waited for: 10 -> 15; matrix products, arithmetic and copies ran while one was open for 12% -> 14% of each run, Pallas kernels for 0% -> 0%
where the time goes in v5:
time: 97.1 us; the launch traced here: 96.7 us
  starting transfers between devices  27.8 us (29%)
  waiting for transfers between devices  26 us (27%)
  matrix products  25.8 us (27%)
  local copies, waits for them, and re-layouts  12 us (12%)
  other arithmetic  3.85 us (4%)
  between operations  1.19 us (1%)
    dot_general x2, matrix products, spread_adjoint(): jnp.einsum('cikq,iapkq->ciap', mixed, band, preferred_element_type=jnp.fl...  9.48 us
    ppermute x6, waiting for transfers between devices, halving_sum(): flat = keep + lax.ppermute(send, axis, pairs)  8.76 us
    ppermute x6, starting transfers between devices, halving_sum(): flat = keep + lax.ppermute(send, axis, pairs)  7.83 us
    ppermute x4, waiting for transfers between devices, halving_sum(): flat = flat + lax.ppermute(flat, axis, pairs)  7.01 us
    dot_general x3, matrix products, band_of(): jnp.einsum('kiad,dpq->iapkq', stencil, lon_picker(col_count), preferred_e...  6.96 us
    ppermute x6, starting transfers between devices, halving_sum(): other = lax.ppermute(flat, axis, pairs)  6.51 us
    unnamed x24, local copies, waits for them, and re-layouts  5.2 us
    ppermute x1, starting transfers between devices, lon_halo(): lax.ppermute(block[..., :width], 'lon', [(i, (i - 1) % count) for i in ra...  5.13 us
  transfers between devices with their start and end apart: 20, of which 15 were waited for; matrix products, arithmetic and copies ran while one was open for 14% of the time, Pallas kernels for 0%

profile of v5, /device:TPU:0, one launch (start us, length us, event | category | flops | bytes accessed | tf_op | source)
XLA Modules:
  0.0 96.7 jit_solution(8604964732502562671)
XLA Ops:
  0.6 1.1 %copy.26 = bf16[1,256,2,128]{1,3,2,0:T(8,128)(2,1)S(1)} copy(bf16[1,256,2,128]{3,2,1,0:T(2,128)(2,1)} %param.13) | data formatting | bytes 262144 | tf_op args[6]
  1.7 1.0 %copy.25 = bf16[1,256,2,128]{1,3,2,0:T(8,128)(2,1)S(1)} copy(bf16[1,256,2,128]{3,2,1,0:T(2,128)(2,1)} %param.7) | data formatting | bytes 262144 | tf_op args[0]
  2.8 5.1 %collective-permute-start.1 = (bf16[512,2,8]{0,2,1:T(8,128)(2,1)S(1)}, bf16[512,2,8]{0,2,1:T(8,128)(2,1)S(1)}, u32[]{:S(2)}, u32[]{:S(2)}) collective-permute-start(bf16[512,2,8]{0,2,1:T(8,128)(2,1)S(1)} %get-tuple-element.21), channel_id=1, source_target_pairs={{0,3},{1,0},{2,1},{3,2},{4,7},{5,4},{6,5},{7,6},{8,11},{9,8},{10,9... | collective-permute-start | bytes 49160 | tf_op jit(solution)/shard_map/ppermute | solution.py:63
  7.9 0.1 fusion.42
  8.0 0.1 fusion.21
  8.1 0.7 broadcast_add_fusion
  8.8 0.9 convolution_convert_fusion.2
  9.7 0.1 reshape.80
  9.8 0.2 copy.28
  10.0 3.4 %collective-permute-done = bf16[512,2,8]{0,2,1:T(8,128)(2,1)S(1)} collective-permute-done((bf16[512,2,8]{0,2,1:T(8,128)(2,1)S(1)}, bf16[512,2,8]{0,2,1:T(8,128)(2,1)S(1)}, u32[]{:S(2)}, u32[]{:S(2)}) %collective-permute-start) | collective-permute-done | bytes 16416 | tf_op jit(solution)/shard_map/ppermute | solution.py:62
  13.5 1.3 %collective-permute-start.3 = (bf16[513,2,144]{0,2,1:T(8,128)(2,1)S(1)}, bf16[513,2,144]{0,2,1:T(8,128)(2,1)S(1)}, u32[]{:S(2)}, u32[]{:S(2)}) collective-permute-start(bf16[513,2,144]{0,2,1:T(8,128)(2,1)S(1)} %pad_maximum_fusion.16), channel_id=1, source_target_pairs={{4,0},{5,1},{6,2},{7,3},{12,8},{13,9},{14,10},{15,11},{20,16},{21,... | collective-permute-start | bytes 886472 | tf_op jit(solution)/shard_map/ppermute | solution.py:53
  14.8 4.6 %collective-permute-start.2 = (bf16[513,2,144]{0,2,1:T(8,128)(2,1)S(1)}, bf16[513,2,144]{0,2,1:T(8,128)(2,1)S(1)}, u32[]{:S(2)}, u32[]{:S(2)}) collective-permute-start(bf16[513,2,144]{0,2,1:T(8,128)(2,1)S(1)} %pad_maximum_fusion.16), channel_id=1, source_target_pairs={{0,4},{1,5},{2,6},{3,7},{8,12},{9,13},{10,14},{11,15},{16,20},{17,... | collective-permute-start | bytes 886472 | tf_op jit(solution)/shard_map/ppermute | solution.py:48
  19.4 1.8 %copy.53 = pred[9,152,144,1,1]{1,0,4,3,2:T(8,128)(4,1)S(1)} copy(pred[9,152,144,1,1]{2,1,0,3,4:T(8,128)(4,1)S(1)} %fusion.21) | data formatting | bytes 393984 | tf_op jit(solution)/shard_map/eq | solution.py:85
  21.2 1.6 %fusion.34 = bf16[136,128,3,2,3]{1,4,3,2,0:T(4,128)(2,1)} fusion(pred[9,136,128,1,1]{2,1,0,3,4:T(8,128)(4,1)S(1)} %fusion.42, bf16[3,2,3,9]{3,2,1,0:T(4,128)(2,1)S(1)} %convolution_convert_fusion.2), kind=kOutput, calls=%fused_computation.36 | convolution fusion | flops 5640192 | bytes 783684 | tf_op jit(solution)/shard_map/kiad,dpq->iapkq/dot_general | solution.py:90
  22.8 1.5 %collective-permute-done.3 = bf16[513,2,144]{0,2,1:T(8,128)(2,1)S(1)} collective-permute-done((bf16[513,2,144]{0,2,1:T(8,128)(2,1)S(1)}, bf16[513,2,144]{0,2,1:T(8,128)(2,1)S(1)}, u32[]{:S(2)}, u32[]{:S(2)}) %collective-permute-start.3) | collective-permute-done | bytes 295520 | tf_op jit(solution)/shard_map/ppermute | solution.py:53
  24.3 1.2 %collective-permute-done.2 = bf16[513,2,144]{0,2,1:T(8,128)(2,1)S(1)} collective-permute-done((bf16[513,2,144]{0,2,1:T(8,128)(2,1)S(1)}, bf16[513,2,144]{0,2,1:T(8,128)(2,1)S(1)}, u32[]{:S(2)}, u32[]{:S(2)}) %collective-permute-start.2) | collective-permute-done | bytes 295520 | tf_op jit(solution)/shard_map/ppermute | solution.py:48
  25.5 0.1 maximum_reduce_fusion
  25.6 0.1 reshape_squeeze.3
  25.7 3.9 %fusion.80 = bf16[152,144,3,6,3]{0,3,4,2,1:T(8,128)(2,1)} fusion(pred[9,152,144,1,1]{1,0,4,3,2:T(8,128)(4,1)S(1)} %copy.53, bf16[6,3,3,9]{3,2,1,0:T(4,128)(2,1)S(1)} %reshape_squeeze.3), kind=kOutput, calls=%fused_computation.126 | convolution fusion | flops 21275136 | bytes 2561868 | tf_op jit(solution)/shard_map/kiad,dpq->iapkq/dot_general | solution.py:90
  29.7 1.5 %convert_bitcast_fusion = bf16[4,3,144,3,136]{2,0,1,3,4:T(4,128)(2,1)S(1)} fusion(bf16[3,6,3,9]{3,1,2,0:T(8,128)(2,1)S(1)} %bitcast.202), kind=kOutput, calls=%fused_computation.8 | convolution fusion | flops 13747968 | bytes 1419264 | tf_op jit(solution)/shard_map/kiad,dpq->iapkq/dot_general | solution.py:90
  31.3 1.7 %fusion.23 = bf16[256,4,3,136]{0,3,2,1:T(8,128)(2,1)} fusion(bf16[4,3,144,3,136]{2,0,1,3,4:T(4,128)(2,1)S(1)} %convert_bitcast_fusion, bf16[256,4,1,144]{0,3,2,1:T(8,128)(2,1)S(1)} %get-tuple-element.14, bf16[256,4,1,144]{0,3,2,1:T(8,128)(2,1)S(1)} %get-tuple-element.13, bf16[256,4,1,144]{0,3,2,1:T(8,128)(2,1)S(1)} %get-tuple-element.12), kind=kOutput, calls=%fused_computation.21 | convolution fusion | flops 362274816 | bytes 3130368 | tf_op jit(solution)/shard_map/ciap,iapkq->cikq/dot_general | solution.py:101
  32.9 6.2 %fusion.12 = f32[256,6,3,152]{0,3,1,2:T(8,128)} fusion(bf16[513,2,144]{0,2,1:T(8,128)(2,1)S(1)} %collective-permute-done.3, bf16[513,2,144]{0,2,1:T(8,128)(2,1)} %copy-done.1, bf16[1,2,144]{0,2,1:T(8,128)(2,1)} %copy-done.3, bf16[512,2,8]{0,2,1:T(8,128)(2,1)S(1)} %collective-permute-done.1, bf16[512,2,8]{0,2,1:T(8,128)(2,1)} %copy-done.6, ...), kind=kOutput, calls=%fused_computation.12 | convolution fusion | flops 948658176 | bytes 6445248 | tf_op jit(solution)/shard_map/cikq,iapkq->ciap/dot_general | solution.py:107
  39.2 3.2 %fusion.46 = (bf16[256,4,136]{0,2,1:T(8,128)(2,1)S(1)}, bf16[256,4,136]{0,2,1:T(8,128)(2,1)}) fusion(f32[256,6,3,152]{0,3,1,2:T(8,128)} %fusion.12, pred[4]{0:T(512)(128)(4,1)S(1)} %compare_and_fusion, bf16[256,4,3,136]{0,3,2,1:T(8,128)(2,1)} %fusion.23, bf16[3,256,256]{2,1,0:T(8,128)(2,1)} %param.8), kind=kOutput, calls=%fused_computation.54 | convolution fusion | flops 217808896 | bytes 3457028 | tf_op jit(solution)/shard_map/koc,cikj->oij/dot_general | solution.py:118
  42.4 0.7 copy-done.8
  43.1 3.3 %fusion.15 = f32[256,4,3,144]{0,3,2,1:T(8,128)} fusion(bf16[4,3,144,3,136]{2,0,1,3,4:T(4,128)(2,1)S(1)} %convert_bitcast_fusion, bf16[3,256,256]{2,1,0:T(8,128)(2,1)} %param.8, bf16[256,4,136]{0,2,1:T(8,128)(2,1)S(1)} %get-tuple-element.15), kind=kOutput, calls=%fused_computation.15 | convolution fusion | flops 575299584 | bytes 3851264 | tf_op jit(solution)/shard_map/cikq,iapkq->ciap/dot_general | solution.py:107
  46.4 1.4 %fusion.29 = f32[3,256,256]{1,2,0:T(8,128)S(1)} fusion(bf16[256,4,3,136]{0,3,2,1:T(8,128)(2,1)} %fusion.23, bf16[256,4,136]{0,2,1:T(8,128)(2,1)} %copy-done.8), kind=kOutput, calls=%fused_computation.28 | convolution fusion | flops 100859904 | bytes 1310720 | tf_op jit(solution)/shard_map/oij,cikj->koc/dot_general | solution.py:128
  47.7 1.1 %slice_bitcast_fusion.2 = (bf16[256,2,1,136]{0,3,1,2:T(8,128)(2,1)S(1)}, bf16[256,2,1,136]{0,3,1,2:T(8,128)(2,1)S(1)}, bf16[256,2,1,136]{0,3,1,2:T(8,128)(2,1)S(1)}) fusion(bf16[256,4,136]{0,2,1:T(8,128)(2,1)} %get-tuple-element.16), kind=kLoop, calls=%fused_computation.112 | loop fusion | bytes 835584 | tf_op jit(solution)/shard_map/stack | solution.py:98
  48.8 0.3 copy.38
  49.1 0.4 copy.71
  49.5 0.8 dynamic_slice.37
  50.3 1.6 %fusion.31 = bf16[256,2,3,128]{0,3,2,1:T(8,128)(2,1)S(1)} fusion(bf16[136,128,3,2,3]{1,4,3,2,0:T(4,128)(2,1)} %fusion.34, bf16[256,2,1,136]{0,3,1,2:T(8,128)(2,1)S(1)} %get-tuple-element.18, bf16[256,2,1,136]{0,3,1,2:T(8,128)(2,1)S(1)} %get-tuple-element.19, bf16[256,2,1,136]{0,3,1,2:T(8,128)(2,1)S(1)} %get-tuple-element.17), kind=kOutput, calls=%fused_computation.32 | convolution fusion | flops 161046528 | bytes 1437696 | tf_op jit(solution)/shard_map/ciap,iapkq->cikq/dot_general | solution.py:101
  51.9 0.3 fusion.27
  52.2 0.3 copy.41
  52.5 0.4 copy.72
  52.9 0.6 collective-permute-start.12
  53.5 1.1 %fusion.76 = bf16[1,256,2,128]{1,3,2,0:T(8,128)(2,1)S(1)} fusion(f32[256,4,3,144]{0,3,2,1:T(8,128)} %fusion.15), kind=kLoop, calls=%fused_computation.114 | loop fusion | flops 196608 | bytes 917504 | tf_op jit(solution)/shard_map/convert_element_type | solution.py:174
  54.7 1.0 %dynamic-slice_add_fusion.1 = f32[98304]{0:T(1024)S(1)} fusion(f32[98304]{0:T(1024)} %collective-permute-done.4, f32[196608]{0:T(1024)S(1)} %bitcast.199, s32[]{:T(128)S(6)} %select_n.128), kind=kLoop, calls=%fused_computation.86 | loop fusion | flops 98304 | bytes 1179652 | tf_op jit(solution)/shard_map/add | solution.py:30
  55.7 1.6 %collective-permute-start.5 = (f32[49152]{0:T(1024)S(1)}, f32[49152]{0:T(1024)S(1)}, u32[]{:S(2)}, u32[]{:S(2)}) collective-permute-start(f32[49152]{0:T(1024)S(1)} %dynamic_slice.39), channel_id=1, source_target_pairs={{0,16},{8,24},{16,0},{24,8},{1,17},{9,25},{17,1},{25,9},{2,18},{10... | collective-permute-start | bytes 589832 | tf_op jit(solution)/shard_map/ppermute | solution.py:30
  57.4 0.6 collective-permute-start.13
  58.0 5.6 %collective-permute-done.5 = f32[49152]{0:T(1024)S(1)} collective-permute-done((f32[49152]{0:T(1024)S(1)}, f32[49152]{0:T(1024)S(1)}, u32[]{:S(2)}, u32[]{:S(2)}) %collective-permute-start.5) | collective-permute-done | bytes 196640 | tf_op jit(solution)/shard_map/ppermute | solution.py:30
  63.6 2.6 %collective-permute-start.6 = (f32[24576]{0:T(1024)S(1)}, f32[24576]{0:T(1024)S(1)}, u32[]{:S(2)}, u32[]{:S(2)}) collective-permute-start(f32[24576]{0:T(1024)S(1)} %dynamic_slice.41), channel_id=1, source_target_pairs={{0,4},{4,0},{1,5},{5,1},{2,6},{6,2},{3,7},{7,3},{8,12},{12,8},{9,1... | collective-permute-start | bytes 294920 | tf_op jit(solution)/shard_map/ppermute | solution.py:30
  66.2 0.7 collective-permute-done.13
  66.9 2.6 %collective-permute-start.14 = (f32[24576]{0:T(1024)S(1)}, f32[24576]{0:T(1024)S(1)}, u32[]{:S(2)}, u32[]{:S(2)}) collective-permute-start(f32[24576]{0:T(1024)S(1)} %dynamic_slice.47), channel_id=1, source_target_pairs={{0,4},{4,0},{1,5},{5,1},{2,6},{6,2},{3,7},{7,3},{8,12},{12,8},{9,1... | collective-permute-start | bytes 294920 | tf_op jit(solution)/shard_map/ppermute | solution.py:30
  69.6 2.5 %collective-permute-done.14 = f32[24576]{0:T(1024)S(1)} collective-permute-done((f32[24576]{0:T(1024)S(1)}, f32[24576]{0:T(1024)S(1)}, u32[]{:S(2)}, u32[]{:S(2)}) %collective-permute-start.14) | collective-permute-done | bytes 98336 | tf_op jit(solution)/shard_map/ppermute | solution.py:30
  72.1 3.0 %collective-permute-done.7 = f32[24576]{0:T(1024)S(1)} collective-permute-done((f32[24576]{0:T(1024)S(1)}, f32[24576]{0:T(1024)S(1)}, u32[]{:S(2)}, u32[]{:S(2)}) %collective-permute-start.7) | collective-permute-done | bytes 98336 | tf_op jit(solution)/shard_map/ppermute | solution.py:33
  75.2 0.3 fusion.33
  75.5 0.8 copy.42
  76.3 0.8 copy.43
  77.1 0.7 collective-permute-done.15
  77.8 2.3 %collective-permute-start.16 = (f32[24576]{0:T(1024)S(1)}, f32[24576]{0:T(1024)S(1)}, u32[]{:S(2)}, u32[]{:S(2)}) collective-permute-start(f32[24576]{0:T(1024)S(1)} %add.171), channel_id=1, source_target_pairs={{0,2},{1,3},{2,0},{3,1},{4,6},{5,7},{6,4},{7,5},{8,10},{9,11},{10,... | collective-permute-start | bytes 294920 | tf_op jit(solution)/shard_map/ppermute | solution.py:33
  80.1 2.9 %collective-permute-done.8 = f32[24576]{0:T(1024)S(1)} collective-permute-done((f32[24576]{0:T(1024)S(1)}, f32[24576]{0:T(1024)S(1)}, u32[]{:S(2)}, u32[]{:S(2)}) %collective-permute-start.8) | collective-permute-done | bytes 98336 | tf_op jit(solution)/shard_map/ppermute | solution.py:33
  82.9 1.6 %collective-permute-start.9 = (bf16[24576]{0:T(1024)(128)(2,1)S(1)}, bf16[24576]{0:T(1024)(128)(2,1)S(1)}, u32[]{:S(2)}, u32[]{:S(2)}) collective-permute-start(bf16[24576]{0:T(1024)(128)(2,1)S(1)} %add_convert_fusion.1), channel_id=1, source_target_pairs={{0,4},{4,0},{1,5},{5,1},{2,6},{6,2},{3,7},{7,3},{8,12},{12,8},{9,1... | collective-permute-start | bytes 147464 | tf_op jit(solution)/shard_map/ppermute | solution.py:38
  84.6 0.5 collective-permute-done.16
  85.1 1.6 %collective-permute-start.17 = (bf16[24576]{0:T(1024)(128)(2,1)S(1)}, bf16[24576]{0:T(1024)(128)(2,1)S(1)}, u32[]{:S(2)}, u32[]{:S(2)}) collective-permute-start(bf16[24576]{0:T(1024)(128)(2,1)S(1)} %add_convert_fusion), channel_id=1, source_target_pairs={{0,4},{4,0},{1,5},{5,1},{2,6},{6,2},{3,7},{7,3},{8,12},{12,8},{9,1... | collective-permute-start | bytes 147464 | tf_op jit(solution)/shard_map/ppermute | solution.py:38
  86.7 0.4 collective-permute-done.9
  87.1 1.6 %collective-permute-start.10 = (bf16[49152]{0:T(1024)(128)(2,1)S(1)}, bf16[49152]{0:T(1024)(128)(2,1)S(1)}, u32[]{:S(2)}, u32[]{:S(2)}) collective-permute-start(bf16[49152]{0:T(1024)(128)(2,1)S(1)} %maximum_select_fusion.4), channel_id=1, source_target_pairs={{0,16},{8,24},{16,0},{24,8},{1,17},{9,25},{17,1},{25,9},{2,18},{10... | collective-permute-start | bytes 294920 | tf_op jit(solution)/shard_map/ppermute | solution.py:38
  88.7 0.5 collective-permute-done.17
  89.2 1.6 %collective-permute-start.18 = (bf16[49152]{0:T(1024)(128)(2,1)S(1)}, bf16[49152]{0:T(1024)(128)(2,1)S(1)}, u32[]{:S(2)}, u32[]{:S(2)}) collective-permute-start(bf16[49152]{0:T(1024)(128)(2,1)S(1)} %maximum_select_fusion.5), channel_id=1, source_target_pairs={{0,16},{8,24},{16,0},{24,8},{1,17},{9,25},{17,1},{25,9},{2,18},{10... | collective-permute-start | bytes 294920 | tf_op jit(solution)/shard_map/ppermute | solution.py:38
  90.8 1.0 %collective-permute-done.10 = bf16[49152]{0:T(1024)(128)(2,1)S(1)} collective-permute-done((bf16[49152]{0:T(1024)(128)(2,1)S(1)}, bf16[49152]{0:T(1024)(128)(2,1)S(1)}, u32[]{:S(2)}, u32[]{:S(2)}) %collective-permute-start.10) | collective-permute-done | bytes 98336 | tf_op jit(solution)/shard_map/ppermute | solution.py:38
  91.9 2.0 %collective-permute-done.18 = bf16[49152]{0:T(1024)(128)(2,1)S(1)} collective-permute-done((bf16[49152]{0:T(1024)(128)(2,1)S(1)}, bf16[49152]{0:T(1024)(128)(2,1)S(1)}, u32[]{:S(2)}, u32[]{:S(2)}) %collective-permute-start.18) | collective-permute-done | bytes 98336 | tf_op jit(solution)/shard_map/ppermute | solution.py:38
  94.1 0.1 fusion.62
  94.1 1.1 %reshape.84 = f32[3,256,256]{2,1,0:T(8,128)} reshape(f32[196608]{0:T(1024)S(1)} %fusion.62) | data formatting | bytes 1572864 | tf_op jit(solution)/shard_map/convert_element_type | solution.py:42
  95.2 0.2 collective-permute-done.19
  95.6 1.1 %reshape.85 = f32[3,256,256]{2,1,0:T(8,128)} reshape(f32[196608]{0:T(1024)S(1)} %fusion.63) | data formatting | bytes 1572864 | tf_op jit(solution)/shard_map/convert_element_type | solution.py:42
  (55 shorter events, 1.1 us)
Async XLA Ops:
  0.6 32.3 %copy-start = (bf16[3,256,256]{2,1,0:T(8,128)(2,1)S(1)}, bf16[3,256,256]{2,1,0:T(8,128)(2,1)}, u32[]{:S(2)}) copy-start(bf16[3,256,256]{2,1,0:T(8,128)(2,1)} %param.9) | copy-start | bytes 1179652
  2.8 7.3 %collective-permute-start.1 = (bf16[512,2,8]{0,2,1:T(8,128)(2,1)S(1)}, bf16[512,2,8]{0,2,1:T(8,128)(2,1)S(1)}, u32[]{:S(2)}, u32[]{:S(2)}) collective-permute-start(bf16[512,2,8]{0,2,1:T(8,128)(2,1)S(1)} %get-tuple-element.21), channel_id=1, source_target_pairs={{0,3},{1,0},{2,1},{3,2},{4,7},{5,4},{6,5},{7,6},{8,11},{9,8},{10,9... | collective-permute-start | bytes 49160 | tf_op jit(solution)/shard_map/ppermute | solution.py:63
  7.9 5.5 %collective-permute-start = (bf16[512,2,8]{0,2,1:T(8,128)(2,1)S(1)}, bf16[512,2,8]{0,2,1:T(8,128)(2,1)S(1)}, u32[]{:S(2)}, u32[]{:S(2)}) collective-permute-start(bf16[512,2,8]{0,2,1:T(8,128)(2,1)S(1)} %get-tuple-element.20), channel_id=1, source_target_pairs={{0,1},{1,2},{2,3},{3,0},{4,5},{5,6},{6,7},{7,4},{8,9},{9,10},{10,1... | collective-permute-start | bytes 49160 | tf_op jit(solution)/shard_map/ppermute | solution.py:62
  10.0 19.6 %copy-start.3 = (bf16[1,2,144]{0,2,1:T(8,128)(2,1)}, bf16[1,2,144]{0,2,1:T(8,128)(2,1)S(1)}, u32[]{:S(2)}) copy-start(bf16[1,2,144]{0,2,1:T(8,128)(2,1)S(1)} %copy.28) | copy-start | bytes 1732
  13.4 16.2 %copy-start.6 = (bf16[512,2,8]{0,2,1:T(8,128)(2,1)}, bf16[512,2,8]{0,2,1:T(8,128)(2,1)S(1)}, u32[]{:S(2)}) copy-start(bf16[512,2,8]{0,2,1:T(8,128)(2,1)S(1)} %collective-permute-done) | copy-start | bytes 49156
  13.5 10.8 %collective-permute-start.3 = (bf16[513,2,144]{0,2,1:T(8,128)(2,1)S(1)}, bf16[513,2,144]{0,2,1:T(8,128)(2,1)S(1)}, u32[]{:S(2)}, u32[]{:S(2)}) collective-permute-start(bf16[513,2,144]{0,2,1:T(8,128)(2,1)S(1)} %pad_maximum_fusion.16), channel_id=1, source_target_pairs={{4,0},{5,1},{6,2},{7,3},{12,8},{13,9},{14,10},{15,11},{20,16},{21,... | collective-permute-start | bytes 886472 | tf_op jit(solution)/shard_map/ppermute | solution.py:53
  14.8 10.7 %collective-permute-start.2 = (bf16[513,2,144]{0,2,1:T(8,128)(2,1)S(1)}, bf16[513,2,144]{0,2,1:T(8,128)(2,1)S(1)}, u32[]{:S(2)}, u32[]{:S(2)}) collective-permute-start(bf16[513,2,144]{0,2,1:T(8,128)(2,1)S(1)} %pad_maximum_fusion.16), channel_id=1, source_target_pairs={{0,4},{1,5},{2,6},{3,7},{8,12},{9,13},{10,14},{11,15},{16,20},{17,... | collective-permute-start | bytes 886472 | tf_op jit(solution)/shard_map/ppermute | solution.py:48
  25.5 4.2 %copy-start.1 = (bf16[513,2,144]{0,2,1:T(8,128)(2,1)}, bf16[513,2,144]{0,2,1:T(8,128)(2,1)S(1)}, u32[]{:S(2)}) copy-start(bf16[513,2,144]{0,2,1:T(8,128)(2,1)S(1)} %collective-permute-done.2) | copy-start | bytes 886468
  29.6 1.5 %copy-start.2 = (bf16[513,2,144]{0,2,1:T(8,128)(2,1)S(1)}, bf16[513,2,144]{0,2,1:T(8,128)(2,1)}, u32[]{:S(2)}) copy-start(bf16[513,2,144]{0,2,1:T(8,128)(2,1)} %copy-done.1) | copy-start | bytes 886468
  29.6 1.6 %copy-start.4 = (bf16[1,2,144]{0,2,1:T(8,128)(2,1)S(1)}, bf16[1,2,144]{0,2,1:T(8,128)(2,1)}, u32[]{:S(2)}) copy-start(bf16[1,2,144]{0,2,1:T(8,128)(2,1)} %copy-done.3) | copy-start | bytes 1732
  29.6 1.5 %copy-start.7 = (bf16[512,2,8]{0,2,1:T(8,128)(2,1)S(1)}, bf16[512,2,8]{0,2,1:T(8,128)(2,1)}, u32[]{:S(2)}) copy-start(bf16[512,2,8]{0,2,1:T(8,128)(2,1)} %copy-done.6) | copy-start | bytes 49156
  42.4 0.7 copy-start.8
  49.1 2.8 %copy-start.5 = (bf16[1,256,2,128]{3,2,1,0:T(2,128)(2,1)S(1)}, bf16[1,256,2,128]{3,2,1,0:T(2,128)(2,1)}, u32[]{:S(2)}) copy-start(bf16[1,256,2,128]{3,2,1,0:T(2,128)(2,1)} %param.13) | copy-start | bytes 393220
  50.3 4.4 %collective-permute-start.4 = (f32[98304]{0:T(1024)}, f32[98304]{0:T(1024)}, u32[]{:S(2)}, u32[]{:S(2)}) collective-permute-start(f32[98304]{0:T(1024)} %dynamic_slice.37), channel_id=1, source_target_pairs={{0,8},{8,0},{16,24},{24,16},{1,9},{9,1},{17,25},{25,17},{2,10},{10... | collective-permute-start | bytes 1179656 | tf_op jit(solution)/shard_map/ppermute | solution.py:30
  52.9 4.4 %collective-permute-start.12 = (f32[98304]{0:T(1024)S(1)}, f32[98304]{0:T(1024)S(1)}, u32[]{:S(2)}, u32[]{:S(2)}) collective-permute-start(f32[98304]{0:T(1024)S(1)} %dynamic_slice.43), channel_id=1, source_target_pairs={{0,8},{8,0},{16,24},{24,16},{1,9},{9,1},{17,25},{25,17},{2,10},{10... | collective-permute-start | bytes 1179656 | tf_op jit(solution)/shard_map/ppermute | solution.py:30
  55.7 7.8 %collective-permute-start.5 = (f32[49152]{0:T(1024)S(1)}, f32[49152]{0:T(1024)S(1)}, u32[]{:S(2)}, u32[]{:S(2)}) collective-permute-start(f32[49152]{0:T(1024)S(1)} %dynamic_slice.39), channel_id=1, source_target_pairs={{0,16},{8,24},{16,0},{24,8},{1,17},{9,25},{17,1},{25,9},{2,18},{10... | collective-permute-start | bytes 589832 | tf_op jit(solution)/shard_map/ppermute | solution.py:30
  57.4 9.5 %collective-permute-start.13 = (f32[49152]{0:T(1024)S(1)}, f32[49152]{0:T(1024)S(1)}, u32[]{:S(2)}, u32[]{:S(2)}) collective-permute-start(f32[49152]{0:T(1024)S(1)} %dynamic_slice.45), channel_id=1, source_target_pairs={{0,16},{8,24},{16,0},{24,8},{1,17},{9,25},{17,1},{25,9},{2,18},{10... | collective-permute-start | bytes 589832 | tf_op jit(solution)/shard_map/ppermute | solution.py:30
  63.6 5.8 %collective-permute-start.6 = (f32[24576]{0:T(1024)S(1)}, f32[24576]{0:T(1024)S(1)}, u32[]{:S(2)}, u32[]{:S(2)}) collective-permute-start(f32[24576]{0:T(1024)S(1)} %dynamic_slice.41), channel_id=1, source_target_pairs={{0,4},{4,0},{1,5},{5,1},{2,6},{6,2},{3,7},{7,3},{8,12},{12,8},{9,1... | collective-permute-start | bytes 294920 | tf_op jit(solution)/shard_map/ppermute | solution.py:30
  66.9 5.1 %collective-permute-start.14 = (f32[24576]{0:T(1024)S(1)}, f32[24576]{0:T(1024)S(1)}, u32[]{:S(2)}, u32[]{:S(2)}) collective-permute-start(f32[24576]{0:T(1024)S(1)} %dynamic_slice.47), channel_id=1, source_target_pairs={{0,4},{4,0},{1,5},{5,1},{2,6},{6,2},{3,7},{7,3},{8,12},{12,8},{9,1... | collective-permute-start | bytes 294920 | tf_op jit(solution)/shard_map/ppermute | solution.py:30
  69.5 5.6 %collective-permute-start.7 = (f32[24576]{0:T(1024)S(1)}, f32[24576]{0:T(1024)S(1)}, u32[]{:S(2)}, u32[]{:S(2)}) collective-permute-start(f32[24576]{0:T(1024)S(1)} %dynamic-slice_add_fusion.5), channel_id=1, source_target_pairs={{0,1},{1,0},{2,3},{3,2},{4,5},{5,4},{6,7},{7,6},{8,9},{9,8},{10,11... | collective-permute-start | bytes 294920 | tf_op jit(solution)/shard_map/ppermute | solution.py:33
  72.1 5.7 %collective-permute-start.15 = (f32[24576]{0:T(1024)S(1)}, f32[24576]{0:T(1024)S(1)}, u32[]{:S(2)}, u32[]{:S(2)}) collective-permute-start(f32[24576]{0:T(1024)S(1)} %dynamic-slice_add_fusion.4), channel_id=1, source_target_pairs={{0,1},{1,0},{2,3},{3,2},{4,5},{5,4},{6,7},{7,6},{8,9},{9,8},{10,11... | collective-permute-start | bytes 294920 | tf_op jit(solution)/shard_map/ppermute | solution.py:33
  75.1 7.8 %collective-permute-start.8 = (f32[24576]{0:T(1024)S(1)}, f32[24576]{0:T(1024)S(1)}, u32[]{:S(2)}, u32[]{:S(2)}) collective-permute-start(f32[24576]{0:T(1024)S(1)} %add.166), channel_id=1, source_target_pairs={{0,2},{1,3},{2,0},{3,1},{4,6},{5,7},{6,4},{7,5},{8,10},{9,11},{10,... | collective-permute-start | bytes 294920 | tf_op jit(solution)/shard_map/ppermute | solution.py:33
  77.8 7.2 %collective-permute-start.16 = (f32[24576]{0:T(1024)S(1)}, f32[24576]{0:T(1024)S(1)}, u32[]{:S(2)}, u32[]{:S(2)}) collective-permute-start(f32[24576]{0:T(1024)S(1)} %add.171), channel_id=1, source_target_pairs={{0,2},{1,3},{2,0},{3,1},{4,6},{5,7},{6,4},{7,5},{8,10},{9,11},{10,... | collective-permute-start | bytes 294920 | tf_op jit(solution)/shard_map/ppermute | solution.py:33
  82.9 4.2 %collective-permute-start.9 = (bf16[24576]{0:T(1024)(128)(2,1)S(1)}, bf16[24576]{0:T(1024)(128)(2,1)S(1)}, u32[]{:S(2)}, u32[]{:S(2)}) collective-permute-start(bf16[24576]{0:T(1024)(128)(2,1)S(1)} %add_convert_fusion.1), channel_id=1, source_target_pairs={{0,4},{4,0},{1,5},{5,1},{2,6},{6,2},{3,7},{7,3},{8,12},{12,8},{9,1... | collective-permute-start | bytes 147464 | tf_op jit(solution)/shard_map/ppermute | solution.py:38
  85.1 4.2 %collective-permute-start.17 = (bf16[24576]{0:T(1024)(128)(2,1)S(1)}, bf16[24576]{0:T(1024)(128)(2,1)S(1)}, u32[]{:S(2)}, u32[]{:S(2)}) collective-permute-start(bf16[24576]{0:T(1024)(128)(2,1)S(1)} %add_convert_fusion), channel_id=1, source_target_pairs={{0,4},{4,0},{1,5},{5,1},{2,6},{6,2},{3,7},{7,3},{8,12},{12,8},{9,1... | collective-permute-start | bytes 147464 | tf_op jit(solution)/shard_map/ppermute | solution.py:38
  87.1 4.7 %collective-permute-start.10 = (bf16[49152]{0:T(1024)(128)(2,1)S(1)}, bf16[49152]{0:T(1024)(128)(2,1)S(1)}, u32[]{:S(2)}, u32[]{:S(2)}) collective-permute-start(bf16[49152]{0:T(1024)(128)(2,1)S(1)} %maximum_select_fusion.4), channel_id=1, source_target_pairs={{0,16},{8,24},{16,0},{24,8},{1,17},{9,25},{17,1},{25,9},{2,18},{10... | collective-permute-start | bytes 294920 | tf_op jit(solution)/shard_map/ppermute | solution.py:38
  89.2 4.7 %collective-permute-start.18 = (bf16[49152]{0:T(1024)(128)(2,1)S(1)}, bf16[49152]{0:T(1024)(128)(2,1)S(1)}, u32[]{:S(2)}, u32[]{:S(2)}) collective-permute-start(bf16[49152]{0:T(1024)(128)(2,1)S(1)} %maximum_select_fusion.5), channel_id=1, source_target_pairs={{0,16},{8,24},{16,0},{24,8},{1,17},{9,25},{17,1},{25,9},{2,18},{10... | collective-permute-start | bytes 294920 | tf_op jit(solution)/shard_map/ppermute | solution.py:38
  91.9 2.2 %collective-permute-start.11 = (bf16[98304]{0:T(1024)(128)(2,1)S(1)}, bf16[98304]{0:T(1024)(128)(2,1)S(1)}, u32[]{:S(2)}, u32[]{:S(2)}) collective-permute-start(bf16[98304]{0:T(1024)(128)(2,1)S(1)} %maximum_select_fusion.2), channel_id=1, source_target_pairs={{0,8},{8,0},{16,24},{24,16},{1,9},{9,1},{17,25},{25,17},{2,10},{10... | collective-permute-start | bytes 589832 | tf_op jit(solution)/shard_map/ppermute | solution.py:38
  94.0 1.5 %collective-permute-start.19 = (bf16[98304]{0:T(1024)(128)(2,1)S(1)}, bf16[98304]{0:T(1024)(128)(2,1)S(1)}, u32[]{:S(2)}, u32[]{:S(2)}) collective-permute-start(bf16[98304]{0:T(1024)(128)(2,1)S(1)} %maximum_select_fusion.3), channel_id=1, source_target_pairs={{0,8},{8,0},{16,24},{24,16},{1,9},{9,1},{17,25},{25,17},{2,10},{10... | collective-permute-start | bytes 589832 | tf_op jit(solution)/shard_map/ppermute | solution.py:38

commit v6 on v5

--- a/solution.py
+++ b/solution.py
@@ -11,7 +11,7 @@
 LON_HALO = 2 * LON_REACH
 
 
-def halving_sum(value, axes, exchanged=2):
+def halving_sum(value, axes, exchanged=2, hold=None):
     stages = []
     for axis in axes:
         bit = 1
@@ -21,6 +21,7 @@
     exchanged = min(exchanged, len(stages))
     halved = stages[: len(stages) - exchanged]
     flat = value.reshape(-1)
+    held = hold
     for axis, bit in halved:
         pairs = [(i, i ^ bit) for i in range(lax.axis_size(axis))]
         upper = (lax.axis_index(axis) // bit) % 2
@@ -28,6 +29,9 @@
         keep = lax.dynamic_slice_in_dim(flat, upper * half, half)
         send = lax.dynamic_slice_in_dim(flat, (1 - upper) * half, half)
         flat = keep + lax.ppermute(send, axis, pairs)
+        if hold is not None:
+            flat, hold = lax.optimization_barrier((flat, hold))
+            held, hold = hold, None
     for axis, bit in stages[len(halved) :]:
         pairs = [(i, i ^ bit) for i in range(lax.axis_size(axis))]
         flat = flat + lax.ppermute(flat, axis, pairs)
@@ -39,7 +43,7 @@
         flat = jnp.where(
             upper == 1, jnp.concatenate([other, flat]), jnp.concatenate([flat, other])
         )
-    return flat.astype(jnp.float32).reshape(value.shape)
+    return flat.astype(jnp.float32).reshape(value.shape), held
 
 
 def lat_halo(block, dim, width):
@@ -75,20 +79,24 @@
     return stencil.astype(jnp.bfloat16)
 
 
-def lon_picker(col_count):
+def lon_picker(col_count, first_source=0, source_count=None):
     span_count = 2 * LON_REACH + 1
-    wide_count = col_count + 2 * LON_REACH
-    table_shape = (span_count, wide_count, col_count)
+    if source_count is None:
+        source_count = col_count + 2 * LON_REACH
+    table_shape = (span_count, source_count, col_count)
     offset_level = lax.broadcasted_iota(jnp.int32, table_shape, 0)
-    source = lax.broadcasted_iota(jnp.int32, table_shape, 1)
+    source = lax.broadcasted_iota(jnp.int32, table_shape, 1) + first_source
     target = lax.broadcasted_iota(jnp.int32, table_shape, 2)
     matches = source - target == offset_level
     return matches.astype(jnp.bfloat16)
 
 
-def band_of(stencil, col_count):
+def band_of(stencil, col_count, first_source=0, source_count=None):
     return jnp.einsum(
-        "kiad,dpq->iapkq", stencil, lon_picker(col_count), preferred_element_type=jnp.float32
+        "kiad,dpq->iapkq",
+        stencil,
+        lon_picker(col_count, first_source, source_count),
+        preferred_element_type=jnp.float32,
     ).astype(jnp.bfloat16)
 
 
@@ -105,7 +113,8 @@
     row_count, col_count = mixed.shape[1], mixed.shape[3]
     lat_taps = 2 * LAT_REACH + 1
     partial = jnp.einsum("cikq,iapkq->ciap", mixed, band, preferred_element_type=jnp.float32)
-    partial = partial[:, :, :, LON_HALO : col_count]
+    if partial.shape[3] != col_count - LON_HALO:
+        partial = partial[:, :, :, LON_HALO : col_count]
     out_rows = row_count - LAT_HALO
     total = partial[:, LAT_HALO : LAT_HALO + out_rows, 0]
     for offset in range(1, lat_taps):
@@ -153,13 +162,12 @@
 
     near_band = band_of(stencil_wide[:, LAT_REACH : LAT_REACH + row_count + 2 * LAT_REACH], col_count + LON_HALO)
     own_band = band_of(stencil, col_count)
-    wide_band = band_of(stencil_wide, col_count + 2 * LON_HALO)
+    wide_band = band_of(stencil_wide, col_count + 2 * LON_HALO, LON_HALO, col_count + LON_HALO)
 
     first_near = spread(source_wide, near_band, basis_count).astype(jnp.bfloat16)
     hidden = mix_channels(first_weight, first_near)
     activation = jnp.where(near_valid, jax.nn.gelu(hidden), 0.0).astype(jnp.bfloat16)
     second_spread = spread(activation, own_band, basis_count).astype(jnp.bfloat16)
-    layer_output = mix_channels(second_weight, second_spread).astype(jnp.bfloat16)
     own_gradient = gradient_wide[:, LAT_HALO : LAT_HALO + row_count, LON_HALO : LON_HALO + col_count]
     second_sum = filter_term(own_gradient, second_spread)
 
@@ -170,15 +178,16 @@
     own_hidden_grad = hidden_grad[:, LAT_REACH : LAT_REACH + row_count, LON_REACH : LON_REACH + col_count]
     own_first = first_near[:, LAT_REACH : LAT_REACH + row_count, :, LON_REACH : LON_REACH + col_count]
     first_sum = filter_term(own_hidden_grad, own_first)
-    first_mixed = unmix(first_weight, hidden_grad)
-    state_grad = spread_adjoint(first_mixed, near_band).astype(jnp.bfloat16)
-
     member_total = state_field.shape[0] * lax.axis_size("ens")
     grad_scale = 1.0 / math.sqrt(
         member_total * row_count * lax.axis_size("lat") * col_count * lax.axis_size("lon")
     )
-    first_grad = halving_sum(first_sum * grad_scale, ("ens", "lat", "lon"))
-    second_grad = halving_sum(second_sum * grad_scale, ("ens", "lat", "lon"))
+    axes = ("ens", "lat", "lon")
+    second_grad, second_spread = halving_sum(second_sum * grad_scale, axes, hold=second_spread)
+    first_grad, hidden_grad = halving_sum(first_sum * grad_scale, axes, hold=hidden_grad)
+    layer_output = mix_channels(second_weight, second_spread).astype(jnp.bfloat16)
+    first_mixed = unmix(first_weight, hidden_grad)
+    state_grad = spread_adjoint(first_mixed, near_band).astype(jnp.bfloat16)
     return (layer_output[None], state_grad[None], first_grad, second_grad)
 
 

time: 97.1 us -> 95.5 us (0.984)
  waiting for transfers between devices: 26 us -> 29.1 us
  matrix products: 25.8 us -> 23.8 us
  local copies, waits for them, and re-layouts: 12 us -> 10.2 us
    ppermute x1, waiting for transfers between devices: 1.45 us -> 4.27 us  [lat_halo(): lax.ppermute(lax.slice_in_dim(block, 0, width, axis=dim), 'lat', [(i + 1,...]
    eq x1 -> x0, local copies, waits for them, and re-layouts: 1.76 us -> none  [lon_picker(): matches = source - target == offset_level]
    dot_general x3, matrix products: 6.96 us -> 5.76 us  [band_of(): jnp.einsum('kiad,dpq->iapkq', stencil, lon_picker(col_count, first_source...]
    dot_general x2, matrix products: 3.24 us -> 2.1 us  [spread(): jnp.einsum('ciap,iapkq->cikq', stacked, band, preferred_element_type=jnp....]
    unnamed x24 -> x16, local copies, waits for them, and re-layouts: 5.2 us -> 6.26 us
    another operation x1, local copies, waits for them, and re-layouts: 1.07 us -> 0.03 us  [spread(): jnp.stack([values[:, offset:offset + row_count] for offset in range(lat_t...]
  transfers between devices with their start and end apart: 20 -> 20, of which waited for: 15 -> 16; matrix products, arithmetic and copies ran while one was open for 14% -> 11% of each run, Pallas kernels for 0% -> 0%
where the time goes in v6:
time: 95.5 us; the launch traced here: 95 us
  waiting for transfers between devices  29.1 us (30%)
  starting transfers between devices  26.9 us (28%)
  matrix products  23.8 us (25%)
  local copies, waits for them, and re-layouts  10.2 us (11%)
  other arithmetic  3.98 us (4%)
  between operations  1.04 us (1%)
    dot_general x2, matrix products, spread_adjoint(): jnp.einsum('cikq,iapkq->ciap', mixed, band, preferred_element_type=jnp.fl...  9.93 us
    ppermute x6, waiting for transfers between devices, halving_sum(): flat = keep + lax.ppermute(send, axis, pairs)  8.34 us
    ppermute x6, starting transfers between devices, halving_sum(): flat = keep + lax.ppermute(send, axis, pairs)  7.83 us
    ppermute x4, waiting for transfers between devices, halving_sum(): flat = flat + lax.ppermute(flat, axis, pairs)  6.96 us
    unnamed x16, local copies, waits for them, and re-layouts  6.26 us
    dot_general x3, matrix products, band_of(): jnp.einsum('kiad,dpq->iapkq', stencil, lon_picker(col_count, first_source...  5.76 us
    ppermute x6, starting transfers between devices, halving_sum(): other = lax.ppermute(flat, axis, pairs)  5.75 us
    ppermute x1, starting transfers between devices, lon_halo(): lax.ppermute(block[..., :width], 'lon', [(i, (i - 1) % count) for i in ra...  5.13 us
  transfers between devices with their start and end apart: 20, of which 16 were waited for; matrix products, arithmetic and copies ran while one was open for 11% of the time, Pallas kernels for 0%

profile of v6, /device:TPU:0, one launch (start us, length us, event | category | flops | bytes accessed | tf_op | source)
XLA Modules:
  0.0 95.0 jit_solution(15691898272043703761)
XLA Ops:
  0.6 1.1 %copy.26 = bf16[1,256,2,128]{1,3,2,0:T(8,128)(2,1)S(1)} copy(bf16[1,256,2,128]{3,2,1,0:T(2,128)(2,1)} %param.13) | data formatting | bytes 262144 | tf_op args[6]
  1.7 1.0 %copy.25 = bf16[1,256,2,128]{1,3,2,0:T(8,128)(2,1)S(1)} copy(bf16[1,256,2,128]{3,2,1,0:T(2,128)(2,1)} %param.7) | data formatting | bytes 262144 | tf_op args[0]
  2.8 5.1 %collective-permute-start.1 = (bf16[512,2,8]{0,2,1:T(8,128)(2,1)S(1)}, bf16[512,2,8]{0,2,1:T(8,128)(2,1)S(1)}, u32[]{:S(2)}, u32[]{:S(2)}) collective-permute-start(bf16[512,2,8]{0,2,1:T(8,128)(2,1)S(1)} %get-tuple-element.29), channel_id=1, source_target_pairs={{0,3},{1,0},{2,1},{3,2},{4,7},{5,4},{6,5},{7,6},{8,11},{9,8},{10,9... | collective-permute-start | bytes 49160 | tf_op jit(solution)/shard_map/ppermute | solution.py:67
  7.9 0.1 fusion.44
  8.0 0.7 broadcast_add_fusion
  8.7 0.9 convolution_convert_fusion.2
  9.6 0.1 reshape.80
  9.7 0.2 fusion.31
  10.0 0.1 copy.28
  10.1 3.3 %collective-permute-done = bf16[512,2,8]{0,2,1:T(8,128)(2,1)S(1)} collective-permute-done((bf16[512,2,8]{0,2,1:T(8,128)(2,1)S(1)}, bf16[512,2,8]{0,2,1:T(8,128)(2,1)S(1)}, u32[]{:S(2)}, u32[]{:S(2)}) %collective-permute-start) | collective-permute-done | bytes 16416 | tf_op jit(solution)/shard_map/ppermute | solution.py:66
  13.5 1.3 %collective-permute-start.3 = (bf16[513,2,144]{0,2,1:T(8,128)(2,1)S(1)}, bf16[513,2,144]{0,2,1:T(8,128)(2,1)S(1)}, u32[]{:S(2)}, u32[]{:S(2)}) collective-permute-start(bf16[513,2,144]{0,2,1:T(8,128)(2,1)S(1)} %pad_maximum_fusion.16), channel_id=1, source_target_pairs={{4,0},{5,1},{6,2},{7,3},{12,8},{13,9},{14,10},{15,11},{20,16},{21,... | collective-permute-start | bytes 886472 | tf_op jit(solution)/shard_map/ppermute | solution.py:57
  14.8 4.6 %collective-permute-start.2 = (bf16[513,2,144]{0,2,1:T(8,128)(2,1)S(1)}, bf16[513,2,144]{0,2,1:T(8,128)(2,1)S(1)}, u32[]{:S(2)}, u32[]{:S(2)}) collective-permute-start(bf16[513,2,144]{0,2,1:T(8,128)(2,1)S(1)} %pad_maximum_fusion.16), channel_id=1, source_target_pairs={{0,4},{1,5},{2,6},{3,7},{8,12},{9,13},{10,14},{11,15},{16,20},{17,... | collective-permute-start | bytes 886472 | tf_op jit(solution)/shard_map/ppermute | solution.py:52
  19.4 0.6 fusion.36
  20.0 4.3 %collective-permute-done.3 = bf16[513,2,144]{0,2,1:T(8,128)(2,1)S(1)} collective-permute-done((bf16[513,2,144]{0,2,1:T(8,128)(2,1)S(1)}, bf16[513,2,144]{0,2,1:T(8,128)(2,1)S(1)}, u32[]{:S(2)}, u32[]{:S(2)}) %collective-permute-start.3) | collective-permute-done | bytes 295520 | tf_op jit(solution)/shard_map/ppermute | solution.py:57
  24.2 1.2 %collective-permute-done.2 = bf16[513,2,144]{0,2,1:T(8,128)(2,1)S(1)} collective-permute-done((bf16[513,2,144]{0,2,1:T(8,128)(2,1)S(1)}, bf16[513,2,144]{0,2,1:T(8,128)(2,1)S(1)}, u32[]{:S(2)}, u32[]{:S(2)}) %collective-permute-start.2) | collective-permute-done | bytes 295520 | tf_op jit(solution)/shard_map/ppermute | solution.py:52
  25.4 0.1 maximum_reduce_fusion
  25.6 0.1 reshape_squeeze.3
  25.7 3.7 %fusion.10 = bf16[136,144,3,6,3]{1,3,4,2,0:T(8,128)(2,1)} fusion(pred[9,136,144,1,1]{2,1,0,3,4:T(8,128)(4,1)S(1)} %fusion.31, bf16[6,3,3,9]{3,2,1,0:T(4,128)(2,1)S(1)} %reshape_squeeze.3), kind=kOutput, calls=%fused_computation.12 | convolution fusion | flops 19035648 | bytes 2292300 | tf_op jit(solution)/shard_map/kiad,dpq->iapkq/dot_general | solution.py:95
  29.4 1.5 %convert_bitcast_fusion = bf16[4,3,144,3,136]{2,0,1,3,4:T(4,128)(2,1)S(1)} fusion(bf16[3,6,3,9]{3,1,2,0:T(8,128)(2,1)S(1)} %bitcast.201), kind=kOutput, calls=%fused_computation.8 | convolution fusion | flops 13747968 | bytes 1419264 | tf_op jit(solution)/shard_map/kiad,dpq->iapkq/dot_general | solution.py:95
  31.0 1.4 %copy-done.1 = bf16[4,3,144,3,136]{2,0,1,3,4:T(4,128)(2,1)} copy-done((bf16[4,3,144,3,136]{2,0,1,3,4:T(4,128)(2,1)}, bf16[4,3,144,3,136]{2,0,1,3,4:T(4,128)(2,1)S(1)}, u32[]{:S(2)}) %copy-start.1) | copy-done | bytes 1410072
  32.3 1.7 %fusion.24 = bf16[256,4,3,136]{0,3,2,1:T(8,128)(2,1)} fusion(bf16[4,3,144,3,136]{2,0,1,3,4:T(4,128)(2,1)S(1)} %convert_bitcast_fusion, bf16[256,4,1,144]{0,3,2,1:T(8,128)(2,1)S(1)} %get-tuple-element.22, bf16[256,4,1,144]{0,3,2,1:T(8,128)(2,1)S(1)} %get-tuple-element.21, bf16[256,4,1,144]{0,3,2,1:T(8,128)(2,1)S(1)} %get-tuple-element.20), kind=kOutput, calls=%fused_computation.21 | convolution fusion | flops 362274816 | bytes 3130368 | tf_op jit(solution)/shard_map/ciap,iapkq->cikq/dot_general | solution.py:109
  34.0 5.9 %fusion.14 = f32[256,6,3,136]{0,3,1,2:T(8,128)} fusion(bf16[513,2,144]{0,2,1:T(8,128)(2,1)S(1)} %collective-permute-done.3, bf16[513,2,144]{0,2,1:T(8,128)(2,1)S(1)} %collective-permute-done.2, bf16[1,2,144]{0,2,1:T(8,128)(2,1)S(1)} %copy.28, bf16[512,2,8]{0,2,1:T(8,128)(2,1)S(1)} %collective-permute-done.1, ...), kind=kOutput, calls=%fused_computation.14 | convolution fusion | flops 884957184 | bytes 5901504 | tf_op jit(solution)/shard_map/cikq,iapkq->ciap/dot_general | solution.py:115
  39.9 3.1 %fusion.48 = (bf16[256,4,136]{0,2,1:T(8,128)(2,1)}, bf16[256,4,136]{0,2,1:T(8,128)(2,1)S(1)}) fusion(f32[256,6,3,136]{0,3,1,2:T(8,128)} %fusion.14, pred[4]{0:T(512)(128)(4,1)S(1)} %compare_and_fusion, bf16[256,4,3,136]{0,3,2,1:T(8,128)(2,1)} %fusion.24, bf16[3,256,256]{2,1,0:T(8,128)(2,1)S(1)} %copy-done), kind=kOutput, calls=%fused_computation.56 | convolution fusion | flops 217808896 | bytes 3457028 | tf_op jit(solution)/shard_map/koc,cikj->oij/dot_general | solution.py:127
  43.1 0.4 fusion.33
  43.5 0.4 copy-done.2
  44.0 0.3 fusion.30
  44.3 0.3 copy.36
  44.6 0.4 copy.71
  45.0 0.8 dynamic_slice.37
  45.8 1.4 %fusion.28 = f32[3,256,256]{1,2,0:T(8,128)S(1)} fusion(bf16[256,4,3,136]{0,3,2,1:T(8,128)(2,1)} %fusion.24, bf16[256,4,136]{0,2,1:T(8,128)(2,1)} %get-tuple-element.9), kind=kOutput, calls=%fused_computation.25 | convolution fusion | flops 100859904 | bytes 1310720 | tf_op jit(solution)/shard_map/oij,cikj->koc/dot_general | solution.py:137
  47.1 0.3 copy.40
  47.4 0.4 copy.72
  47.9 0.6 collective-permute-start.5
  48.4 1.0 %dynamic-slice_add_fusion.1 = f32[98304]{0:T(1024)S(1)} fusion(f32[98304]{0:T(1024)} %collective-permute-done.4, f32[196608]{0:T(1024)S(1)} %bitcast.198, s32[]{:T(128)S(6)} %select_n.121), kind=kLoop, calls=%fused_computation.88 | loop fusion | flops 98304 | bytes 1179652 | tf_op jit(solution)/shard_map/add | solution.py:31
  49.5 0.3 collective-permute-done.5
  49.9 4.0 %fusion.17 = f32[256,4,3,144]{0,3,2,1:T(8,128)} fusion(bf16[4,3,144,3,136]{2,0,1,3,4:T(4,128)(2,1)} %copy-done.1, bf16[3,256,256]{2,1,0:T(8,128)(2,1)S(1)} %copy-done, bf16[256,4,136]{0,2,1:T(8,128)(2,1)S(1)} %copy-done.4), kind=kOutput, calls=%fused_computation.17 | convolution fusion | flops 575299584 | bytes 3851264 | tf_op jit(solution)/shard_map/cikq,iapkq->ciap/dot_general | solution.py:115
  53.9 1.6 %collective-permute-start.6 = (f32[49152]{0:T(1024)S(1)}, f32[49152]{0:T(1024)S(1)}, u32[]{:S(2)}, u32[]{:S(2)}) collective-permute-start(f32[49152]{0:T(1024)S(1)} %dynamic_slice.41), channel_id=1, source_target_pairs={{0,16},{8,24},{16,0},{24,8},{1,17},{9,25},{17,1},{25,9},{2,18},{10... | collective-permute-start | bytes 589832 | tf_op jit(solution)/shard_map/ppermute | solution.py:31
  55.5 0.6 collective-permute-start.13
  56.1 1.1 %fusion.78 = bf16[1,256,2,128]{1,3,2,0:T(8,128)(2,1)S(1)} fusion(f32[256,4,3,144]{0,3,2,1:T(8,128)} %fusion.17), kind=kLoop, calls=%fused_computation.116 | loop fusion | flops 196608 | bytes 917504 | tf_op jit(solution)/shard_map/convert_element_type | solution.py:190
  57.2 4.5 %collective-permute-done.6 = f32[49152]{0:T(1024)S(1)} collective-permute-done((f32[49152]{0:T(1024)S(1)}, f32[49152]{0:T(1024)S(1)}, u32[]{:S(2)}, u32[]{:S(2)}) %collective-permute-start.6) | collective-permute-done | bytes 196640 | tf_op jit(solution)/shard_map/ppermute | solution.py:31
  61.8 2.6 %collective-permute-start.7 = (f32[24576]{0:T(1024)S(1)}, f32[24576]{0:T(1024)S(1)}, u32[]{:S(2)}, u32[]{:S(2)}) collective-permute-start(f32[24576]{0:T(1024)S(1)} %dynamic_slice.43), channel_id=1, source_target_pairs={{0,4},{4,0},{1,5},{5,1},{2,6},{6,2},{3,7},{7,3},{8,12},{12,8},{9,1... | collective-permute-start | bytes 294920 | tf_op jit(solution)/shard_map/ppermute | solution.py:31
  64.3 1.0 %collective-permute-done.13 = f32[49152]{0:T(1024)S(1)} collective-permute-done((f32[49152]{0:T(1024)S(1)}, f32[49152]{0:T(1024)S(1)}, u32[]{:S(2)}, u32[]{:S(2)}) %collective-permute-start.13) | collective-permute-done | bytes 196640 | tf_op jit(solution)/shard_map/ppermute | solution.py:31
  65.4 2.6 %collective-permute-start.14 = (f32[24576]{0:T(1024)S(1)}, f32[24576]{0:T(1024)S(1)}, u32[]{:S(2)}, u32[]{:S(2)}) collective-permute-start(f32[24576]{0:T(1024)S(1)} %dynamic_slice.47), channel_id=1, source_target_pairs={{0,4},{4,0},{1,5},{5,1},{2,6},{6,2},{3,7},{7,3},{8,12},{12,8},{9,1... | collective-permute-start | bytes 294920 | tf_op jit(solution)/shard_map/ppermute | solution.py:31
  68.0 2.5 %collective-permute-done.14 = f32[24576]{0:T(1024)S(1)} collective-permute-done((f32[24576]{0:T(1024)S(1)}, f32[24576]{0:T(1024)S(1)}, u32[]{:S(2)}, u32[]{:S(2)}) %collective-permute-start.14) | collective-permute-done | bytes 98336 | tf_op jit(solution)/shard_map/ppermute | solution.py:31
  70.6 2.8 %collective-permute-done.8 = f32[24576]{0:T(1024)S(1)} collective-permute-done((f32[24576]{0:T(1024)S(1)}, f32[24576]{0:T(1024)S(1)}, u32[]{:S(2)}, u32[]{:S(2)}) %collective-permute-start.8) | collective-permute-done | bytes 98336 | tf_op jit(solution)/shard_map/ppermute | solution.py:37
  73.5 0.3 fusion.35
  73.8 0.8 copy.42
  74.6 0.8 copy.43
  75.4 0.9 collective-permute-done.15
  76.3 2.1 %collective-permute-start.16 = (f32[24576]{0:T(1024)S(1)}, f32[24576]{0:T(1024)S(1)}, u32[]{:S(2)}, u32[]{:S(2)}) collective-permute-start(f32[24576]{0:T(1024)S(1)} %add.180), channel_id=1, source_target_pairs={{0,2},{1,3},{2,0},{3,1},{4,6},{5,7},{6,4},{7,5},{8,10},{9,11},{10,... | collective-permute-start | bytes 294920 | tf_op jit(solution)/shard_map/ppermute | solution.py:37
  78.4 2.9 %collective-permute-done.9 = f32[24576]{0:T(1024)S(1)} collective-permute-done((f32[24576]{0:T(1024)S(1)}, f32[24576]{0:T(1024)S(1)}, u32[]{:S(2)}, u32[]{:S(2)}) %collective-permute-start.9) | collective-permute-done | bytes 98336 | tf_op jit(solution)/shard_map/ppermute | solution.py:37
  81.3 1.8 %collective-permute-start.10 = (bf16[24576]{0:T(1024)(128)(2,1)S(1)}, bf16[24576]{0:T(1024)(128)(2,1)S(1)}, u32[]{:S(2)}, u32[]{:S(2)}) collective-permute-start(bf16[24576]{0:T(1024)(128)(2,1)S(1)} %add_convert_fusion.1), channel_id=1, source_target_pairs={{0,4},{4,0},{1,5},{5,1},{2,6},{6,2},{3,7},{7,3},{8,12},{12,8},{9,1... | collective-permute-start | bytes 147464 | tf_op jit(solution)/shard_map/ppermute | solution.py:42
  83.1 0.3 collective-permute-done.16
  83.4 0.7 collective-permute-start.17
  84.2 1.3 %collective-permute-done.10 = bf16[24576]{0:T(1024)(128)(2,1)S(1)} collective-permute-done((bf16[24576]{0:T(1024)(128)(2,1)S(1)}, bf16[24576]{0:T(1024)(128)(2,1)S(1)}, u32[]{:S(2)}, u32[]{:S(2)}) %collective-permute-start.10) | collective-permute-done | bytes 49184 | tf_op jit(solution)/shard_map/ppermute | solution.py:42
  85.5 1.6 %collective-permute-start.11 = (bf16[49152]{0:T(1024)(128)(2,1)S(1)}, bf16[49152]{0:T(1024)(128)(2,1)S(1)}, u32[]{:S(2)}, u32[]{:S(2)}) collective-permute-start(bf16[49152]{0:T(1024)(128)(2,1)S(1)} %maximum_select_fusion.4), channel_id=1, source_target_pairs={{0,16},{8,24},{16,0},{24,8},{1,17},{9,25},{17,1},{25,9},{2,18},{10... | collective-permute-start | bytes 294920 | tf_op jit(solution)/shard_map/ppermute | solution.py:42
  87.1 0.5 collective-permute-done.17
  87.6 1.6 %collective-permute-start.18 = (bf16[49152]{0:T(1024)(128)(2,1)S(1)}, bf16[49152]{0:T(1024)(128)(2,1)S(1)}, u32[]{:S(2)}, u32[]{:S(2)}) collective-permute-start(bf16[49152]{0:T(1024)(128)(2,1)S(1)} %maximum_select_fusion.5), channel_id=1, source_target_pairs={{0,16},{8,24},{16,0},{24,8},{1,17},{9,25},{17,1},{25,9},{2,18},{10... | collective-permute-start | bytes 294920 | tf_op jit(solution)/shard_map/ppermute | solution.py:42
  89.2 1.0 %collective-permute-done.11 = bf16[49152]{0:T(1024)(128)(2,1)S(1)} collective-permute-done((bf16[49152]{0:T(1024)(128)(2,1)S(1)}, bf16[49152]{0:T(1024)(128)(2,1)S(1)}, u32[]{:S(2)}, u32[]{:S(2)}) %collective-permute-start.11) | collective-permute-done | bytes 98336 | tf_op jit(solution)/shard_map/ppermute | solution.py:42
  90.3 2.0 %collective-permute-done.18 = bf16[49152]{0:T(1024)(128)(2,1)S(1)} collective-permute-done((bf16[49152]{0:T(1024)(128)(2,1)S(1)}, bf16[49152]{0:T(1024)(128)(2,1)S(1)}, u32[]{:S(2)}, u32[]{:S(2)}) %collective-permute-start.18) | collective-permute-done | bytes 98336 | tf_op jit(solution)/shard_map/ppermute | solution.py:42
  92.4 0.1 fusion.64
  92.5 1.1 %reshape.84 = f32[3,256,256]{2,1,0:T(8,128)} reshape(f32[196608]{0:T(1024)S(1)} %fusion.64) | data formatting | bytes 1572864 | tf_op jit(solution)/shard_map/convert_element_type | solution.py:46
  93.6 0.2 collective-permute-done.19
  93.9 1.1 %reshape.85 = f32[3,256,256]{2,1,0:T(8,128)} reshape(f32[196608]{0:T(1024)S(1)} %fusion.65) | data formatting | bytes 1572864 | tf_op jit(solution)/shard_map/convert_element_type | solution.py:46
  (47 shorter events, 1.1 us)
Async XLA Ops:
  0.6 39.3 %copy-start = (bf16[3,256,256]{2,1,0:T(8,128)(2,1)S(1)}, bf16[3,256,256]{2,1,0:T(8,128)(2,1)}, u32[]{:S(2)}) copy-start(bf16[3,256,256]{2,1,0:T(8,128)(2,1)} %param.8) | copy-start | bytes 1179652
  2.8 7.4 %collective-permute-start.1 = (bf16[512,2,8]{0,2,1:T(8,128)(2,1)S(1)}, bf16[512,2,8]{0,2,1:T(8,128)(2,1)S(1)}, u32[]{:S(2)}, u32[]{:S(2)}) collective-permute-start(bf16[512,2,8]{0,2,1:T(8,128)(2,1)S(1)} %get-tuple-element.29), channel_id=1, source_target_pairs={{0,3},{1,0},{2,1},{3,2},{4,7},{5,4},{6,5},{7,6},{8,11},{9,8},{10,9... | collective-permute-start | bytes 49160 | tf_op jit(solution)/shard_map/ppermute | solution.py:67
  7.9 5.5 %collective-permute-start = (bf16[512,2,8]{0,2,1:T(8,128)(2,1)S(1)}, bf16[512,2,8]{0,2,1:T(8,128)(2,1)S(1)}, u32[]{:S(2)}, u32[]{:S(2)}) collective-permute-start(bf16[512,2,8]{0,2,1:T(8,128)(2,1)S(1)} %get-tuple-element.28), channel_id=1, source_target_pairs={{0,1},{1,2},{2,3},{3,0},{4,5},{5,6},{6,7},{7,4},{8,9},{9,10},{10,1... | collective-permute-start | bytes 49160 | tf_op jit(solution)/shard_map/ppermute | solution.py:66
  13.5 10.8 %collective-permute-start.3 = (bf16[513,2,144]{0,2,1:T(8,128)(2,1)S(1)}, bf16[513,2,144]{0,2,1:T(8,128)(2,1)S(1)}, u32[]{:S(2)}, u32[]{:S(2)}) collective-permute-start(bf16[513,2,144]{0,2,1:T(8,128)(2,1)S(1)} %pad_maximum_fusion.16), channel_id=1, source_target_pairs={{4,0},{5,1},{6,2},{7,3},{12,8},{13,9},{14,10},{15,11},{20,16},{21,... | collective-permute-start | bytes 886472 | tf_op jit(solution)/shard_map/ppermute | solution.py:57
  14.8 10.7 %collective-permute-start.2 = (bf16[513,2,144]{0,2,1:T(8,128)(2,1)S(1)}, bf16[513,2,144]{0,2,1:T(8,128)(2,1)S(1)}, u32[]{:S(2)}, u32[]{:S(2)}) collective-permute-start(bf16[513,2,144]{0,2,1:T(8,128)(2,1)S(1)} %pad_maximum_fusion.16), channel_id=1, source_target_pairs={{0,4},{1,5},{2,6},{3,7},{8,12},{9,13},{10,14},{11,15},{16,20},{17,... | collective-permute-start | bytes 886472 | tf_op jit(solution)/shard_map/ppermute | solution.py:52
  30.9 1.4 %copy-start.1 = (bf16[4,3,144,3,136]{2,0,1,3,4:T(4,128)(2,1)}, bf16[4,3,144,3,136]{2,0,1,3,4:T(4,128)(2,1)S(1)}, u32[]{:S(2)}) copy-start(bf16[4,3,144,3,136]{2,0,1,3,4:T(4,128)(2,1)S(1)} %convert_bitcast_fusion) | copy-start | bytes 4230148
  32.3 1.7 %copy-start.3 = (bf16[3,256,256]{2,1,0:T(8,128)(2,1)S(1)}, bf16[3,256,256]{2,1,0:T(8,128)(2,1)}, u32[]{:S(2)}) copy-start(bf16[3,256,256]{2,1,0:T(8,128)(2,1)} %param.9) | copy-start | bytes 1179652
  43.1 0.9 copy-start.2
  45.8 2.7 %collective-permute-start.4 = (f32[98304]{0:T(1024)}, f32[98304]{0:T(1024)}, u32[]{:S(2)}, u32[]{:S(2)}) collective-permute-start(f32[98304]{0:T(1024)} %dynamic_slice.37), channel_id=1, source_target_pairs={{0,8},{8,0},{16,24},{24,16},{1,9},{9,1},{17,25},{25,17},{2,10},{10... | collective-permute-start | bytes 1179656 | tf_op jit(solution)/shard_map/ppermute | solution.py:31
  47.4 2.4 %copy-start.4 = (bf16[256,4,136]{0,2,1:T(8,128)(2,1)S(1)}, bf16[256,4,136]{0,2,1:T(8,128)(2,1)}, u32[]{:S(2)}) copy-start(bf16[256,4,136]{0,2,1:T(8,128)(2,1)} %get-tuple-element.9) | copy-start | bytes 835588
  47.9 1.9 %collective-permute-start.5 = (f32[98304]{0:T(1024)S(1)}, f32[98304]{0:T(1024)S(1)}, u32[]{:S(2)}, u32[]{:S(2)}) collective-permute-start(f32[98304]{0:T(1024)S(1)} %dynamic_slice.39), channel_id=1, source_target_pairs={{0,8},{8,0},{16,24},{24,16},{1,9},{9,1},{17,25},{25,17},{2,10},{10... | collective-permute-start | bytes 1179656 | tf_op jit(solution)/shard_map/ppermute | solution.py:31
  53.9 7.8 %collective-permute-start.6 = (f32[49152]{0:T(1024)S(1)}, f32[49152]{0:T(1024)S(1)}, u32[]{:S(2)}, u32[]{:S(2)}) collective-permute-start(f32[49152]{0:T(1024)S(1)} %dynamic_slice.41), channel_id=1, source_target_pairs={{0,16},{8,24},{16,0},{24,8},{1,17},{9,25},{17,1},{25,9},{2,18},{10... | collective-permute-start | bytes 589832 | tf_op jit(solution)/shard_map/ppermute | solution.py:31
  55.5 9.9 %collective-permute-start.13 = (f32[49152]{0:T(1024)S(1)}, f32[49152]{0:T(1024)S(1)}, u32[]{:S(2)}, u32[]{:S(2)}) collective-permute-start(f32[49152]{0:T(1024)S(1)} %dynamic_slice.45), channel_id=1, source_target_pairs={{0,16},{8,24},{16,0},{24,8},{1,17},{9,25},{17,1},{25,9},{2,18},{10... | collective-permute-start | bytes 589832 | tf_op jit(solution)/shard_map/ppermute | solution.py:31
  61.8 6.2 %collective-permute-start.7 = (f32[24576]{0:T(1024)S(1)}, f32[24576]{0:T(1024)S(1)}, u32[]{:S(2)}, u32[]{:S(2)}) collective-permute-start(f32[24576]{0:T(1024)S(1)} %dynamic_slice.43), channel_id=1, source_target_pairs={{0,4},{4,0},{1,5},{5,1},{2,6},{6,2},{3,7},{7,3},{8,12},{12,8},{9,1... | collective-permute-start | bytes 294920 | tf_op jit(solution)/shard_map/ppermute | solution.py:31
  65.4 5.1 %collective-permute-start.14 = (f32[24576]{0:T(1024)S(1)}, f32[24576]{0:T(1024)S(1)}, u32[]{:S(2)}, u32[]{:S(2)}) collective-permute-start(f32[24576]{0:T(1024)S(1)} %dynamic_slice.47), channel_id=1, source_target_pairs={{0,4},{4,0},{1,5},{5,1},{2,6},{6,2},{3,7},{7,3},{8,12},{12,8},{9,1... | collective-permute-start | bytes 294920 | tf_op jit(solution)/shard_map/ppermute | solution.py:31
  68.0 5.5 %collective-permute-start.8 = (f32[24576]{0:T(1024)S(1)}, f32[24576]{0:T(1024)S(1)}, u32[]{:S(2)}, u32[]{:S(2)}) collective-permute-start(f32[24576]{0:T(1024)S(1)} %dynamic-slice_add_fusion.5), channel_id=1, source_target_pairs={{0,1},{1,0},{2,3},{3,2},{4,5},{5,4},{6,7},{7,6},{8,9},{9,8},{10,11... | collective-permute-start | bytes 294920 | tf_op jit(solution)/shard_map/ppermute | solution.py:37
  70.6 5.7 %collective-permute-start.15 = (f32[24576]{0:T(1024)S(1)}, f32[24576]{0:T(1024)S(1)}, u32[]{:S(2)}, u32[]{:S(2)}) collective-permute-start(f32[24576]{0:T(1024)S(1)} %dynamic-slice_add_fusion.4), channel_id=1, source_target_pairs={{0,1},{1,0},{2,3},{3,2},{4,5},{5,4},{6,7},{7,6},{8,9},{9,8},{10,11... | collective-permute-start | bytes 294920 | tf_op jit(solution)/shard_map/ppermute | solution.py:37
  73.4 7.9 %collective-permute-start.9 = (f32[24576]{0:T(1024)S(1)}, f32[24576]{0:T(1024)S(1)}, u32[]{:S(2)}, u32[]{:S(2)}) collective-permute-start(f32[24576]{0:T(1024)S(1)} %add.176), channel_id=1, source_target_pairs={{0,2},{1,3},{2,0},{3,1},{4,6},{5,7},{6,4},{7,5},{8,10},{9,11},{10,... | collective-permute-start | bytes 294920 | tf_op jit(solution)/shard_map/ppermute | solution.py:37
  76.3 7.1 %collective-permute-start.16 = (f32[24576]{0:T(1024)S(1)}, f32[24576]{0:T(1024)S(1)}, u32[]{:S(2)}, u32[]{:S(2)}) collective-permute-start(f32[24576]{0:T(1024)S(1)} %add.180), channel_id=1, source_target_pairs={{0,2},{1,3},{2,0},{3,1},{4,6},{5,7},{6,4},{7,5},{8,10},{9,11},{10,... | collective-permute-start | bytes 294920 | tf_op jit(solution)/shard_map/ppermute | solution.py:37
  81.3 4.2 %collective-permute-start.10 = (bf16[24576]{0:T(1024)(128)(2,1)S(1)}, bf16[24576]{0:T(1024)(128)(2,1)S(1)}, u32[]{:S(2)}, u32[]{:S(2)}) collective-permute-start(bf16[24576]{0:T(1024)(128)(2,1)S(1)} %add_convert_fusion.1), channel_id=1, source_target_pairs={{0,4},{4,0},{1,5},{5,1},{2,6},{6,2},{3,7},{7,3},{8,12},{12,8},{9,1... | collective-permute-start | bytes 147464 | tf_op jit(solution)/shard_map/ppermute | solution.py:42
  83.4 4.2 %collective-permute-start.17 = (bf16[24576]{0:T(1024)(128)(2,1)S(1)}, bf16[24576]{0:T(1024)(128)(2,1)S(1)}, u32[]{:S(2)}, u32[]{:S(2)}) collective-permute-start(bf16[24576]{0:T(1024)(128)(2,1)S(1)} %add_convert_fusion), channel_id=1, source_target_pairs={{0,4},{4,0},{1,5},{5,1},{2,6},{6,2},{3,7},{7,3},{8,12},{12,8},{9,1... | collective-permute-start | bytes 147464 | tf_op jit(solution)/shard_map/ppermute | solution.py:42
  85.5 4.7 %collective-permute-start.11 = (bf16[49152]{0:T(1024)(128)(2,1)S(1)}, bf16[49152]{0:T(1024)(128)(2,1)S(1)}, u32[]{:S(2)}, u32[]{:S(2)}) collective-permute-start(bf16[49152]{0:T(1024)(128)(2,1)S(1)} %maximum_select_fusion.4), channel_id=1, source_target_pairs={{0,16},{8,24},{16,0},{24,8},{1,17},{9,25},{17,1},{25,9},{2,18},{10... | collective-permute-start | bytes 294920 | tf_op jit(solution)/shard_map/ppermute | solution.py:42
  87.6 4.7 %collective-permute-start.18 = (bf16[49152]{0:T(1024)(128)(2,1)S(1)}, bf16[49152]{0:T(1024)(128)(2,1)S(1)}, u32[]{:S(2)}, u32[]{:S(2)}) collective-permute-start(bf16[49152]{0:T(1024)(128)(2,1)S(1)} %maximum_select_fusion.5), channel_id=1, source_target_pairs={{0,16},{8,24},{16,0},{24,8},{1,17},{9,25},{17,1},{25,9},{2,18},{10... | collective-permute-start | bytes 294920 | tf_op jit(solution)/shard_map/ppermute | solution.py:42
  90.3 2.2 %collective-permute-start.12 = (bf16[98304]{0:T(1024)(128)(2,1)S(1)}, bf16[98304]{0:T(1024)(128)(2,1)S(1)}, u32[]{:S(2)}, u32[]{:S(2)}) collective-permute-start(bf16[98304]{0:T(1024)(128)(2,1)S(1)} %maximum_select_fusion.2), channel_id=1, source_target_pairs={{0,8},{8,0},{16,24},{24,16},{1,9},{9,1},{17,25},{25,17},{2,10},{10... | collective-permute-start | bytes 589832 | tf_op jit(solution)/shard_map/ppermute | solution.py:42
  92.4 1.5 %collective-permute-start.19 = (bf16[98304]{0:T(1024)(128)(2,1)S(1)}, bf16[98304]{0:T(1024)(128)(2,1)S(1)}, u32[]{:S(2)}, u32[]{:S(2)}) collective-permute-start(bf16[98304]{0:T(1024)(128)(2,1)S(1)} %maximum_select_fusion.3), channel_id=1, source_target_pairs={{0,8},{8,0},{16,24},{24,16},{1,9},{9,1},{17,25},{25,17},{2,10},{10... | collective-permute-start | bytes 589832 | tf_op jit(solution)/shard_map/ppermute | solution.py:42

commit v7 on v6

--- a/solution.py
+++ b/solution.py
@@ -20,7 +20,7 @@
             bit *= 2
     exchanged = min(exchanged, len(stages))
     halved = stages[: len(stages) - exchanged]
-    flat = value.reshape(-1)
+    flat = value.reshape(-1, value.shape[-1])
     held = hold
     for axis, bit in halved:
         pairs = [(i, i ^ bit) for i in range(lax.axis_size(axis))]

time: 95.5 us -> 91.9 us (0.962)
  local copies, waits for them, and re-layouts: 10.2 us -> 7.01 us
  other arithmetic: 3.98 us -> 6.05 us
  starting transfers between devices: 26.9 us -> 25.4 us
    convert_element_type x2 -> x0, local copies, waits for them, and re-layouts: 2.2 us -> none  [halving_sum(): return (flat.astype(jnp.float32).reshape(value.shape), held)]
    convert_element_type x2, other arithmetic: 0.16 us -> 1.89 us  [halving_sum(): return (flat.astype(jnp.float32).reshape(value.shape), held)]
    ppermute x4, waiting for transfers between devices: 6.96 us -> 8.68 us  [halving_sum(): flat = flat + lax.ppermute(flat, axis, pairs)]
    ppermute x6, waiting for transfers between devices: 8.34 us -> 6.83 us  [halving_sum(): flat = keep + lax.ppermute(send, axis, pairs)]
    unnamed x16 -> x18, local copies, waits for them, and re-layouts: 6.26 us -> 5.75 us
  transfers between devices with their start and end apart: 20 -> 20, of which waited for: 16 -> 13; matrix products, arithmetic and copies ran while one was open for 11% -> 16% of each run, Pallas kernels for 0% -> 0%
where the time goes in v7:
time: 91.9 us; the launch traced here: 91.4 us
  waiting for transfers between devices  28.7 us (31%)
  starting transfers between devices  25.4 us (28%)
  matrix products  23.1 us (25%)
  local copies, waits for them, and re-layouts  7.01 us (8%)
  other arithmetic  6.05 us (7%)
  between operations  1.05 us (1%)
    dot_general x2, matrix products, spread_adjoint(): jnp.einsum('cikq,iapkq->ciap', mixed, band, preferred_element_type=jnp.fl...  10.2 us
    ppermute x4, waiting for transfers between devices, halving_sum(): flat = flat + lax.ppermute(flat, axis, pairs)  8.68 us
    ppermute x6, starting transfers between devices, halving_sum(): flat = keep + lax.ppermute(send, axis, pairs)  7.82 us
    ppermute x6, waiting for transfers between devices, halving_sum(): flat = keep + lax.ppermute(send, axis, pairs)  6.83 us
    dot_general x3, matrix products, band_of(): jnp.einsum('kiad,dpq->iapkq', stencil, lon_picker(col_count, first_source...  6.66 us
    unnamed x18, local copies, waits for them, and re-layouts  5.75 us
    ppermute x6, waiting for transfers between devices, halving_sum(): other = lax.ppermute(flat, axis, pairs)  5.36 us
    ppermute x1, starting transfers between devices, lon_halo(): lax.ppermute(block[..., :width], 'lon', [(i, (i - 1) % count) for i in ra...  5.13 us
  transfers between devices with their start and end apart: 20, of which 13 were waited for; matrix products, arithmetic and copies ran while one was open for 16% of the time, Pallas kernels for 0%

profile of v7, /device:TPU:0, one launch (start us, length us, event | category | flops | bytes accessed | tf_op | source)
XLA Modules:
  0.0 91.4 jit_solution(1770438618933769642)
XLA Ops:
  0.6 1.1 %copy.26 = bf16[1,256,2,128]{1,3,2,0:T(8,128)(2,1)S(1)} copy(bf16[1,256,2,128]{3,2,1,0:T(2,128)(2,1)} %param.13) | data formatting | bytes 262144 | tf_op args[6]
  1.7 1.0 %copy.25 = bf16[1,256,2,128]{1,3,2,0:T(8,128)(2,1)S(1)} copy(bf16[1,256,2,128]{3,2,1,0:T(2,128)(2,1)} %param.7) | data formatting | bytes 262144 | tf_op args[0]
  2.8 5.1 %collective-permute-start.1 = (bf16[512,2,8]{0,2,1:T(8,128)(2,1)S(1)}, bf16[512,2,8]{0,2,1:T(8,128)(2,1)S(1)}, u32[]{:S(2)}, u32[]{:S(2)}) collective-permute-start(bf16[512,2,8]{0,2,1:T(8,128)(2,1)S(1)} %get-tuple-element.29), channel_id=1, source_target_pairs={{0,3},{1,0},{2,1},{3,2},{4,7},{5,4},{6,5},{7,6},{8,11},{9,8},{10,9... | collective-permute-start | bytes 49160 | tf_op jit(solution)/shard_map/ppermute | solution.py:67
  7.9 0.1 fusion.42
  8.0 0.7 broadcast_add_fusion
  8.7 0.9 convolution_convert_fusion.2
  9.6 0.1 reshape.80
  9.7 0.2 fusion.29
  10.0 0.1 copy.28
  10.1 3.3 %collective-permute-done = bf16[512,2,8]{0,2,1:T(8,128)(2,1)S(1)} collective-permute-done((bf16[512,2,8]{0,2,1:T(8,128)(2,1)S(1)}, bf16[512,2,8]{0,2,1:T(8,128)(2,1)S(1)}, u32[]{:S(2)}, u32[]{:S(2)}) %collective-permute-start) | collective-permute-done | bytes 16416 | tf_op jit(solution)/shard_map/ppermute | solution.py:66
  13.5 1.3 %collective-permute-start.3 = (bf16[513,2,144]{0,2,1:T(8,128)(2,1)S(1)}, bf16[513,2,144]{0,2,1:T(8,128)(2,1)S(1)}, u32[]{:S(2)}, u32[]{:S(2)}) collective-permute-start(bf16[513,2,144]{0,2,1:T(8,128)(2,1)S(1)} %pad_maximum_fusion.16), channel_id=1, source_target_pairs={{4,0},{5,1},{6,2},{7,3},{12,8},{13,9},{14,10},{15,11},{20,16},{21,... | collective-permute-start | bytes 886472 | tf_op jit(solution)/shard_map/ppermute | solution.py:57
  14.8 4.6 %collective-permute-start.2 = (bf16[513,2,144]{0,2,1:T(8,128)(2,1)S(1)}, bf16[513,2,144]{0,2,1:T(8,128)(2,1)S(1)}, u32[]{:S(2)}, u32[]{:S(2)}) collective-permute-start(bf16[513,2,144]{0,2,1:T(8,128)(2,1)S(1)} %pad_maximum_fusion.16), channel_id=1, source_target_pairs={{0,4},{1,5},{2,6},{3,7},{8,12},{9,13},{10,14},{11,15},{16,20},{17,... | collective-permute-start | bytes 886472 | tf_op jit(solution)/shard_map/ppermute | solution.py:52
  19.4 1.5 %fusion.34 = bf16[136,128,3,2,3]{1,4,3,2,0:T(4,128)(2,1)} fusion(pred[9,136,128,1,1]{2,1,0,3,4:T(8,128)(4,1)S(1)} %fusion.42, bf16[3,2,3,9]{3,2,1,0:T(4,128)(2,1)S(1)} %convolution_convert_fusion.2), kind=kOutput, calls=%fused_computation.36 | convolution fusion | flops 5640192 | bytes 783684 | tf_op jit(solution)/shard_map/kiad,dpq->iapkq/dot_general | solution.py:95
  20.9 3.4 %collective-permute-done.3 = bf16[513,2,144]{0,2,1:T(8,128)(2,1)S(1)} collective-permute-done((bf16[513,2,144]{0,2,1:T(8,128)(2,1)S(1)}, bf16[513,2,144]{0,2,1:T(8,128)(2,1)S(1)}, u32[]{:S(2)}, u32[]{:S(2)}) %collective-permute-start.3) | collective-permute-done | bytes 295520 | tf_op jit(solution)/shard_map/ppermute | solution.py:57
  24.2 1.2 %collective-permute-done.2 = bf16[513,2,144]{0,2,1:T(8,128)(2,1)S(1)} collective-permute-done((bf16[513,2,144]{0,2,1:T(8,128)(2,1)S(1)}, bf16[513,2,144]{0,2,1:T(8,128)(2,1)S(1)}, u32[]{:S(2)}, u32[]{:S(2)}) %collective-permute-start.2) | collective-permute-done | bytes 295520 | tf_op jit(solution)/shard_map/ppermute | solution.py:52
  25.4 0.1 maximum_reduce_fusion
  25.6 0.1 reshape_squeeze.3
  25.7 3.7 %fusion.10 = bf16[136,144,3,6,3]{1,3,4,2,0:T(8,128)(2,1)} fusion(pred[9,136,144,1,1]{2,1,0,3,4:T(8,128)(4,1)S(1)} %fusion.29, bf16[6,3,3,9]{3,2,1,0:T(4,128)(2,1)S(1)} %reshape_squeeze.3), kind=kOutput, calls=%fused_computation.12 | convolution fusion | flops 19035648 | bytes 2292300 | tf_op jit(solution)/shard_map/kiad,dpq->iapkq/dot_general | solution.py:95
  29.4 1.5 %convert_bitcast_fusion = bf16[4,3,144,3,136]{2,0,1,3,4:T(4,128)(2,1)S(1)} fusion(bf16[3,6,3,9]{3,1,2,0:T(8,128)(2,1)S(1)} %bitcast.199), kind=kOutput, calls=%fused_computation.8 | convolution fusion | flops 13747968 | bytes 1419264 | tf_op jit(solution)/shard_map/kiad,dpq->iapkq/dot_general | solution.py:95
  31.0 1.3 %copy-done.1 = bf16[4,3,144,3,136]{2,0,1,3,4:T(4,128)(2,1)} copy-done((bf16[4,3,144,3,136]{2,0,1,3,4:T(4,128)(2,1)}, bf16[4,3,144,3,136]{2,0,1,3,4:T(4,128)(2,1)S(1)}, u32[]{:S(2)}) %copy-start.1) | copy-done | bytes 1410072
  32.3 0.8 fusion.24
  33.1 0.2 copy-done.3
  33.3 6.2 %fusion.14 = f32[256,6,3,136]{0,3,1,2:T(8,128)} fusion(bf16[513,2,144]{0,2,1:T(8,128)(2,1)S(1)} %collective-permute-done.3, bf16[513,2,144]{0,2,1:T(8,128)(2,1)S(1)} %collective-permute-done.2, bf16[1,2,144]{0,2,1:T(8,128)(2,1)S(1)} %copy.28, bf16[512,2,8]{0,2,1:T(8,128)(2,1)S(1)} %collective-permute-done.1, ...), kind=kOutput, calls=%fused_computation.14 | convolution fusion | flops 884957184 | bytes 5901504 | tf_op jit(solution)/shard_map/cikq,iapkq->ciap/dot_general | solution.py:115
  39.6 2.2 %fusion.46 = (bf16[256,4,136]{0,2,1:T(8,128)(2,1)S(1)}, bf16[256,4,136]{0,2,1:T(8,128)(2,1)S(1)}) fusion(f32[256,6,3,136]{0,3,1,2:T(8,128)} %fusion.14, pred[4]{0:T(512)(128)(4,1)S(1)} %compare_and_fusion, bf16[256,4,3,136]{0,3,2,1:T(8,128)(2,1)S(1)} %fusion.24, bf16[3,256,256]{2,1,0:T(8,128)(2,1)S(1)} %copy-done), kind=kOutput, calls=%fused_computation.54 | convolution fusion | flops 217808896 | bytes 3457028 | tf_op jit(solution)/shard_map/koc,cikj->oij/dot_general | solution.py:127
  41.9 0.4 fusion.31
  42.3 0.5 copy-done.2
  42.8 0.3 fusion.27
  43.1 0.1 collective-permute-start.4
  43.2 1.3 %fusion.28 = f32[256,3,256]{0,2,1:T(8,128)S(1)} fusion(bf16[256,4,3,136]{0,3,2,1:T(8,128)(2,1)} %copy-done.5, bf16[256,4,136]{0,2,1:T(8,128)(2,1)S(1)} %get-tuple-element.9), kind=kOutput, calls=%fused_computation.26 | convolution fusion | flops 100859904 | bytes 1310720 | tf_op jit(solution)/shard_map/oij,cikj->koc/dot_general | solution.py:137
  44.6 0.8 constant_dynamic-slice_fusion.4
  45.4 0.5 collective-permute-start.5
  45.9 1.6 %collective-permute-done.5 = f32[384,256]{1,0:T(8,128)} collective-permute-done((f32[384,256]{1,0:T(8,128)}, f32[384,256]{1,0:T(8,128)}, u32[]{:S(2)}, u32[]{:S(2)}) %collective-permute-start.5) | collective-permute-done | bytes 393248 | tf_op jit(solution)/shard_map/ppermute | solution.py:31
  47.5 1.0 %dynamic-slice_add_fusion = f32[384,256]{1,0:T(8,128)S(1)} fusion(f32[384,256]{1,0:T(8,128)} %collective-permute-done.5, f32[768,256]{1,0:T(8,128)S(1)} %bitcast.198, s32[]{:T(128)S(6)} %select_n.121), kind=kLoop, calls=%fused_computation.83 | loop fusion | flops 98304 | bytes 1179652 | tf_op jit(solution)/shard_map/add | solution.py:31
  48.6 1.6 %collective-permute-start.6 = (f32[192,256]{1,0:T(8,128)S(1)}, f32[192,256]{1,0:T(8,128)S(1)}, u32[]{:S(2)}, u32[]{:S(2)}) collective-permute-start(f32[192,256]{1,0:T(8,128)S(1)} %constant_dynamic-slice_fusion.3), channel_id=1, source_target_pairs={{0,16},{8,24},{16,0},{24,8},{1,17},{9,25},{17,1},{25,9},{2,18},{10... | collective-permute-start | bytes 589832 | tf_op jit(solution)/shard_map/ppermute | solution.py:31
  50.2 0.6 collective-permute-start.13
  50.8 4.0 %fusion.17 = f32[256,4,3,144]{0,3,2,1:T(8,128)} fusion(bf16[4,3,144,3,136]{2,0,1,3,4:T(4,128)(2,1)} %copy-done.1, bf16[3,256,256]{2,1,0:T(8,128)(2,1)S(1)} %copy-done, bf16[256,4,136]{0,2,1:T(8,128)(2,1)} %copy-done.6), kind=kOutput, calls=%fused_computation.17 | convolution fusion | flops 575299584 | bytes 3851264 | tf_op jit(solution)/shard_map/cikq,iapkq->ciap/dot_general | solution.py:115
  54.8 1.7 %collective-permute-done.6 = f32[192,256]{1,0:T(8,128)S(1)} collective-permute-done((f32[192,256]{1,0:T(8,128)S(1)}, f32[192,256]{1,0:T(8,128)S(1)}, u32[]{:S(2)}, u32[]{:S(2)}) %collective-permute-start.6) | collective-permute-done | bytes 196640 | tf_op jit(solution)/shard_map/ppermute | solution.py:31
  56.5 2.6 %collective-permute-start.7 = (f32[96,256]{1,0:T(8,128)S(1)}, f32[96,256]{1,0:T(8,128)S(1)}, u32[]{:S(2)}, u32[]{:S(2)}) collective-permute-start(f32[96,256]{1,0:T(8,128)S(1)} %constant_dynamic-slice_fusion.2), channel_id=1, source_target_pairs={{0,4},{4,0},{1,5},{5,1},{2,6},{6,2},{3,7},{7,3},{8,12},{12,8},{9,1... | collective-permute-start | bytes 294920 | tf_op jit(solution)/shard_map/ppermute | solution.py:31
  59.1 1.0 %collective-permute-done.13 = f32[192,256]{1,0:T(8,128)S(1)} collective-permute-done((f32[192,256]{1,0:T(8,128)S(1)}, f32[192,256]{1,0:T(8,128)S(1)}, u32[]{:S(2)}, u32[]{:S(2)}) %collective-permute-start.13) | collective-permute-done | bytes 196640 | tf_op jit(solution)/shard_map/ppermute | solution.py:31
  60.1 2.6 %collective-permute-start.14 = (f32[96,256]{1,0:T(8,128)S(1)}, f32[96,256]{1,0:T(8,128)S(1)}, u32[]{:S(2)}, u32[]{:S(2)}) collective-permute-start(f32[96,256]{1,0:T(8,128)S(1)} %constant_dynamic-slice_fusion), channel_id=1, source_target_pairs={{0,4},{4,0},{1,5},{5,1},{2,6},{6,2},{3,7},{7,3},{8,12},{12,8},{9,1... | collective-permute-start | bytes 294920 | tf_op jit(solution)/shard_map/ppermute | solution.py:31
  62.7 0.1 collective-permute-start.8
  62.8 2.5 %collective-permute-done.14 = f32[96,256]{1,0:T(8,128)S(1)} collective-permute-done((f32[96,256]{1,0:T(8,128)S(1)}, f32[96,256]{1,0:T(8,128)S(1)}, u32[]{:S(2)}, u32[]{:S(2)}) %collective-permute-start.14) | collective-permute-done | bytes 98336 | tf_op jit(solution)/shard_map/ppermute | solution.py:31
  65.3 0.1 collective-permute-start.15
  65.4 2.8 %collective-permute-done.8 = f32[96,256]{1,0:T(8,128)S(1)} collective-permute-done((f32[96,256]{1,0:T(8,128)S(1)}, f32[96,256]{1,0:T(8,128)S(1)}, u32[]{:S(2)}, u32[]{:S(2)}) %collective-permute-start.8) | collective-permute-done | bytes 98336 | tf_op jit(solution)/shard_map/ppermute | solution.py:37
  68.2 0.1 collective-permute-start.9
  68.3 1.2 %fusion.74 = bf16[1,256,2,128]{1,3,2,0:T(8,128)(2,1)S(1)} fusion(f32[256,4,3,144]{0,3,2,1:T(8,128)} %fusion.17), kind=kLoop, calls=%fused_computation.112 | loop fusion | flops 196608 | bytes 917504 | tf_op jit(solution)/shard_map/convert_element_type | solution.py:190
  69.4 1.6 %collective-permute-done.15 = f32[96,256]{1,0:T(8,128)S(1)} collective-permute-done((f32[96,256]{1,0:T(8,128)S(1)}, f32[96,256]{1,0:T(8,128)S(1)}, u32[]{:S(2)}, u32[]{:S(2)}) %collective-permute-start.15) | collective-permute-done | bytes 98336 | tf_op jit(solution)/shard_map/ppermute | solution.py:37
  71.0 1.4 %collective-permute-start.16 = (f32[96,256]{1,0:T(8,128)S(1)}, f32[96,256]{1,0:T(8,128)S(1)}, u32[]{:S(2)}, u32[]{:S(2)}) collective-permute-start(f32[96,256]{1,0:T(8,128)S(1)} %add.180), channel_id=1, source_target_pairs={{0,2},{1,3},{2,0},{3,1},{4,6},{5,7},{6,4},{7,5},{8,10},{9,11},{10,... | collective-permute-start | bytes 294920 | tf_op jit(solution)/shard_map/ppermute | solution.py:37
  72.4 4.3 %collective-permute-done.9 = f32[96,256]{1,0:T(8,128)S(1)} collective-permute-done((f32[96,256]{1,0:T(8,128)S(1)}, f32[96,256]{1,0:T(8,128)S(1)}, u32[]{:S(2)}, u32[]{:S(2)}) %collective-permute-start.9) | collective-permute-done | bytes 98336 | tf_op jit(solution)/shard_map/ppermute | solution.py:37
  76.7 1.1 %collective-permute-start.10 = (bf16[96,256]{1,0:T(8,128)(2,1)S(1)}, bf16[96,256]{1,0:T(8,128)(2,1)S(1)}, u32[]{:S(2)}, u32[]{:S(2)}) collective-permute-start(bf16[96,256]{1,0:T(8,128)(2,1)S(1)} %add_convert_fusion.1), channel_id=1, source_target_pairs={{0,4},{4,0},{1,5},{5,1},{2,6},{6,2},{3,7},{7,3},{8,12},{12,8},{9,1... | collective-permute-start | bytes 147464 | tf_op jit(solution)/shard_map/ppermute | solution.py:42
  77.9 1.0 %collective-permute-start.17 = (bf16[96,256]{1,0:T(8,128)(2,1)S(1)}, bf16[96,256]{1,0:T(8,128)(2,1)S(1)}, u32[]{:S(2)}, u32[]{:S(2)}) collective-permute-start(bf16[96,256]{1,0:T(8,128)(2,1)S(1)} %add_convert_fusion), channel_id=1, source_target_pairs={{0,4},{4,0},{1,5},{5,1},{2,6},{6,2},{3,7},{7,3},{8,12},{12,8},{9,1... | collective-permute-start | bytes 147464 | tf_op jit(solution)/shard_map/ppermute | solution.py:42
  78.9 2.0 %collective-permute-done.10 = bf16[96,256]{1,0:T(8,128)(2,1)S(1)} collective-permute-done((bf16[96,256]{1,0:T(8,128)(2,1)S(1)}, bf16[96,256]{1,0:T(8,128)(2,1)S(1)}, u32[]{:S(2)}, u32[]{:S(2)}) %collective-permute-start.10) | collective-permute-done | bytes 49184 | tf_op jit(solution)/shard_map/ppermute | solution.py:42
  80.9 1.6 %collective-permute-start.11 = (bf16[192,256]{1,0:T(8,128)(2,1)S(1)}, bf16[192,256]{1,0:T(8,128)(2,1)S(1)}, u32[]{:S(2)}, u32[]{:S(2)}) collective-permute-start(bf16[192,256]{1,0:T(8,128)(2,1)S(1)} %maximum_select_fusion.4), channel_id=1, source_target_pairs={{0,16},{8,24},{16,0},{24,8},{1,17},{9,25},{17,1},{25,9},{2,18},{10... | collective-permute-start | bytes 294920 | tf_op jit(solution)/shard_map/ppermute | solution.py:42
  82.5 1.1 %collective-permute-start.18 = (bf16[192,256]{1,0:T(8,128)(2,1)S(1)}, bf16[192,256]{1,0:T(8,128)(2,1)S(1)}, u32[]{:S(2)}, u32[]{:S(2)}) collective-permute-start(bf16[192,256]{1,0:T(8,128)(2,1)S(1)} %maximum_select_fusion.5), channel_id=1, source_target_pairs={{0,16},{8,24},{16,0},{24,8},{1,17},{9,25},{17,1},{25,9},{2,18},{10... | collective-permute-start | bytes 294920 | tf_op jit(solution)/shard_map/ppermute | solution.py:42
  83.6 2.0 %collective-permute-done.11 = bf16[192,256]{1,0:T(8,128)(2,1)S(1)} collective-permute-done((bf16[192,256]{1,0:T(8,128)(2,1)S(1)}, bf16[192,256]{1,0:T(8,128)(2,1)S(1)}, u32[]{:S(2)}, u32[]{:S(2)}) %collective-permute-start.11) | collective-permute-done | bytes 98336 | tf_op jit(solution)/shard_map/ppermute | solution.py:42
  85.6 0.1 collective-permute-start.12
  85.7 1.4 %collective-permute-done.18 = bf16[192,256]{1,0:T(8,128)(2,1)S(1)} collective-permute-done((bf16[192,256]{1,0:T(8,128)(2,1)S(1)}, bf16[192,256]{1,0:T(8,128)(2,1)S(1)}, u32[]{:S(2)}, u32[]{:S(2)}) %collective-permute-start.18) | collective-permute-done | bytes 98336 | tf_op jit(solution)/shard_map/ppermute | solution.py:42
  87.3 0.3 fusion.33
  87.6 0.8 copy.40
  88.4 0.8 copy.41
  89.2 0.2 maximum_select_fusion
  89.3 0.9 %convert.5 = f32[3,256,256]{2,1,0:T(8,128)} convert(bf16[3,256,256]{2,1,0:T(8,128)(2,1)S(1)} %bitcast.196) | non-fusion elementwise | flops 196608 | bytes 1179648 | tf_op jit(solution)/shard_map/convert_element_type | solution.py:46
  90.3 0.2 maximum_select_fusion.1
  90.4 0.9 %convert.6 = f32[3,256,256]{2,1,0:T(8,128)} convert(bf16[3,256,256]{2,1,0:T(8,128)(2,1)S(1)} %bitcast.195) | non-fusion elementwise | flops 196608 | bytes 1179648 | tf_op jit(solution)/shard_map/convert_element_type | solution.py:46
  (47 shorter events, 0.7 us)
Async XLA Ops:
  0.6 38.9 %copy-start = (bf16[3,256,256]{2,1,0:T(8,128)(2,1)S(1)}, bf16[3,256,256]{2,1,0:T(8,128)(2,1)}, u32[]{:S(2)}) copy-start(bf16[3,256,256]{2,1,0:T(8,128)(2,1)} %param.8) | copy-start | bytes 1179652
  2.8 7.4 %collective-permute-start.1 = (bf16[512,2,8]{0,2,1:T(8,128)(2,1)S(1)}, bf16[512,2,8]{0,2,1:T(8,128)(2,1)S(1)}, u32[]{:S(2)}, u32[]{:S(2)}) collective-permute-start(bf16[512,2,8]{0,2,1:T(8,128)(2,1)S(1)} %get-tuple-element.29), channel_id=1, source_target_pairs={{0,3},{1,0},{2,1},{3,2},{4,7},{5,4},{6,5},{7,6},{8,11},{9,8},{10,9... | collective-permute-start | bytes 49160 | tf_op jit(solution)/shard_map/ppermute | solution.py:67
  7.9 5.5 %collective-permute-start = (bf16[512,2,8]{0,2,1:T(8,128)(2,1)S(1)}, bf16[512,2,8]{0,2,1:T(8,128)(2,1)S(1)}, u32[]{:S(2)}, u32[]{:S(2)}) collective-permute-start(bf16[512,2,8]{0,2,1:T(8,128)(2,1)S(1)} %get-tuple-element.28), channel_id=1, source_target_pairs={{0,1},{1,2},{2,3},{3,0},{4,5},{5,6},{6,7},{7,4},{8,9},{9,10},{10,1... | collective-permute-start | bytes 49160 | tf_op jit(solution)/shard_map/ppermute | solution.py:66
  13.5 10.8 %collective-permute-start.3 = (bf16[513,2,144]{0,2,1:T(8,128)(2,1)S(1)}, bf16[513,2,144]{0,2,1:T(8,128)(2,1)S(1)}, u32[]{:S(2)}, u32[]{:S(2)}) collective-permute-start(bf16[513,2,144]{0,2,1:T(8,128)(2,1)S(1)} %pad_maximum_fusion.16), channel_id=1, source_target_pairs={{4,0},{5,1},{6,2},{7,3},{12,8},{13,9},{14,10},{15,11},{20,16},{21,... | collective-permute-start | bytes 886472 | tf_op jit(solution)/shard_map/ppermute | solution.py:57
  14.8 10.7 %collective-permute-start.2 = (bf16[513,2,144]{0,2,1:T(8,128)(2,1)S(1)}, bf16[513,2,144]{0,2,1:T(8,128)(2,1)S(1)}, u32[]{:S(2)}, u32[]{:S(2)}) collective-permute-start(bf16[513,2,144]{0,2,1:T(8,128)(2,1)S(1)} %pad_maximum_fusion.16), channel_id=1, source_target_pairs={{0,4},{1,5},{2,6},{3,7},{8,12},{9,13},{10,14},{11,15},{16,20},{17,... | collective-permute-start | bytes 886472 | tf_op jit(solution)/shard_map/ppermute | solution.py:52
  30.9 1.4 %copy-start.1 = (bf16[4,3,144,3,136]{2,0,1,3,4:T(4,128)(2,1)}, bf16[4,3,144,3,136]{2,0,1,3,4:T(4,128)(2,1)S(1)}, u32[]{:S(2)}) copy-start(bf16[4,3,144,3,136]{2,0,1,3,4:T(4,128)(2,1)S(1)} %convert_bitcast_fusion) | copy-start | bytes 4230148
  32.3 1.0 %copy-start.3 = (bf16[3,256,256]{2,1,0:T(8,128)(2,1)S(1)}, bf16[3,256,256]{2,1,0:T(8,128)(2,1)}, u32[]{:S(2)}) copy-start(bf16[3,256,256]{2,1,0:T(8,128)(2,1)} %param.9) | copy-start | bytes 1179652
  33.3 6.2 %copy-start.5 = (bf16[256,4,3,136]{0,3,2,1:T(8,128)(2,1)}, bf16[256,4,3,136]{0,3,2,1:T(8,128)(2,1)S(1)}, u32[]{:S(2)}) copy-start(bf16[256,4,3,136]{0,3,2,1:T(8,128)(2,1)S(1)} %fusion.24) | copy-start | bytes 2506756
  39.6 2.3 %copy-start.4 = (bf16[136,128,3,2,3]{1,4,3,2,0:T(4,128)(2,1)S(1)}, bf16[136,128,3,2,3]{1,4,3,2,0:T(4,128)(2,1)}, u32[]{:S(2)}) copy-start(bf16[136,128,3,2,3]{1,4,3,2,0:T(4,128)(2,1)} %fusion.34) | copy-start | bytes 1880068
  41.8 1.4 %copy-start.6 = (bf16[256,4,136]{0,2,1:T(8,128)(2,1)}, bf16[256,4,136]{0,2,1:T(8,128)(2,1)S(1)}, u32[]{:S(2)}) copy-start(bf16[256,4,136]{0,2,1:T(8,128)(2,1)S(1)} %get-tuple-element.9) | copy-start | bytes 835588
  41.8 1.0 %copy-start.2 = (bf16[1,256,2,128]{3,2,1,0:T(2,128)(2,1)S(1)}, bf16[1,256,2,128]{3,2,1,0:T(2,128)(2,1)}, u32[]{:S(2)}) copy-start(bf16[1,256,2,128]{3,2,1,0:T(2,128)(2,1)} %param.13) | copy-start | bytes 393220
  43.1 2.7 %collective-permute-start.4 = (f32[384,256]{1,0:T(8,128)S(1)}, f32[384,256]{1,0:T(8,128)S(1)}, u32[]{:S(2)}, u32[]{:S(2)}) collective-permute-start(f32[384,256]{1,0:T(8,128)S(1)} %constant_dynamic-slice_fusion.5), channel_id=1, source_target_pairs={{0,8},{8,0},{16,24},{24,16},{1,9},{9,1},{17,25},{25,17},{2,10},{10... | collective-permute-start | bytes 1179656 | tf_op jit(solution)/shard_map/ppermute | solution.py:31
  45.4 2.2 %collective-permute-start.5 = (f32[384,256]{1,0:T(8,128)}, f32[384,256]{1,0:T(8,128)}, u32[]{:S(2)}, u32[]{:S(2)}) collective-permute-start(f32[384,256]{1,0:T(8,128)} %constant_dynamic-slice_fusion.4), channel_id=1, source_target_pairs={{0,8},{8,0},{16,24},{24,16},{1,9},{9,1},{17,25},{25,17},{2,10},{10... | collective-permute-start | bytes 1179656 | tf_op jit(solution)/shard_map/ppermute | solution.py:31
  48.6 7.8 %collective-permute-start.6 = (f32[192,256]{1,0:T(8,128)S(1)}, f32[192,256]{1,0:T(8,128)S(1)}, u32[]{:S(2)}, u32[]{:S(2)}) collective-permute-start(f32[192,256]{1,0:T(8,128)S(1)} %constant_dynamic-slice_fusion.3), channel_id=1, source_target_pairs={{0,16},{8,24},{16,0},{24,8},{1,17},{9,25},{17,1},{25,9},{2,18},{10... | collective-permute-start | bytes 589832 | tf_op jit(solution)/shard_map/ppermute | solution.py:31
  50.2 9.9 %collective-permute-start.13 = (f32[192,256]{1,0:T(8,128)S(1)}, f32[192,256]{1,0:T(8,128)S(1)}, u32[]{:S(2)}, u32[]{:S(2)}) collective-permute-start(f32[192,256]{1,0:T(8,128)S(1)} %constant_dynamic-slice_fusion.1), channel_id=1, source_target_pairs={{0,16},{8,24},{16,0},{24,8},{1,17},{9,25},{17,1},{25,9},{2,18},{10... | collective-permute-start | bytes 589832 | tf_op jit(solution)/shard_map/ppermute | solution.py:31
  56.5 6.2 %collective-permute-start.7 = (f32[96,256]{1,0:T(8,128)S(1)}, f32[96,256]{1,0:T(8,128)S(1)}, u32[]{:S(2)}, u32[]{:S(2)}) collective-permute-start(f32[96,256]{1,0:T(8,128)S(1)} %constant_dynamic-slice_fusion.2), channel_id=1, source_target_pairs={{0,4},{4,0},{1,5},{5,1},{2,6},{6,2},{3,7},{7,3},{8,12},{12,8},{9,1... | collective-permute-start | bytes 294920 | tf_op jit(solution)/shard_map/ppermute | solution.py:31
  60.1 5.1 %collective-permute-start.14 = (f32[96,256]{1,0:T(8,128)S(1)}, f32[96,256]{1,0:T(8,128)S(1)}, u32[]{:S(2)}, u32[]{:S(2)}) collective-permute-start(f32[96,256]{1,0:T(8,128)S(1)} %constant_dynamic-slice_fusion), channel_id=1, source_target_pairs={{0,4},{4,0},{1,5},{5,1},{2,6},{6,2},{3,7},{7,3},{8,12},{12,8},{9,1... | collective-permute-start | bytes 294920 | tf_op jit(solution)/shard_map/ppermute | solution.py:31
  62.7 5.5 %collective-permute-start.8 = (f32[96,256]{1,0:T(8,128)S(1)}, f32[96,256]{1,0:T(8,128)S(1)}, u32[]{:S(2)}, u32[]{:S(2)}) collective-permute-start(f32[96,256]{1,0:T(8,128)S(1)} %dynamic-slice_add_fusion.5), channel_id=1, source_target_pairs={{0,1},{1,0},{2,3},{3,2},{4,5},{5,4},{6,7},{7,6},{8,9},{9,8},{10,11... | collective-permute-start | bytes 294920 | tf_op jit(solution)/shard_map/ppermute | solution.py:37
  65.3 5.7 %collective-permute-start.15 = (f32[96,256]{1,0:T(8,128)S(1)}, f32[96,256]{1,0:T(8,128)S(1)}, u32[]{:S(2)}, u32[]{:S(2)}) collective-permute-start(f32[96,256]{1,0:T(8,128)S(1)} %dynamic-slice_add_fusion.4), channel_id=1, source_target_pairs={{0,1},{1,0},{2,3},{3,2},{4,5},{5,4},{6,7},{7,6},{8,9},{9,8},{10,11... | collective-permute-start | bytes 294920 | tf_op jit(solution)/shard_map/ppermute | solution.py:37
  68.2 8.5 %collective-permute-start.9 = (f32[96,256]{1,0:T(8,128)S(1)}, f32[96,256]{1,0:T(8,128)S(1)}, u32[]{:S(2)}, u32[]{:S(2)}) collective-permute-start(f32[96,256]{1,0:T(8,128)S(1)} %add.176), channel_id=1, source_target_pairs={{0,2},{1,3},{2,0},{3,1},{4,6},{5,7},{6,4},{7,5},{8,10},{9,11},{10,... | collective-permute-start | bytes 294920 | tf_op jit(solution)/shard_map/ppermute | solution.py:37
  71.0 6.8 %collective-permute-start.16 = (f32[96,256]{1,0:T(8,128)S(1)}, f32[96,256]{1,0:T(8,128)S(1)}, u32[]{:S(2)}, u32[]{:S(2)}) collective-permute-start(f32[96,256]{1,0:T(8,128)S(1)} %add.180), channel_id=1, source_target_pairs={{0,2},{1,3},{2,0},{3,1},{4,6},{5,7},{6,4},{7,5},{8,10},{9,11},{10,... | collective-permute-start | bytes 294920 | tf_op jit(solution)/shard_map/ppermute | solution.py:37
  76.7 4.2 %collective-permute-start.10 = (bf16[96,256]{1,0:T(8,128)(2,1)S(1)}, bf16[96,256]{1,0:T(8,128)(2,1)S(1)}, u32[]{:S(2)}, u32[]{:S(2)}) collective-permute-start(bf16[96,256]{1,0:T(8,128)(2,1)S(1)} %add_convert_fusion.1), channel_id=1, source_target_pairs={{0,4},{4,0},{1,5},{5,1},{2,6},{6,2},{3,7},{7,3},{8,12},{12,8},{9,1... | collective-permute-start | bytes 147464 | tf_op jit(solution)/shard_map/ppermute | solution.py:42
  77.9 4.6 %collective-permute-start.17 = (bf16[96,256]{1,0:T(8,128)(2,1)S(1)}, bf16[96,256]{1,0:T(8,128)(2,1)S(1)}, u32[]{:S(2)}, u32[]{:S(2)}) collective-permute-start(bf16[96,256]{1,0:T(8,128)(2,1)S(1)} %add_convert_fusion), channel_id=1, source_target_pairs={{0,4},{4,0},{1,5},{5,1},{2,6},{6,2},{3,7},{7,3},{8,12},{12,8},{9,1... | collective-permute-start | bytes 147464 | tf_op jit(solution)/shard_map/ppermute | solution.py:42
  80.9 4.7 %collective-permute-start.11 = (bf16[192,256]{1,0:T(8,128)(2,1)S(1)}, bf16[192,256]{1,0:T(8,128)(2,1)S(1)}, u32[]{:S(2)}, u32[]{:S(2)}) collective-permute-start(bf16[192,256]{1,0:T(8,128)(2,1)S(1)} %maximum_select_fusion.4), channel_id=1, source_target_pairs={{0,16},{8,24},{16,0},{24,8},{1,17},{9,25},{17,1},{25,9},{2,18},{10... | collective-permute-start | bytes 294920 | tf_op jit(solution)/shard_map/ppermute | solution.py:42
  82.5 4.7 %collective-permute-start.18 = (bf16[192,256]{1,0:T(8,128)(2,1)S(1)}, bf16[192,256]{1,0:T(8,128)(2,1)S(1)}, u32[]{:S(2)}, u32[]{:S(2)}) collective-permute-start(bf16[192,256]{1,0:T(8,128)(2,1)S(1)} %maximum_select_fusion.5), channel_id=1, source_target_pairs={{0,16},{8,24},{16,0},{24,8},{1,17},{9,25},{17,1},{25,9},{2,18},{10... | collective-permute-start | bytes 294920 | tf_op jit(solution)/shard_map/ppermute | solution.py:42
  85.6 3.5 %collective-permute-start.12 = (bf16[384,256]{1,0:T(8,128)(2,1)S(1)}, bf16[384,256]{1,0:T(8,128)(2,1)S(1)}, u32[]{:S(2)}, u32[]{:S(2)}) collective-permute-start(bf16[384,256]{1,0:T(8,128)(2,1)S(1)} %maximum_select_fusion.2), channel_id=1, source_target_pairs={{0,8},{8,0},{16,24},{24,16},{1,9},{9,1},{17,25},{25,17},{2,10},{10... | collective-permute-start | bytes 589832 | tf_op jit(solution)/shard_map/ppermute | solution.py:42
  87.2 3.1 %collective-permute-start.19 = (bf16[384,256]{1,0:T(8,128)(2,1)S(1)}, bf16[384,256]{1,0:T(8,128)(2,1)S(1)}, u32[]{:S(2)}, u32[]{:S(2)}) collective-permute-start(bf16[384,256]{1,0:T(8,128)(2,1)S(1)} %maximum_select_fusion.3), channel_id=1, source_target_pairs={{0,8},{8,0},{16,24},{24,16},{1,9},{9,1},{17,25},{25,17},{2,10},{10... | collective-permute-start | bytes 589832 | tf_op jit(solution)/shard_map/ppermute | solution.py:42

commit v8 on v7

--- a/solution.py
+++ b/solution.py
@@ -46,26 +46,40 @@
     return flat.astype(jnp.float32).reshape(value.shape), held
 
 
-def lat_halo(block, dim, width):
-    count = lax.axis_size("lat")
-    rows = block.shape[dim]
-    above = lax.ppermute(
-        lax.slice_in_dim(block, rows - width, rows, axis=dim),
-        "lat",
-        [(i, i + 1) for i in range(count - 1)],
-    )
-    below = lax.ppermute(
-        lax.slice_in_dim(block, 0, width, axis=dim), "lat", [(i + 1, i) for i in range(count - 1)]
-    )
-    return jnp.concatenate([above, block, below], axis=dim)
-
-
-def lon_halo(block, width):
-    count = lax.axis_size("lon")
-    cols = block.shape[-1]
-    left = lax.ppermute(block[..., cols - width :], "lon", [(i, (i + 1) % count) for i in range(count)])
-    right = lax.ppermute(block[..., :width], "lon", [(i, (i - 1) % count) for i in range(count)])
-    return jnp.concatenate([left, block, right], axis=-1)
+def neighbour_piece(block, lat_step, lon_step, lat_width, lon_width):
+    lat_count, lon_count = lax.axis_size("lat"), lax.axis_size("lon")
+    rows, cols = block.shape[1], block.shape[2]
+    if lat_step:
+        block = block[:, rows - lat_width :] if lat_step < 0 else block[:, :lat_width]
+    if lon_step:
+        block = block[:, :, cols - lon_width :] if lon_step < 0 else block[:, :, :lon_width]
+    if not lat_step:
+        pairs = [(lo, (lo - lon_step) % lon_count) for lo in range(lon_count)]
+        return lax.ppermute(block, "lon", pairs)
+    pairs = [
+        (la * lon_count + lo, (la - lat_step) * lon_count + (lo - lon_step) % lon_count)
+        for la in range(lat_count)
+        for lo in range(lon_count)
+        if 0 <= la - lat_step < lat_count
+    ]
+    if not lon_step:
+        pairs = [(s // lon_count, t // lon_count) for s, t in pairs if s % lon_count == 0]
+        return lax.ppermute(block, "lat", pairs)
+    return lax.ppermute(block, ("lat", "lon"), pairs)
+
+
+def framed_of(block, extra, lat_width, lon_width):
+    channels = block.shape[0]
+    tall = jnp.concatenate([block, extra], axis=0)
+    above = neighbour_piece(tall, -1, 0, lat_width, lon_width)
+    below = neighbour_piece(tall, 1, 0, lat_width, lon_width)
+    bands = []
+    for lat_step, centre in ((-1, above[:channels]), (0, block), (1, below[:channels])):
+        left = neighbour_piece(block, lat_step, -1, lat_width, lon_width)
+        right = neighbour_piece(block, lat_step, 1, lat_width, lon_width)
+        bands.append(jnp.concatenate([left, centre, right], axis=2))
+    extra_rows = jnp.concatenate([above[channels:], extra, below[channels:]], axis=1)
+    return jnp.concatenate(bands, axis=1), extra_rows
 
 
 def coefficients(quadrature, lat_offsets, lon_offsets):
@@ -144,13 +158,13 @@
     stencil = coefficients(quadrature, lat_offsets, lon_offsets)
     basis_count = stencil.shape[0]
 
-    packed = lon_halo(jnp.concatenate([source, gradient], axis=0), LON_HALO)
+    packed = jnp.concatenate([source, gradient], axis=0)
     taps_per_row = stencil.size // row_count
     stencil_rows = jnp.transpose(stencil, (1, 0, 2, 3)).reshape(row_count, taps_per_row)
-    stencil_rows = jnp.pad(stencil_rows, ((0, 0), (0, packed.shape[2] - taps_per_row)))
-    framed = lat_halo(jnp.concatenate([packed, stencil_rows[None]], axis=0), 1, LAT_HALO)
-    source_wide, gradient_wide = framed[:channels], framed[channels : 2 * channels]
-    stencil_wide = framed[2 * channels, :, :taps_per_row].reshape(
+    stencil_rows = jnp.pad(stencil_rows, ((0, 0), (0, col_count - taps_per_row)))
+    framed, stencil_wide = framed_of(packed, stencil_rows[None], LAT_HALO, LON_HALO)
+    source_wide, gradient_wide = framed[:channels], framed[channels:]
+    stencil_wide = stencil_wide[0, :, :taps_per_row].reshape(
         row_count + 2 * LAT_HALO, stencil.shape[0], stencil.shape[2], stencil.shape[3]
     )
     stencil_wide = jnp.transpose(stencil_wide, (1, 0, 2, 3))

time: 91.9 us -> 102 us (1.11)
  starting transfers between devices: 25.4 us -> 44.4 us
  waiting for transfers between devices: 28.7 us -> 19.6 us
  matrix products: 23.1 us -> 24.7 us
  local copies, waits for them, and re-layouts: 7.01 us -> 5.63 us
    ppermute x4 -> x8, starting transfers between devices: 11 us -> 24.7 us  [the longest x4 12.1 us: neighbour_piece(): return lax.ppermute(block, ('lat', 'lon'), pairs)]
    ppermute x4 -> x8, waiting for transfers between devices: 7.87 us -> 1.16 us  [the longest x4 1.15 us: neighbour_piece(): return lax.ppermute(block, ('lat', 'lon'), pairs)]
    ppermute x6, starting transfers between devices: 7.82 us -> 11.9 us  [halving_sum(): flat = keep + lax.ppermute(send, axis, pairs)]
    unnamed x18, local copies, waits for them, and re-layouts: 5.75 us -> 4.14 us
    ppermute x4, waiting for transfers between devices: 8.68 us -> 7.57 us  [halving_sum(): flat = flat + lax.ppermute(flat, axis, pairs)]
  transfers between devices with their start and end apart: 20 -> 24, of which waited for: 13 -> 10; matrix products, arithmetic and copies ran while one was open for 16% -> 18% of each run, Pallas kernels for 0% -> 0%
where the time goes in v8:
time: 102 us; the launch traced here: 101 us
  starting transfers between devices  44.4 us (44%)
  matrix products  24.7 us (24%)
  waiting for transfers between devices  19.6 us (19%)
  local copies, waits for them, and re-layouts  5.63 us (6%)
  other arithmetic  5.63 us (6%)
  between operations  1.14 us (1%)
    ppermute x4, starting transfers between devices, neighbour_piece(): return lax.ppermute(block, ('lat', 'lon'), pairs)  12.1 us
    ppermute x6, starting transfers between devices, halving_sum(): flat = keep + lax.ppermute(send, axis, pairs)  11.9 us
    dot_general x2, matrix products, spread_adjoint(): jnp.einsum('cikq,iapkq->ciap', mixed, band, preferred_element_type=jnp.fl...  10 us
    dot_general x3, matrix products, band_of(): jnp.einsum('kiad,dpq->iapkq', stencil, lon_picker(col_count, first_source...  7.58 us
    ppermute x4, waiting for transfers between devices, halving_sum(): flat = flat + lax.ppermute(flat, axis, pairs)  7.57 us
    ppermute x2, starting transfers between devices, neighbour_piece(): return lax.ppermute(block, 'lon', pairs)  6.4 us
    ppermute x2, starting transfers between devices, neighbour_piece(): return lax.ppermute(block, 'lat', pairs)  6.23 us
    ppermute x6, waiting for transfers between devices, halving_sum(): flat = keep + lax.ppermute(send, axis, pairs)  5.82 us
  transfers between devices with their start and end apart: 24, of which 10 were waited for; matrix products, arithmetic and copies ran while one was open for 18% of the time, Pallas kernels for 0%

profile of v8, /device:TPU:0, one launch (start us, length us, event | category | flops | bytes accessed | tf_op | source)
XLA Modules:
  0.0 101.2 jit_solution(8615283057499583924)
XLA Ops:
  0.6 0.8 broadcast_add_fusion
  1.4 0.9 convolution_convert_fusion.3
  2.3 0.1 reshape.80
  2.4 0.1 copy.46
  2.6 1.0 %copy.44 = bf16[1,256,2,128]{1,3,2,0:T(8,128)(2,1)S(1)} copy(bf16[1,256,2,128]{3,2,1,0:T(2,128)(2,1)} %param.13) | data formatting | bytes 262144 | tf_op args[6]
  3.6 1.0 %copy.43 = bf16[1,256,2,128]{1,3,2,0:T(8,128)(2,1)S(1)} copy(bf16[1,256,2,128]{3,2,1,0:T(2,128)(2,1)} %param.7) | data formatting | bytes 262144 | tf_op args[0]
  4.6 1.3 %collective-permute-start.1 = (bf16[513,2,128]{0,2,1:T(8,128)(2,1)S(1)}, bf16[513,2,128]{0,2,1:T(8,128)(2,1)S(1)}, u32[]{:S(2)}, u32[]{:S(2)}) collective-permute-start(bf16[513,2,128]{0,2,1:T(8,128)(2,1)S(1)} %pad_maximum_fusion.17), channel_id=1, source_target_pairs={{4,0},{5,1},{6,2},{7,3},{12,8},{13,9},{14,10},{15,11},{20,16},{21,... | collective-permute-start | bytes 787976 | tf_op jit(solution)/shard_map/ppermute | solution.py:67
  5.9 4.9 %collective-permute-start = (bf16[513,2,128]{0,2,1:T(8,128)(2,1)S(1)}, bf16[513,2,128]{0,2,1:T(8,128)(2,1)S(1)}, u32[]{:S(2)}, u32[]{:S(2)}) collective-permute-start(bf16[513,2,128]{0,2,1:T(8,128)(2,1)S(1)} %pad_maximum_fusion.17), channel_id=1, source_target_pairs={{0,4},{1,5},{2,6},{3,7},{8,12},{9,13},{10,14},{11,15},{16,20},{17,... | collective-permute-start | bytes 787976 | tf_op jit(solution)/shard_map/ppermute | solution.py:67
  10.9 1.3 %collective-permute-start.7 = (bf16[512,2,8]{0,2,1:T(8,128)(2,1)S(1)}, bf16[512,2,8]{0,2,1:T(8,128)(2,1)S(1)}, u32[]{:S(2)}, u32[]{:S(2)}) collective-permute-start(bf16[512,2,8]{0,2,1:T(8,128)(2,1)S(1)} %get-tuple-element.32), channel_id=1, source_target_pairs={{4,3},{5,0},{6,1},{7,2},{12,11},{13,8},{14,9},{15,10},{20,19},{21,... | collective-permute-start | bytes 49160 | tf_op jit(solution)/shard_map/ppermute | solution.py:68
  12.2 4.8 %collective-permute-start.5 = (bf16[512,2,8]{0,2,1:T(8,128)(2,1)S(1)}, bf16[512,2,8]{0,2,1:T(8,128)(2,1)S(1)}, u32[]{:S(2)}, u32[]{:S(2)}) collective-permute-start(bf16[512,2,8]{0,2,1:T(8,128)(2,1)S(1)} %get-tuple-element.32), channel_id=1, source_target_pairs={{0,3},{1,0},{2,1},{3,2},{4,7},{5,4},{6,5},{7,6},{8,11},{9,8},{10,9... | collective-permute-start | bytes 49160 | tf_op jit(solution)/shard_map/ppermute | solution.py:58
  17.0 4.3 %collective-permute-start.3 = (bf16[512,2,8]{0,2,1:T(8,128)(2,1)S(1)}, bf16[512,2,8]{0,2,1:T(8,128)(2,1)S(1)}, u32[]{:S(2)}, u32[]{:S(2)}) collective-permute-start(bf16[512,2,8]{0,2,1:T(8,128)(2,1)S(1)} %get-tuple-element.32), channel_id=1, source_target_pairs={{0,7},{1,4},{2,5},{3,6},{8,15},{9,12},{10,13},{11,14},{16,23},{17,... | collective-permute-start | bytes 49160 | tf_op jit(solution)/shard_map/ppermute | solution.py:68
  21.3 1.5 %fusion.22 = bf16[2,3,136,3,128]{4,1,0,3,2:T(4,128)(2,1)} fusion(bf16[3,2,3,9]{3,2,1,0:T(4,128)(2,1)S(1)} %convolution_convert_fusion.3), kind=kOutput, calls=%fused_computation.20 | convolution fusion | flops 6266880 | bytes 627012 | tf_op jit(solution)/shard_map/kiad,dpq->iapkq/dot_general | solution.py:109
  22.8 1.3 %collective-permute-start.6 = (bf16[512,2,8]{0,2,1:T(8,128)(2,1)S(1)}, bf16[512,2,8]{0,2,1:T(8,128)(2,1)S(1)}, u32[]{:S(2)}, u32[]{:S(2)}) collective-permute-start(bf16[512,2,8]{0,2,1:T(8,128)(2,1)S(1)} %get-tuple-element.31), channel_id=1, source_target_pairs={{4,1},{5,2},{6,3},{7,0},{12,9},{13,10},{14,11},{15,8},{20,17},{21,... | collective-permute-start | bytes 49160 | tf_op jit(solution)/shard_map/ppermute | solution.py:68
  24.2 0.1 copy.48
  24.2 1.6 %collective-permute-start.4 = (bf16[512,2,8]{0,2,1:T(8,128)(2,1)S(1)}, bf16[512,2,8]{0,2,1:T(8,128)(2,1)S(1)}, u32[]{:S(2)}, u32[]{:S(2)}) collective-permute-start(bf16[512,2,8]{0,2,1:T(8,128)(2,1)S(1)} %get-tuple-element.31), channel_id=1, source_target_pairs={{0,1},{1,2},{2,3},{3,0},{4,5},{5,6},{6,7},{7,4},{8,9},{9,10},{10,1... | collective-permute-start | bytes 49160 | tf_op jit(solution)/shard_map/ppermute | solution.py:58
  25.9 0.1 copy.47
  26.0 0.1 reshape_squeeze.3
  26.1 4.6 %convert_bitcast_fusion = bf16[6,3,136,3,144]{4,1,0,3,2:T(4,128)(2,1)} fusion(s32[136]{0:T(256)S(1)} %iota_add_fusion, bf16[3,6,3,9]{3,1,2,0:T(8,128)(2,1)S(1)} %bitcast.202), kind=kOutput, calls=%fused_computation | convolution fusion | flops 20445696 | bytes 2116588 | tf_op jit(solution)/shard_map/kiad,dpq->iapkq/dot_general | solution.py:109
  30.7 1.5 %convert_bitcast_fusion.1 = bf16[4,3,144,3,136]{2,0,1,3,4:T(4,128)(2,1)S(1)} fusion(bf16[3,6,3,9]{3,1,2,0:T(8,128)(2,1)S(1)} %bitcast.203), kind=kOutput, calls=%fused_computation.7 | convolution fusion | flops 13747968 | bytes 1419264 | tf_op jit(solution)/shard_map/kiad,dpq->iapkq/dot_general | solution.py:109
  32.2 5.2 %collective-permute-start.2 = (bf16[512,2,8]{0,2,1:T(8,128)(2,1)S(1)}, bf16[512,2,8]{0,2,1:T(8,128)(2,1)S(1)}, u32[]{:S(2)}, u32[]{:S(2)}) collective-permute-start(bf16[512,2,8]{0,2,1:T(8,128)(2,1)S(1)} %get-tuple-element.31), channel_id=1, source_target_pairs={{0,5},{1,6},{2,7},{3,4},{8,13},{9,14},{10,15},{11,12},{16,21},{17,... | collective-permute-start | bytes 49160 | tf_op jit(solution)/shard_map/ppermute | solution.py:68
  37.5 1.1 %collective-permute-done.2 = bf16[512,2,8]{0,2,1:T(8,128)(2,1)S(1)} collective-permute-done((bf16[512,2,8]{0,2,1:T(8,128)(2,1)S(1)}, bf16[512,2,8]{0,2,1:T(8,128)(2,1)S(1)}, u32[]{:S(2)}, u32[]{:S(2)}) %collective-permute-start.2) | collective-permute-done | bytes 16416 | tf_op jit(solution)/shard_map/ppermute | solution.py:68
  38.7 1.7 %fusion.24 = bf16[256,4,3,136]{0,3,2,1:T(8,128)(2,1)} fusion(bf16[4,3,144,3,136]{2,0,1,3,4:T(4,128)(2,1)S(1)} %convert_bitcast_fusion.1, bf16[256,4,1,144]{0,3,2,1:T(8,128)(2,1)S(1)} %fusion.75, bf16[256,4,1,144]{0,3,2,1:T(8,128)(2,1)S(1)} %get-tuple-element.25, bf16[256,4,1,144]{0,3,2,1:T(8,128)(2,1)S(1)} %get-tuple-element.24), kind=kOutput, calls=%fused_computation.22 | convolution fusion | flops 362274816 | bytes 3130368 | tf_op jit(solution)/shard_map/ciap,iapkq->cikq/dot_general | solution.py:123
  40.4 6.0 %fusion.13 = f32[256,6,3,136]{0,3,1,2:T(8,128)} fusion(bf16[6,3,136,3,144]{4,1,0,3,2:T(4,128)(2,1)} %convert_bitcast_fusion, bf16[512,2,8]{0,2,1:T(8,128)(2,1)S(1)} %collective-permute-done.7, bf16[512,2,128]{0,2,1:T(8,128)(2,1)S(1)} %slice.114, bf16[512,2,8]{0,2,1:T(8,128)(2,1)S(1)} %collective-permute-done.6, ...), kind=kOutput, calls=%fused_computation.13 | convolution fusion | flops 886284288 | bytes 5899776 | tf_op jit(solution)/shard_map/cikq,iapkq->ciap/dot_general | solution.py:129
  46.5 2.2 %fusion.44 = (bf16[256,4,136]{0,2,1:T(8,128)(2,1)S(1)}, bf16[256,4,136]{0,2,1:T(8,128)(2,1)S(1)}) fusion(f32[256,6,3,136]{0,3,1,2:T(8,128)} %fusion.13, pred[4]{0:T(512)(128)(4,1)S(1)} %compare_and_fusion, bf16[256,4,3,136]{0,3,2,1:T(8,128)(2,1)S(1)} %copy-done.5, bf16[3,256,256]{2,1,0:T(8,128)(2,1)S(1)} %copy-done), kind=kOutput, calls=%fused_computation.51 | convolution fusion | flops 217808896 | bytes 3457028 | tf_op jit(solution)/shard_map/koc,cikj->oij/dot_general | solution.py:141
  48.8 0.4 fusion.30
  49.2 0.5 copy-done.2
  49.7 0.3 fusion.27
  50.1 0.1 collective-permute-start.8
  50.1 1.3 %fusion.28 = f32[256,3,256]{0,2,1:T(8,128)S(1)} fusion(bf16[256,4,3,136]{0,3,2,1:T(8,128)(2,1)} %fusion.24, bf16[256,4,136]{0,2,1:T(8,128)(2,1)S(1)} %get-tuple-element.9), kind=kOutput, calls=%fused_computation.27 | convolution fusion | flops 100859904 | bytes 1310720 | tf_op jit(solution)/shard_map/oij,cikj->koc/dot_general | solution.py:151
  51.5 0.8 constant_dynamic-slice_fusion.4
  52.3 0.5 collective-permute-start.9
  52.8 1.6 %collective-permute-done.9 = f32[384,256]{1,0:T(8,128)} collective-permute-done((f32[384,256]{1,0:T(8,128)}, f32[384,256]{1,0:T(8,128)}, u32[]{:S(2)}, u32[]{:S(2)}) %collective-permute-start.9) | collective-permute-done | bytes 393248 | tf_op jit(solution)/shard_map/ppermute | solution.py:31
  54.4 1.0 %dynamic-slice_add_fusion = f32[384,256]{1,0:T(8,128)S(1)} fusion(f32[384,256]{1,0:T(8,128)} %collective-permute-done.9, f32[768,256]{1,0:T(8,128)S(1)} %bitcast.201, s32[]{:T(128)S(6)} %select_n.121), kind=kLoop, calls=%fused_computation.85 | loop fusion | flops 98304 | bytes 1179652 | tf_op jit(solution)/shard_map/add | solution.py:31
  55.5 1.6 %collective-permute-start.10 = (f32[192,256]{1,0:T(8,128)S(1)}, f32[192,256]{1,0:T(8,128)S(1)}, u32[]{:S(2)}, u32[]{:S(2)}) collective-permute-start(f32[192,256]{1,0:T(8,128)S(1)} %constant_dynamic-slice_fusion.3), channel_id=1, source_target_pairs={{0,16},{8,24},{16,0},{24,8},{1,17},{9,25},{17,1},{25,9},{2,18},{10... | collective-permute-start | bytes 589832 | tf_op jit(solution)/shard_map/ppermute | solution.py:31
  57.1 0.6 collective-permute-start.17
  57.7 4.0 %fusion.16 = f32[256,4,3,144]{0,3,2,1:T(8,128)} fusion(bf16[4,3,144,3,136]{2,0,1,3,4:T(4,128)(2,1)} %copy-done.1, bf16[3,256,256]{2,1,0:T(8,128)(2,1)S(1)} %copy-done, bf16[256,4,136]{0,2,1:T(8,128)(2,1)} %copy-done.6), kind=kOutput, calls=%fused_computation.16 | convolution fusion | flops 575299584 | bytes 3851264 | tf_op jit(solution)/shard_map/cikq,iapkq->ciap/dot_general | solution.py:129
  61.7 1.7 %collective-permute-done.10 = f32[192,256]{1,0:T(8,128)S(1)} collective-permute-done((f32[192,256]{1,0:T(8,128)S(1)}, f32[192,256]{1,0:T(8,128)S(1)}, u32[]{:S(2)}, u32[]{:S(2)}) %collective-permute-start.10) | collective-permute-done | bytes 196640 | tf_op jit(solution)/shard_map/ppermute | solution.py:31
  63.4 5.6 %collective-permute-start.11 = (f32[96,256]{1,0:T(8,128)S(1)}, f32[96,256]{1,0:T(8,128)S(1)}, u32[]{:S(2)}, u32[]{:S(2)}) collective-permute-start(f32[96,256]{1,0:T(8,128)S(1)} %constant_dynamic-slice_fusion.2), channel_id=1, source_target_pairs={{0,4},{4,0},{1,5},{5,1},{2,6},{6,2},{3,7},{7,3},{8,12},{12,8},{9,1... | collective-permute-start | bytes 294920 | tf_op jit(solution)/shard_map/ppermute | solution.py:31
  69.1 3.6 %collective-permute-start.18 = (f32[96,256]{1,0:T(8,128)S(1)}, f32[96,256]{1,0:T(8,128)S(1)}, u32[]{:S(2)}, u32[]{:S(2)}) collective-permute-start(f32[96,256]{1,0:T(8,128)S(1)} %constant_dynamic-slice_fusion), channel_id=1, source_target_pairs={{0,4},{4,0},{1,5},{5,1},{2,6},{6,2},{3,7},{7,3},{8,12},{12,8},{9,1... | collective-permute-start | bytes 294920 | tf_op jit(solution)/shard_map/ppermute | solution.py:31
  72.7 0.1 collective-permute-start.12
  72.7 2.5 %collective-permute-done.18 = f32[96,256]{1,0:T(8,128)S(1)} collective-permute-done((f32[96,256]{1,0:T(8,128)S(1)}, f32[96,256]{1,0:T(8,128)S(1)}, u32[]{:S(2)}, u32[]{:S(2)}) %collective-permute-start.18) | collective-permute-done | bytes 98336 | tf_op jit(solution)/shard_map/ppermute | solution.py:31
  75.2 0.1 collective-permute-start.19
  75.3 2.8 %collective-permute-done.12 = f32[96,256]{1,0:T(8,128)S(1)} collective-permute-done((f32[96,256]{1,0:T(8,128)S(1)}, f32[96,256]{1,0:T(8,128)S(1)}, u32[]{:S(2)}, u32[]{:S(2)}) %collective-permute-start.12) | collective-permute-done | bytes 98336 | tf_op jit(solution)/shard_map/ppermute | solution.py:37
  78.1 0.1 collective-permute-start.13
  78.2 1.2 %fusion.82 = bf16[1,256,2,128]{1,3,2,0:T(8,128)(2,1)S(1)} fusion(f32[256,4,3,144]{0,3,2,1:T(8,128)} %fusion.16), kind=kLoop, calls=%fused_computation.115 | loop fusion | flops 196608 | bytes 917504 | tf_op jit(solution)/shard_map/convert_element_type | solution.py:204
  79.4 0.7 collective-permute-done.19
  80.1 2.3 %collective-permute-start.20 = (f32[96,256]{1,0:T(8,128)S(1)}, f32[96,256]{1,0:T(8,128)S(1)}, u32[]{:S(2)}, u32[]{:S(2)}) collective-permute-start(f32[96,256]{1,0:T(8,128)S(1)} %add.180), channel_id=1, source_target_pairs={{0,2},{1,3},{2,0},{3,1},{4,6},{5,7},{6,4},{7,5},{8,10},{9,11},{10,... | collective-permute-start | bytes 294920 | tf_op jit(solution)/shard_map/ppermute | solution.py:37
  82.4 4.1 %collective-permute-done.13 = f32[96,256]{1,0:T(8,128)S(1)} collective-permute-done((f32[96,256]{1,0:T(8,128)S(1)}, f32[96,256]{1,0:T(8,128)S(1)}, u32[]{:S(2)}, u32[]{:S(2)}) %collective-permute-start.13) | collective-permute-done | bytes 98336 | tf_op jit(solution)/shard_map/ppermute | solution.py:37
  86.5 1.3 %collective-permute-start.14 = (bf16[96,256]{1,0:T(8,128)(2,1)S(1)}, bf16[96,256]{1,0:T(8,128)(2,1)S(1)}, u32[]{:S(2)}, u32[]{:S(2)}) collective-permute-start(bf16[96,256]{1,0:T(8,128)(2,1)S(1)} %add_convert_fusion.1), channel_id=1, source_target_pairs={{0,4},{4,0},{1,5},{5,1},{2,6},{6,2},{3,7},{7,3},{8,12},{12,8},{9,1... | collective-permute-start | bytes 147464 | tf_op jit(solution)/shard_map/ppermute | solution.py:42
  87.8 1.0 %collective-permute-start.21 = (bf16[96,256]{1,0:T(8,128)(2,1)S(1)}, bf16[96,256]{1,0:T(8,128)(2,1)S(1)}, u32[]{:S(2)}, u32[]{:S(2)}) collective-permute-start(bf16[96,256]{1,0:T(8,128)(2,1)S(1)} %add_convert_fusion), channel_id=1, source_target_pairs={{0,4},{4,0},{1,5},{5,1},{2,6},{6,2},{3,7},{7,3},{8,12},{12,8},{9,1... | collective-permute-start | bytes 147464 | tf_op jit(solution)/shard_map/ppermute | solution.py:42
  88.9 1.8 %collective-permute-done.14 = bf16[96,256]{1,0:T(8,128)(2,1)S(1)} collective-permute-done((bf16[96,256]{1,0:T(8,128)(2,1)S(1)}, bf16[96,256]{1,0:T(8,128)(2,1)S(1)}, u32[]{:S(2)}, u32[]{:S(2)}) %collective-permute-start.14) | collective-permute-done | bytes 49184 | tf_op jit(solution)/shard_map/ppermute | solution.py:42
  90.7 1.6 %collective-permute-start.15 = (bf16[192,256]{1,0:T(8,128)(2,1)S(1)}, bf16[192,256]{1,0:T(8,128)(2,1)S(1)}, u32[]{:S(2)}, u32[]{:S(2)}) collective-permute-start(bf16[192,256]{1,0:T(8,128)(2,1)S(1)} %maximum_select_fusion.4), channel_id=1, source_target_pairs={{0,16},{8,24},{16,0},{24,8},{1,17},{9,25},{17,1},{25,9},{2,18},{10... | collective-permute-start | bytes 294920 | tf_op jit(solution)/shard_map/ppermute | solution.py:42
  92.3 1.3 %collective-permute-start.22 = (bf16[192,256]{1,0:T(8,128)(2,1)S(1)}, bf16[192,256]{1,0:T(8,128)(2,1)S(1)}, u32[]{:S(2)}, u32[]{:S(2)}) collective-permute-start(bf16[192,256]{1,0:T(8,128)(2,1)S(1)} %maximum_select_fusion.5), channel_id=1, source_target_pairs={{0,16},{8,24},{16,0},{24,8},{1,17},{9,25},{17,1},{25,9},{2,18},{10... | collective-permute-start | bytes 294920 | tf_op jit(solution)/shard_map/ppermute | solution.py:42
  93.6 1.8 %collective-permute-done.15 = bf16[192,256]{1,0:T(8,128)(2,1)S(1)} collective-permute-done((bf16[192,256]{1,0:T(8,128)(2,1)S(1)}, bf16[192,256]{1,0:T(8,128)(2,1)S(1)}, u32[]{:S(2)}, u32[]{:S(2)}) %collective-permute-start.15) | collective-permute-done | bytes 98336 | tf_op jit(solution)/shard_map/ppermute | solution.py:42
  95.4 0.1 collective-permute-start.16
  95.5 1.4 %collective-permute-done.22 = bf16[192,256]{1,0:T(8,128)(2,1)S(1)} collective-permute-done((bf16[192,256]{1,0:T(8,128)(2,1)S(1)}, bf16[192,256]{1,0:T(8,128)(2,1)S(1)}, u32[]{:S(2)}, u32[]{:S(2)}) %collective-permute-start.22) | collective-permute-done | bytes 98336 | tf_op jit(solution)/shard_map/ppermute | solution.py:42
  97.0 0.1 collective-permute-start.23
  97.1 0.3 fusion.32
  97.4 0.8 copy.63
  98.2 0.8 copy.64
  99.0 0.2 maximum_select_fusion
  99.1 0.9 convert.5
  100.1 0.2 maximum_select_fusion.1
  100.2 0.9 convert.6
  (60 shorter events, 0.8 us)
Async XLA Ops:
  0.6 45.8 %copy-start = (bf16[3,256,256]{2,1,0:T(8,128)(2,1)S(1)}, bf16[3,256,256]{2,1,0:T(8,128)(2,1)}, u32[]{:S(2)}) copy-start(bf16[3,256,256]{2,1,0:T(8,128)(2,1)} %param.8) | copy-start | bytes 1179652
  4.6 18.2 %collective-permute-start.1 = (bf16[513,2,128]{0,2,1:T(8,128)(2,1)S(1)}, bf16[513,2,128]{0,2,1:T(8,128)(2,1)S(1)}, u32[]{:S(2)}, u32[]{:S(2)}) collective-permute-start(bf16[513,2,128]{0,2,1:T(8,128)(2,1)S(1)} %pad_maximum_fusion.17), channel_id=1, source_target_pairs={{4,0},{5,1},{6,2},{7,3},{12,8},{13,9},{14,10},{15,11},{20,16},{21,... | collective-permute-start | bytes 787976 | tf_op jit(solution)/shard_map/ppermute | solution.py:67
  5.9 18.3 %collective-permute-start = (bf16[513,2,128]{0,2,1:T(8,128)(2,1)S(1)}, bf16[513,2,128]{0,2,1:T(8,128)(2,1)S(1)}, u32[]{:S(2)}, u32[]{:S(2)}) collective-permute-start(bf16[513,2,128]{0,2,1:T(8,128)(2,1)S(1)} %pad_maximum_fusion.17), channel_id=1, source_target_pairs={{0,4},{1,5},{2,6},{3,7},{8,12},{9,13},{10,14},{11,15},{16,20},{17,... | collective-permute-start | bytes 787976 | tf_op jit(solution)/shard_map/ppermute | solution.py:67
  10.9 21.3 %collective-permute-start.7 = (bf16[512,2,8]{0,2,1:T(8,128)(2,1)S(1)}, bf16[512,2,8]{0,2,1:T(8,128)(2,1)S(1)}, u32[]{:S(2)}, u32[]{:S(2)}) collective-permute-start(bf16[512,2,8]{0,2,1:T(8,128)(2,1)S(1)} %get-tuple-element.32), channel_id=1, source_target_pairs={{4,3},{5,0},{6,1},{7,2},{12,11},{13,8},{14,9},{15,10},{20,19},{21,... | collective-permute-start | bytes 49160 | tf_op jit(solution)/shard_map/ppermute | solution.py:68
  12.2 25.2 %collective-permute-start.5 = (bf16[512,2,8]{0,2,1:T(8,128)(2,1)S(1)}, bf16[512,2,8]{0,2,1:T(8,128)(2,1)S(1)}, u32[]{:S(2)}, u32[]{:S(2)}) collective-permute-start(bf16[512,2,8]{0,2,1:T(8,128)(2,1)S(1)} %get-tuple-element.32), channel_id=1, source_target_pairs={{0,3},{1,0},{2,1},{3,2},{4,7},{5,4},{6,5},{7,6},{8,11},{9,8},{10,9... | collective-permute-start | bytes 49160 | tf_op jit(solution)/shard_map/ppermute | solution.py:58
  17.0 20.5 %collective-permute-start.3 = (bf16[512,2,8]{0,2,1:T(8,128)(2,1)S(1)}, bf16[512,2,8]{0,2,1:T(8,128)(2,1)S(1)}, u32[]{:S(2)}, u32[]{:S(2)}) collective-permute-start(bf16[512,2,8]{0,2,1:T(8,128)(2,1)S(1)} %get-tuple-element.32), channel_id=1, source_target_pairs={{0,7},{1,4},{2,5},{3,6},{8,15},{9,12},{10,13},{11,14},{16,23},{17,... | collective-permute-start | bytes 49160 | tf_op jit(solution)/shard_map/ppermute | solution.py:68
  22.8 14.6 %collective-permute-start.6 = (bf16[512,2,8]{0,2,1:T(8,128)(2,1)S(1)}, bf16[512,2,8]{0,2,1:T(8,128)(2,1)S(1)}, u32[]{:S(2)}, u32[]{:S(2)}) collective-permute-start(bf16[512,2,8]{0,2,1:T(8,128)(2,1)S(1)} %get-tuple-element.31), channel_id=1, source_target_pairs={{4,1},{5,2},{6,3},{7,0},{12,9},{13,10},{14,11},{15,8},{20,17},{21,... | collective-permute-start | bytes 49160 | tf_op jit(solution)/shard_map/ppermute | solution.py:68
  24.2 13.2 %collective-permute-start.4 = (bf16[512,2,8]{0,2,1:T(8,128)(2,1)S(1)}, bf16[512,2,8]{0,2,1:T(8,128)(2,1)S(1)}, u32[]{:S(2)}, u32[]{:S(2)}) collective-permute-start(bf16[512,2,8]{0,2,1:T(8,128)(2,1)S(1)} %get-tuple-element.31), channel_id=1, source_target_pairs={{0,1},{1,2},{2,3},{3,0},{4,5},{5,6},{6,7},{7,4},{8,9},{9,10},{10,1... | collective-permute-start | bytes 49160 | tf_op jit(solution)/shard_map/ppermute | solution.py:58
  32.2 6.5 %copy-start.1 = (bf16[4,3,144,3,136]{2,0,1,3,4:T(4,128)(2,1)}, bf16[4,3,144,3,136]{2,0,1,3,4:T(4,128)(2,1)S(1)}, u32[]{:S(2)}) copy-start(bf16[4,3,144,3,136]{2,0,1,3,4:T(4,128)(2,1)S(1)} %convert_bitcast_fusion.1) | copy-start | bytes 4230148
  32.2 6.4 %collective-permute-start.2 = (bf16[512,2,8]{0,2,1:T(8,128)(2,1)S(1)}, bf16[512,2,8]{0,2,1:T(8,128)(2,1)S(1)}, u32[]{:S(2)}, u32[]{:S(2)}) collective-permute-start(bf16[512,2,8]{0,2,1:T(8,128)(2,1)S(1)} %get-tuple-element.31), channel_id=1, source_target_pairs={{0,5},{1,6},{2,7},{3,4},{8,13},{9,14},{10,15},{11,12},{16,21},{17,... | collective-permute-start | bytes 49160 | tf_op jit(solution)/shard_map/ppermute | solution.py:68
  38.7 1.7 %copy-start.3 = (bf16[3,256,256]{2,1,0:T(8,128)(2,1)S(1)}, bf16[3,256,256]{2,1,0:T(8,128)(2,1)}, u32[]{:S(2)}) copy-start(bf16[3,256,256]{2,1,0:T(8,128)(2,1)} %param.9) | copy-start | bytes 1179652
  40.4 6.0 %copy-start.5 = (bf16[256,4,3,136]{0,3,2,1:T(8,128)(2,1)S(1)}, bf16[256,4,3,136]{0,3,2,1:T(8,128)(2,1)}, u32[]{:S(2)}) copy-start(bf16[256,4,3,136]{0,3,2,1:T(8,128)(2,1)} %fusion.24) | copy-start | bytes 2506756
  46.5 2.3 %copy-start.4 = (bf16[2,3,136,3,128]{4,1,0,3,2:T(4,128)(2,1)S(1)}, bf16[2,3,136,3,128]{4,1,0,3,2:T(4,128)(2,1)}, u32[]{:S(2)}) copy-start(bf16[2,3,136,3,128]{4,1,0,3,2:T(4,128)(2,1)} %fusion.22) | copy-start | bytes 1880068
  48.7 1.4 %copy-start.6 = (bf16[256,4,136]{0,2,1:T(8,128)(2,1)}, bf16[256,4,136]{0,2,1:T(8,128)(2,1)S(1)}, u32[]{:S(2)}) copy-start(bf16[256,4,136]{0,2,1:T(8,128)(2,1)S(1)} %get-tuple-element.9) | copy-start | bytes 835588
  48.7 1.0 copy-start.2
  50.1 2.7 %collective-permute-start.8 = (f32[384,256]{1,0:T(8,128)S(1)}, f32[384,256]{1,0:T(8,128)S(1)}, u32[]{:S(2)}, u32[]{:S(2)}) collective-permute-start(f32[384,256]{1,0:T(8,128)S(1)} %constant_dynamic-slice_fusion.5), channel_id=1, source_target_pairs={{0,8},{8,0},{16,24},{24,16},{1,9},{9,1},{17,25},{25,17},{2,10},{10... | collective-permute-start | bytes 1179656 | tf_op jit(solution)/shard_map/ppermute | solution.py:31
  52.3 2.2 %collective-permute-start.9 = (f32[384,256]{1,0:T(8,128)}, f32[384,256]{1,0:T(8,128)}, u32[]{:S(2)}, u32[]{:S(2)}) collective-permute-start(f32[384,256]{1,0:T(8,128)} %constant_dynamic-slice_fusion.4), channel_id=1, source_target_pairs={{0,8},{8,0},{16,24},{24,16},{1,9},{9,1},{17,25},{25,17},{2,10},{10... | collective-permute-start | bytes 1179656 | tf_op jit(solution)/shard_map/ppermute | solution.py:31
  55.5 7.8 %collective-permute-start.10 = (f32[192,256]{1,0:T(8,128)S(1)}, f32[192,256]{1,0:T(8,128)S(1)}, u32[]{:S(2)}, u32[]{:S(2)}) collective-permute-start(f32[192,256]{1,0:T(8,128)S(1)} %constant_dynamic-slice_fusion.3), channel_id=1, source_target_pairs={{0,16},{8,24},{16,0},{24,8},{1,17},{9,25},{17,1},{25,9},{2,18},{10... | collective-permute-start | bytes 589832 | tf_op jit(solution)/shard_map/ppermute | solution.py:31
  57.1 11.9 %collective-permute-start.17 = (f32[192,256]{1,0:T(8,128)S(1)}, f32[192,256]{1,0:T(8,128)S(1)}, u32[]{:S(2)}, u32[]{:S(2)}) collective-permute-start(f32[192,256]{1,0:T(8,128)S(1)} %constant_dynamic-slice_fusion.1), channel_id=1, source_target_pairs={{0,16},{8,24},{16,0},{24,8},{1,17},{9,25},{17,1},{25,9},{2,18},{10... | collective-permute-start | bytes 589832 | tf_op jit(solution)/shard_map/ppermute | solution.py:31
  63.4 9.2 %collective-permute-start.11 = (f32[96,256]{1,0:T(8,128)S(1)}, f32[96,256]{1,0:T(8,128)S(1)}, u32[]{:S(2)}, u32[]{:S(2)}) collective-permute-start(f32[96,256]{1,0:T(8,128)S(1)} %constant_dynamic-slice_fusion.2), channel_id=1, source_target_pairs={{0,4},{4,0},{1,5},{5,1},{2,6},{6,2},{3,7},{7,3},{8,12},{12,8},{9,1... | collective-permute-start | bytes 294920 | tf_op jit(solution)/shard_map/ppermute | solution.py:31
  69.1 6.2 %collective-permute-start.18 = (f32[96,256]{1,0:T(8,128)S(1)}, f32[96,256]{1,0:T(8,128)S(1)}, u32[]{:S(2)}, u32[]{:S(2)}) collective-permute-start(f32[96,256]{1,0:T(8,128)S(1)} %constant_dynamic-slice_fusion), channel_id=1, source_target_pairs={{0,4},{4,0},{1,5},{5,1},{2,6},{6,2},{3,7},{7,3},{8,12},{12,8},{9,1... | collective-permute-start | bytes 294920 | tf_op jit(solution)/shard_map/ppermute | solution.py:31
  72.7 5.5 %collective-permute-start.12 = (f32[96,256]{1,0:T(8,128)S(1)}, f32[96,256]{1,0:T(8,128)S(1)}, u32[]{:S(2)}, u32[]{:S(2)}) collective-permute-start(f32[96,256]{1,0:T(8,128)S(1)} %dynamic-slice_add_fusion.5), channel_id=1, source_target_pairs={{0,1},{1,0},{2,3},{3,2},{4,5},{5,4},{6,7},{7,6},{8,9},{9,8},{10,11... | collective-permute-start | bytes 294920 | tf_op jit(solution)/shard_map/ppermute | solution.py:37
  75.2 4.8 %collective-permute-start.19 = (f32[96,256]{1,0:T(8,128)S(1)}, f32[96,256]{1,0:T(8,128)S(1)}, u32[]{:S(2)}, u32[]{:S(2)}) collective-permute-start(f32[96,256]{1,0:T(8,128)S(1)} %dynamic-slice_add_fusion.4), channel_id=1, source_target_pairs={{0,1},{1,0},{2,3},{3,2},{4,5},{5,4},{6,7},{7,6},{8,9},{9,8},{10,11... | collective-permute-start | bytes 294920 | tf_op jit(solution)/shard_map/ppermute | solution.py:37
  78.1 8.4 %collective-permute-start.13 = (f32[96,256]{1,0:T(8,128)S(1)}, f32[96,256]{1,0:T(8,128)S(1)}, u32[]{:S(2)}, u32[]{:S(2)}) collective-permute-start(f32[96,256]{1,0:T(8,128)S(1)} %add.176), channel_id=1, source_target_pairs={{0,2},{1,3},{2,0},{3,1},{4,6},{5,7},{6,4},{7,5},{8,10},{9,11},{10,... | collective-permute-start | bytes 294920 | tf_op jit(solution)/shard_map/ppermute | solution.py:37
  80.1 7.8 %collective-permute-start.20 = (f32[96,256]{1,0:T(8,128)S(1)}, f32[96,256]{1,0:T(8,128)S(1)}, u32[]{:S(2)}, u32[]{:S(2)}) collective-permute-start(f32[96,256]{1,0:T(8,128)S(1)} %add.180), channel_id=1, source_target_pairs={{0,2},{1,3},{2,0},{3,1},{4,6},{5,7},{6,4},{7,5},{8,10},{9,11},{10,... | collective-permute-start | bytes 294920 | tf_op jit(solution)/shard_map/ppermute | solution.py:37
  86.5 4.2 %collective-permute-start.14 = (bf16[96,256]{1,0:T(8,128)(2,1)S(1)}, bf16[96,256]{1,0:T(8,128)(2,1)S(1)}, u32[]{:S(2)}, u32[]{:S(2)}) collective-permute-start(bf16[96,256]{1,0:T(8,128)(2,1)S(1)} %add_convert_fusion.1), channel_id=1, source_target_pairs={{0,4},{4,0},{1,5},{5,1},{2,6},{6,2},{3,7},{7,3},{8,12},{12,8},{9,1... | collective-permute-start | bytes 147464 | tf_op jit(solution)/shard_map/ppermute | solution.py:42
  87.8 4.4 %collective-permute-start.21 = (bf16[96,256]{1,0:T(8,128)(2,1)S(1)}, bf16[96,256]{1,0:T(8,128)(2,1)S(1)}, u32[]{:S(2)}, u32[]{:S(2)}) collective-permute-start(bf16[96,256]{1,0:T(8,128)(2,1)S(1)} %add_convert_fusion), channel_id=1, source_target_pairs={{0,4},{4,0},{1,5},{5,1},{2,6},{6,2},{3,7},{7,3},{8,12},{12,8},{9,1... | collective-permute-start | bytes 147464 | tf_op jit(solution)/shard_map/ppermute | solution.py:42
  90.7 4.7 %collective-permute-start.15 = (bf16[192,256]{1,0:T(8,128)(2,1)S(1)}, bf16[192,256]{1,0:T(8,128)(2,1)S(1)}, u32[]{:S(2)}, u32[]{:S(2)}) collective-permute-start(bf16[192,256]{1,0:T(8,128)(2,1)S(1)} %maximum_select_fusion.4), channel_id=1, source_target_pairs={{0,16},{8,24},{16,0},{24,8},{1,17},{9,25},{17,1},{25,9},{2,18},{10... | collective-permute-start | bytes 294920 | tf_op jit(solution)/shard_map/ppermute | solution.py:42
  92.3 4.7 %collective-permute-start.22 = (bf16[192,256]{1,0:T(8,128)(2,1)S(1)}, bf16[192,256]{1,0:T(8,128)(2,1)S(1)}, u32[]{:S(2)}, u32[]{:S(2)}) collective-permute-start(bf16[192,256]{1,0:T(8,128)(2,1)S(1)} %maximum_select_fusion.5), channel_id=1, source_target_pairs={{0,16},{8,24},{16,0},{24,8},{1,17},{9,25},{17,1},{25,9},{2,18},{10... | collective-permute-start | bytes 294920 | tf_op jit(solution)/shard_map/ppermute | solution.py:42
  95.4 3.5 %collective-permute-start.16 = (bf16[384,256]{1,0:T(8,128)(2,1)S(1)}, bf16[384,256]{1,0:T(8,128)(2,1)S(1)}, u32[]{:S(2)}, u32[]{:S(2)}) collective-permute-start(bf16[384,256]{1,0:T(8,128)(2,1)S(1)} %maximum_select_fusion.2), channel_id=1, source_target_pairs={{0,8},{8,0},{16,24},{24,16},{1,9},{9,1},{17,25},{25,17},{2,10},{10... | collective-permute-start | bytes 589832 | tf_op jit(solution)/shard_map/ppermute | solution.py:42
  97.0 3.1 %collective-permute-start.23 = (bf16[384,256]{1,0:T(8,128)(2,1)S(1)}, bf16[384,256]{1,0:T(8,128)(2,1)S(1)}, u32[]{:S(2)}, u32[]{:S(2)}) collective-permute-start(bf16[384,256]{1,0:T(8,128)(2,1)S(1)} %maximum_select_fusion.3), channel_id=1, source_target_pairs={{0,8},{8,0},{16,24},{24,16},{1,9},{9,1},{17,25},{25,17},{2,10},{10... | collective-permute-start | bytes 589832 | tf_op jit(solution)/shard_map/ppermute | solution.py:42

commit v9 on v7

--- a/solution.py
+++ b/solution.py
@@ -49,6 +49,13 @@
 def lat_halo(block, dim, width):
     count = lax.axis_size("lat")
     rows = block.shape[dim]
+    if count == 2 and width == rows:
+        other = lax.ppermute(block, "lat", [(0, 1), (1, 0)])
+        lower = lax.axis_index("lat") == 0
+        blank = jnp.zeros_like(other)
+        above = jnp.where(lower, blank, other)
+        below = jnp.where(lower, other, blank)
+        return jnp.concatenate([above, block, below], axis=dim)
     above = lax.ppermute(
         lax.slice_in_dim(block, rows - width, rows, axis=dim),
         "lat",

time: 91.9 us -> 88.3 us (0.961)
  starting transfers between devices: 25.4 us -> 18.2 us
  waiting for transfers between devices: 28.7 us -> 32.4 us
    ppermute x2 -> x1, starting transfers between devices: 5.88 us -> 1.58 us  [lat_halo(): other = lax.ppermute(block, 'lat', [(0, 1), (1, 0)])]
    ppermute x6, starting transfers between devices: 7.82 us -> 5.86 us  [halving_sum(): flat = keep + lax.ppermute(send, axis, pairs)]
    ppermute x6, waiting for transfers between devices: 6.83 us -> 8.31 us  [halving_sum(): flat = keep + lax.ppermute(send, axis, pairs)]
    ppermute x2 -> x1, waiting for transfers between devices: 4.58 us -> 5.9 us  [lat_halo(): other = lax.ppermute(block, 'lat', [(0, 1), (1, 0)])]
  transfers between devices with their start and end apart: 20 -> 19, of which waited for: 13 -> 13; matrix products, arithmetic and copies ran while one was open for 16% -> 16% of each run, Pallas kernels for 0% -> 0%
where the time goes in v9:
time: 88.3 us; the launch traced here: 87.8 us
  waiting for transfers between devices  32.4 us (37%)
  matrix products  23.1 us (26%)
  starting transfers between devices  18.2 us (21%)
  local copies, waits for them, and re-layouts  7.02 us (8%)
  other arithmetic  6.12 us (7%)
  between operations  1.01 us (1%)
    dot_general x2, matrix products, spread_adjoint(): jnp.einsum('cikq,iapkq->ciap', mixed, band, preferred_element_type=jnp.fl...  10.2 us
    ppermute x4, waiting for transfers between devices, halving_sum(): flat = flat + lax.ppermute(flat, axis, pairs)  9.36 us
    ppermute x6, waiting for transfers between devices, halving_sum(): flat = keep + lax.ppermute(send, axis, pairs)  8.31 us
    dot_general x3, matrix products, band_of(): jnp.einsum('kiad,dpq->iapkq', stencil, lon_picker(col_count, first_source...  6.66 us
    ppermute x1, waiting for transfers between devices, lat_halo(): other = lax.ppermute(block, 'lat', [(0, 1), (1, 0)])  5.9 us
    ppermute x6, starting transfers between devices, halving_sum(): flat = keep + lax.ppermute(send, axis, pairs)  5.86 us
    unnamed x18, local copies, waits for them, and re-layouts  5.76 us
    ppermute x6, waiting for transfers between devices, halving_sum(): other = lax.ppermute(flat, axis, pairs)  5.49 us
  transfers between devices with their start and end apart: 19, of which 13 were waited for; matrix products, arithmetic and copies ran while one was open for 16% of the time, Pallas kernels for 0%

profile of v9, /device:TPU:0, one launch (start us, length us, event | category | flops | bytes accessed | tf_op | source)
XLA Modules:
  0.0 87.8 jit_solution(15729111301004924335)
XLA Ops:
  0.6 1.1 %copy.26 = bf16[1,256,2,128]{1,3,2,0:T(8,128)(2,1)S(1)} copy(bf16[1,256,2,128]{3,2,1,0:T(2,128)(2,1)} %param.13) | data formatting | bytes 262144 | tf_op args[6]
  1.7 1.0 %copy.25 = bf16[1,256,2,128]{1,3,2,0:T(8,128)(2,1)S(1)} copy(bf16[1,256,2,128]{3,2,1,0:T(2,128)(2,1)} %param.7) | data formatting | bytes 262144 | tf_op args[0]
  2.8 5.1 %collective-permute-start.1 = (bf16[512,2,8]{0,2,1:T(8,128)(2,1)S(1)}, bf16[512,2,8]{0,2,1:T(8,128)(2,1)S(1)}, u32[]{:S(2)}, u32[]{:S(2)}) collective-permute-start(bf16[512,2,8]{0,2,1:T(8,128)(2,1)S(1)} %get-tuple-element.31), channel_id=1, source_target_pairs={{0,3},{1,0},{2,1},{3,2},{4,7},{5,4},{6,5},{7,6},{8,11},{9,8},{10,9... | collective-permute-start | bytes 49160 | tf_op jit(solution)/shard_map/ppermute | solution.py:74
  7.9 0.1 fusion.42
  8.0 0.7 broadcast_add_fusion
  8.7 0.9 %convolution_convert_fusion.2 = bf16[3,2,3,9]{3,2,1,0:T(4,128)(2,1)S(1)} fusion(s32[2,3,12]{2,0,1:T(2,128)S(1)} %get-tuple-element.32, f32[2,3,12]{2,0,1:T(2,128)} %param.10, s32[2,3,12]{2,0,1:T(2,128)S(1)} %get-tuple-element.33), kind=kOutput, calls=%fused_computation.38 | convolution fusion | flops 24570 | bytes 1188 | tf_op jit(solution)/shard_map/rks,rksa,rksd->krad/dot_general | solution.py:83
  9.6 0.1 reshape.80
  9.7 0.2 fusion.29
  10.0 0.1 copy.28
  10.1 3.3 %collective-permute-done = bf16[512,2,8]{0,2,1:T(8,128)(2,1)S(1)} collective-permute-done((bf16[512,2,8]{0,2,1:T(8,128)(2,1)S(1)}, bf16[512,2,8]{0,2,1:T(8,128)(2,1)S(1)}, u32[]{:S(2)}, u32[]{:S(2)}) %collective-permute-start) | collective-permute-done | bytes 16416 | tf_op jit(solution)/shard_map/ppermute | solution.py:73
  13.5 1.6 %collective-permute-start.2 = (bf16[513,2,144]{0,2,1:T(8,128)(2,1)S(1)}, bf16[513,2,144]{0,2,1:T(8,128)(2,1)S(1)}, u32[]{:S(2)}, u32[]{:S(2)}) collective-permute-start(bf16[513,2,144]{0,2,1:T(8,128)(2,1)S(1)} %pad_maximum_fusion.16), channel_id=1, source_target_pairs={{0,4},{4,0},{1,5},{5,1},{2,6},{6,2},{3,7},{7,3},{8,12},{12,8},{9,1... | collective-permute-start | bytes 886472 | tf_op jit(solution)/shard_map/ppermute | solution.py:53
  15.0 1.5 %fusion.34 = bf16[136,128,3,2,3]{1,4,3,2,0:T(4,128)(2,1)} fusion(pred[9,136,128,1,1]{2,1,0,3,4:T(8,128)(4,1)S(1)} %fusion.42, bf16[3,2,3,9]{3,2,1,0:T(4,128)(2,1)S(1)} %convolution_convert_fusion.2), kind=kOutput, calls=%fused_computation.36 | convolution fusion | flops 5640192 | bytes 783684 | tf_op jit(solution)/shard_map/kiad,dpq->iapkq/dot_general | solution.py:102
  16.5 5.9 %collective-permute-done.2 = bf16[513,2,144]{0,2,1:T(8,128)(2,1)S(1)} collective-permute-done((bf16[513,2,144]{0,2,1:T(8,128)(2,1)S(1)}, bf16[513,2,144]{0,2,1:T(8,128)(2,1)S(1)}, u32[]{:S(2)}, u32[]{:S(2)}) %collective-permute-start.2) | collective-permute-done | bytes 295520 | tf_op jit(solution)/shard_map/ppermute | solution.py:53
  22.5 0.2 maximum_reduce_fusion
  22.6 0.1 reshape_squeeze.3
  22.8 3.7 %fusion.10 = bf16[136,144,3,6,3]{1,3,4,2,0:T(8,128)(2,1)} fusion(pred[9,136,144,1,1]{2,1,0,3,4:T(8,128)(4,1)S(1)} %fusion.29, bf16[6,3,3,9]{3,2,1,0:T(4,128)(2,1)S(1)} %reshape_squeeze.3), kind=kOutput, calls=%fused_computation.12 | convolution fusion | flops 19035648 | bytes 2292300 | tf_op jit(solution)/shard_map/kiad,dpq->iapkq/dot_general | solution.py:102
  26.4 1.5 %convert_bitcast_fusion = bf16[4,3,144,3,136]{2,0,1,3,4:T(4,128)(2,1)S(1)} fusion(bf16[3,6,3,9]{3,1,2,0:T(8,128)(2,1)S(1)} %bitcast.199), kind=kOutput, calls=%fused_computation.8 | convolution fusion | flops 13747968 | bytes 1419264 | tf_op jit(solution)/shard_map/kiad,dpq->iapkq/dot_general | solution.py:102
  28.0 1.4 %copy-done.1 = bf16[4,3,144,3,136]{2,0,1,3,4:T(4,128)(2,1)} copy-done((bf16[4,3,144,3,136]{2,0,1,3,4:T(4,128)(2,1)}, bf16[4,3,144,3,136]{2,0,1,3,4:T(4,128)(2,1)S(1)}, u32[]{:S(2)}) %copy-start.1) | copy-done | bytes 1410072
  29.4 0.8 fusion.24
  30.2 0.2 copy-done.3
  30.4 6.2 %fusion.14 = f32[256,6,3,136]{0,3,1,2:T(8,128)} fusion(bf16[513,2,144]{0,2,1:T(8,128)(2,1)S(1)} %get-tuple-element.26, bf16[513,2,144]{0,2,1:T(8,128)(2,1)S(1)} %get-tuple-element.25, bf16[1,2,144]{0,2,1:T(8,128)(2,1)S(1)} %copy.28, bf16[512,2,8]{0,2,1:T(8,128)(2,1)S(1)} %collective-permute-done.1, bf16[512,2,8]{0,2,1:T(8,128)(2,1)S(1)} %collective-permute-done, ...), kind=kOutput, calls=%fused_computation.14 | convolution fusion | flops 884957184 | bytes 5901504 | tf_op jit(solution)/shard_map/cikq,iapkq->ciap/dot_general | solution.py:122
  36.6 2.2 %fusion.46 = (bf16[256,4,136]{0,2,1:T(8,128)(2,1)S(1)}, bf16[256,4,136]{0,2,1:T(8,128)(2,1)S(1)}) fusion(f32[256,6,3,136]{0,3,1,2:T(8,128)} %fusion.14, pred[4]{0:T(512)(128)(4,1)S(1)} %compare_and_fusion, bf16[256,4,3,136]{0,3,2,1:T(8,128)(2,1)S(1)} %fusion.24, bf16[3,256,256]{2,1,0:T(8,128)(2,1)S(1)} %copy-done), kind=kOutput, calls=%fused_computation.54 | convolution fusion | flops 217808896 | bytes 3457028 | tf_op jit(solution)/shard_map/koc,cikj->oij/dot_general | solution.py:134
  38.9 0.4 fusion.31
  39.4 0.5 copy-done.2
  39.9 0.3 fusion.27
  40.2 0.1 collective-permute-start.3
  40.3 1.3 %fusion.28 = f32[256,3,256]{0,2,1:T(8,128)S(1)} fusion(bf16[256,4,3,136]{0,3,2,1:T(8,128)(2,1)} %copy-done.5, bf16[256,4,136]{0,2,1:T(8,128)(2,1)S(1)} %get-tuple-element.9), kind=kOutput, calls=%fused_computation.26 | convolution fusion | flops 100859904 | bytes 1310720 | tf_op jit(solution)/shard_map/oij,cikj->koc/dot_general | solution.py:144
  41.6 0.8 constant_dynamic-slice_fusion.4
  42.4 0.5 collective-permute-start.4
  43.0 1.6 %collective-permute-done.4 = f32[384,256]{1,0:T(8,128)} collective-permute-done((f32[384,256]{1,0:T(8,128)}, f32[384,256]{1,0:T(8,128)}, u32[]{:S(2)}, u32[]{:S(2)}) %collective-permute-start.4) | collective-permute-done | bytes 393248 | tf_op jit(solution)/shard_map/ppermute | solution.py:31
  44.6 1.0 %dynamic-slice_add_fusion = f32[384,256]{1,0:T(8,128)S(1)} fusion(f32[384,256]{1,0:T(8,128)} %collective-permute-done.4, f32[768,256]{1,0:T(8,128)S(1)} %bitcast.198, s32[]{:T(128)S(6)} %select_n.136), kind=kLoop, calls=%fused_computation.83 | loop fusion | flops 98304 | bytes 1179652 | tf_op jit(solution)/shard_map/add | solution.py:31
  45.7 1.6 %collective-permute-start.5 = (f32[192,256]{1,0:T(8,128)S(1)}, f32[192,256]{1,0:T(8,128)S(1)}, u32[]{:S(2)}, u32[]{:S(2)}) collective-permute-start(f32[192,256]{1,0:T(8,128)S(1)} %constant_dynamic-slice_fusion.3), channel_id=1, source_target_pairs={{0,16},{8,24},{16,0},{24,8},{1,17},{9,25},{17,1},{25,9},{2,18},{10... | collective-permute-start | bytes 589832 | tf_op jit(solution)/shard_map/ppermute | solution.py:31
  47.2 0.6 collective-permute-start.12
  47.8 4.0 %fusion.17 = f32[256,4,3,144]{0,3,2,1:T(8,128)} fusion(bf16[4,3,144,3,136]{2,0,1,3,4:T(4,128)(2,1)} %copy-done.1, bf16[3,256,256]{2,1,0:T(8,128)(2,1)S(1)} %copy-done, bf16[256,4,136]{0,2,1:T(8,128)(2,1)} %copy-done.6), kind=kOutput, calls=%fused_computation.17 | convolution fusion | flops 575299584 | bytes 3851264 | tf_op jit(solution)/shard_map/cikq,iapkq->ciap/dot_general | solution.py:122
  51.8 1.7 %collective-permute-done.5 = f32[192,256]{1,0:T(8,128)S(1)} collective-permute-done((f32[192,256]{1,0:T(8,128)S(1)}, f32[192,256]{1,0:T(8,128)S(1)}, u32[]{:S(2)}, u32[]{:S(2)}) %collective-permute-start.5) | collective-permute-done | bytes 196640 | tf_op jit(solution)/shard_map/ppermute | solution.py:31
  53.6 1.6 %collective-permute-start.6 = (f32[96,256]{1,0:T(8,128)S(1)}, f32[96,256]{1,0:T(8,128)S(1)}, u32[]{:S(2)}, u32[]{:S(2)}) collective-permute-start(f32[96,256]{1,0:T(8,128)S(1)} %constant_dynamic-slice_fusion.2), channel_id=1, source_target_pairs={{0,4},{4,0},{1,5},{5,1},{2,6},{6,2},{3,7},{7,3},{8,12},{12,8},{9,1... | collective-permute-start | bytes 294920 | tf_op jit(solution)/shard_map/ppermute | solution.py:31
  55.1 2.0 %collective-permute-done.12 = f32[192,256]{1,0:T(8,128)S(1)} collective-permute-done((f32[192,256]{1,0:T(8,128)S(1)}, f32[192,256]{1,0:T(8,128)S(1)}, u32[]{:S(2)}, u32[]{:S(2)}) %collective-permute-start.12) | collective-permute-done | bytes 196640 | tf_op jit(solution)/shard_map/ppermute | solution.py:31
  57.2 1.6 %collective-permute-start.13 = (f32[96,256]{1,0:T(8,128)S(1)}, f32[96,256]{1,0:T(8,128)S(1)}, u32[]{:S(2)}, u32[]{:S(2)}) collective-permute-start(f32[96,256]{1,0:T(8,128)S(1)} %constant_dynamic-slice_fusion), channel_id=1, source_target_pairs={{0,4},{4,0},{1,5},{5,1},{2,6},{6,2},{3,7},{7,3},{8,12},{12,8},{9,1... | collective-permute-start | bytes 294920 | tf_op jit(solution)/shard_map/ppermute | solution.py:31
  58.8 0.1 collective-permute-start.7
  58.9 3.0 %collective-permute-done.13 = f32[96,256]{1,0:T(8,128)S(1)} collective-permute-done((f32[96,256]{1,0:T(8,128)S(1)}, f32[96,256]{1,0:T(8,128)S(1)}, u32[]{:S(2)}, u32[]{:S(2)}) %collective-permute-start.13) | collective-permute-done | bytes 98336 | tf_op jit(solution)/shard_map/ppermute | solution.py:31
  61.9 0.1 collective-permute-start.14
  62.0 2.0 %collective-permute-done.7 = f32[96,256]{1,0:T(8,128)S(1)} collective-permute-done((f32[96,256]{1,0:T(8,128)S(1)}, f32[96,256]{1,0:T(8,128)S(1)}, u32[]{:S(2)}, u32[]{:S(2)}) %collective-permute-start.7) | collective-permute-done | bytes 98336 | tf_op jit(solution)/shard_map/ppermute | solution.py:37
  64.0 0.1 collective-permute-start.8
  64.1 1.2 %fusion.74 = bf16[1,256,2,128]{1,3,2,0:T(8,128)(2,1)S(1)} fusion(f32[256,4,3,144]{0,3,2,1:T(8,128)} %fusion.17), kind=kLoop, calls=%fused_computation.114 | loop fusion | flops 196608 | bytes 917504 | tf_op jit(solution)/shard_map/convert_element_type | solution.py:197
  65.3 2.3 %collective-permute-done.14 = f32[96,256]{1,0:T(8,128)S(1)} collective-permute-done((f32[96,256]{1,0:T(8,128)S(1)}, f32[96,256]{1,0:T(8,128)S(1)}, u32[]{:S(2)}, u32[]{:S(2)}) %collective-permute-start.14) | collective-permute-done | bytes 98336 | tf_op jit(solution)/shard_map/ppermute | solution.py:37
  67.6 0.7 collective-permute-start.15
  68.3 4.8 %collective-permute-done.8 = f32[96,256]{1,0:T(8,128)S(1)} collective-permute-done((f32[96,256]{1,0:T(8,128)S(1)}, f32[96,256]{1,0:T(8,128)S(1)}, u32[]{:S(2)}, u32[]{:S(2)}) %collective-permute-start.8) | collective-permute-done | bytes 98336 | tf_op jit(solution)/shard_map/ppermute | solution.py:37
  73.1 0.8 collective-permute-start.9
  73.9 0.2 collective-permute-done.15
  74.1 1.1 %collective-permute-start.16 = (bf16[96,256]{1,0:T(8,128)(2,1)S(1)}, bf16[96,256]{1,0:T(8,128)(2,1)S(1)}, u32[]{:S(2)}, u32[]{:S(2)}) collective-permute-start(bf16[96,256]{1,0:T(8,128)(2,1)S(1)} %add_convert_fusion), channel_id=1, source_target_pairs={{0,4},{4,0},{1,5},{5,1},{2,6},{6,2},{3,7},{7,3},{8,12},{12,8},{9,1... | collective-permute-start | bytes 147464 | tf_op jit(solution)/shard_map/ppermute | solution.py:42
  75.3 2.0 %collective-permute-done.9 = bf16[96,256]{1,0:T(8,128)(2,1)S(1)} collective-permute-done((bf16[96,256]{1,0:T(8,128)(2,1)S(1)}, bf16[96,256]{1,0:T(8,128)(2,1)S(1)}, u32[]{:S(2)}, u32[]{:S(2)}) %collective-permute-start.9) | collective-permute-done | bytes 49184 | tf_op jit(solution)/shard_map/ppermute | solution.py:42
  77.3 1.6 %collective-permute-start.10 = (bf16[192,256]{1,0:T(8,128)(2,1)S(1)}, bf16[192,256]{1,0:T(8,128)(2,1)S(1)}, u32[]{:S(2)}, u32[]{:S(2)}) collective-permute-start(bf16[192,256]{1,0:T(8,128)(2,1)S(1)} %maximum_select_fusion.4), channel_id=1, source_target_pairs={{0,16},{8,24},{16,0},{24,8},{1,17},{9,25},{17,1},{25,9},{2,18},{10... | collective-permute-start | bytes 294920 | tf_op jit(solution)/shard_map/ppermute | solution.py:42
  78.8 1.0 %collective-permute-start.17 = (bf16[192,256]{1,0:T(8,128)(2,1)S(1)}, bf16[192,256]{1,0:T(8,128)(2,1)S(1)}, u32[]{:S(2)}, u32[]{:S(2)}) collective-permute-start(bf16[192,256]{1,0:T(8,128)(2,1)S(1)} %maximum_select_fusion.5), channel_id=1, source_target_pairs={{0,16},{8,24},{16,0},{24,8},{1,17},{9,25},{17,1},{25,9},{2,18},{10... | collective-permute-start | bytes 294920 | tf_op jit(solution)/shard_map/ppermute | solution.py:42
  79.9 2.1 %collective-permute-done.10 = bf16[192,256]{1,0:T(8,128)(2,1)S(1)} collective-permute-done((bf16[192,256]{1,0:T(8,128)(2,1)S(1)}, bf16[192,256]{1,0:T(8,128)(2,1)S(1)}, u32[]{:S(2)}, u32[]{:S(2)}) %collective-permute-start.10) | collective-permute-done | bytes 98336 | tf_op jit(solution)/shard_map/ppermute | solution.py:42
  82.0 0.1 collective-permute-start.11
  82.1 1.4 %collective-permute-done.17 = bf16[192,256]{1,0:T(8,128)(2,1)S(1)} collective-permute-done((bf16[192,256]{1,0:T(8,128)(2,1)S(1)}, bf16[192,256]{1,0:T(8,128)(2,1)S(1)}, u32[]{:S(2)}, u32[]{:S(2)}) %collective-permute-start.17) | collective-permute-done | bytes 98336 | tf_op jit(solution)/shard_map/ppermute | solution.py:42
  83.6 0.1 collective-permute-start.18
  83.7 0.3 fusion.33
  84.0 0.8 copy.40
  84.8 0.8 copy.41
  85.5 0.2 maximum_select_fusion
  85.7 0.9 %convert.5 = f32[3,256,256]{2,1,0:T(8,128)} convert(bf16[3,256,256]{2,1,0:T(8,128)(2,1)S(1)} %bitcast.196) | non-fusion elementwise | flops 196608 | bytes 1179648 | tf_op jit(solution)/shard_map/convert_element_type | solution.py:46
  86.7 0.2 maximum_select_fusion.1
  86.8 0.9 %convert.6 = f32[3,256,256]{2,1,0:T(8,128)} convert(bf16[3,256,256]{2,1,0:T(8,128)(2,1)S(1)} %bitcast.195) | non-fusion elementwise | flops 196608 | bytes 1179648 | tf_op jit(solution)/shard_map/convert_element_type | solution.py:46
  (46 shorter events, 0.7 us)
Async XLA Ops:
  0.6 36.0 %copy-start = (bf16[3,256,256]{2,1,0:T(8,128)(2,1)S(1)}, bf16[3,256,256]{2,1,0:T(8,128)(2,1)}, u32[]{:S(2)}) copy-start(bf16[3,256,256]{2,1,0:T(8,128)(2,1)} %param.8) | copy-start | bytes 1179652
  2.8 7.4 %collective-permute-start.1 = (bf16[512,2,8]{0,2,1:T(8,128)(2,1)S(1)}, bf16[512,2,8]{0,2,1:T(8,128)(2,1)S(1)}, u32[]{:S(2)}, u32[]{:S(2)}) collective-permute-start(bf16[512,2,8]{0,2,1:T(8,128)(2,1)S(1)} %get-tuple-element.31), channel_id=1, source_target_pairs={{0,3},{1,0},{2,1},{3,2},{4,7},{5,4},{6,5},{7,6},{8,11},{9,8},{10,9... | collective-permute-start | bytes 49160 | tf_op jit(solution)/shard_map/ppermute | solution.py:74
  7.9 5.5 %collective-permute-start = (bf16[512,2,8]{0,2,1:T(8,128)(2,1)S(1)}, bf16[512,2,8]{0,2,1:T(8,128)(2,1)S(1)}, u32[]{:S(2)}, u32[]{:S(2)}) collective-permute-start(bf16[512,2,8]{0,2,1:T(8,128)(2,1)S(1)} %get-tuple-element.30), channel_id=1, source_target_pairs={{0,1},{1,2},{2,3},{3,0},{4,5},{5,6},{6,7},{7,4},{8,9},{9,10},{10,1... | collective-permute-start | bytes 49160 | tf_op jit(solution)/shard_map/ppermute | solution.py:73
  13.5 9.0 %collective-permute-start.2 = (bf16[513,2,144]{0,2,1:T(8,128)(2,1)S(1)}, bf16[513,2,144]{0,2,1:T(8,128)(2,1)S(1)}, u32[]{:S(2)}, u32[]{:S(2)}) collective-permute-start(bf16[513,2,144]{0,2,1:T(8,128)(2,1)S(1)} %pad_maximum_fusion.16), channel_id=1, source_target_pairs={{0,4},{4,0},{1,5},{5,1},{2,6},{6,2},{3,7},{7,3},{8,12},{12,8},{9,1... | collective-permute-start | bytes 886472 | tf_op jit(solution)/shard_map/ppermute | solution.py:53
  28.0 1.4 %copy-start.1 = (bf16[4,3,144,3,136]{2,0,1,3,4:T(4,128)(2,1)}, bf16[4,3,144,3,136]{2,0,1,3,4:T(4,128)(2,1)S(1)}, u32[]{:S(2)}) copy-start(bf16[4,3,144,3,136]{2,0,1,3,4:T(4,128)(2,1)S(1)} %convert_bitcast_fusion) | copy-start | bytes 4230148
  29.4 1.0 %copy-start.3 = (bf16[3,256,256]{2,1,0:T(8,128)(2,1)S(1)}, bf16[3,256,256]{2,1,0:T(8,128)(2,1)}, u32[]{:S(2)}) copy-start(bf16[3,256,256]{2,1,0:T(8,128)(2,1)} %param.9) | copy-start | bytes 1179652
  30.4 6.2 %copy-start.5 = (bf16[256,4,3,136]{0,3,2,1:T(8,128)(2,1)}, bf16[256,4,3,136]{0,3,2,1:T(8,128)(2,1)S(1)}, u32[]{:S(2)}) copy-start(bf16[256,4,3,136]{0,3,2,1:T(8,128)(2,1)S(1)} %fusion.24) | copy-start | bytes 2506756
  36.6 2.3 %copy-start.4 = (bf16[136,128,3,2,3]{1,4,3,2,0:T(4,128)(2,1)S(1)}, bf16[136,128,3,2,3]{1,4,3,2,0:T(4,128)(2,1)}, u32[]{:S(2)}) copy-start(bf16[136,128,3,2,3]{1,4,3,2,0:T(4,128)(2,1)} %fusion.34) | copy-start | bytes 1880068
  38.9 1.4 %copy-start.6 = (bf16[256,4,136]{0,2,1:T(8,128)(2,1)}, bf16[256,4,136]{0,2,1:T(8,128)(2,1)S(1)}, u32[]{:S(2)}) copy-start(bf16[256,4,136]{0,2,1:T(8,128)(2,1)S(1)} %get-tuple-element.9) | copy-start | bytes 835588
  38.9 1.0 %copy-start.2 = (bf16[1,256,2,128]{3,2,1,0:T(2,128)(2,1)S(1)}, bf16[1,256,2,128]{3,2,1,0:T(2,128)(2,1)}, u32[]{:S(2)}) copy-start(bf16[1,256,2,128]{3,2,1,0:T(2,128)(2,1)} %param.13) | copy-start | bytes 393220
  40.2 2.7 %collective-permute-start.3 = (f32[384,256]{1,0:T(8,128)S(1)}, f32[384,256]{1,0:T(8,128)S(1)}, u32[]{:S(2)}, u32[]{:S(2)}) collective-permute-start(f32[384,256]{1,0:T(8,128)S(1)} %constant_dynamic-slice_fusion.5), channel_id=1, source_target_pairs={{0,8},{8,0},{16,24},{24,16},{1,9},{9,1},{17,25},{25,17},{2,10},{10... | collective-permute-start | bytes 1179656 | tf_op jit(solution)/shard_map/ppermute | solution.py:31
  42.4 2.2 %collective-permute-start.4 = (f32[384,256]{1,0:T(8,128)}, f32[384,256]{1,0:T(8,128)}, u32[]{:S(2)}, u32[]{:S(2)}) collective-permute-start(f32[384,256]{1,0:T(8,128)} %constant_dynamic-slice_fusion.4), channel_id=1, source_target_pairs={{0,8},{8,0},{16,24},{24,16},{1,9},{9,1},{17,25},{25,17},{2,10},{10... | collective-permute-start | bytes 1179656 | tf_op jit(solution)/shard_map/ppermute | solution.py:31
  45.7 7.8 %collective-permute-start.5 = (f32[192,256]{1,0:T(8,128)S(1)}, f32[192,256]{1,0:T(8,128)S(1)}, u32[]{:S(2)}, u32[]{:S(2)}) collective-permute-start(f32[192,256]{1,0:T(8,128)S(1)} %constant_dynamic-slice_fusion.3), channel_id=1, source_target_pairs={{0,16},{8,24},{16,0},{24,8},{1,17},{9,25},{17,1},{25,9},{2,18},{10... | collective-permute-start | bytes 589832 | tf_op jit(solution)/shard_map/ppermute | solution.py:31
  47.2 9.9 %collective-permute-start.12 = (f32[192,256]{1,0:T(8,128)S(1)}, f32[192,256]{1,0:T(8,128)S(1)}, u32[]{:S(2)}, u32[]{:S(2)}) collective-permute-start(f32[192,256]{1,0:T(8,128)S(1)} %constant_dynamic-slice_fusion.1), channel_id=1, source_target_pairs={{0,16},{8,24},{16,0},{24,8},{1,17},{9,25},{17,1},{25,9},{2,18},{10... | collective-permute-start | bytes 589832 | tf_op jit(solution)/shard_map/ppermute | solution.py:31
  53.6 5.2 %collective-permute-start.6 = (f32[96,256]{1,0:T(8,128)S(1)}, f32[96,256]{1,0:T(8,128)S(1)}, u32[]{:S(2)}, u32[]{:S(2)}) collective-permute-start(f32[96,256]{1,0:T(8,128)S(1)} %constant_dynamic-slice_fusion.2), channel_id=1, source_target_pairs={{0,4},{4,0},{1,5},{5,1},{2,6},{6,2},{3,7},{7,3},{8,12},{12,8},{9,1... | collective-permute-start | bytes 294920 | tf_op jit(solution)/shard_map/ppermute | solution.py:31
  57.2 4.7 %collective-permute-start.13 = (f32[96,256]{1,0:T(8,128)S(1)}, f32[96,256]{1,0:T(8,128)S(1)}, u32[]{:S(2)}, u32[]{:S(2)}) collective-permute-start(f32[96,256]{1,0:T(8,128)S(1)} %constant_dynamic-slice_fusion), channel_id=1, source_target_pairs={{0,4},{4,0},{1,5},{5,1},{2,6},{6,2},{3,7},{7,3},{8,12},{12,8},{9,1... | collective-permute-start | bytes 294920 | tf_op jit(solution)/shard_map/ppermute | solution.py:31
  58.8 5.2 %collective-permute-start.7 = (f32[96,256]{1,0:T(8,128)S(1)}, f32[96,256]{1,0:T(8,128)S(1)}, u32[]{:S(2)}, u32[]{:S(2)}) collective-permute-start(f32[96,256]{1,0:T(8,128)S(1)} %dynamic-slice_add_fusion.5), channel_id=1, source_target_pairs={{0,1},{1,0},{2,3},{3,2},{4,5},{5,4},{6,7},{7,6},{8,9},{9,8},{10,11... | collective-permute-start | bytes 294920 | tf_op jit(solution)/shard_map/ppermute | solution.py:37
  61.9 5.7 %collective-permute-start.14 = (f32[96,256]{1,0:T(8,128)S(1)}, f32[96,256]{1,0:T(8,128)S(1)}, u32[]{:S(2)}, u32[]{:S(2)}) collective-permute-start(f32[96,256]{1,0:T(8,128)S(1)} %dynamic-slice_add_fusion.4), channel_id=1, source_target_pairs={{0,1},{1,0},{2,3},{3,2},{4,5},{5,4},{6,7},{7,6},{8,9},{9,8},{10,11... | collective-permute-start | bytes 294920 | tf_op jit(solution)/shard_map/ppermute | solution.py:37
  64.0 9.1 %collective-permute-start.8 = (f32[96,256]{1,0:T(8,128)S(1)}, f32[96,256]{1,0:T(8,128)S(1)}, u32[]{:S(2)}, u32[]{:S(2)}) collective-permute-start(f32[96,256]{1,0:T(8,128)S(1)} %add.176), channel_id=1, source_target_pairs={{0,2},{1,3},{2,0},{3,1},{4,6},{5,7},{6,4},{7,5},{8,10},{9,11},{10,... | collective-permute-start | bytes 294920 | tf_op jit(solution)/shard_map/ppermute | solution.py:37
  67.6 6.5 %collective-permute-start.15 = (f32[96,256]{1,0:T(8,128)S(1)}, f32[96,256]{1,0:T(8,128)S(1)}, u32[]{:S(2)}, u32[]{:S(2)}) collective-permute-start(f32[96,256]{1,0:T(8,128)S(1)} %add.180), channel_id=1, source_target_pairs={{0,2},{1,3},{2,0},{3,1},{4,6},{5,7},{6,4},{7,5},{8,10},{9,11},{10,... | collective-permute-start | bytes 294920 | tf_op jit(solution)/shard_map/ppermute | solution.py:37
  73.1 4.2 %collective-permute-start.9 = (bf16[96,256]{1,0:T(8,128)(2,1)S(1)}, bf16[96,256]{1,0:T(8,128)(2,1)S(1)}, u32[]{:S(2)}, u32[]{:S(2)}) collective-permute-start(bf16[96,256]{1,0:T(8,128)(2,1)S(1)} %add_convert_fusion.1), channel_id=1, source_target_pairs={{0,4},{4,0},{1,5},{5,1},{2,6},{6,2},{3,7},{7,3},{8,12},{12,8},{9,1... | collective-permute-start | bytes 147464 | tf_op jit(solution)/shard_map/ppermute | solution.py:42
  74.1 4.7 %collective-permute-start.16 = (bf16[96,256]{1,0:T(8,128)(2,1)S(1)}, bf16[96,256]{1,0:T(8,128)(2,1)S(1)}, u32[]{:S(2)}, u32[]{:S(2)}) collective-permute-start(bf16[96,256]{1,0:T(8,128)(2,1)S(1)} %add_convert_fusion), channel_id=1, source_target_pairs={{0,4},{4,0},{1,5},{5,1},{2,6},{6,2},{3,7},{7,3},{8,12},{12,8},{9,1... | collective-permute-start | bytes 147464 | tf_op jit(solution)/shard_map/ppermute | solution.py:42
  77.3 4.7 %collective-permute-start.10 = (bf16[192,256]{1,0:T(8,128)(2,1)S(1)}, bf16[192,256]{1,0:T(8,128)(2,1)S(1)}, u32[]{:S(2)}, u32[]{:S(2)}) collective-permute-start(bf16[192,256]{1,0:T(8,128)(2,1)S(1)} %maximum_select_fusion.4), channel_id=1, source_target_pairs={{0,16},{8,24},{16,0},{24,8},{1,17},{9,25},{17,1},{25,9},{2,18},{10... | collective-permute-start | bytes 294920 | tf_op jit(solution)/shard_map/ppermute | solution.py:42
  78.8 4.7 %collective-permute-start.17 = (bf16[192,256]{1,0:T(8,128)(2,1)S(1)}, bf16[192,256]{1,0:T(8,128)(2,1)S(1)}, u32[]{:S(2)}, u32[]{:S(2)}) collective-permute-start(bf16[192,256]{1,0:T(8,128)(2,1)S(1)} %maximum_select_fusion.5), channel_id=1, source_target_pairs={{0,16},{8,24},{16,0},{24,8},{1,17},{9,25},{17,1},{25,9},{2,18},{10... | collective-permute-start | bytes 294920 | tf_op jit(solution)/shard_map/ppermute | solution.py:42
  82.0 3.5 %collective-permute-start.11 = (bf16[384,256]{1,0:T(8,128)(2,1)S(1)}, bf16[384,256]{1,0:T(8,128)(2,1)S(1)}, u32[]{:S(2)}, u32[]{:S(2)}) collective-permute-start(bf16[384,256]{1,0:T(8,128)(2,1)S(1)} %maximum_select_fusion.2), channel_id=1, source_target_pairs={{0,8},{8,0},{16,24},{24,16},{1,9},{9,1},{17,25},{25,17},{2,10},{10... | collective-permute-start | bytes 589832 | tf_op jit(solution)/shard_map/ppermute | solution.py:42
  83.6 3.1 %collective-permute-start.18 = (bf16[384,256]{1,0:T(8,128)(2,1)S(1)}, bf16[384,256]{1,0:T(8,128)(2,1)S(1)}, u32[]{:S(2)}, u32[]{:S(2)}) collective-permute-start(bf16[384,256]{1,0:T(8,128)(2,1)S(1)} %maximum_select_fusion.3), channel_id=1, source_target_pairs={{0,8},{8,0},{16,24},{24,16},{1,9},{9,1},{17,25},{25,17},{2,10},{10... | collective-permute-start | bytes 589832 | tf_op jit(solution)/shard_map/ppermute | solution.py:42

commit v10 on v9

--- a/solution.py
+++ b/solution.py
@@ -130,6 +130,16 @@
     return total
 
 
+def spread_adjoint_rows(mixed, band):
+    col_count = mixed.shape[3]
+    partial = jnp.einsum("cikq,iapkq->ciap", mixed, band, preferred_element_type=jnp.float32)
+    if partial.shape[3] != col_count - LON_HALO:
+        partial = partial[:, :, :, LON_HALO : col_count]
+    below = jnp.pad(partial[:, 1:, 0], ((0, 0), (0, 1), (0, 0)))
+    above = jnp.pad(partial[:, :-1, 2], ((0, 0), (1, 0), (0, 0)))
+    return partial[:, :, 1] + below + above
+
+
 def mix_channels(weight, spreaded):
     return jnp.einsum("koc,cikj->oij", weight, spreaded, preferred_element_type=jnp.float32)
 
@@ -178,8 +188,22 @@
     own_gradient = gradient_wide[:, LAT_HALO : LAT_HALO + row_count, LON_HALO : LON_HALO + col_count]
     second_sum = filter_term(own_gradient, second_spread)
 
-    second_mixed = unmix(second_weight, gradient_wide)
-    activation_grad = spread_adjoint(second_mixed, wide_band).astype(jnp.bfloat16)
+    if lax.axis_size("lat") == 2 and row_count == LAT_HALO:
+        lower = lax.axis_index("lat") == 0
+        grid_gradient = jnp.where(lower, gradient_wide[:, row_count:], gradient_wide[:, : 2 * row_count])
+        grid_stencil = jnp.where(lower, stencil_wide[:, row_count:], stencil_wide[:, : 2 * row_count])
+        grid_band = band_of(grid_stencil, col_count + 2 * LON_HALO, LON_HALO, col_count + LON_HALO)
+        second_mixed = unmix(second_weight, grid_gradient)
+        grid_grad = spread_adjoint_rows(second_mixed, grid_band).astype(jnp.bfloat16)
+        edge = jnp.zeros_like(grid_grad[:, :LAT_REACH])
+        activation_grad = jnp.where(
+            lower,
+            jnp.concatenate([edge, grid_grad[:, : 2 * row_count - LAT_REACH]], axis=1),
+            jnp.concatenate([grid_grad[:, LAT_REACH:], edge], axis=1),
+        )
+    else:
+        second_mixed = unmix(second_weight, gradient_wide)
+        activation_grad = spread_adjoint(second_mixed, wide_band).astype(jnp.bfloat16)
     hidden_grad = jax.vjp(jax.nn.gelu, hidden)[1](activation_grad.astype(jnp.float32))[0]
     hidden_grad = jnp.where(near_valid, hidden_grad, 0.0).astype(jnp.bfloat16)
     own_hidden_grad = hidden_grad[:, LAT_REACH : LAT_REACH + row_count, LON_REACH : LON_REACH + col_count]

time: 88.3 us -> 81.9 us (0.928)
  matrix products: 23.1 us -> 17.9 us
    dot_general x2 -> x1, matrix products: 10.2 us -> 3.98 us  [spread_adjoint(): jnp.einsum('cikq,iapkq->ciap', mixed, band, preferred_element_type=jnp.fl...]
    dot_general x0 -> x1, matrix products: none -> 2.71 us  [spread_adjoint_rows(): jnp.einsum('cikq,iapkq->ciap', mixed, band, preferred_element_type=jnp.fl...]
    dot_general x2, matrix products: 2.54 us -> 1.09 us  [mix_channels(): jnp.einsum('koc,cikj->oij', weight, spreaded, preferred_element_type=jnp....]
    dot_general x2, matrix products: 1.6 us -> 0.59 us  [filter_term(): jnp.einsum('oij,cikj->koc', gradient, spreaded, preferred_element_type=jn...]
    add x6, other arithmetic: 1.17 us -> 0.18 us  [halving_sum(): flat = keep + lax.ppermute(send, axis, pairs)]
    unnamed x18 -> x16, local copies, waits for them, and re-layouts: 5.76 us -> 5.71 us
  transfers between devices with their start and end apart: 19 -> 19, of which waited for: 13 -> 14; matrix products, arithmetic and copies ran while one was open for 16% -> 16% of each run, Pallas kernels for 0% -> 0%
where the time goes in v10:
time: 81.9 us; the launch traced here: 81.6 us
  waiting for transfers between devices  32.1 us (39%)
  starting transfers between devices  18.2 us (22%)
  matrix products  17.9 us (22%)
  local copies, waits for them, and re-layouts  7.06 us (9%)
  other arithmetic  5.25 us (6%)
  between operations  1.05 us (1%)
    ppermute x4, waiting for transfers between devices, halving_sum(): flat = flat + lax.ppermute(flat, axis, pairs)  9.31 us
    ppermute x6, waiting for transfers between devices, halving_sum(): flat = keep + lax.ppermute(send, axis, pairs)  8.17 us
    dot_general x3, matrix products, band_of(): jnp.einsum('kiad,dpq->iapkq', stencil, lon_picker(col_count, first_source...  7.41 us
    ppermute x6, starting transfers between devices, halving_sum(): flat = keep + lax.ppermute(send, axis, pairs)  5.89 us
    ppermute x1, waiting for transfers between devices, lat_halo(): other = lax.ppermute(block, 'lat', [(0, 1), (1, 0)])  5.85 us
    unnamed x16, local copies, waits for them, and re-layouts  5.71 us
    ppermute x6, waiting for transfers between devices, halving_sum(): other = lax.ppermute(flat, axis, pairs)  5.49 us
    ppermute x1, starting transfers between devices, lon_halo(): lax.ppermute(block[..., :width], 'lon', [(i, (i - 1) % count) for i in ra...  5.13 us
  transfers between devices with their start and end apart: 19, of which 14 were waited for; matrix products, arithmetic and copies ran while one was open for 16% of the time, Pallas kernels for 0%

profile of v10, /device:TPU:0, one launch (start us, length us, event | category | flops | bytes accessed | tf_op | source)
XLA Modules:
  0.0 81.6 jit_solution(7339975835738334850)
XLA Ops:
  0.6 1.1 %copy.26 = bf16[1,256,2,128]{1,3,2,0:T(8,128)(2,1)S(1)} copy(bf16[1,256,2,128]{3,2,1,0:T(2,128)(2,1)} %param.13) | data formatting | bytes 262144 | tf_op args[6]
  1.7 1.0 %copy.25 = bf16[1,256,2,128]{1,3,2,0:T(8,128)(2,1)S(1)} copy(bf16[1,256,2,128]{3,2,1,0:T(2,128)(2,1)} %param.7) | data formatting | bytes 262144 | tf_op args[0]
  2.8 5.1 %collective-permute-start.1 = (bf16[512,2,8]{0,2,1:T(8,128)(2,1)S(1)}, bf16[512,2,8]{0,2,1:T(8,128)(2,1)S(1)}, u32[]{:S(2)}, u32[]{:S(2)}) collective-permute-start(bf16[512,2,8]{0,2,1:T(8,128)(2,1)S(1)} %get-tuple-element.35), channel_id=1, source_target_pairs={{0,3},{1,0},{2,1},{3,2},{4,7},{5,4},{6,5},{7,6},{8,11},{9,8},{10,9... | collective-permute-start | bytes 49160 | tf_op jit(solution)/shard_map/ppermute | solution.py:74
  7.9 0.1 fusion.42
  8.0 0.7 broadcast_add_fusion
  8.7 0.9 %convolution_convert_fusion.2 = bf16[3,2,3,9]{3,2,1,0:T(4,128)(2,1)S(1)} fusion(s32[2,3,12]{2,0,1:T(2,128)S(1)} %get-tuple-element.36, f32[2,3,12]{2,0,1:T(2,128)} %param.10, s32[2,3,12]{2,0,1:T(2,128)S(1)} %get-tuple-element.37), kind=kOutput, calls=%fused_computation.38 | convolution fusion | flops 24570 | bytes 1188 | tf_op jit(solution)/shard_map/rks,rksa,rksd->krad/dot_general | solution.py:83
  9.6 0.1 reshape.75
  9.7 0.2 fusion.29
  10.0 0.1 copy.28
  10.1 3.3 %collective-permute-done = bf16[512,2,8]{0,2,1:T(8,128)(2,1)S(1)} collective-permute-done((bf16[512,2,8]{0,2,1:T(8,128)(2,1)S(1)}, bf16[512,2,8]{0,2,1:T(8,128)(2,1)S(1)}, u32[]{:S(2)}, u32[]{:S(2)}) %collective-permute-start) | collective-permute-done | bytes 16416 | tf_op jit(solution)/shard_map/ppermute | solution.py:73
  13.5 1.6 %collective-permute-start.2 = (bf16[513,2,144]{0,2,1:T(8,128)(2,1)S(1)}, bf16[513,2,144]{0,2,1:T(8,128)(2,1)S(1)}, u32[]{:S(2)}, u32[]{:S(2)}) collective-permute-start(bf16[513,2,144]{0,2,1:T(8,128)(2,1)S(1)} %pad_maximum_fusion), channel_id=1, source_target_pairs={{0,4},{4,0},{1,5},{5,1},{2,6},{6,2},{3,7},{7,3},{8,12},{12,8},{9,1... | collective-permute-start | bytes 886472 | tf_op jit(solution)/shard_map/ppermute | solution.py:53
  15.1 1.5 %fusion.34 = bf16[136,128,3,2,3]{1,4,3,2,0:T(4,128)(2,1)} fusion(pred[9,136,128,1,1]{2,1,0,3,4:T(8,128)(4,1)S(1)} %fusion.42, bf16[3,2,3,9]{3,2,1,0:T(4,128)(2,1)S(1)} %convolution_convert_fusion.2), kind=kOutput, calls=%fused_computation.36 | convolution fusion | flops 5640192 | bytes 783684 | tf_op jit(solution)/shard_map/kiad,dpq->iapkq/dot_general | solution.py:102
  16.6 5.9 %collective-permute-done.2 = bf16[513,2,144]{0,2,1:T(8,128)(2,1)S(1)} collective-permute-done((bf16[513,2,144]{0,2,1:T(8,128)(2,1)S(1)}, bf16[513,2,144]{0,2,1:T(8,128)(2,1)S(1)}, u32[]{:S(2)}, u32[]{:S(2)}) %collective-permute-start.2) | collective-permute-done | bytes 295520 | tf_op jit(solution)/shard_map/ppermute | solution.py:53
  22.5 0.2 maximum_reduce_fusion
  22.6 0.1 reshape_squeeze.3
  22.8 3.0 %convert_bitcast_fusion = bf16[4,3,144,3,136]{2,0,1,3,4:T(4,128)(2,1)} fusion(bf16[3,6,3,9]{3,1,2,0:T(8,128)(2,1)S(1)} %bitcast.205), kind=kOutput, calls=%fused_computation.8 | convolution fusion | flops 13747968 | bytes 1419264 | tf_op jit(solution)/shard_map/kiad,dpq->iapkq/dot_general | solution.py:102
  25.7 2.9 %fusion.10 = bf16[136,144,3,4,3]{1,3,4,2,0:T(4,128)(2,1)} fusion(pred[9,136,144,1,1]{2,1,0,3,4:T(8,128)(4,1)S(1)} %fusion.29, bf16[3,6,3,9]{3,1,2,0:T(8,128)(2,1)S(1)} %bitcast.206, pred[]{:T(512)S(6)} %eq.72), kind=kOutput, calls=%fused_computation.12 | convolution fusion | flops 12690756 | bytes 1587277 | tf_op jit(solution)/shard_map/kiad,dpq->iapkq/dot_general | solution.py:102
  28.7 2.7 %fusion.19 = f32[256,4,3,136]{0,3,1,2:T(8,128)S(1)} fusion(bf16[3,256,256]{2,1,0:T(8,128)(2,1)} %param.9, bf16[513,2,144]{0,2,1:T(8,128)(2,1)S(1)} %get-tuple-element.27, bf16[1,2,144]{0,2,1:T(8,128)(2,1)S(1)} %copy.28, bf16[512,2,8]{0,2,1:T(8,128)(2,1)S(1)} %collective-permute-done.1, bf16[512,2,8]{0,2,1:T(8,128)(2,1)S(1)} %collective-permute-done, ...), kind=kOutput, calls=%fused_computation.16 | convolution fusion | flops 591593472 | bytes 4360897 | tf_op jit(solution)/shard_map/cikq,iapkq->ciap/dot_general | solution.py:135
  31.4 0.1 fusion.56
  31.6 0.1 maximum_bitcast_fusion.4
  31.7 1.5 %copy-done.1 = bf16[4,3,144,3,136]{2,0,1,3,4:T(4,128)(2,1)S(1)} copy-done((bf16[4,3,144,3,136]{2,0,1,3,4:T(4,128)(2,1)S(1)}, bf16[4,3,144,3,136]{2,0,1,3,4:T(4,128)(2,1)}, u32[]{:S(2)}) %copy-start.1) | copy-done | bytes 1410072
  33.1 0.8 fusion.24
  33.9 0.8 fusion.46
  34.8 0.3 copy-done.4
  35.1 0.4 fusion.31
  35.5 0.3 copy-done.2
  35.8 0.3 fusion.27
  36.1 0.1 collective-permute-start.3
  36.2 0.3 fusion.28
  36.5 0.8 constant_dynamic-slice_fusion.4
  37.3 0.5 collective-permute-start.4
  37.8 0.1 collective-permute-done.3
  38.0 1.4 %collective-permute-done.4 = f32[384,256]{1,0:T(8,128)S(1)} collective-permute-done((f32[384,256]{1,0:T(8,128)}, f32[384,256]{1,0:T(8,128)S(1)}, u32[]{:S(2)}, u32[]{:S(2)}) %collective-permute-start.4) | collective-permute-done | bytes 393248 | tf_op jit(solution)/shard_map/ppermute | solution.py:31
  39.5 1.5 %collective-permute-start.5 = (f32[192,256]{1,0:T(8,128)S(1)}, f32[192,256]{1,0:T(8,128)S(1)}, u32[]{:S(2)}, u32[]{:S(2)}) collective-permute-start(f32[192,256]{1,0:T(8,128)S(1)} %constant_dynamic-slice_fusion.3), channel_id=1, source_target_pairs={{0,16},{8,24},{16,0},{24,8},{1,17},{9,25},{17,1},{25,9},{2,18},{10... | collective-permute-start | bytes 589832 | tf_op jit(solution)/shard_map/ppermute | solution.py:31
  41.0 0.6 collective-permute-start.12
  41.6 4.0 %fusion.14 = f32[256,4,3,144]{0,3,2,1:T(8,128)} fusion(bf16[4,3,144,3,136]{2,0,1,3,4:T(4,128)(2,1)} %convert_bitcast_fusion, bf16[3,256,256]{2,1,0:T(8,128)(2,1)S(1)} %copy-done, bf16[256,4,136]{0,2,1:T(8,128)(2,1)} %copy-done.5), kind=kOutput, calls=%fused_computation.15 | convolution fusion | flops 575299584 | bytes 3851264 | tf_op jit(solution)/shard_map/cikq,iapkq->ciap/dot_general | solution.py:122
  45.6 1.7 %collective-permute-done.5 = f32[192,256]{1,0:T(8,128)S(1)} collective-permute-done((f32[192,256]{1,0:T(8,128)S(1)}, f32[192,256]{1,0:T(8,128)S(1)}, u32[]{:S(2)}, u32[]{:S(2)}) %collective-permute-start.5) | collective-permute-done | bytes 196640 | tf_op jit(solution)/shard_map/ppermute | solution.py:31
  47.4 1.6 %collective-permute-start.6 = (f32[96,256]{1,0:T(8,128)S(1)}, f32[96,256]{1,0:T(8,128)S(1)}, u32[]{:S(2)}, u32[]{:S(2)}) collective-permute-start(f32[96,256]{1,0:T(8,128)S(1)} %constant_dynamic-slice_fusion.2), channel_id=1, source_target_pairs={{0,4},{4,0},{1,5},{5,1},{2,6},{6,2},{3,7},{7,3},{8,12},{12,8},{9,1... | collective-permute-start | bytes 294920 | tf_op jit(solution)/shard_map/ppermute | solution.py:31
  48.9 2.0 %collective-permute-done.12 = f32[192,256]{1,0:T(8,128)S(1)} collective-permute-done((f32[192,256]{1,0:T(8,128)S(1)}, f32[192,256]{1,0:T(8,128)S(1)}, u32[]{:S(2)}, u32[]{:S(2)}) %collective-permute-start.12) | collective-permute-done | bytes 196640 | tf_op jit(solution)/shard_map/ppermute | solution.py:31
  51.0 1.6 %collective-permute-start.13 = (f32[96,256]{1,0:T(8,128)S(1)}, f32[96,256]{1,0:T(8,128)S(1)}, u32[]{:S(2)}, u32[]{:S(2)}) collective-permute-start(f32[96,256]{1,0:T(8,128)S(1)} %constant_dynamic-slice_fusion), channel_id=1, source_target_pairs={{0,4},{4,0},{1,5},{5,1},{2,6},{6,2},{3,7},{7,3},{8,12},{12,8},{9,1... | collective-permute-start | bytes 294920 | tf_op jit(solution)/shard_map/ppermute | solution.py:31
  52.6 0.1 collective-permute-start.7
  52.7 3.0 %collective-permute-done.13 = f32[96,256]{1,0:T(8,128)S(1)} collective-permute-done((f32[96,256]{1,0:T(8,128)S(1)}, f32[96,256]{1,0:T(8,128)S(1)}, u32[]{:S(2)}, u32[]{:S(2)}) %collective-permute-start.13) | collective-permute-done | bytes 98336 | tf_op jit(solution)/shard_map/ppermute | solution.py:31
  55.7 0.1 collective-permute-start.14
  55.7 2.1 %collective-permute-done.7 = f32[96,256]{1,0:T(8,128)S(1)} collective-permute-done((f32[96,256]{1,0:T(8,128)S(1)}, f32[96,256]{1,0:T(8,128)S(1)}, u32[]{:S(2)}, u32[]{:S(2)}) %collective-permute-start.7) | collective-permute-done | bytes 98336 | tf_op jit(solution)/shard_map/ppermute | solution.py:37
  57.8 0.1 collective-permute-start.8
  57.9 1.2 %fusion.79 = bf16[1,256,2,128]{1,3,2,0:T(8,128)(2,1)S(1)} fusion(f32[256,4,3,144]{0,3,2,1:T(8,128)} %fusion.14), kind=kLoop, calls=%fused_computation.119 | loop fusion | flops 196608 | bytes 917504 | tf_op jit(solution)/shard_map/convert_element_type | solution.py:221
  59.1 2.3 %collective-permute-done.14 = f32[96,256]{1,0:T(8,128)S(1)} collective-permute-done((f32[96,256]{1,0:T(8,128)S(1)}, f32[96,256]{1,0:T(8,128)S(1)}, u32[]{:S(2)}, u32[]{:S(2)}) %collective-permute-start.14) | collective-permute-done | bytes 98336 | tf_op jit(solution)/shard_map/ppermute | solution.py:37
  61.4 0.7 collective-permute-start.15
  62.1 4.8 %collective-permute-done.8 = f32[96,256]{1,0:T(8,128)S(1)} collective-permute-done((f32[96,256]{1,0:T(8,128)S(1)}, f32[96,256]{1,0:T(8,128)S(1)}, u32[]{:S(2)}, u32[]{:S(2)}) %collective-permute-start.8) | collective-permute-done | bytes 98336 | tf_op jit(solution)/shard_map/ppermute | solution.py:37
  66.9 0.9 %collective-permute-start.9 = (bf16[96,256]{1,0:T(8,128)(2,1)S(1)}, bf16[96,256]{1,0:T(8,128)(2,1)S(1)}, u32[]{:S(2)}, u32[]{:S(2)}) collective-permute-start(bf16[96,256]{1,0:T(8,128)(2,1)S(1)} %add_convert_fusion.1), channel_id=1, source_target_pairs={{0,4},{4,0},{1,5},{5,1},{2,6},{6,2},{3,7},{7,3},{8,12},{12,8},{9,1... | collective-permute-start | bytes 147464 | tf_op jit(solution)/shard_map/ppermute | solution.py:42
  67.7 0.2 collective-permute-done.15
  67.9 1.1 %collective-permute-start.16 = (bf16[96,256]{1,0:T(8,128)(2,1)S(1)}, bf16[96,256]{1,0:T(8,128)(2,1)S(1)}, u32[]{:S(2)}, u32[]{:S(2)}) collective-permute-start(bf16[96,256]{1,0:T(8,128)(2,1)S(1)} %add_convert_fusion), channel_id=1, source_target_pairs={{0,4},{4,0},{1,5},{5,1},{2,6},{6,2},{3,7},{7,3},{8,12},{12,8},{9,1... | collective-permute-start | bytes 147464 | tf_op jit(solution)/shard_map/ppermute | solution.py:42
  69.0 2.0 %collective-permute-done.9 = bf16[96,256]{1,0:T(8,128)(2,1)S(1)} collective-permute-done((bf16[96,256]{1,0:T(8,128)(2,1)S(1)}, bf16[96,256]{1,0:T(8,128)(2,1)S(1)}, u32[]{:S(2)}, u32[]{:S(2)}) %collective-permute-start.9) | collective-permute-done | bytes 49184 | tf_op jit(solution)/shard_map/ppermute | solution.py:42
  71.0 1.6 %collective-permute-start.10 = (bf16[192,256]{1,0:T(8,128)(2,1)S(1)}, bf16[192,256]{1,0:T(8,128)(2,1)S(1)}, u32[]{:S(2)}, u32[]{:S(2)}) collective-permute-start(bf16[192,256]{1,0:T(8,128)(2,1)S(1)} %maximum_select_fusion.4), channel_id=1, source_target_pairs={{0,16},{8,24},{16,0},{24,8},{1,17},{9,25},{17,1},{25,9},{2,18},{10... | collective-permute-start | bytes 294920 | tf_op jit(solution)/shard_map/ppermute | solution.py:42
  72.6 1.0 %collective-permute-start.17 = (bf16[192,256]{1,0:T(8,128)(2,1)S(1)}, bf16[192,256]{1,0:T(8,128)(2,1)S(1)}, u32[]{:S(2)}, u32[]{:S(2)}) collective-permute-start(bf16[192,256]{1,0:T(8,128)(2,1)S(1)} %maximum_select_fusion.5), channel_id=1, source_target_pairs={{0,16},{8,24},{16,0},{24,8},{1,17},{9,25},{17,1},{25,9},{2,18},{10... | collective-permute-start | bytes 294920 | tf_op jit(solution)/shard_map/ppermute | solution.py:42
  73.7 2.1 %collective-permute-done.10 = bf16[192,256]{1,0:T(8,128)(2,1)S(1)} collective-permute-done((bf16[192,256]{1,0:T(8,128)(2,1)S(1)}, bf16[192,256]{1,0:T(8,128)(2,1)S(1)}, u32[]{:S(2)}, u32[]{:S(2)}) %collective-permute-start.10) | collective-permute-done | bytes 98336 | tf_op jit(solution)/shard_map/ppermute | solution.py:42
  75.9 1.5 %collective-permute-done.17 = bf16[192,256]{1,0:T(8,128)(2,1)S(1)} collective-permute-done((bf16[192,256]{1,0:T(8,128)(2,1)S(1)}, bf16[192,256]{1,0:T(8,128)(2,1)S(1)}, u32[]{:S(2)}, u32[]{:S(2)}) %collective-permute-start.17) | collective-permute-done | bytes 98336 | tf_op jit(solution)/shard_map/ppermute | solution.py:42
  77.5 0.3 fusion.33
  77.8 0.8 copy.40
  78.6 0.8 copy.41
  79.4 0.2 maximum_select_fusion
  79.5 0.9 %convert.3 = f32[3,256,256]{2,1,0:T(8,128)} convert(bf16[3,256,256]{2,1,0:T(8,128)(2,1)S(1)} %bitcast.202) | non-fusion elementwise | flops 196608 | bytes 1179648 | tf_op jit(solution)/shard_map/convert_element_type | solution.py:46
  80.5 0.2 maximum_select_fusion.1
  80.6 0.9 %convert.4 = f32[3,256,256]{2,1,0:T(8,128)} convert(bf16[3,256,256]{2,1,0:T(8,128)(2,1)S(1)} %bitcast.201) | non-fusion elementwise | flops 196608 | bytes 1179648 | tf_op jit(solution)/shard_map/convert_element_type | solution.py:46
  (47 shorter events, 0.9 us)
Async XLA Ops:
  0.6 33.3 %copy-start = (bf16[3,256,256]{2,1,0:T(8,128)(2,1)S(1)}, bf16[3,256,256]{2,1,0:T(8,128)(2,1)}, u32[]{:S(2)}) copy-start(bf16[3,256,256]{2,1,0:T(8,128)(2,1)} %param.8) | copy-start | bytes 1179652
  2.8 7.4 %collective-permute-start.1 = (bf16[512,2,8]{0,2,1:T(8,128)(2,1)S(1)}, bf16[512,2,8]{0,2,1:T(8,128)(2,1)S(1)}, u32[]{:S(2)}, u32[]{:S(2)}) collective-permute-start(bf16[512,2,8]{0,2,1:T(8,128)(2,1)S(1)} %get-tuple-element.35), channel_id=1, source_target_pairs={{0,3},{1,0},{2,1},{3,2},{4,7},{5,4},{6,5},{7,6},{8,11},{9,8},{10,9... | collective-permute-start | bytes 49160 | tf_op jit(solution)/shard_map/ppermute | solution.py:74
  7.9 5.5 %collective-permute-start = (bf16[512,2,8]{0,2,1:T(8,128)(2,1)S(1)}, bf16[512,2,8]{0,2,1:T(8,128)(2,1)S(1)}, u32[]{:S(2)}, u32[]{:S(2)}) collective-permute-start(bf16[512,2,8]{0,2,1:T(8,128)(2,1)S(1)} %get-tuple-element.34), channel_id=1, source_target_pairs={{0,1},{1,2},{2,3},{3,0},{4,5},{5,6},{6,7},{7,4},{8,9},{9,10},{10,1... | collective-permute-start | bytes 49160 | tf_op jit(solution)/shard_map/ppermute | solution.py:73
  13.5 9.0 %collective-permute-start.2 = (bf16[513,2,144]{0,2,1:T(8,128)(2,1)S(1)}, bf16[513,2,144]{0,2,1:T(8,128)(2,1)S(1)}, u32[]{:S(2)}, u32[]{:S(2)}) collective-permute-start(bf16[513,2,144]{0,2,1:T(8,128)(2,1)S(1)} %pad_maximum_fusion), channel_id=1, source_target_pairs={{0,4},{4,0},{1,5},{5,1},{2,6},{6,2},{3,7},{7,3},{8,12},{12,8},{9,1... | collective-permute-start | bytes 886472 | tf_op jit(solution)/shard_map/ppermute | solution.py:53
  31.4 1.7 %copy-start.1 = (bf16[4,3,144,3,136]{2,0,1,3,4:T(4,128)(2,1)S(1)}, bf16[4,3,144,3,136]{2,0,1,3,4:T(4,128)(2,1)}, u32[]{:S(2)}) copy-start(bf16[4,3,144,3,136]{2,0,1,3,4:T(4,128)(2,1)} %convert_bitcast_fusion) | copy-start | bytes 4230148
  33.9 1.2 %copy-start.4 = (bf16[136,128,3,2,3]{1,4,3,2,0:T(4,128)(2,1)S(1)}, bf16[136,128,3,2,3]{1,4,3,2,0:T(4,128)(2,1)}, u32[]{:S(2)}) copy-start(bf16[136,128,3,2,3]{1,4,3,2,0:T(4,128)(2,1)} %fusion.34) | copy-start | bytes 1880068
  34.7 1.8 %copy-start.5 = (bf16[256,4,136]{0,2,1:T(8,128)(2,1)}, bf16[256,4,136]{0,2,1:T(8,128)(2,1)S(1)}, u32[]{:S(2)}) copy-start(bf16[256,4,136]{0,2,1:T(8,128)(2,1)S(1)} %get-tuple-element.9) | copy-start | bytes 835588
  34.7 1.1 %copy-start.2 = (bf16[1,256,2,128]{3,2,1,0:T(2,128)(2,1)S(1)}, bf16[1,256,2,128]{3,2,1,0:T(2,128)(2,1)}, u32[]{:S(2)}) copy-start(bf16[1,256,2,128]{3,2,1,0:T(2,128)(2,1)} %param.13) | copy-start | bytes 393220
  36.1 1.8 %collective-permute-start.3 = (f32[384,256]{1,0:T(8,128)S(1)}, f32[384,256]{1,0:T(8,128)S(1)}, u32[]{:S(2)}, u32[]{:S(2)}) collective-permute-start(f32[384,256]{1,0:T(8,128)S(1)} %constant_dynamic-slice_fusion.5), channel_id=1, source_target_pairs={{0,8},{8,0},{16,24},{24,16},{1,9},{9,1},{17,25},{25,17},{2,10},{10... | collective-permute-start | bytes 1179656 | tf_op jit(solution)/shard_map/ppermute | solution.py:31
  37.3 2.1 %collective-permute-start.4 = (f32[384,256]{1,0:T(8,128)}, f32[384,256]{1,0:T(8,128)S(1)}, u32[]{:S(2)}, u32[]{:S(2)}) collective-permute-start(f32[384,256]{1,0:T(8,128)} %constant_dynamic-slice_fusion.4), channel_id=1, source_target_pairs={{0,8},{8,0},{16,24},{24,16},{1,9},{9,1},{17,25},{25,17},{2,10},{10... | collective-permute-start | bytes 1179656 | tf_op jit(solution)/shard_map/ppermute | solution.py:31
  39.5 7.8 %collective-permute-start.5 = (f32[192,256]{1,0:T(8,128)S(1)}, f32[192,256]{1,0:T(8,128)S(1)}, u32[]{:S(2)}, u32[]{:S(2)}) collective-permute-start(f32[192,256]{1,0:T(8,128)S(1)} %constant_dynamic-slice_fusion.3), channel_id=1, source_target_pairs={{0,16},{8,24},{16,0},{24,8},{1,17},{9,25},{17,1},{25,9},{2,18},{10... | collective-permute-start | bytes 589832 | tf_op jit(solution)/shard_map/ppermute | solution.py:31
  41.0 9.9 %collective-permute-start.12 = (f32[192,256]{1,0:T(8,128)S(1)}, f32[192,256]{1,0:T(8,128)S(1)}, u32[]{:S(2)}, u32[]{:S(2)}) collective-permute-start(f32[192,256]{1,0:T(8,128)S(1)} %constant_dynamic-slice_fusion.1), channel_id=1, source_target_pairs={{0,16},{8,24},{16,0},{24,8},{1,17},{9,25},{17,1},{25,9},{2,18},{10... | collective-permute-start | bytes 589832 | tf_op jit(solution)/shard_map/ppermute | solution.py:31
  47.3 30.2 %copy-start.3 = (bf16[3,256,256]{2,1,0:T(8,128)(2,1)S(1)}, bf16[3,256,256]{2,1,0:T(8,128)(2,1)}, u32[]{:S(2)}) copy-start(bf16[3,256,256]{2,1,0:T(8,128)(2,1)} %param.9) | copy-start | bytes 1179652
  47.4 5.2 %collective-permute-start.6 = (f32[96,256]{1,0:T(8,128)S(1)}, f32[96,256]{1,0:T(8,128)S(1)}, u32[]{:S(2)}, u32[]{:S(2)}) collective-permute-start(f32[96,256]{1,0:T(8,128)S(1)} %constant_dynamic-slice_fusion.2), channel_id=1, source_target_pairs={{0,4},{4,0},{1,5},{5,1},{2,6},{6,2},{3,7},{7,3},{8,12},{12,8},{9,1... | collective-permute-start | bytes 294920 | tf_op jit(solution)/shard_map/ppermute | solution.py:31
  51.0 4.7 %collective-permute-start.13 = (f32[96,256]{1,0:T(8,128)S(1)}, f32[96,256]{1,0:T(8,128)S(1)}, u32[]{:S(2)}, u32[]{:S(2)}) collective-permute-start(f32[96,256]{1,0:T(8,128)S(1)} %constant_dynamic-slice_fusion), channel_id=1, source_target_pairs={{0,4},{4,0},{1,5},{5,1},{2,6},{6,2},{3,7},{7,3},{8,12},{12,8},{9,1... | collective-permute-start | bytes 294920 | tf_op jit(solution)/shard_map/ppermute | solution.py:31
  52.6 5.2 %collective-permute-start.7 = (f32[96,256]{1,0:T(8,128)S(1)}, f32[96,256]{1,0:T(8,128)S(1)}, u32[]{:S(2)}, u32[]{:S(2)}) collective-permute-start(f32[96,256]{1,0:T(8,128)S(1)} %dynamic-slice_add_fusion.5), channel_id=1, source_target_pairs={{0,1},{1,0},{2,3},{3,2},{4,5},{5,4},{6,7},{7,6},{8,9},{9,8},{10,11... | collective-permute-start | bytes 294920 | tf_op jit(solution)/shard_map/ppermute | solution.py:37
  55.7 5.7 %collective-permute-start.14 = (f32[96,256]{1,0:T(8,128)S(1)}, f32[96,256]{1,0:T(8,128)S(1)}, u32[]{:S(2)}, u32[]{:S(2)}) collective-permute-start(f32[96,256]{1,0:T(8,128)S(1)} %dynamic-slice_add_fusion.4), channel_id=1, source_target_pairs={{0,1},{1,0},{2,3},{3,2},{4,5},{5,4},{6,7},{7,6},{8,9},{9,8},{10,11... | collective-permute-start | bytes 294920 | tf_op jit(solution)/shard_map/ppermute | solution.py:37
  57.8 9.0 %collective-permute-start.8 = (f32[96,256]{1,0:T(8,128)S(1)}, f32[96,256]{1,0:T(8,128)S(1)}, u32[]{:S(2)}, u32[]{:S(2)}) collective-permute-start(f32[96,256]{1,0:T(8,128)S(1)} %add.182), channel_id=1, source_target_pairs={{0,2},{1,3},{2,0},{3,1},{4,6},{5,7},{6,4},{7,5},{8,10},{9,11},{10,... | collective-permute-start | bytes 294920 | tf_op jit(solution)/shard_map/ppermute | solution.py:37
  61.4 6.5 %collective-permute-start.15 = (f32[96,256]{1,0:T(8,128)S(1)}, f32[96,256]{1,0:T(8,128)S(1)}, u32[]{:S(2)}, u32[]{:S(2)}) collective-permute-start(f32[96,256]{1,0:T(8,128)S(1)} %add.186), channel_id=1, source_target_pairs={{0,2},{1,3},{2,0},{3,1},{4,6},{5,7},{6,4},{7,5},{8,10},{9,11},{10,... | collective-permute-start | bytes 294920 | tf_op jit(solution)/shard_map/ppermute | solution.py:37
  66.9 4.2 %collective-permute-start.9 = (bf16[96,256]{1,0:T(8,128)(2,1)S(1)}, bf16[96,256]{1,0:T(8,128)(2,1)S(1)}, u32[]{:S(2)}, u32[]{:S(2)}) collective-permute-start(bf16[96,256]{1,0:T(8,128)(2,1)S(1)} %add_convert_fusion.1), channel_id=1, source_target_pairs={{0,4},{4,0},{1,5},{5,1},{2,6},{6,2},{3,7},{7,3},{8,12},{12,8},{9,1... | collective-permute-start | bytes 147464 | tf_op jit(solution)/shard_map/ppermute | solution.py:42
  67.9 4.7 %collective-permute-start.16 = (bf16[96,256]{1,0:T(8,128)(2,1)S(1)}, bf16[96,256]{1,0:T(8,128)(2,1)S(1)}, u32[]{:S(2)}, u32[]{:S(2)}) collective-permute-start(bf16[96,256]{1,0:T(8,128)(2,1)S(1)} %add_convert_fusion), channel_id=1, source_target_pairs={{0,4},{4,0},{1,5},{5,1},{2,6},{6,2},{3,7},{7,3},{8,12},{12,8},{9,1... | collective-permute-start | bytes 147464 | tf_op jit(solution)/shard_map/ppermute | solution.py:42
  71.0 4.7 %collective-permute-start.10 = (bf16[192,256]{1,0:T(8,128)(2,1)S(1)}, bf16[192,256]{1,0:T(8,128)(2,1)S(1)}, u32[]{:S(2)}, u32[]{:S(2)}) collective-permute-start(bf16[192,256]{1,0:T(8,128)(2,1)S(1)} %maximum_select_fusion.4), channel_id=1, source_target_pairs={{0,16},{8,24},{16,0},{24,8},{1,17},{9,25},{17,1},{25,9},{2,18},{10... | collective-permute-start | bytes 294920 | tf_op jit(solution)/shard_map/ppermute | solution.py:42
  72.6 4.7 %collective-permute-start.17 = (bf16[192,256]{1,0:T(8,128)(2,1)S(1)}, bf16[192,256]{1,0:T(8,128)(2,1)S(1)}, u32[]{:S(2)}, u32[]{:S(2)}) collective-permute-start(bf16[192,256]{1,0:T(8,128)(2,1)S(1)} %maximum_select_fusion.5), channel_id=1, source_target_pairs={{0,16},{8,24},{16,0},{24,8},{1,17},{9,25},{17,1},{25,9},{2,18},{10... | collective-permute-start | bytes 294920 | tf_op jit(solution)/shard_map/ppermute | solution.py:42
  75.8 3.6 %collective-permute-start.11 = (bf16[384,256]{1,0:T(8,128)(2,1)S(1)}, bf16[384,256]{1,0:T(8,128)(2,1)S(1)}, u32[]{:S(2)}, u32[]{:S(2)}) collective-permute-start(bf16[384,256]{1,0:T(8,128)(2,1)S(1)} %maximum_select_fusion.2), channel_id=1, source_target_pairs={{0,8},{8,0},{16,24},{24,16},{1,9},{9,1},{17,25},{25,17},{2,10},{10... | collective-permute-start | bytes 589832 | tf_op jit(solution)/shard_map/ppermute | solution.py:42
  77.4 3.1 %collective-permute-start.18 = (bf16[384,256]{1,0:T(8,128)(2,1)S(1)}, bf16[384,256]{1,0:T(8,128)(2,1)S(1)}, u32[]{:S(2)}, u32[]{:S(2)}) collective-permute-start(bf16[384,256]{1,0:T(8,128)(2,1)S(1)} %maximum_select_fusion.3), channel_id=1, source_target_pairs={{0,8},{8,0},{16,24},{24,16},{1,9},{9,1},{17,25},{25,17},{2,10},{10... | collective-permute-start | bytes 589832 | tf_op jit(solution)/shard_map/ppermute | solution.py:42

commit v11 on v10

--- a/solution.py
+++ b/solution.py
@@ -36,10 +36,12 @@
         pairs = [(i, i ^ bit) for i in range(lax.axis_size(axis))]
         flat = flat + lax.ppermute(flat, axis, pairs)
     flat = flat.astype(jnp.bfloat16)
-    for axis, bit in reversed(halved):
+    for step, (axis, bit) in enumerate(reversed(halved)):
         pairs = [(i, i ^ bit) for i in range(lax.axis_size(axis))]
         upper = (lax.axis_index(axis) // bit) % 2
         other = lax.ppermute(flat, axis, pairs)
+        if step == len(halved) - 1:
+            flat, other = flat.astype(jnp.float32), other.astype(jnp.float32)
         flat = jnp.where(
             upper == 1, jnp.concatenate([other, flat]), jnp.concatenate([flat, other])
         )

time: 81.9 us -> 81.7 us (level)
    convert_element_type x2 -> x4, other arithmetic: 1.89 us -> 0.21 us  [halving_sum(): flat, other = (flat.astype(jnp.float32), other.astype(jnp.float32))]
    select_n x6 -> x4, other arithmetic: 0.47 us -> 1.92 us  [halving_sum(): jnp.where(upper == 1, jnp.concatenate([other, flat]), jnp.concatenate([fl...]
where the time goes in v11:
time: 81.7 us; the launch traced here: 81.3 us
  waiting for transfers between devices  32.2 us (39%)
  starting transfers between devices  18.2 us (22%)
  matrix products  17.9 us (22%)
  local copies, waits for them, and re-layouts  7.06 us (9%)
  other arithmetic  5.01 us (6%)
  between operations  1.05 us (1%)
    ppermute x4, waiting for transfers between devices, halving_sum(): flat = flat + lax.ppermute(flat, axis, pairs)  9.36 us
    ppermute x6, waiting for transfers between devices, halving_sum(): flat = keep + lax.ppermute(send, axis, pairs)  8.21 us
    dot_general x3, matrix products, band_of(): jnp.einsum('kiad,dpq->iapkq', stencil, lon_picker(col_count, first_source...  7.43 us
    ppermute x1, waiting for transfers between devices, lat_halo(): other = lax.ppermute(block, 'lat', [(0, 1), (1, 0)])  5.85 us
    ppermute x6, starting transfers between devices, halving_sum(): flat = keep + lax.ppermute(send, axis, pairs)  5.85 us
    unnamed x16, local copies, waits for them, and re-layouts  5.71 us
    ppermute x6, waiting for transfers between devices, halving_sum(): other = lax.ppermute(flat, axis, pairs)  5.48 us
    ppermute x1, starting transfers between devices, lon_halo(): lax.ppermute(block[..., :width], 'lon', [(i, (i - 1) % count) for i in ra...  5.13 us
  transfers between devices with their start and end apart: 19, of which 14 were waited for; matrix products, arithmetic and copies ran while one was open for 16% of the time, Pallas kernels for 0%

profile of v11, /device:TPU:0, one launch (start us, length us, event | category | flops | bytes accessed | tf_op | source)
XLA Modules:
  0.0 81.3 jit_solution(1352537662338272467)
XLA Ops:
  0.6 1.1 %copy.26 = bf16[1,256,2,128]{1,3,2,0:T(8,128)(2,1)S(1)} copy(bf16[1,256,2,128]{3,2,1,0:T(2,128)(2,1)} %param.13) | data formatting | bytes 262144 | tf_op args[6]
  1.7 1.0 %copy.25 = bf16[1,256,2,128]{1,3,2,0:T(8,128)(2,1)S(1)} copy(bf16[1,256,2,128]{3,2,1,0:T(2,128)(2,1)} %param.7) | data formatting | bytes 262144 | tf_op args[0]
  2.8 5.1 %collective-permute-start.1 = (bf16[512,2,8]{0,2,1:T(8,128)(2,1)S(1)}, bf16[512,2,8]{0,2,1:T(8,128)(2,1)S(1)}, u32[]{:S(2)}, u32[]{:S(2)}) collective-permute-start(bf16[512,2,8]{0,2,1:T(8,128)(2,1)S(1)} %get-tuple-element.39), channel_id=1, source_target_pairs={{0,3},{1,0},{2,1},{3,2},{4,7},{5,4},{6,5},{7,6},{8,11},{9,8},{10,9... | collective-permute-start | bytes 49160 | tf_op jit(solution)/shard_map/ppermute | solution.py:76
  7.9 0.1 fusion.42
  8.0 0.7 broadcast_add_fusion
  8.7 0.9 %convolution_convert_fusion.2 = bf16[3,2,3,9]{3,2,1,0:T(4,128)(2,1)S(1)} fusion(s32[2,3,12]{2,0,1:T(2,128)S(1)} %get-tuple-element.40, f32[2,3,12]{2,0,1:T(2,128)} %param.10, s32[2,3,12]{2,0,1:T(2,128)S(1)} %get-tuple-element.41), kind=kOutput, calls=%fused_computation.38 | convolution fusion | flops 24570 | bytes 1188 | tf_op jit(solution)/shard_map/rks,rksa,rksd->krad/dot_general | solution.py:85
  9.6 0.1 reshape.71
  9.7 0.2 fusion.29
  10.0 0.1 copy.28
  10.1 3.3 %collective-permute-done = bf16[512,2,8]{0,2,1:T(8,128)(2,1)S(1)} collective-permute-done((bf16[512,2,8]{0,2,1:T(8,128)(2,1)S(1)}, bf16[512,2,8]{0,2,1:T(8,128)(2,1)S(1)}, u32[]{:S(2)}, u32[]{:S(2)}) %collective-permute-start) | collective-permute-done | bytes 16416 | tf_op jit(solution)/shard_map/ppermute | solution.py:75
  13.5 1.6 %collective-permute-start.2 = (bf16[513,2,144]{0,2,1:T(8,128)(2,1)S(1)}, bf16[513,2,144]{0,2,1:T(8,128)(2,1)S(1)}, u32[]{:S(2)}, u32[]{:S(2)}) collective-permute-start(bf16[513,2,144]{0,2,1:T(8,128)(2,1)S(1)} %pad_maximum_fusion), channel_id=1, source_target_pairs={{0,4},{4,0},{1,5},{5,1},{2,6},{6,2},{3,7},{7,3},{8,12},{12,8},{9,1... | collective-permute-start | bytes 886472 | tf_op jit(solution)/shard_map/ppermute | solution.py:55
  15.1 1.5 %fusion.34 = bf16[136,128,3,2,3]{1,4,3,2,0:T(4,128)(2,1)} fusion(pred[9,136,128,1,1]{2,1,0,3,4:T(8,128)(4,1)S(1)} %fusion.42, bf16[3,2,3,9]{3,2,1,0:T(4,128)(2,1)S(1)} %convolution_convert_fusion.2), kind=kOutput, calls=%fused_computation.36 | convolution fusion | flops 5640192 | bytes 783684 | tf_op jit(solution)/shard_map/kiad,dpq->iapkq/dot_general | solution.py:104
  16.6 5.8 %collective-permute-done.2 = bf16[513,2,144]{0,2,1:T(8,128)(2,1)S(1)} collective-permute-done((bf16[513,2,144]{0,2,1:T(8,128)(2,1)S(1)}, bf16[513,2,144]{0,2,1:T(8,128)(2,1)S(1)}, u32[]{:S(2)}, u32[]{:S(2)}) %collective-permute-start.2) | collective-permute-done | bytes 295520 | tf_op jit(solution)/shard_map/ppermute | solution.py:55
  22.5 0.2 maximum_reduce_fusion
  22.6 0.1 reshape_squeeze.3
  22.8 3.0 %convert_bitcast_fusion = bf16[4,3,144,3,136]{2,0,1,3,4:T(4,128)(2,1)} fusion(bf16[3,6,3,9]{3,1,2,0:T(8,128)(2,1)S(1)} %bitcast.203), kind=kOutput, calls=%fused_computation.8 | convolution fusion | flops 13747968 | bytes 1419264 | tf_op jit(solution)/shard_map/kiad,dpq->iapkq/dot_general | solution.py:104
  25.7 2.9 %fusion.10 = bf16[136,144,3,4,3]{1,3,4,2,0:T(4,128)(2,1)} fusion(pred[9,136,144,1,1]{2,1,0,3,4:T(8,128)(4,1)S(1)} %fusion.29, bf16[3,6,3,9]{3,1,2,0:T(8,128)(2,1)S(1)} %bitcast.204, pred[]{:T(512)S(6)} %eq.72), kind=kOutput, calls=%fused_computation.12 | convolution fusion | flops 12690756 | bytes 1587277 | tf_op jit(solution)/shard_map/kiad,dpq->iapkq/dot_general | solution.py:104
  28.7 2.7 %fusion.19 = f32[256,4,3,136]{0,3,1,2:T(8,128)S(1)} fusion(bf16[3,256,256]{2,1,0:T(8,128)(2,1)} %param.9, bf16[513,2,144]{0,2,1:T(8,128)(2,1)S(1)} %get-tuple-element.31, bf16[1,2,144]{0,2,1:T(8,128)(2,1)S(1)} %copy.28, bf16[512,2,8]{0,2,1:T(8,128)(2,1)S(1)} %collective-permute-done.1, bf16[512,2,8]{0,2,1:T(8,128)(2,1)S(1)} %collective-permute-done, ...), kind=kOutput, calls=%fused_computation.16 | convolution fusion | flops 591593472 | bytes 4360897 | tf_op jit(solution)/shard_map/cikq,iapkq->ciap/dot_general | solution.py:137
  31.4 0.1 fusion.56
  31.6 0.1 maximum_bitcast_fusion.4
  31.7 1.5 %copy-done.1 = bf16[4,3,144,3,136]{2,0,1,3,4:T(4,128)(2,1)S(1)} copy-done((bf16[4,3,144,3,136]{2,0,1,3,4:T(4,128)(2,1)S(1)}, bf16[4,3,144,3,136]{2,0,1,3,4:T(4,128)(2,1)}, u32[]{:S(2)}) %copy-start.1) | copy-done | bytes 1410072
  33.1 0.8 fusion.24
  33.9 0.8 fusion.46
  34.8 0.3 copy-done.4
  35.1 0.4 fusion.31
  35.5 0.3 copy-done.2
  35.8 0.3 fusion.27
  36.1 0.1 collective-permute-start.3
  36.2 0.3 fusion.28
  36.5 0.8 constant_dynamic-slice_fusion.4
  37.3 0.5 collective-permute-start.4
  37.8 0.1 collective-permute-done.3
  38.0 1.4 %collective-permute-done.4 = f32[384,256]{1,0:T(8,128)S(1)} collective-permute-done((f32[384,256]{1,0:T(8,128)}, f32[384,256]{1,0:T(8,128)S(1)}, u32[]{:S(2)}, u32[]{:S(2)}) %collective-permute-start.4) | collective-permute-done | bytes 393248 | tf_op jit(solution)/shard_map/ppermute | solution.py:31
  39.5 1.5 %collective-permute-start.5 = (f32[192,256]{1,0:T(8,128)S(1)}, f32[192,256]{1,0:T(8,128)S(1)}, u32[]{:S(2)}, u32[]{:S(2)}) collective-permute-start(f32[192,256]{1,0:T(8,128)S(1)} %constant_dynamic-slice_fusion.3), channel_id=1, source_target_pairs={{0,16},{8,24},{16,0},{24,8},{1,17},{9,25},{17,1},{25,9},{2,18},{10... | collective-permute-start | bytes 589832 | tf_op jit(solution)/shard_map/ppermute | solution.py:31
  41.0 0.6 collective-permute-start.12
  41.6 4.0 %fusion.14 = f32[256,4,3,144]{0,3,2,1:T(8,128)} fusion(bf16[4,3,144,3,136]{2,0,1,3,4:T(4,128)(2,1)} %convert_bitcast_fusion, bf16[3,256,256]{2,1,0:T(8,128)(2,1)S(1)} %copy-done, bf16[256,4,136]{0,2,1:T(8,128)(2,1)} %copy-done.5), kind=kOutput, calls=%fused_computation.15 | convolution fusion | flops 575299584 | bytes 3851264 | tf_op jit(solution)/shard_map/cikq,iapkq->ciap/dot_general | solution.py:124
  45.6 1.7 %collective-permute-done.5 = f32[192,256]{1,0:T(8,128)S(1)} collective-permute-done((f32[192,256]{1,0:T(8,128)S(1)}, f32[192,256]{1,0:T(8,128)S(1)}, u32[]{:S(2)}, u32[]{:S(2)}) %collective-permute-start.5) | collective-permute-done | bytes 196640 | tf_op jit(solution)/shard_map/ppermute | solution.py:31
  47.4 1.6 %collective-permute-start.6 = (f32[96,256]{1,0:T(8,128)S(1)}, f32[96,256]{1,0:T(8,128)S(1)}, u32[]{:S(2)}, u32[]{:S(2)}) collective-permute-start(f32[96,256]{1,0:T(8,128)S(1)} %constant_dynamic-slice_fusion.2), channel_id=1, source_target_pairs={{0,4},{4,0},{1,5},{5,1},{2,6},{6,2},{3,7},{7,3},{8,12},{12,8},{9,1... | collective-permute-start | bytes 294920 | tf_op jit(solution)/shard_map/ppermute | solution.py:31
  48.9 2.0 %collective-permute-done.12 = f32[192,256]{1,0:T(8,128)S(1)} collective-permute-done((f32[192,256]{1,0:T(8,128)S(1)}, f32[192,256]{1,0:T(8,128)S(1)}, u32[]{:S(2)}, u32[]{:S(2)}) %collective-permute-start.12) | collective-permute-done | bytes 196640 | tf_op jit(solution)/shard_map/ppermute | solution.py:31
  51.0 1.6 %collective-permute-start.13 = (f32[96,256]{1,0:T(8,128)S(1)}, f32[96,256]{1,0:T(8,128)S(1)}, u32[]{:S(2)}, u32[]{:S(2)}) collective-permute-start(f32[96,256]{1,0:T(8,128)S(1)} %constant_dynamic-slice_fusion), channel_id=1, source_target_pairs={{0,4},{4,0},{1,5},{5,1},{2,6},{6,2},{3,7},{7,3},{8,12},{12,8},{9,1... | collective-permute-start | bytes 294920 | tf_op jit(solution)/shard_map/ppermute | solution.py:31
  52.6 0.1 collective-permute-start.7
  52.7 3.0 %collective-permute-done.13 = f32[96,256]{1,0:T(8,128)S(1)} collective-permute-done((f32[96,256]{1,0:T(8,128)S(1)}, f32[96,256]{1,0:T(8,128)S(1)}, u32[]{:S(2)}, u32[]{:S(2)}) %collective-permute-start.13) | collective-permute-done | bytes 98336 | tf_op jit(solution)/shard_map/ppermute | solution.py:31
  55.7 0.1 collective-permute-start.14
  55.8 2.0 %collective-permute-done.7 = f32[96,256]{1,0:T(8,128)S(1)} collective-permute-done((f32[96,256]{1,0:T(8,128)S(1)}, f32[96,256]{1,0:T(8,128)S(1)}, u32[]{:S(2)}, u32[]{:S(2)}) %collective-permute-start.7) | collective-permute-done | bytes 98336 | tf_op jit(solution)/shard_map/ppermute | solution.py:37
  57.9 1.2 %fusion.79 = bf16[1,256,2,128]{1,3,2,0:T(8,128)(2,1)S(1)} fusion(f32[256,4,3,144]{0,3,2,1:T(8,128)} %fusion.14), kind=kLoop, calls=%fused_computation.119 | loop fusion | flops 196608 | bytes 917504 | tf_op jit(solution)/shard_map/convert_element_type | solution.py:223
  59.0 2.3 %collective-permute-done.14 = f32[96,256]{1,0:T(8,128)S(1)} collective-permute-done((f32[96,256]{1,0:T(8,128)S(1)}, f32[96,256]{1,0:T(8,128)S(1)}, u32[]{:S(2)}, u32[]{:S(2)}) %collective-permute-start.14) | collective-permute-done | bytes 98336 | tf_op jit(solution)/shard_map/ppermute | solution.py:37
  61.4 0.7 collective-permute-start.15
  62.1 4.8 %collective-permute-done.8 = f32[96,256]{1,0:T(8,128)S(1)} collective-permute-done((f32[96,256]{1,0:T(8,128)S(1)}, f32[96,256]{1,0:T(8,128)S(1)}, u32[]{:S(2)}, u32[]{:S(2)}) %collective-permute-start.8) | collective-permute-done | bytes 98336 | tf_op jit(solution)/shard_map/ppermute | solution.py:37
  66.9 0.8 %collective-permute-start.9 = (bf16[96,256]{1,0:T(8,128)(2,1)S(1)}, bf16[96,256]{1,0:T(8,128)(2,1)S(1)}, u32[]{:S(2)}, u32[]{:S(2)}) collective-permute-start(bf16[96,256]{1,0:T(8,128)(2,1)S(1)} %add_convert_fusion.1), channel_id=1, source_target_pairs={{0,4},{4,0},{1,5},{5,1},{2,6},{6,2},{3,7},{7,3},{8,12},{12,8},{9,1... | collective-permute-start | bytes 147464 | tf_op jit(solution)/shard_map/ppermute | solution.py:42
  67.7 0.2 collective-permute-done.15
  67.9 1.1 %collective-permute-start.16 = (bf16[96,256]{1,0:T(8,128)(2,1)S(1)}, bf16[96,256]{1,0:T(8,128)(2,1)S(1)}, u32[]{:S(2)}, u32[]{:S(2)}) collective-permute-start(bf16[96,256]{1,0:T(8,128)(2,1)S(1)} %add_convert_fusion), channel_id=1, source_target_pairs={{0,4},{4,0},{1,5},{5,1},{2,6},{6,2},{3,7},{7,3},{8,12},{12,8},{9,1... | collective-permute-start | bytes 147464 | tf_op jit(solution)/shard_map/ppermute | solution.py:42
  69.1 2.0 %collective-permute-done.9 = bf16[96,256]{1,0:T(8,128)(2,1)S(1)} collective-permute-done((bf16[96,256]{1,0:T(8,128)(2,1)S(1)}, bf16[96,256]{1,0:T(8,128)(2,1)S(1)}, u32[]{:S(2)}, u32[]{:S(2)}) %collective-permute-start.9) | collective-permute-done | bytes 49184 | tf_op jit(solution)/shard_map/ppermute | solution.py:42
  71.1 1.6 %collective-permute-start.10 = (bf16[192,256]{1,0:T(8,128)(2,1)S(1)}, bf16[192,256]{1,0:T(8,128)(2,1)S(1)}, u32[]{:S(2)}, u32[]{:S(2)}) collective-permute-start(bf16[192,256]{1,0:T(8,128)(2,1)S(1)} %maximum_select_fusion.4), channel_id=1, source_target_pairs={{0,16},{8,24},{16,0},{24,8},{1,17},{9,25},{17,1},{25,9},{2,18},{10... | collective-permute-start | bytes 294920 | tf_op jit(solution)/shard_map/ppermute | solution.py:42
  72.7 1.0 %collective-permute-start.17 = (bf16[192,256]{1,0:T(8,128)(2,1)S(1)}, bf16[192,256]{1,0:T(8,128)(2,1)S(1)}, u32[]{:S(2)}, u32[]{:S(2)}) collective-permute-start(bf16[192,256]{1,0:T(8,128)(2,1)S(1)} %maximum_select_fusion.5), channel_id=1, source_target_pairs={{0,16},{8,24},{16,0},{24,8},{1,17},{9,25},{17,1},{25,9},{2,18},{10... | collective-permute-start | bytes 294920 | tf_op jit(solution)/shard_map/ppermute | solution.py:42
  73.7 2.1 %collective-permute-done.10 = bf16[192,256]{1,0:T(8,128)(2,1)S(1)} collective-permute-done((bf16[192,256]{1,0:T(8,128)(2,1)S(1)}, bf16[192,256]{1,0:T(8,128)(2,1)S(1)}, u32[]{:S(2)}, u32[]{:S(2)}) %collective-permute-start.10) | collective-permute-done | bytes 98336 | tf_op jit(solution)/shard_map/ppermute | solution.py:42
  75.8 0.1 fusion.97
  75.8 0.1 collective-permute-start.11
  75.9 1.4 %collective-permute-done.17 = bf16[192,256]{1,0:T(8,128)(2,1)S(1)} collective-permute-done((bf16[192,256]{1,0:T(8,128)(2,1)S(1)}, bf16[192,256]{1,0:T(8,128)(2,1)S(1)}, u32[]{:S(2)}, u32[]{:S(2)}) %collective-permute-start.17) | collective-permute-done | bytes 98336 | tf_op jit(solution)/shard_map/ppermute | solution.py:42
  77.4 0.1 fusion.96
  77.5 0.3 fusion.33
  77.8 0.8 copy.40
  78.6 0.8 copy.41
  79.4 0.9 %maximum_select_fusion = f32[768,256]{1,0:T(8,128)} fusion(f32[384,256]{1,0:T(8,128)S(1)} %get-tuple-element.22, f32[384,256]{1,0:T(8,128)S(1)} %convert_element_type.134, pred[]{:T(512)S(6)} %eq.74), kind=kLoop, calls=%fused_computation.46 | loop fusion | flops 589824 | bytes 1572865 | tf_op jit(solution)/shard_map/jit(_where)/select_n | solution.py:45
  80.4 0.9 %maximum_select_fusion.1 = f32[768,256]{1,0:T(8,128)} fusion(f32[384,256]{1,0:T(8,128)S(1)} %get-tuple-element.20, f32[384,256]{1,0:T(8,128)S(1)} %convert_element_type.137, pred[]{:T(512)S(6)} %eq.74), kind=kLoop, calls=%fused_computation.47 | loop fusion | flops 589824 | bytes 1572865 | tf_op jit(solution)/shard_map/jit(_where)/select_n | solution.py:45
  (47 shorter events, 0.9 us)
Async XLA Ops:
  0.6 33.3 %copy-start = (bf16[3,256,256]{2,1,0:T(8,128)(2,1)S(1)}, bf16[3,256,256]{2,1,0:T(8,128)(2,1)}, u32[]{:S(2)}) copy-start(bf16[3,256,256]{2,1,0:T(8,128)(2,1)} %param.8) | copy-start | bytes 1179652
  2.8 7.4 %collective-permute-start.1 = (bf16[512,2,8]{0,2,1:T(8,128)(2,1)S(1)}, bf16[512,2,8]{0,2,1:T(8,128)(2,1)S(1)}, u32[]{:S(2)}, u32[]{:S(2)}) collective-permute-start(bf16[512,2,8]{0,2,1:T(8,128)(2,1)S(1)} %get-tuple-element.39), channel_id=1, source_target_pairs={{0,3},{1,0},{2,1},{3,2},{4,7},{5,4},{6,5},{7,6},{8,11},{9,8},{10,9... | collective-permute-start | bytes 49160 | tf_op jit(solution)/shard_map/ppermute | solution.py:76
  7.9 5.5 %collective-permute-start = (bf16[512,2,8]{0,2,1:T(8,128)(2,1)S(1)}, bf16[512,2,8]{0,2,1:T(8,128)(2,1)S(1)}, u32[]{:S(2)}, u32[]{:S(2)}) collective-permute-start(bf16[512,2,8]{0,2,1:T(8,128)(2,1)S(1)} %get-tuple-element.38), channel_id=1, source_target_pairs={{0,1},{1,2},{2,3},{3,0},{4,5},{5,6},{6,7},{7,4},{8,9},{9,10},{10,1... | collective-permute-start | bytes 49160 | tf_op jit(solution)/shard_map/ppermute | solution.py:75
  13.5 9.0 %collective-permute-start.2 = (bf16[513,2,144]{0,2,1:T(8,128)(2,1)S(1)}, bf16[513,2,144]{0,2,1:T(8,128)(2,1)S(1)}, u32[]{:S(2)}, u32[]{:S(2)}) collective-permute-start(bf16[513,2,144]{0,2,1:T(8,128)(2,1)S(1)} %pad_maximum_fusion), channel_id=1, source_target_pairs={{0,4},{4,0},{1,5},{5,1},{2,6},{6,2},{3,7},{7,3},{8,12},{12,8},{9,1... | collective-permute-start | bytes 886472 | tf_op jit(solution)/shard_map/ppermute | solution.py:55
  31.4 1.7 %copy-start.1 = (bf16[4,3,144,3,136]{2,0,1,3,4:T(4,128)(2,1)S(1)}, bf16[4,3,144,3,136]{2,0,1,3,4:T(4,128)(2,1)}, u32[]{:S(2)}) copy-start(bf16[4,3,144,3,136]{2,0,1,3,4:T(4,128)(2,1)} %convert_bitcast_fusion) | copy-start | bytes 4230148
  33.9 1.2 %copy-start.4 = (bf16[136,128,3,2,3]{1,4,3,2,0:T(4,128)(2,1)S(1)}, bf16[136,128,3,2,3]{1,4,3,2,0:T(4,128)(2,1)}, u32[]{:S(2)}) copy-start(bf16[136,128,3,2,3]{1,4,3,2,0:T(4,128)(2,1)} %fusion.34) | copy-start | bytes 1880068
  34.7 1.8 %copy-start.5 = (bf16[256,4,136]{0,2,1:T(8,128)(2,1)}, bf16[256,4,136]{0,2,1:T(8,128)(2,1)S(1)}, u32[]{:S(2)}) copy-start(bf16[256,4,136]{0,2,1:T(8,128)(2,1)S(1)} %get-tuple-element.9) | copy-start | bytes 835588
  34.7 1.1 %copy-start.2 = (bf16[1,256,2,128]{3,2,1,0:T(2,128)(2,1)S(1)}, bf16[1,256,2,128]{3,2,1,0:T(2,128)(2,1)}, u32[]{:S(2)}) copy-start(bf16[1,256,2,128]{3,2,1,0:T(2,128)(2,1)} %param.13) | copy-start | bytes 393220
  36.1 1.8 %collective-permute-start.3 = (f32[384,256]{1,0:T(8,128)S(1)}, f32[384,256]{1,0:T(8,128)S(1)}, u32[]{:S(2)}, u32[]{:S(2)}) collective-permute-start(f32[384,256]{1,0:T(8,128)S(1)} %constant_dynamic-slice_fusion.5), channel_id=1, source_target_pairs={{0,8},{8,0},{16,24},{24,16},{1,9},{9,1},{17,25},{25,17},{2,10},{10... | collective-permute-start | bytes 1179656 | tf_op jit(solution)/shard_map/ppermute | solution.py:31
  37.3 2.1 %collective-permute-start.4 = (f32[384,256]{1,0:T(8,128)}, f32[384,256]{1,0:T(8,128)S(1)}, u32[]{:S(2)}, u32[]{:S(2)}) collective-permute-start(f32[384,256]{1,0:T(8,128)} %constant_dynamic-slice_fusion.4), channel_id=1, source_target_pairs={{0,8},{8,0},{16,24},{24,16},{1,9},{9,1},{17,25},{25,17},{2,10},{10... | collective-permute-start | bytes 1179656 | tf_op jit(solution)/shard_map/ppermute | solution.py:31
  39.5 7.8 %collective-permute-start.5 = (f32[192,256]{1,0:T(8,128)S(1)}, f32[192,256]{1,0:T(8,128)S(1)}, u32[]{:S(2)}, u32[]{:S(2)}) collective-permute-start(f32[192,256]{1,0:T(8,128)S(1)} %constant_dynamic-slice_fusion.3), channel_id=1, source_target_pairs={{0,16},{8,24},{16,0},{24,8},{1,17},{9,25},{17,1},{25,9},{2,18},{10... | collective-permute-start | bytes 589832 | tf_op jit(solution)/shard_map/ppermute | solution.py:31
  41.0 9.9 %collective-permute-start.12 = (f32[192,256]{1,0:T(8,128)S(1)}, f32[192,256]{1,0:T(8,128)S(1)}, u32[]{:S(2)}, u32[]{:S(2)}) collective-permute-start(f32[192,256]{1,0:T(8,128)S(1)} %constant_dynamic-slice_fusion.1), channel_id=1, source_target_pairs={{0,16},{8,24},{16,0},{24,8},{1,17},{9,25},{17,1},{25,9},{2,18},{10... | collective-permute-start | bytes 589832 | tf_op jit(solution)/shard_map/ppermute | solution.py:31
  47.4 5.2 %collective-permute-start.6 = (f32[96,256]{1,0:T(8,128)S(1)}, f32[96,256]{1,0:T(8,128)S(1)}, u32[]{:S(2)}, u32[]{:S(2)}) collective-permute-start(f32[96,256]{1,0:T(8,128)S(1)} %constant_dynamic-slice_fusion.2), channel_id=1, source_target_pairs={{0,4},{4,0},{1,5},{5,1},{2,6},{6,2},{3,7},{7,3},{8,12},{12,8},{9,1... | collective-permute-start | bytes 294920 | tf_op jit(solution)/shard_map/ppermute | solution.py:31
  51.0 26.6 %copy-start.3 = (bf16[3,256,256]{2,1,0:T(8,128)(2,1)S(1)}, bf16[3,256,256]{2,1,0:T(8,128)(2,1)}, u32[]{:S(2)}) copy-start(bf16[3,256,256]{2,1,0:T(8,128)(2,1)} %param.9) | copy-start | bytes 1179652
  51.0 4.7 %collective-permute-start.13 = (f32[96,256]{1,0:T(8,128)S(1)}, f32[96,256]{1,0:T(8,128)S(1)}, u32[]{:S(2)}, u32[]{:S(2)}) collective-permute-start(f32[96,256]{1,0:T(8,128)S(1)} %constant_dynamic-slice_fusion), channel_id=1, source_target_pairs={{0,4},{4,0},{1,5},{5,1},{2,6},{6,2},{3,7},{7,3},{8,12},{12,8},{9,1... | collective-permute-start | bytes 294920 | tf_op jit(solution)/shard_map/ppermute | solution.py:31
  52.6 5.2 %collective-permute-start.7 = (f32[96,256]{1,0:T(8,128)S(1)}, f32[96,256]{1,0:T(8,128)S(1)}, u32[]{:S(2)}, u32[]{:S(2)}) collective-permute-start(f32[96,256]{1,0:T(8,128)S(1)} %dynamic-slice_add_fusion.5), channel_id=1, source_target_pairs={{0,1},{1,0},{2,3},{3,2},{4,5},{5,4},{6,7},{7,6},{8,9},{9,8},{10,11... | collective-permute-start | bytes 294920 | tf_op jit(solution)/shard_map/ppermute | solution.py:37
  55.7 5.7 %collective-permute-start.14 = (f32[96,256]{1,0:T(8,128)S(1)}, f32[96,256]{1,0:T(8,128)S(1)}, u32[]{:S(2)}, u32[]{:S(2)}) collective-permute-start(f32[96,256]{1,0:T(8,128)S(1)} %dynamic-slice_add_fusion.4), channel_id=1, source_target_pairs={{0,1},{1,0},{2,3},{3,2},{4,5},{5,4},{6,7},{7,6},{8,9},{9,8},{10,11... | collective-permute-start | bytes 294920 | tf_op jit(solution)/shard_map/ppermute | solution.py:37
  57.8 9.1 %collective-permute-start.8 = (f32[96,256]{1,0:T(8,128)S(1)}, f32[96,256]{1,0:T(8,128)S(1)}, u32[]{:S(2)}, u32[]{:S(2)}) collective-permute-start(f32[96,256]{1,0:T(8,128)S(1)} %add.182), channel_id=1, source_target_pairs={{0,2},{1,3},{2,0},{3,1},{4,6},{5,7},{6,4},{7,5},{8,10},{9,11},{10,... | collective-permute-start | bytes 294920 | tf_op jit(solution)/shard_map/ppermute | solution.py:37
  61.4 6.5 %collective-permute-start.15 = (f32[96,256]{1,0:T(8,128)S(1)}, f32[96,256]{1,0:T(8,128)S(1)}, u32[]{:S(2)}, u32[]{:S(2)}) collective-permute-start(f32[96,256]{1,0:T(8,128)S(1)} %add.186), channel_id=1, source_target_pairs={{0,2},{1,3},{2,0},{3,1},{4,6},{5,7},{6,4},{7,5},{8,10},{9,11},{10,... | collective-permute-start | bytes 294920 | tf_op jit(solution)/shard_map/ppermute | solution.py:37
  66.9 4.2 %collective-permute-start.9 = (bf16[96,256]{1,0:T(8,128)(2,1)S(1)}, bf16[96,256]{1,0:T(8,128)(2,1)S(1)}, u32[]{:S(2)}, u32[]{:S(2)}) collective-permute-start(bf16[96,256]{1,0:T(8,128)(2,1)S(1)} %add_convert_fusion.1), channel_id=1, source_target_pairs={{0,4},{4,0},{1,5},{5,1},{2,6},{6,2},{3,7},{7,3},{8,12},{12,8},{9,1... | collective-permute-start | bytes 147464 | tf_op jit(solution)/shard_map/ppermute | solution.py:42
  67.9 4.7 %collective-permute-start.16 = (bf16[96,256]{1,0:T(8,128)(2,1)S(1)}, bf16[96,256]{1,0:T(8,128)(2,1)S(1)}, u32[]{:S(2)}, u32[]{:S(2)}) collective-permute-start(bf16[96,256]{1,0:T(8,128)(2,1)S(1)} %add_convert_fusion), channel_id=1, source_target_pairs={{0,4},{4,0},{1,5},{5,1},{2,6},{6,2},{3,7},{7,3},{8,12},{12,8},{9,1... | collective-permute-start | bytes 147464 | tf_op jit(solution)/shard_map/ppermute | solution.py:42
  71.1 4.7 %collective-permute-start.10 = (bf16[192,256]{1,0:T(8,128)(2,1)S(1)}, bf16[192,256]{1,0:T(8,128)(2,1)S(1)}, u32[]{:S(2)}, u32[]{:S(2)}) collective-permute-start(bf16[192,256]{1,0:T(8,128)(2,1)S(1)} %maximum_select_fusion.4), channel_id=1, source_target_pairs={{0,16},{8,24},{16,0},{24,8},{1,17},{9,25},{17,1},{25,9},{2,18},{10... | collective-permute-start | bytes 294920 | tf_op jit(solution)/shard_map/ppermute | solution.py:42
  72.7 4.7 %collective-permute-start.17 = (bf16[192,256]{1,0:T(8,128)(2,1)S(1)}, bf16[192,256]{1,0:T(8,128)(2,1)S(1)}, u32[]{:S(2)}, u32[]{:S(2)}) collective-permute-start(bf16[192,256]{1,0:T(8,128)(2,1)S(1)} %maximum_select_fusion.5), channel_id=1, source_target_pairs={{0,16},{8,24},{16,0},{24,8},{1,17},{9,25},{17,1},{25,9},{2,18},{10... | collective-permute-start | bytes 294920 | tf_op jit(solution)/shard_map/ppermute | solution.py:42
  75.8 3.6 %collective-permute-start.11 = (bf16[384,256]{1,0:T(8,128)(2,1)S(1)}, bf16[384,256]{1,0:T(8,128)(2,1)S(1)}, u32[]{:S(2)}, u32[]{:S(2)}) collective-permute-start(bf16[384,256]{1,0:T(8,128)(2,1)S(1)} %get-tuple-element.23), channel_id=1, source_target_pairs={{0,8},{8,0},{16,24},{24,16},{1,9},{9,1},{17,25},{25,17},{2,10},{10... | collective-permute-start | bytes 589832 | tf_op jit(solution)/shard_map/ppermute | solution.py:42
  77.4 2.9 %collective-permute-start.18 = (bf16[384,256]{1,0:T(8,128)(2,1)S(1)}, bf16[384,256]{1,0:T(8,128)(2,1)S(1)}, u32[]{:S(2)}, u32[]{:S(2)}) collective-permute-start(bf16[384,256]{1,0:T(8,128)(2,1)S(1)} %get-tuple-element.21), channel_id=1, source_target_pairs={{0,8},{8,0},{16,24},{24,16},{1,9},{9,1},{17,25},{25,17},{2,10},{10... | collective-permute-start | bytes 589832 | tf_op jit(solution)/shard_map/ppermute | solution.py:42

commit v12 on v11

--- a/solution.py
+++ b/solution.py
@@ -163,16 +163,10 @@
     stencil = coefficients(quadrature, lat_offsets, lon_offsets)
     basis_count = stencil.shape[0]
 
+    stencil_wide = lat_halo(stencil, 1, LAT_HALO)
     packed = lon_halo(jnp.concatenate([source, gradient], axis=0), LON_HALO)
-    taps_per_row = stencil.size // row_count
-    stencil_rows = jnp.transpose(stencil, (1, 0, 2, 3)).reshape(row_count, taps_per_row)
-    stencil_rows = jnp.pad(stencil_rows, ((0, 0), (0, packed.shape[2] - taps_per_row)))
-    framed = lat_halo(jnp.concatenate([packed, stencil_rows[None]], axis=0), 1, LAT_HALO)
-    source_wide, gradient_wide = framed[:channels], framed[channels : 2 * channels]
-    stencil_wide = framed[2 * channels, :, :taps_per_row].reshape(
-        row_count + 2 * LAT_HALO, stencil.shape[0], stencil.shape[2], stencil.shape[3]
-    )
-    stencil_wide = jnp.transpose(stencil_wide, (1, 0, 2, 3))
+    framed = lat_halo(packed, 1, LAT_HALO)
+    source_wide, gradient_wide = framed[:channels], framed[channels:]
 
     total_rows = row_count * lax.axis_size("lat")
     first_row = lax.axis_index("lat") * row_count

time: 81.7 us -> 83.3 us (1.020)
  waiting for transfers between devices: 32.2 us -> 22.9 us
  starting transfers between devices: 18.2 us -> 23.1 us
  matrix products: 17.9 us -> 20.9 us
  other arithmetic: 5.01 us -> 7.06 us
    ppermute x4, waiting for transfers between devices: 9.36 us -> 5.05 us  [halving_sum(): flat = flat + lax.ppermute(flat, axis, pairs)]
    ppermute x4, starting transfers between devices: 0.88 us -> 4.84 us  [halving_sum(): flat = flat + lax.ppermute(flat, axis, pairs)]
    ppermute x1, waiting for transfers between devices: 3.28 us -> 0.01 us  [lon_halo(): lax.ppermute(block[..., cols - width:], 'lon', [(i, (i + 1) % count) for...]
    dot_general x1, matrix products: 2.7 us -> 5.14 us  [spread_adjoint_rows(): jnp.einsum('cikq,iapkq->ciap', mixed, band, preferred_element_type=jnp.fl...]
    ppermute x1 -> x2, waiting for transfers between devices: 5.85 us -> 3.71 us  [lat_halo(): other = lax.ppermute(block, 'lat', [(0, 1), (1, 0)])]
    ppermute x1 -> x2, starting transfers between devices: 1.58 us -> 3.17 us  [lat_halo(): other = lax.ppermute(block, 'lat', [(0, 1), (1, 0)])]
    ppermute x6, waiting for transfers between devices: 8.21 us -> 9.73 us  [halving_sum(): flat = keep + lax.ppermute(send, axis, pairs)]
    ppermute x6, starting transfers between devices: 5.85 us -> 4.44 us  [halving_sum(): flat = keep + lax.ppermute(send, axis, pairs)]
  transfers between devices with their start and end apart: 19 -> 20, of which waited for: 14 -> 15; matrix products, arithmetic and copies ran while one was open for 16% -> 24% of each run, Pallas kernels for 0% -> 0%
where the time goes in v12:
time: 83.3 us; the launch traced here: 82.8 us
  starting transfers between devices  23.1 us (28%)
  waiting for transfers between devices  22.9 us (27%)
  matrix products  20.9 us (25%)
  local copies, waits for them, and re-layouts  7.76 us (9%)
  other arithmetic  7.06 us (8%)
  between operations  1.06 us (1%)
    ppermute x6, waiting for transfers between devices, halving_sum(): flat = keep + lax.ppermute(send, axis, pairs)  9.73 us
    dot_general x3, matrix products, band_of(): jnp.einsum('kiad,dpq->iapkq', stencil, lon_picker(col_count, first_source...  8.07 us
    ppermute x6, starting transfers between devices, halving_sum(): other = lax.ppermute(flat, axis, pairs)  5.51 us
    dot_general x1, matrix products, spread_adjoint_rows(): jnp.einsum('cikq,iapkq->ciap', mixed, band, preferred_element_type=jnp.fl...  5.14 us
    ppermute x1, starting transfers between devices, lon_halo(): lax.ppermute(block[..., :width], 'lon', [(i, (i - 1) % count) for i in ra...  5.13 us
    ppermute x4, waiting for transfers between devices, halving_sum(): flat = flat + lax.ppermute(flat, axis, pairs)  5.05 us
    unnamed x20, local copies, waits for them, and re-layouts  4.86 us
    ppermute x4, starting transfers between devices, halving_sum(): flat = flat + lax.ppermute(flat, axis, pairs)  4.84 us
  transfers between devices with their start and end apart: 20, of which 15 were waited for; matrix products, arithmetic and copies ran while one was open for 24% of the time, Pallas kernels for 0%

profile of v12, /device:TPU:0, one launch (start us, length us, event | category | flops | bytes accessed | tf_op | source)
XLA Modules:
  0.0 82.8 jit_solution(18367548205941252061)
XLA Ops:
  0.6 1.1 %copy.13 = bf16[1,256,2,128]{1,3,2,0:T(8,128)(2,1)S(1)} copy(bf16[1,256,2,128]{3,2,1,0:T(2,128)(2,1)} %param.13) | data formatting | bytes 262144 | tf_op args[6]
  1.7 1.0 %copy.12 = bf16[1,256,2,128]{1,3,2,0:T(8,128)(2,1)S(1)} copy(bf16[1,256,2,128]{3,2,1,0:T(2,128)(2,1)} %param.7) | data formatting | bytes 262144 | tf_op args[0]
  2.8 5.1 %collective-permute-start.2 = (bf16[512,2,8]{0,2,1:T(8,128)(2,1)S(1)}, bf16[512,2,8]{0,2,1:T(8,128)(2,1)S(1)}, u32[]{:S(2)}, u32[]{:S(2)}) collective-permute-start(bf16[512,2,8]{0,2,1:T(8,128)(2,1)S(1)} %get-tuple-element.34), channel_id=1, source_target_pairs={{0,3},{1,0},{2,1},{3,2},{4,7},{5,4},{6,5},{7,6},{8,11},{9,8},{10,9... | collective-permute-start | bytes 49160 | tf_op jit(solution)/shard_map/ppermute | solution.py:76
  7.9 0.7 broadcast_add_fusion
  8.6 0.9 %convolution_convert_fusion.2 = bf16[3,2,3,9]{3,2,1,0:T(4,128)(2,1)S(1)} fusion(s32[2,3,12]{2,0,1:T(2,128)S(1)} %get-tuple-element.37, f32[2,3,12]{2,0,1:T(2,128)} %param.10, s32[2,3,12]{2,0,1:T(2,128)S(1)} %get-tuple-element.38), kind=kOutput, calls=%fused_computation.38 | convolution fusion | flops 24570 | bytes 1188 | tf_op jit(solution)/shard_map/rks,rksa,rksd->krad/dot_general | solution.py:85
  9.5 1.6 %collective-permute-start = (bf16[3,2,3,9]{3,2,1,0:T(4,128)(2,1)S(1)}, bf16[3,2,3,9]{3,2,1,0:T(4,128)(2,1)S(1)}, u32[]{:S(2)}, u32[]{:S(2)}) collective-permute-start(bf16[3,2,3,9]{3,2,1,0:T(4,128)(2,1)S(1)} %convolution_convert_fusion.2), channel_id=1, source_target_pairs={{0,4},{4,0},{1,5},{5,1},{2,6},{6,2},{3,7},{7,3},{8,12},{12,8},{9,1... | collective-permute-start | bytes 980 | tf_op jit(solution)/shard_map/ppermute | solution.py:55
  11.1 0.1 fusion.42
  11.2 1.6 %fusion.34 = bf16[136,128,3,2,3]{1,4,3,2,0:T(4,128)(2,1)} fusion(pred[9,136,128,1,1]{2,1,0,3,4:T(8,128)(4,1)S(1)} %fusion.42, bf16[3,2,3,9]{3,2,1,0:T(4,128)(2,1)S(1)} %convolution_convert_fusion.2), kind=kOutput, calls=%fused_computation.36 | convolution fusion | flops 5640192 | bytes 783684 | tf_op jit(solution)/shard_map/kiad,dpq->iapkq/dot_general | solution.py:104
  12.8 0.2 fusion.29
  13.0 0.2 collective-permute-done
  13.2 3.6 %fusion.10 = bf16[136,144,3,4,3]{1,4,3,2,0:T(4,128)(2,1)} fusion(pred[9,136,144,1,1]{2,1,0,3,4:T(8,128)(4,1)S(1)} %fusion.29, bf16[3,2,3,9]{3,2,1,0:T(4,128)(2,1)S(1)} %get-tuple-element.36, bf16[3,2,3,9]{3,2,1,0:T(4,128)(2,1)S(1)} %convolution_convert_fusion.2, bf16[3,2,3,9]{3,2,1,0:T(4,128)(2,1)S(1)} %get-tuple-element.35, pred[]{:T(512)S(6)} %eq.73), kind=kOutput, calls=%fused_computation.12 | convolution fusion | flops 12693348 | bytes 1587277 | tf_op jit(solution)/shard_map/kiad,dpq->iapkq/dot_general | solution.py:104
  16.8 1.6 %collective-permute-start.3 = (bf16[512,2,144]{0,2,1:T(8,128)(2,1)S(1)}, bf16[512,2,144]{0,2,1:T(8,128)(2,1)S(1)}, u32[]{:S(2)}, u32[]{:S(2)}) collective-permute-start(bf16[512,2,144]{0,2,1:T(8,128)(2,1)S(1)} %pad_maximum_fusion.6), channel_id=1, source_target_pairs={{0,4},{4,0},{1,5},{5,1},{2,6},{6,2},{3,7},{7,3},{8,12},{12,8},{9,1... | collective-permute-start | bytes 884744 | tf_op jit(solution)/shard_map/ppermute | solution.py:55
  18.4 3.0 %convert_bitcast_fusion = bf16[4,3,144,3,136]{2,0,1,3,4:T(4,128)(2,1)} fusion(bf16[3,4,3,9]{3,2,1,0:T(4,128)(2,1)S(1)} %pad_maximum_fusion.9), kind=kOutput, calls=%fused_computation.8 | convolution fusion | flops 13747968 | bytes 1410696 | tf_op jit(solution)/shard_map/kiad,dpq->iapkq/dot_general | solution.py:104
  21.3 3.6 %collective-permute-done.3 = bf16[512,2,144]{0,2,1:T(8,128)(2,1)S(1)} collective-permute-done((bf16[512,2,144]{0,2,1:T(8,128)(2,1)S(1)}, bf16[512,2,144]{0,2,1:T(8,128)(2,1)S(1)}, u32[]{:S(2)}, u32[]{:S(2)}) %collective-permute-start.3) | collective-permute-done | bytes 294944 | tf_op jit(solution)/shard_map/ppermute | solution.py:55
  25.0 0.1 maximum_maximum_fusion
  25.1 0.8 slice_bitcast_fusion.3
  25.8 0.1 copy-done.3
  25.9 5.1 %fusion.19 = f32[256,4,3,136]{0,3,1,2:T(8,128)} fusion(bf16[3,256,256]{2,1,0:T(8,128)(2,1)S(1)} %copy-done.3, bf16[512,4,144]{0,2,1:T(8,128)(2,1)S(1)} %get-tuple-element.24, bf16[512,4,144]{0,2,1:T(8,128)(2,1)S(1)} %get-tuple-element.25, pred[]{:T(512)S(6)} %eq.73, bf16[136,144,3,4,3]{1,4,3,2,0:T(4,128)(2,1)} %fusion.10), kind=kOutput, calls=%fused_computation.16 | convolution fusion | flops 588054528 | bytes 4064257 | tf_op jit(solution)/shard_map/cikq,iapkq->ciap/dot_general | solution.py:137
  31.1 1.2 %slice_bitcast_fusion.2 = (f32[256,3,136]{0,2,1:T(8,128)S(1)}, f32[256,3,136]{0,2,1:T(8,128)S(1)}) fusion(f32[256,4,3,136]{0,3,1,2:T(8,128)} %fusion.19), kind=kLoop, calls=%fused_computation.72 | loop fusion | bytes 1671168 | tf_op jit(solution)/shard_map/squeeze | solution.py:140
  32.3 1.3 %fusion.56 = bf16[256,4,136]{0,2,1:T(8,128)(2,1)S(1)} fusion(f32[256,4,3,136]{0,3,1,2:T(8,128)} %fusion.19, f32[256,3,136]{0,2,1:T(8,128)S(1)} %get-tuple-element.21, f32[256,3,136]{0,2,1:T(8,128)S(1)} %get-tuple-element.20), kind=kLoop, calls=%fused_computation.69 | loop fusion | flops 417792 | bytes 1671168 | tf_op jit(solution)/shard_map/convert_element_type | solution.py:193
  33.7 0.5 copy-done.1
  34.2 0.8 fusion.24
  35.0 0.8 fusion.46
  35.8 0.3 copy-done.5
  36.1 0.4 fusion.31
  36.6 0.3 copy-done.2
  36.8 0.3 fusion.27
  37.2 0.1 collective-permute-start.4
  37.2 0.3 fusion.28
  37.6 0.8 constant_dynamic-slice_fusion.4
  38.4 0.5 collective-permute-start.5
  38.8 0.1 collective-permute-done.4
  39.0 1.5 %collective-permute-done.5 = f32[384,256]{1,0:T(8,128)} collective-permute-done((f32[384,256]{1,0:T(8,128)}, f32[384,256]{1,0:T(8,128)}, u32[]{:S(2)}, u32[]{:S(2)}) %collective-permute-start.5) | collective-permute-done | bytes 393248 | tf_op jit(solution)/shard_map/ppermute | solution.py:31
  40.5 1.0 %dynamic-slice_add_fusion = f32[384,256]{1,0:T(8,128)S(1)} fusion(f32[384,256]{1,0:T(8,128)} %collective-permute-done.5, f32[768,256]{1,0:T(8,128)S(1)} %bitcast.194, s32[]{:T(128)S(6)} %select_n.179), kind=kLoop, calls=%fused_computation.80 | loop fusion | flops 98304 | bytes 1179652 | tf_op jit(solution)/shard_map/add | solution.py:31
  41.6 1.6 %collective-permute-start.6 = (f32[192,256]{1,0:T(8,128)S(1)}, f32[192,256]{1,0:T(8,128)S(1)}, u32[]{:S(2)}, u32[]{:S(2)}) collective-permute-start(f32[192,256]{1,0:T(8,128)S(1)} %constant_dynamic-slice_fusion.3), channel_id=1, source_target_pairs={{0,16},{8,24},{16,0},{24,8},{1,17},{9,25},{17,1},{25,9},{2,18},{10... | collective-permute-start | bytes 589832 | tf_op jit(solution)/shard_map/ppermute | solution.py:31
  43.2 0.6 collective-permute-start.13
  43.8 4.0 %fusion.14 = f32[256,4,3,144]{0,3,2,1:T(8,128)} fusion(bf16[4,3,144,3,136]{2,0,1,3,4:T(4,128)(2,1)} %convert_bitcast_fusion, bf16[3,256,256]{2,1,0:T(8,128)(2,1)S(1)} %copy-done, bf16[256,4,136]{0,2,1:T(8,128)(2,1)S(1)} %copy-done.7), kind=kOutput, calls=%fused_computation.15 | convolution fusion | flops 575299584 | bytes 3851264 | tf_op jit(solution)/shard_map/cikq,iapkq->ciap/dot_general | solution.py:124
  47.8 1.7 %collective-permute-done.6 = f32[192,256]{1,0:T(8,128)S(1)} collective-permute-done((f32[192,256]{1,0:T(8,128)S(1)}, f32[192,256]{1,0:T(8,128)S(1)}, u32[]{:S(2)}, u32[]{:S(2)}) %collective-permute-start.6) | collective-permute-done | bytes 196640 | tf_op jit(solution)/shard_map/ppermute | solution.py:31
  49.5 0.9 %collective-permute-start.7 = (f32[96,256]{1,0:T(8,128)S(1)}, f32[96,256]{1,0:T(8,128)S(1)}, u32[]{:S(2)}, u32[]{:S(2)}) collective-permute-start(f32[96,256]{1,0:T(8,128)S(1)} %constant_dynamic-slice_fusion.2), channel_id=1, source_target_pairs={{0,4},{4,0},{1,5},{5,1},{2,6},{6,2},{3,7},{7,3},{8,12},{12,8},{9,1... | collective-permute-start | bytes 294920 | tf_op jit(solution)/shard_map/ppermute | solution.py:31
  50.4 2.7 %collective-permute-done.13 = f32[192,256]{1,0:T(8,128)S(1)} collective-permute-done((f32[192,256]{1,0:T(8,128)S(1)}, f32[192,256]{1,0:T(8,128)S(1)}, u32[]{:S(2)}, u32[]{:S(2)}) %collective-permute-start.13) | collective-permute-done | bytes 196640 | tf_op jit(solution)/shard_map/ppermute | solution.py:31
  53.1 0.9 %collective-permute-start.14 = (f32[96,256]{1,0:T(8,128)S(1)}, f32[96,256]{1,0:T(8,128)S(1)}, u32[]{:S(2)}, u32[]{:S(2)}) collective-permute-start(f32[96,256]{1,0:T(8,128)S(1)} %constant_dynamic-slice_fusion), channel_id=1, source_target_pairs={{0,4},{4,0},{1,5},{5,1},{2,6},{6,2},{3,7},{7,3},{8,12},{12,8},{9,1... | collective-permute-start | bytes 294920 | tf_op jit(solution)/shard_map/ppermute | solution.py:31
  54.0 0.2 collective-permute-done.7
  54.2 0.1 collective-permute-start.8
  54.3 3.5 %collective-permute-done.14 = f32[96,256]{1,0:T(8,128)S(1)} collective-permute-done((f32[96,256]{1,0:T(8,128)S(1)}, f32[96,256]{1,0:T(8,128)S(1)}, u32[]{:S(2)}, u32[]{:S(2)}) %collective-permute-start.14) | collective-permute-done | bytes 98336 | tf_op jit(solution)/shard_map/ppermute | solution.py:31
  57.9 1.0 %collective-permute-done.8 = f32[96,256]{1,0:T(8,128)S(1)} collective-permute-done((f32[96,256]{1,0:T(8,128)S(1)}, f32[96,256]{1,0:T(8,128)S(1)}, u32[]{:S(2)}, u32[]{:S(2)}) %collective-permute-start.8) | collective-permute-done | bytes 98336 | tf_op jit(solution)/shard_map/ppermute | solution.py:37
  58.9 3.1 %collective-permute-start.9 = (f32[96,256]{1,0:T(8,128)S(1)}, f32[96,256]{1,0:T(8,128)S(1)}, u32[]{:S(2)}, u32[]{:S(2)}) collective-permute-start(f32[96,256]{1,0:T(8,128)S(1)} %add.180), channel_id=1, source_target_pairs={{0,2},{1,3},{2,0},{3,1},{4,6},{5,7},{6,4},{7,5},{8,10},{9,11},{10,... | collective-permute-start | bytes 294920 | tf_op jit(solution)/shard_map/ppermute | solution.py:37
  62.1 1.1 %fusion.76 = bf16[1,256,2,128]{1,3,2,0:T(8,128)(2,1)S(1)} fusion(f32[256,4,3,144]{0,3,2,1:T(8,128)} %fusion.14), kind=kLoop, calls=%fused_computation.108 | loop fusion | flops 196608 | bytes 917504 | tf_op jit(solution)/shard_map/convert_element_type | solution.py:217
  63.3 1.6 %collective-permute-start.16 = (f32[96,256]{1,0:T(8,128)S(1)}, f32[96,256]{1,0:T(8,128)S(1)}, u32[]{:S(2)}, u32[]{:S(2)}) collective-permute-start(f32[96,256]{1,0:T(8,128)S(1)} %add.184), channel_id=1, source_target_pairs={{0,2},{1,3},{2,0},{3,1},{4,6},{5,7},{6,4},{7,5},{8,10},{9,11},{10,... | collective-permute-start | bytes 294920 | tf_op jit(solution)/shard_map/ppermute | solution.py:37
  64.8 2.4 %collective-permute-done.9 = f32[96,256]{1,0:T(8,128)S(1)} collective-permute-done((f32[96,256]{1,0:T(8,128)S(1)}, f32[96,256]{1,0:T(8,128)S(1)}, u32[]{:S(2)}, u32[]{:S(2)}) %collective-permute-start.9) | collective-permute-done | bytes 98336 | tf_op jit(solution)/shard_map/ppermute | solution.py:37
  67.3 1.1 %collective-permute-start.10 = (bf16[96,256]{1,0:T(8,128)(2,1)S(1)}, bf16[96,256]{1,0:T(8,128)(2,1)S(1)}, u32[]{:S(2)}, u32[]{:S(2)}) collective-permute-start(bf16[96,256]{1,0:T(8,128)(2,1)S(1)} %add_convert_fusion.1), channel_id=1, source_target_pairs={{0,4},{4,0},{1,5},{5,1},{2,6},{6,2},{3,7},{7,3},{8,12},{12,8},{9,1... | collective-permute-start | bytes 147464 | tf_op jit(solution)/shard_map/ppermute | solution.py:42
  68.4 1.6 %collective-permute-done.16 = f32[96,256]{1,0:T(8,128)S(1)} collective-permute-done((f32[96,256]{1,0:T(8,128)S(1)}, f32[96,256]{1,0:T(8,128)S(1)}, u32[]{:S(2)}, u32[]{:S(2)}) %collective-permute-start.16) | collective-permute-done | bytes 98336 | tf_op jit(solution)/shard_map/ppermute | solution.py:37
  70.0 1.2 %collective-permute-start.17 = (bf16[96,256]{1,0:T(8,128)(2,1)S(1)}, bf16[96,256]{1,0:T(8,128)(2,1)S(1)}, u32[]{:S(2)}, u32[]{:S(2)}) collective-permute-start(bf16[96,256]{1,0:T(8,128)(2,1)S(1)} %add_convert_fusion), channel_id=1, source_target_pairs={{0,4},{4,0},{1,5},{5,1},{2,6},{6,2},{3,7},{7,3},{8,12},{12,8},{9,1... | collective-permute-start | bytes 147464 | tf_op jit(solution)/shard_map/ppermute | solution.py:42
  71.1 0.6 collective-permute-done.10
  71.7 1.6 %collective-permute-start.11 = (bf16[192,256]{1,0:T(8,128)(2,1)S(1)}, bf16[192,256]{1,0:T(8,128)(2,1)S(1)}, u32[]{:S(2)}, u32[]{:S(2)}) collective-permute-start(bf16[192,256]{1,0:T(8,128)(2,1)S(1)} %maximum_select_fusion.4), channel_id=1, source_target_pairs={{0,16},{8,24},{16,0},{24,8},{1,17},{9,25},{17,1},{25,9},{2,18},{10... | collective-permute-start | bytes 294920 | tf_op jit(solution)/shard_map/ppermute | solution.py:42
  73.3 0.8 collective-permute-done.17
  74.1 1.6 %collective-permute-start.18 = (bf16[192,256]{1,0:T(8,128)(2,1)S(1)}, bf16[192,256]{1,0:T(8,128)(2,1)S(1)}, u32[]{:S(2)}, u32[]{:S(2)}) collective-permute-start(bf16[192,256]{1,0:T(8,128)(2,1)S(1)} %maximum_select_fusion.5), channel_id=1, source_target_pairs={{0,16},{8,24},{16,0},{24,8},{1,17},{9,25},{17,1},{25,9},{2,18},{10... | collective-permute-start | bytes 294920 | tf_op jit(solution)/shard_map/ppermute | solution.py:42
  75.7 0.7 collective-permute-done.11
  76.5 0.1 collective-permute-start.12
  76.6 2.2 %collective-permute-done.18 = bf16[192,256]{1,0:T(8,128)(2,1)S(1)} collective-permute-done((bf16[192,256]{1,0:T(8,128)(2,1)S(1)}, bf16[192,256]{1,0:T(8,128)(2,1)S(1)}, u32[]{:S(2)}, u32[]{:S(2)}) %collective-permute-start.18) | collective-permute-done | bytes 98336 | tf_op jit(solution)/shard_map/ppermute | solution.py:42
  79.0 0.3 fusion.33
  79.3 0.8 copy.24
  80.1 0.8 copy.25
  80.9 0.9 %maximum_select_fusion = f32[768,256]{1,0:T(8,128)} fusion(f32[384,256]{1,0:T(8,128)S(1)} %get-tuple-element.18, f32[384,256]{1,0:T(8,128)S(1)} %convert_element_type.127, pred[]{:T(512)S(6)} %eq.75), kind=kLoop, calls=%fused_computation.46 | loop fusion | flops 589824 | bytes 1572865 | tf_op jit(solution)/shard_map/jit(_where)/select_n | solution.py:45
  81.8 0.9 %maximum_select_fusion.1 = f32[768,256]{1,0:T(8,128)} fusion(f32[384,256]{1,0:T(8,128)S(1)} %get-tuple-element.16, f32[384,256]{1,0:T(8,128)S(1)} %convert_element_type.130, pred[]{:T(512)S(6)} %eq.75), kind=kLoop, calls=%fused_computation.47 | loop fusion | flops 589824 | bytes 1572865 | tf_op jit(solution)/shard_map/jit(_where)/select_n | solution.py:45
  (50 shorter events, 0.9 us)
Async XLA Ops:
  0.6 34.3 %copy-start = (bf16[3,256,256]{2,1,0:T(8,128)(2,1)S(1)}, bf16[3,256,256]{2,1,0:T(8,128)(2,1)}, u32[]{:S(2)}) copy-start(bf16[3,256,256]{2,1,0:T(8,128)(2,1)} %param.8) | copy-start | bytes 1179652
  2.8 14.0 %collective-permute-start.2 = (bf16[512,2,8]{0,2,1:T(8,128)(2,1)S(1)}, bf16[512,2,8]{0,2,1:T(8,128)(2,1)S(1)}, u32[]{:S(2)}, u32[]{:S(2)}) collective-permute-start(bf16[512,2,8]{0,2,1:T(8,128)(2,1)S(1)} %get-tuple-element.34), channel_id=1, source_target_pairs={{0,3},{1,0},{2,1},{3,2},{4,7},{5,4},{6,5},{7,6},{8,11},{9,8},{10,9... | collective-permute-start | bytes 49160 | tf_op jit(solution)/shard_map/ppermute | solution.py:76
  7.9 8.9 %collective-permute-start.1 = (bf16[512,2,8]{0,2,1:T(8,128)(2,1)S(1)}, bf16[512,2,8]{0,2,1:T(8,128)(2,1)S(1)}, u32[]{:S(2)}, u32[]{:S(2)}) collective-permute-start(bf16[512,2,8]{0,2,1:T(8,128)(2,1)S(1)} %get-tuple-element.33), channel_id=1, source_target_pairs={{0,1},{1,2},{2,3},{3,0},{4,5},{5,6},{6,7},{7,4},{8,9},{9,10},{10,1... | collective-permute-start | bytes 49160 | tf_op jit(solution)/shard_map/ppermute | solution.py:75
  9.5 3.7 %collective-permute-start = (bf16[3,2,3,9]{3,2,1,0:T(4,128)(2,1)S(1)}, bf16[3,2,3,9]{3,2,1,0:T(4,128)(2,1)S(1)}, u32[]{:S(2)}, u32[]{:S(2)}) collective-permute-start(bf16[3,2,3,9]{3,2,1,0:T(4,128)(2,1)S(1)} %convolution_convert_fusion.2), channel_id=1, source_target_pairs={{0,4},{4,0},{1,5},{5,1},{2,6},{6,2},{3,7},{7,3},{8,12},{12,8},{9,1... | collective-permute-start | bytes 980 | tf_op jit(solution)/shard_map/ppermute | solution.py:55
  16.8 8.1 %collective-permute-start.3 = (bf16[512,2,144]{0,2,1:T(8,128)(2,1)S(1)}, bf16[512,2,144]{0,2,1:T(8,128)(2,1)S(1)}, u32[]{:S(2)}, u32[]{:S(2)}) collective-permute-start(bf16[512,2,144]{0,2,1:T(8,128)(2,1)S(1)} %pad_maximum_fusion.6), channel_id=1, source_target_pairs={{0,4},{4,0},{1,5},{5,1},{2,6},{6,2},{3,7},{7,3},{8,12},{12,8},{9,1... | collective-permute-start | bytes 884744 | tf_op jit(solution)/shard_map/ppermute | solution.py:55
  24.9 1.0 %copy-start.3 = (bf16[3,256,256]{2,1,0:T(8,128)(2,1)S(1)}, bf16[3,256,256]{2,1,0:T(8,128)(2,1)}, u32[]{:S(2)}) copy-start(bf16[3,256,256]{2,1,0:T(8,128)(2,1)} %param.9) | copy-start | bytes 1179652
  32.3 1.9 %copy-start.1 = (bf16[4,3,144,3,136]{2,0,1,3,4:T(4,128)(2,1)S(1)}, bf16[4,3,144,3,136]{2,0,1,3,4:T(4,128)(2,1)}, u32[]{:S(2)}) copy-start(bf16[4,3,144,3,136]{2,0,1,3,4:T(4,128)(2,1)} %convert_bitcast_fusion) | copy-start | bytes 4230148
  32.3 1.9 %copy-start.4 = (bf16[256,4,1,144]{0,3,2,1:T(8,128)(2,1)S(1)}, bf16[256,4,1,144]{0,3,2,1:T(8,128)(2,1)}, u32[]{:S(2)}) copy-start(bf16[256,4,1,144]{0,3,2,1:T(8,128)(2,1)} %get-tuple-element.40) | copy-start | bytes 884740
  35.0 1.2 %copy-start.5 = (bf16[136,128,3,2,3]{1,4,3,2,0:T(4,128)(2,1)S(1)}, bf16[136,128,3,2,3]{1,4,3,2,0:T(4,128)(2,1)}, u32[]{:S(2)}) copy-start(bf16[136,128,3,2,3]{1,4,3,2,0:T(4,128)(2,1)} %fusion.34) | copy-start | bytes 1880068
  35.8 1.5 %copy-start.6 = (bf16[256,4,136]{0,2,1:T(8,128)(2,1)}, bf16[256,4,136]{0,2,1:T(8,128)(2,1)S(1)}, u32[]{:S(2)}) copy-start(bf16[256,4,136]{0,2,1:T(8,128)(2,1)S(1)} %get-tuple-element.9) | copy-start | bytes 835588
  35.8 1.1 %copy-start.2 = (bf16[1,256,2,128]{3,2,1,0:T(2,128)(2,1)S(1)}, bf16[1,256,2,128]{3,2,1,0:T(2,128)(2,1)}, u32[]{:S(2)}) copy-start(bf16[1,256,2,128]{3,2,1,0:T(2,128)(2,1)} %param.13) | copy-start | bytes 393220
  37.2 1.8 %collective-permute-start.4 = (f32[384,256]{1,0:T(8,128)S(1)}, f32[384,256]{1,0:T(8,128)S(1)}, u32[]{:S(2)}, u32[]{:S(2)}) collective-permute-start(f32[384,256]{1,0:T(8,128)S(1)} %constant_dynamic-slice_fusion.5), channel_id=1, source_target_pairs={{0,8},{8,0},{16,24},{24,16},{1,9},{9,1},{17,25},{25,17},{2,10},{10... | collective-permute-start | bytes 1179656 | tf_op jit(solution)/shard_map/ppermute | solution.py:31
  38.4 2.2 %collective-permute-start.5 = (f32[384,256]{1,0:T(8,128)}, f32[384,256]{1,0:T(8,128)}, u32[]{:S(2)}, u32[]{:S(2)}) collective-permute-start(f32[384,256]{1,0:T(8,128)} %constant_dynamic-slice_fusion.4), channel_id=1, source_target_pairs={{0,8},{8,0},{16,24},{24,16},{1,9},{9,1},{17,25},{25,17},{2,10},{10... | collective-permute-start | bytes 1179656 | tf_op jit(solution)/shard_map/ppermute | solution.py:31
  39.0 4.8 %copy-start.7 = (bf16[256,4,136]{0,2,1:T(8,128)(2,1)S(1)}, bf16[256,4,136]{0,2,1:T(8,128)(2,1)}, u32[]{:S(2)}) copy-start(bf16[256,4,136]{0,2,1:T(8,128)(2,1)} %copy-done.6) | copy-start | bytes 835588
  41.6 7.8 %collective-permute-start.6 = (f32[192,256]{1,0:T(8,128)S(1)}, f32[192,256]{1,0:T(8,128)S(1)}, u32[]{:S(2)}, u32[]{:S(2)}) collective-permute-start(f32[192,256]{1,0:T(8,128)S(1)} %constant_dynamic-slice_fusion.3), channel_id=1, source_target_pairs={{0,16},{8,24},{16,0},{24,8},{1,17},{9,25},{17,1},{25,9},{2,18},{10... | collective-permute-start | bytes 589832 | tf_op jit(solution)/shard_map/ppermute | solution.py:31
  43.2 9.9 %collective-permute-start.13 = (f32[192,256]{1,0:T(8,128)S(1)}, f32[192,256]{1,0:T(8,128)S(1)}, u32[]{:S(2)}, u32[]{:S(2)}) collective-permute-start(f32[192,256]{1,0:T(8,128)S(1)} %constant_dynamic-slice_fusion.1), channel_id=1, source_target_pairs={{0,16},{8,24},{16,0},{24,8},{1,17},{9,25},{17,1},{25,9},{2,18},{10... | collective-permute-start | bytes 589832 | tf_op jit(solution)/shard_map/ppermute | solution.py:31
  49.5 4.7 %collective-permute-start.7 = (f32[96,256]{1,0:T(8,128)S(1)}, f32[96,256]{1,0:T(8,128)S(1)}, u32[]{:S(2)}, u32[]{:S(2)}) collective-permute-start(f32[96,256]{1,0:T(8,128)S(1)} %constant_dynamic-slice_fusion.2), channel_id=1, source_target_pairs={{0,4},{4,0},{1,5},{5,1},{2,6},{6,2},{3,7},{7,3},{8,12},{12,8},{9,1... | collective-permute-start | bytes 294920 | tf_op jit(solution)/shard_map/ppermute | solution.py:31
  53.1 4.7 %collective-permute-start.14 = (f32[96,256]{1,0:T(8,128)S(1)}, f32[96,256]{1,0:T(8,128)S(1)}, u32[]{:S(2)}, u32[]{:S(2)}) collective-permute-start(f32[96,256]{1,0:T(8,128)S(1)} %constant_dynamic-slice_fusion), channel_id=1, source_target_pairs={{0,4},{4,0},{1,5},{5,1},{2,6},{6,2},{3,7},{7,3},{8,12},{12,8},{9,1... | collective-permute-start | bytes 294920 | tf_op jit(solution)/shard_map/ppermute | solution.py:31
  54.2 4.7 %collective-permute-start.8 = (f32[96,256]{1,0:T(8,128)S(1)}, f32[96,256]{1,0:T(8,128)S(1)}, u32[]{:S(2)}, u32[]{:S(2)}) collective-permute-start(f32[96,256]{1,0:T(8,128)S(1)} %dynamic-slice_add_fusion.5), channel_id=1, source_target_pairs={{0,1},{1,0},{2,3},{3,2},{4,5},{5,4},{6,7},{7,6},{8,9},{9,8},{10,11... | collective-permute-start | bytes 294920 | tf_op jit(solution)/shard_map/ppermute | solution.py:37
  57.8 5.4 %collective-permute-start.15 = (f32[96,256]{1,0:T(8,128)S(1)}, f32[96,256]{1,0:T(8,128)S(1)}, u32[]{:S(2)}, u32[]{:S(2)}) collective-permute-start(f32[96,256]{1,0:T(8,128)S(1)} %dynamic-slice_add_fusion.4), channel_id=1, source_target_pairs={{0,1},{1,0},{2,3},{3,2},{4,5},{5,4},{6,7},{7,6},{8,9},{9,8},{10,11... | collective-permute-start | bytes 294920 | tf_op jit(solution)/shard_map/ppermute | solution.py:37
  58.9 8.3 %collective-permute-start.9 = (f32[96,256]{1,0:T(8,128)S(1)}, f32[96,256]{1,0:T(8,128)S(1)}, u32[]{:S(2)}, u32[]{:S(2)}) collective-permute-start(f32[96,256]{1,0:T(8,128)S(1)} %add.180), channel_id=1, source_target_pairs={{0,2},{1,3},{2,0},{3,1},{4,6},{5,7},{6,4},{7,5},{8,10},{9,11},{10,... | collective-permute-start | bytes 294920 | tf_op jit(solution)/shard_map/ppermute | solution.py:37
  63.3 6.7 %collective-permute-start.16 = (f32[96,256]{1,0:T(8,128)S(1)}, f32[96,256]{1,0:T(8,128)S(1)}, u32[]{:S(2)}, u32[]{:S(2)}) collective-permute-start(f32[96,256]{1,0:T(8,128)S(1)} %add.184), channel_id=1, source_target_pairs={{0,2},{1,3},{2,0},{3,1},{4,6},{5,7},{6,4},{7,5},{8,10},{9,11},{10,... | collective-permute-start | bytes 294920 | tf_op jit(solution)/shard_map/ppermute | solution.py:37
  67.3 4.4 %collective-permute-start.10 = (bf16[96,256]{1,0:T(8,128)(2,1)S(1)}, bf16[96,256]{1,0:T(8,128)(2,1)S(1)}, u32[]{:S(2)}, u32[]{:S(2)}) collective-permute-start(bf16[96,256]{1,0:T(8,128)(2,1)S(1)} %add_convert_fusion.1), channel_id=1, source_target_pairs={{0,4},{4,0},{1,5},{5,1},{2,6},{6,2},{3,7},{7,3},{8,12},{12,8},{9,1... | collective-permute-start | bytes 147464 | tf_op jit(solution)/shard_map/ppermute | solution.py:42
  70.0 4.2 %collective-permute-start.17 = (bf16[96,256]{1,0:T(8,128)(2,1)S(1)}, bf16[96,256]{1,0:T(8,128)(2,1)S(1)}, u32[]{:S(2)}, u32[]{:S(2)}) collective-permute-start(bf16[96,256]{1,0:T(8,128)(2,1)S(1)} %add_convert_fusion), channel_id=1, source_target_pairs={{0,4},{4,0},{1,5},{5,1},{2,6},{6,2},{3,7},{7,3},{8,12},{12,8},{9,1... | collective-permute-start | bytes 147464 | tf_op jit(solution)/shard_map/ppermute | solution.py:42
  71.7 4.7 %collective-permute-start.11 = (bf16[192,256]{1,0:T(8,128)(2,1)S(1)}, bf16[192,256]{1,0:T(8,128)(2,1)S(1)}, u32[]{:S(2)}, u32[]{:S(2)}) collective-permute-start(bf16[192,256]{1,0:T(8,128)(2,1)S(1)} %maximum_select_fusion.4), channel_id=1, source_target_pairs={{0,16},{8,24},{16,0},{24,8},{1,17},{9,25},{17,1},{25,9},{2,18},{10... | collective-permute-start | bytes 294920 | tf_op jit(solution)/shard_map/ppermute | solution.py:42
  74.1 4.7 %collective-permute-start.18 = (bf16[192,256]{1,0:T(8,128)(2,1)S(1)}, bf16[192,256]{1,0:T(8,128)(2,1)S(1)}, u32[]{:S(2)}, u32[]{:S(2)}) collective-permute-start(bf16[192,256]{1,0:T(8,128)(2,1)S(1)} %maximum_select_fusion.5), channel_id=1, source_target_pairs={{0,16},{8,24},{16,0},{24,8},{1,17},{9,25},{17,1},{25,9},{2,18},{10... | collective-permute-start | bytes 294920 | tf_op jit(solution)/shard_map/ppermute | solution.py:42
  76.5 4.3 %collective-permute-start.12 = (bf16[384,256]{1,0:T(8,128)(2,1)S(1)}, bf16[384,256]{1,0:T(8,128)(2,1)S(1)}, u32[]{:S(2)}, u32[]{:S(2)}) collective-permute-start(bf16[384,256]{1,0:T(8,128)(2,1)S(1)} %get-tuple-element.19), channel_id=1, source_target_pairs={{0,8},{8,0},{16,24},{24,16},{1,9},{9,1},{17,25},{25,17},{2,10},{10... | collective-permute-start | bytes 589832 | tf_op jit(solution)/shard_map/ppermute | solution.py:42
  78.9 2.9 %collective-permute-start.19 = (bf16[384,256]{1,0:T(8,128)(2,1)S(1)}, bf16[384,256]{1,0:T(8,128)(2,1)S(1)}, u32[]{:S(2)}, u32[]{:S(2)}) collective-permute-start(bf16[384,256]{1,0:T(8,128)(2,1)S(1)} %get-tuple-element.17), channel_id=1, source_target_pairs={{0,8},{8,0},{16,24},{24,16},{1,9},{9,1},{17,25},{25,17},{2,10},{10... | collective-permute-start | bytes 589832 | tf_op jit(solution)/shard_map/ppermute | solution.py:42

commit v13 on v11

--- a/solution.py
+++ b/solution.py
@@ -11,7 +11,7 @@
 LON_HALO = 2 * LON_REACH
 
 
-def halving_sum(value, axes, exchanged=2, hold=None):
+def halving_sum(value, axes, exchanged=3, hold=None):
     stages = []
     for axis in axes:
         bit = 1

time: 81.7 us -> 84.5 us (1.034)
  waiting for transfers between devices: 32.2 us -> 37.4 us
  matrix products: 17.9 us -> 16.6 us
  other arithmetic: 5.01 us -> 3.95 us
    ppermute x4 -> x6, waiting for transfers between devices: 9.36 us -> 18.6 us  [halving_sum(): flat = flat + lax.ppermute(flat, axis, pairs)]
    ppermute x4 -> x6, starting transfers between devices: 0.88 us -> 4.75 us  [halving_sum(): flat = flat + lax.ppermute(flat, axis, pairs)]
    ppermute x6 -> x4, starting transfers between devices: 5.85 us -> 3.25 us  [halving_sum(): flat = keep + lax.ppermute(send, axis, pairs)]
    ppermute x6 -> x4, waiting for transfers between devices: 5.48 us -> 2.96 us  [halving_sum(): other = lax.ppermute(flat, axis, pairs)]
    ppermute x6 -> x4, waiting for transfers between devices: 8.21 us -> 6.72 us  [halving_sum(): flat = keep + lax.ppermute(send, axis, pairs)]
    ppermute x6 -> x4, starting transfers between devices: 4.71 us -> 3.27 us  [halving_sum(): other = lax.ppermute(flat, axis, pairs)]
    dot_general x1, matrix products: 3.98 us -> 2.74 us  [spread_adjoint(): jnp.einsum('cikq,iapkq->ciap', mixed, band, preferred_element_type=jnp.fl...]
    convert_element_type x1, other arithmetic: 1.16 us -> 0.04 us  [body(): state_grad = spread_adjoint(first_mixed, near_band).astype(jnp.bfloat16)]
  transfers between devices with their start and end apart: 19 -> 17, of which waited for: 14 -> 13; matrix products, arithmetic and copies ran while one was open for 16% -> 13% of each run, Pallas kernels for 0% -> 0%
where the time goes in v13:
time: 84.5 us; the launch traced here: 84.1 us
  waiting for transfers between devices  37.4 us (44%)
  starting transfers between devices  18 us (21%)
  matrix products  16.6 us (20%)
  local copies, waits for them, and re-layouts  7.2 us (9%)
  other arithmetic  3.95 us (5%)
  between operations  1.01 us (1%)
    ppermute x6, waiting for transfers between devices, halving_sum(): flat = flat + lax.ppermute(flat, axis, pairs)  18.6 us
    dot_general x3, matrix products, band_of(): jnp.einsum('kiad,dpq->iapkq', stencil, lon_picker(col_count, first_source...  7.41 us
    ppermute x4, waiting for transfers between devices, halving_sum(): flat = keep + lax.ppermute(send, axis, pairs)  6.72 us
    unnamed x16, local copies, waits for them, and re-layouts  5.89 us
    ppermute x1, waiting for transfers between devices, lat_halo(): other = lax.ppermute(block, 'lat', [(0, 1), (1, 0)])  5.85 us
    ppermute x1, starting transfers between devices, lon_halo(): lax.ppermute(block[..., :width], 'lon', [(i, (i - 1) % count) for i in ra...  5.13 us
    ppermute x6, starting transfers between devices, halving_sum(): flat = flat + lax.ppermute(flat, axis, pairs)  4.75 us
    ppermute x1, waiting for transfers between devices, lon_halo(): lax.ppermute(block[..., cols - width:], 'lon', [(i, (i + 1) % count) for...  3.28 us
  transfers between devices with their start and end apart: 17, of which 13 were waited for; matrix products, arithmetic and copies ran while one was open for 13% of the time, Pallas kernels for 0%

profile of v13, /device:TPU:0, one launch (start us, length us, event | category | flops | bytes accessed | tf_op | source)
XLA Modules:
  0.0 84.1 jit_solution(15528180214036425328)
XLA Ops:
  0.6 1.1 %copy.26 = bf16[1,256,2,128]{1,3,2,0:T(8,128)(2,1)S(1)} copy(bf16[1,256,2,128]{3,2,1,0:T(2,128)(2,1)} %param.13) | data formatting | bytes 262144 | tf_op args[6]
  1.7 1.0 %copy.25 = bf16[1,256,2,128]{1,3,2,0:T(8,128)(2,1)S(1)} copy(bf16[1,256,2,128]{3,2,1,0:T(2,128)(2,1)} %param.7) | data formatting | bytes 262144 | tf_op args[0]
  2.8 5.1 %collective-permute-start.1 = (bf16[512,2,8]{0,2,1:T(8,128)(2,1)S(1)}, bf16[512,2,8]{0,2,1:T(8,128)(2,1)S(1)}, u32[]{:S(2)}, u32[]{:S(2)}) collective-permute-start(bf16[512,2,8]{0,2,1:T(8,128)(2,1)S(1)} %get-tuple-element.39), channel_id=1, source_target_pairs={{0,3},{1,0},{2,1},{3,2},{4,7},{5,4},{6,5},{7,6},{8,11},{9,8},{10,9... | collective-permute-start | bytes 49160 | tf_op jit(solution)/shard_map/ppermute | solution.py:76
  7.9 0.1 fusion.42
  8.0 0.7 broadcast_add_fusion
  8.7 0.9 %convolution_convert_fusion.2 = bf16[3,2,3,9]{3,2,1,0:T(4,128)(2,1)S(1)} fusion(s32[2,3,12]{2,0,1:T(2,128)S(1)} %get-tuple-element.40, f32[2,3,12]{2,0,1:T(2,128)} %param.10, s32[2,3,12]{2,0,1:T(2,128)S(1)} %get-tuple-element.41), kind=kOutput, calls=%fused_computation.38 | convolution fusion | flops 24570 | bytes 1188 | tf_op jit(solution)/shard_map/rks,rksa,rksd->krad/dot_general | solution.py:85
  9.6 0.1 reshape.71
  9.7 0.2 fusion.29
  10.0 0.1 copy.28
  10.1 3.3 %collective-permute-done = bf16[512,2,8]{0,2,1:T(8,128)(2,1)S(1)} collective-permute-done((bf16[512,2,8]{0,2,1:T(8,128)(2,1)S(1)}, bf16[512,2,8]{0,2,1:T(8,128)(2,1)S(1)}, u32[]{:S(2)}, u32[]{:S(2)}) %collective-permute-start) | collective-permute-done | bytes 16416 | tf_op jit(solution)/shard_map/ppermute | solution.py:75
  13.5 1.6 %collective-permute-start.2 = (bf16[513,2,144]{0,2,1:T(8,128)(2,1)S(1)}, bf16[513,2,144]{0,2,1:T(8,128)(2,1)S(1)}, u32[]{:S(2)}, u32[]{:S(2)}) collective-permute-start(bf16[513,2,144]{0,2,1:T(8,128)(2,1)S(1)} %pad_maximum_fusion), channel_id=1, source_target_pairs={{0,4},{4,0},{1,5},{5,1},{2,6},{6,2},{3,7},{7,3},{8,12},{12,8},{9,1... | collective-permute-start | bytes 886472 | tf_op jit(solution)/shard_map/ppermute | solution.py:55
  15.1 1.5 %fusion.34 = bf16[136,128,3,2,3]{1,4,3,2,0:T(4,128)(2,1)} fusion(pred[9,136,128,1,1]{2,1,0,3,4:T(8,128)(4,1)S(1)} %fusion.42, bf16[3,2,3,9]{3,2,1,0:T(4,128)(2,1)S(1)} %convolution_convert_fusion.2), kind=kOutput, calls=%fused_computation.36 | convolution fusion | flops 5640192 | bytes 783684 | tf_op jit(solution)/shard_map/kiad,dpq->iapkq/dot_general | solution.py:104
  16.6 5.9 %collective-permute-done.2 = bf16[513,2,144]{0,2,1:T(8,128)(2,1)S(1)} collective-permute-done((bf16[513,2,144]{0,2,1:T(8,128)(2,1)S(1)}, bf16[513,2,144]{0,2,1:T(8,128)(2,1)S(1)}, u32[]{:S(2)}, u32[]{:S(2)}) %collective-permute-start.2) | collective-permute-done | bytes 295520 | tf_op jit(solution)/shard_map/ppermute | solution.py:55
  22.4 0.1 broadcast_select_fusion.1
  22.5 0.2 maximum_reduce_fusion
  22.6 0.1 reshape_squeeze.3
  22.8 3.0 %convert_bitcast_fusion = bf16[4,3,144,3,136]{2,0,1,3,4:T(4,128)(2,1)} fusion(bf16[3,6,3,9]{3,1,2,0:T(8,128)(2,1)S(1)} %bitcast.203), kind=kOutput, calls=%fused_computation.8 | convolution fusion | flops 13747968 | bytes 1419264 | tf_op jit(solution)/shard_map/kiad,dpq->iapkq/dot_general | solution.py:104
  25.7 2.9 %fusion.10 = bf16[136,144,3,4,3]{1,3,4,2,0:T(4,128)(2,1)} fusion(pred[9,136,144,1,1]{2,1,0,3,4:T(8,128)(4,1)S(1)} %fusion.29, bf16[3,6,3,9]{3,1,2,0:T(8,128)(2,1)S(1)} %bitcast.204, pred[]{:T(512)S(6)} %eq.64), kind=kOutput, calls=%fused_computation.12 | convolution fusion | flops 12690756 | bytes 1587277 | tf_op jit(solution)/shard_map/kiad,dpq->iapkq/dot_general | solution.py:104
  28.7 2.7 %fusion.19 = f32[256,4,3,136]{0,3,1,2:T(8,128)S(1)} fusion(bf16[3,256,256]{2,1,0:T(8,128)(2,1)} %param.9, bf16[513,2,144]{0,2,1:T(8,128)(2,1)S(1)} %get-tuple-element.31, bf16[1,2,144]{0,2,1:T(8,128)(2,1)S(1)} %copy.28, bf16[512,2,8]{0,2,1:T(8,128)(2,1)S(1)} %collective-permute-done.1, bf16[512,2,8]{0,2,1:T(8,128)(2,1)S(1)} %collective-permute-done, ...), kind=kOutput, calls=%fused_computation.16 | convolution fusion | flops 591593472 | bytes 4360897 | tf_op jit(solution)/shard_map/cikq,iapkq->ciap/dot_general | solution.py:137
  31.4 0.1 slice_bitcast_fusion.2
  31.4 0.1 fusion.56
  31.6 0.1 maximum_bitcast_fusion.4
  31.7 1.5 %copy-done.1 = bf16[4,3,144,3,136]{2,0,1,3,4:T(4,128)(2,1)S(1)} copy-done((bf16[4,3,144,3,136]{2,0,1,3,4:T(4,128)(2,1)S(1)}, bf16[4,3,144,3,136]{2,0,1,3,4:T(4,128)(2,1)}, u32[]{:S(2)}) %copy-start.1) | copy-done | bytes 1410072
  33.1 0.8 fusion.24
  33.9 0.8 fusion.46
  34.8 0.3 fusion.28
  35.1 0.3 copy-done.5
  35.4 0.1 collective-permute-start.4
  35.5 0.4 copy-done.4
  36.0 0.4 fusion.31
  36.4 0.3 fusion.27
  36.7 0.8 constant_dynamic-slice_fusion.3
  37.5 0.1 collective-permute-start.3
  37.6 1.6 %collective-permute-start.5 = (f32[192,256]{1,0:T(8,128)S(1)}, f32[192,256]{1,0:T(8,128)S(1)}, u32[]{:S(2)}, u32[]{:S(2)}) collective-permute-start(f32[192,256]{1,0:T(8,128)S(1)} %constant_dynamic-slice_fusion.1), channel_id=1, source_target_pairs={{0,16},{8,24},{16,0},{24,8},{1,17},{9,25},{17,1},{25,9},{2,18},{10... | collective-permute-start | bytes 589832 | tf_op jit(solution)/shard_map/ppermute | solution.py:31
  39.2 0.2 collective-permute-done.3
  39.5 1.6 %collective-permute-start.11 = (f32[192,256]{1,0:T(8,128)S(1)}, f32[192,256]{1,0:T(8,128)S(1)}, u32[]{:S(2)}, u32[]{:S(2)}) collective-permute-start(f32[192,256]{1,0:T(8,128)S(1)} %constant_dynamic-slice_fusion), channel_id=1, source_target_pairs={{0,16},{8,24},{16,0},{24,8},{1,17},{9,25},{17,1},{25,9},{2,18},{10... | collective-permute-start | bytes 589832 | tf_op jit(solution)/shard_map/ppermute | solution.py:31
  41.0 4.4 %collective-permute-done.5 = f32[192,256]{1,0:T(8,128)S(1)} collective-permute-done((f32[192,256]{1,0:T(8,128)S(1)}, f32[192,256]{1,0:T(8,128)S(1)}, u32[]{:S(2)}, u32[]{:S(2)}) %collective-permute-start.5) | collective-permute-done | bytes 196640 | tf_op jit(solution)/shard_map/ppermute | solution.py:31
  45.5 1.6 %collective-permute-start.6 = (f32[192,256]{1,0:T(8,128)S(1)}, f32[192,256]{1,0:T(8,128)S(1)}, u32[]{:S(2)}, u32[]{:S(2)}) collective-permute-start(f32[192,256]{1,0:T(8,128)S(1)} %dynamic-slice_add_fusion.3), channel_id=1, source_target_pairs={{0,4},{4,0},{1,5},{5,1},{2,6},{6,2},{3,7},{7,3},{8,12},{12,8},{9,1... | collective-permute-start | bytes 589832 | tf_op jit(solution)/shard_map/ppermute | solution.py:37
  47.1 2.1 %collective-permute-done.11 = f32[192,256]{1,0:T(8,128)S(1)} collective-permute-done((f32[192,256]{1,0:T(8,128)S(1)}, f32[192,256]{1,0:T(8,128)S(1)}, u32[]{:S(2)}, u32[]{:S(2)}) %collective-permute-start.11) | collective-permute-done | bytes 196640 | tf_op jit(solution)/shard_map/ppermute | solution.py:31
  49.2 1.6 %collective-permute-start.12 = (f32[192,256]{1,0:T(8,128)S(1)}, f32[192,256]{1,0:T(8,128)S(1)}, u32[]{:S(2)}, u32[]{:S(2)}) collective-permute-start(f32[192,256]{1,0:T(8,128)S(1)} %dynamic-slice_add_fusion.2), channel_id=1, source_target_pairs={{0,4},{4,0},{1,5},{5,1},{2,6},{6,2},{3,7},{7,3},{8,12},{12,8},{9,1... | collective-permute-start | bytes 589832 | tf_op jit(solution)/shard_map/ppermute | solution.py:37
  50.8 0.7 collective-permute-done.6
  51.5 0.1 collective-permute-start.7
  51.5 2.7 %fusion.14 = f32[256,4,3,144]{0,3,2,1:T(8,128)S(1)} fusion(bf16[4,3,144,3,136]{2,0,1,3,4:T(4,128)(2,1)} %convert_bitcast_fusion, bf16[3,256,256]{2,1,0:T(8,128)(2,1)S(1)} %copy-done, bf16[256,4,136]{0,2,1:T(8,128)(2,1)} %copy-done.5), kind=kOutput, calls=%fused_computation.15 | convolution fusion | flops 575299584 | bytes 3851264 | tf_op jit(solution)/shard_map/cikq,iapkq->ciap/dot_general | solution.py:124
  54.3 1.3 %collective-permute-done.12 = f32[192,256]{1,0:T(8,128)S(1)} collective-permute-done((f32[192,256]{1,0:T(8,128)S(1)}, f32[192,256]{1,0:T(8,128)S(1)}, u32[]{:S(2)}, u32[]{:S(2)}) %collective-permute-start.12) | collective-permute-done | bytes 196640 | tf_op jit(solution)/shard_map/ppermute | solution.py:37
  55.7 0.7 collective-permute-start.13
  56.4 0.9 %collective-permute-done.7 = f32[192,256]{1,0:T(8,128)S(1)} collective-permute-done((f32[192,256]{1,0:T(8,128)S(1)}, f32[192,256]{1,0:T(8,128)S(1)}, u32[]{:S(2)}, u32[]{:S(2)}) %collective-permute-start.7) | collective-permute-done | bytes 196640 | tf_op jit(solution)/shard_map/ppermute | solution.py:37
  57.4 0.5 collective-permute-start.8
  57.9 6.3 %collective-permute-done.13 = f32[192,256]{1,0:T(8,128)S(1)} collective-permute-done((f32[192,256]{1,0:T(8,128)S(1)}, f32[192,256]{1,0:T(8,128)S(1)}, u32[]{:S(2)}, u32[]{:S(2)}) %collective-permute-start.13) | collective-permute-done | bytes 196640 | tf_op jit(solution)/shard_map/ppermute | solution.py:37
  64.2 0.3 collective-permute-start.14
  64.5 8.1 %collective-permute-done.8 = f32[192,256]{1,0:T(8,128)S(1)} collective-permute-done((f32[192,256]{1,0:T(8,128)S(1)}, f32[192,256]{1,0:T(8,128)S(1)}, u32[]{:S(2)}, u32[]{:S(2)}) %collective-permute-start.8) | collective-permute-done | bytes 196640 | tf_op jit(solution)/shard_map/ppermute | solution.py:37
  72.7 1.6 %collective-permute-start.9 = (bf16[192,256]{1,0:T(8,128)(2,1)S(1)}, bf16[192,256]{1,0:T(8,128)(2,1)S(1)}, u32[]{:S(2)}, u32[]{:S(2)}) collective-permute-start(bf16[192,256]{1,0:T(8,128)(2,1)S(1)} %add_convert_fusion.1), channel_id=1, source_target_pairs={{0,16},{8,24},{16,0},{24,8},{1,17},{9,25},{17,1},{25,9},{2,18},{10... | collective-permute-start | bytes 294920 | tf_op jit(solution)/shard_map/ppermute | solution.py:42
  74.2 1.2 %collective-permute-done.14 = f32[192,256]{1,0:T(8,128)S(1)} collective-permute-done((f32[192,256]{1,0:T(8,128)S(1)}, f32[192,256]{1,0:T(8,128)S(1)}, u32[]{:S(2)}, u32[]{:S(2)}) %collective-permute-start.14) | collective-permute-done | bytes 196640 | tf_op jit(solution)/shard_map/ppermute | solution.py:37
  75.5 1.6 %collective-permute-start.15 = (bf16[192,256]{1,0:T(8,128)(2,1)S(1)}, bf16[192,256]{1,0:T(8,128)(2,1)S(1)}, u32[]{:S(2)}, u32[]{:S(2)}) collective-permute-start(bf16[192,256]{1,0:T(8,128)(2,1)S(1)} %add_convert_fusion), channel_id=1, source_target_pairs={{0,16},{8,24},{16,0},{24,8},{1,17},{9,25},{17,1},{25,9},{2,18},{10... | collective-permute-start | bytes 294920 | tf_op jit(solution)/shard_map/ppermute | solution.py:42
  77.0 0.9 %collective-permute-done.9 = bf16[192,256]{1,0:T(8,128)(2,1)S(1)} collective-permute-done((bf16[192,256]{1,0:T(8,128)(2,1)S(1)}, bf16[192,256]{1,0:T(8,128)(2,1)S(1)}, u32[]{:S(2)}, u32[]{:S(2)}) %collective-permute-start.9) | collective-permute-done | bytes 98336 | tf_op jit(solution)/shard_map/ppermute | solution.py:42
  77.9 0.1 fusion.97
  78.0 0.1 collective-permute-start.10
  78.1 2.1 %collective-permute-done.15 = bf16[192,256]{1,0:T(8,128)(2,1)S(1)} collective-permute-done((bf16[192,256]{1,0:T(8,128)(2,1)S(1)}, bf16[192,256]{1,0:T(8,128)(2,1)S(1)}, u32[]{:S(2)}, u32[]{:S(2)}) %collective-permute-start.15) | collective-permute-done | bytes 98336 | tf_op jit(solution)/shard_map/ppermute | solution.py:42
  80.1 0.1 fusion.96
  80.2 0.1 collective-permute-start.16
  80.3 0.3 fusion.33
  80.6 0.8 copy.40
  81.4 0.8 copy.41
  82.2 0.9 %maximum_select_fusion = f32[768,256]{1,0:T(8,128)} fusion(f32[384,256]{1,0:T(8,128)S(1)} %get-tuple-element.22, f32[384,256]{1,0:T(8,128)S(1)} %convert_element_type.134, pred[]{:T(512)S(6)} %eq.66), kind=kLoop, calls=%fused_computation.46 | loop fusion | flops 589824 | bytes 1572865 | tf_op jit(solution)/shard_map/jit(_where)/select_n | solution.py:45
  83.2 0.9 %maximum_select_fusion.1 = f32[768,256]{1,0:T(8,128)} fusion(f32[384,256]{1,0:T(8,128)S(1)} %get-tuple-element.20, f32[384,256]{1,0:T(8,128)S(1)} %convert_element_type.137, pred[]{:T(512)S(6)} %eq.66), kind=kLoop, calls=%fused_computation.47 | loop fusion | flops 589824 | bytes 1572865 | tf_op jit(solution)/shard_map/jit(_where)/select_n | solution.py:45
  (39 shorter events, 0.6 us)
Async XLA Ops:
  0.6 33.3 %copy-start = (bf16[3,256,256]{2,1,0:T(8,128)(2,1)S(1)}, bf16[3,256,256]{2,1,0:T(8,128)(2,1)}, u32[]{:S(2)}) copy-start(bf16[3,256,256]{2,1,0:T(8,128)(2,1)} %param.8) | copy-start | bytes 1179652
  2.8 7.4 %collective-permute-start.1 = (bf16[512,2,8]{0,2,1:T(8,128)(2,1)S(1)}, bf16[512,2,8]{0,2,1:T(8,128)(2,1)S(1)}, u32[]{:S(2)}, u32[]{:S(2)}) collective-permute-start(bf16[512,2,8]{0,2,1:T(8,128)(2,1)S(1)} %get-tuple-element.39), channel_id=1, source_target_pairs={{0,3},{1,0},{2,1},{3,2},{4,7},{5,4},{6,5},{7,6},{8,11},{9,8},{10,9... | collective-permute-start | bytes 49160 | tf_op jit(solution)/shard_map/ppermute | solution.py:76
  7.9 5.5 %collective-permute-start = (bf16[512,2,8]{0,2,1:T(8,128)(2,1)S(1)}, bf16[512,2,8]{0,2,1:T(8,128)(2,1)S(1)}, u32[]{:S(2)}, u32[]{:S(2)}) collective-permute-start(bf16[512,2,8]{0,2,1:T(8,128)(2,1)S(1)} %get-tuple-element.38), channel_id=1, source_target_pairs={{0,1},{1,2},{2,3},{3,0},{4,5},{5,6},{6,7},{7,4},{8,9},{9,10},{10,1... | collective-permute-start | bytes 49160 | tf_op jit(solution)/shard_map/ppermute | solution.py:75
  13.5 9.0 %collective-permute-start.2 = (bf16[513,2,144]{0,2,1:T(8,128)(2,1)S(1)}, bf16[513,2,144]{0,2,1:T(8,128)(2,1)S(1)}, u32[]{:S(2)}, u32[]{:S(2)}) collective-permute-start(bf16[513,2,144]{0,2,1:T(8,128)(2,1)S(1)} %pad_maximum_fusion), channel_id=1, source_target_pairs={{0,4},{4,0},{1,5},{5,1},{2,6},{6,2},{3,7},{7,3},{8,12},{12,8},{9,1... | collective-permute-start | bytes 886472 | tf_op jit(solution)/shard_map/ppermute | solution.py:55
  31.4 1.7 %copy-start.1 = (bf16[4,3,144,3,136]{2,0,1,3,4:T(4,128)(2,1)S(1)}, bf16[4,3,144,3,136]{2,0,1,3,4:T(4,128)(2,1)}, u32[]{:S(2)}) copy-start(bf16[4,3,144,3,136]{2,0,1,3,4:T(4,128)(2,1)} %convert_bitcast_fusion) | copy-start | bytes 4230148
  34.7 0.7 copy-start.5
  34.7 1.3 %copy-start.4 = (bf16[136,128,3,2,3]{1,4,3,2,0:T(4,128)(2,1)S(1)}, bf16[136,128,3,2,3]{1,4,3,2,0:T(4,128)(2,1)}, u32[]{:S(2)}) copy-start(bf16[136,128,3,2,3]{1,4,3,2,0:T(4,128)(2,1)} %fusion.34) | copy-start | bytes 1880068
  34.8 1.6 %copy-start.2 = (bf16[1,256,2,128]{3,2,1,0:T(2,128)(2,1)S(1)}, bf16[1,256,2,128]{3,2,1,0:T(2,128)(2,1)}, u32[]{:S(2)}) copy-start(bf16[1,256,2,128]{3,2,1,0:T(2,128)(2,1)} %param.13) | copy-start | bytes 393220
  35.4 2.1 %collective-permute-start.4 = (f32[384,256]{1,0:T(8,128)S(1)}, f32[384,256]{1,0:T(8,128)S(1)}, u32[]{:S(2)}, u32[]{:S(2)}) collective-permute-start(f32[384,256]{1,0:T(8,128)S(1)} %constant_dynamic-slice_fusion.2), channel_id=1, source_target_pairs={{0,8},{8,0},{16,24},{24,16},{1,9},{9,1},{17,25},{25,17},{2,10},{10... | collective-permute-start | bytes 1179656 | tf_op jit(solution)/shard_map/ppermute | solution.py:31
  37.5 1.9 %collective-permute-start.3 = (f32[384,256]{1,0:T(8,128)}, f32[384,256]{1,0:T(8,128)S(1)}, u32[]{:S(2)}, u32[]{:S(2)}) collective-permute-start(f32[384,256]{1,0:T(8,128)} %constant_dynamic-slice_fusion.3), channel_id=1, source_target_pairs={{0,8},{8,0},{16,24},{24,16},{1,9},{9,1},{17,25},{25,17},{2,10},{10... | collective-permute-start | bytes 1179656 | tf_op jit(solution)/shard_map/ppermute | solution.py:31
  37.6 7.8 %collective-permute-start.5 = (f32[192,256]{1,0:T(8,128)S(1)}, f32[192,256]{1,0:T(8,128)S(1)}, u32[]{:S(2)}, u32[]{:S(2)}) collective-permute-start(f32[192,256]{1,0:T(8,128)S(1)} %constant_dynamic-slice_fusion.1), channel_id=1, source_target_pairs={{0,16},{8,24},{16,0},{24,8},{1,17},{9,25},{17,1},{25,9},{2,18},{10... | collective-permute-start | bytes 589832 | tf_op jit(solution)/shard_map/ppermute | solution.py:31
  39.5 9.7 %collective-permute-start.11 = (f32[192,256]{1,0:T(8,128)S(1)}, f32[192,256]{1,0:T(8,128)S(1)}, u32[]{:S(2)}, u32[]{:S(2)}) collective-permute-start(f32[192,256]{1,0:T(8,128)S(1)} %constant_dynamic-slice_fusion), channel_id=1, source_target_pairs={{0,16},{8,24},{16,0},{24,8},{1,17},{9,25},{17,1},{25,9},{2,18},{10... | collective-permute-start | bytes 589832 | tf_op jit(solution)/shard_map/ppermute | solution.py:31
  45.5 6.0 %collective-permute-start.6 = (f32[192,256]{1,0:T(8,128)S(1)}, f32[192,256]{1,0:T(8,128)S(1)}, u32[]{:S(2)}, u32[]{:S(2)}) collective-permute-start(f32[192,256]{1,0:T(8,128)S(1)} %dynamic-slice_add_fusion.3), channel_id=1, source_target_pairs={{0,4},{4,0},{1,5},{5,1},{2,6},{6,2},{3,7},{7,3},{8,12},{12,8},{9,1... | collective-permute-start | bytes 589832 | tf_op jit(solution)/shard_map/ppermute | solution.py:37
  49.2 6.5 %collective-permute-start.12 = (f32[192,256]{1,0:T(8,128)S(1)}, f32[192,256]{1,0:T(8,128)S(1)}, u32[]{:S(2)}, u32[]{:S(2)}) collective-permute-start(f32[192,256]{1,0:T(8,128)S(1)} %dynamic-slice_add_fusion.2), channel_id=1, source_target_pairs={{0,4},{4,0},{1,5},{5,1},{2,6},{6,2},{3,7},{7,3},{8,12},{12,8},{9,1... | collective-permute-start | bytes 589832 | tf_op jit(solution)/shard_map/ppermute | solution.py:37
  51.5 5.9 %collective-permute-start.7 = (f32[192,256]{1,0:T(8,128)S(1)}, f32[192,256]{1,0:T(8,128)S(1)}, u32[]{:S(2)}, u32[]{:S(2)}) collective-permute-start(f32[192,256]{1,0:T(8,128)S(1)} %add.163), channel_id=1, source_target_pairs={{0,1},{1,0},{2,3},{3,2},{4,5},{5,4},{6,7},{7,6},{8,9},{9,8},{10,11... | collective-permute-start | bytes 589832 | tf_op jit(solution)/shard_map/ppermute | solution.py:37
  54.3 26.0 %copy-start.3 = (bf16[3,256,256]{2,1,0:T(8,128)(2,1)S(1)}, bf16[3,256,256]{2,1,0:T(8,128)(2,1)}, u32[]{:S(2)}) copy-start(bf16[3,256,256]{2,1,0:T(8,128)(2,1)} %param.9) | copy-start | bytes 1179652
  55.7 8.5 %collective-permute-start.13 = (f32[192,256]{1,0:T(8,128)S(1)}, f32[192,256]{1,0:T(8,128)S(1)}, u32[]{:S(2)}, u32[]{:S(2)}) collective-permute-start(f32[192,256]{1,0:T(8,128)S(1)} %add.167), channel_id=1, source_target_pairs={{0,1},{1,0},{2,3},{3,2},{4,5},{5,4},{6,7},{7,6},{8,9},{9,8},{10,11... | collective-permute-start | bytes 589832 | tf_op jit(solution)/shard_map/ppermute | solution.py:37
  57.4 15.3 %collective-permute-start.8 = (f32[192,256]{1,0:T(8,128)S(1)}, f32[192,256]{1,0:T(8,128)S(1)}, u32[]{:S(2)}, u32[]{:S(2)}) collective-permute-start(f32[192,256]{1,0:T(8,128)S(1)} %add.164), channel_id=1, source_target_pairs={{0,2},{1,3},{2,0},{3,1},{4,6},{5,7},{6,4},{7,5},{8,10},{9,11},{10,... | collective-permute-start | bytes 589832 | tf_op jit(solution)/shard_map/ppermute | solution.py:37
  64.2 11.2 %collective-permute-start.14 = (f32[192,256]{1,0:T(8,128)S(1)}, f32[192,256]{1,0:T(8,128)S(1)}, u32[]{:S(2)}, u32[]{:S(2)}) collective-permute-start(f32[192,256]{1,0:T(8,128)S(1)} %add.168), channel_id=1, source_target_pairs={{0,2},{1,3},{2,0},{3,1},{4,6},{5,7},{6,4},{7,5},{8,10},{9,11},{10,... | collective-permute-start | bytes 589832 | tf_op jit(solution)/shard_map/ppermute | solution.py:37
  72.7 5.2 %collective-permute-start.9 = (bf16[192,256]{1,0:T(8,128)(2,1)S(1)}, bf16[192,256]{1,0:T(8,128)(2,1)S(1)}, u32[]{:S(2)}, u32[]{:S(2)}) collective-permute-start(bf16[192,256]{1,0:T(8,128)(2,1)S(1)} %add_convert_fusion.1), channel_id=1, source_target_pairs={{0,16},{8,24},{16,0},{24,8},{1,17},{9,25},{17,1},{25,9},{2,18},{10... | collective-permute-start | bytes 294920 | tf_op jit(solution)/shard_map/ppermute | solution.py:42
  75.5 4.7 %collective-permute-start.15 = (bf16[192,256]{1,0:T(8,128)(2,1)S(1)}, bf16[192,256]{1,0:T(8,128)(2,1)S(1)}, u32[]{:S(2)}, u32[]{:S(2)}) collective-permute-start(bf16[192,256]{1,0:T(8,128)(2,1)S(1)} %add_convert_fusion), channel_id=1, source_target_pairs={{0,16},{8,24},{16,0},{24,8},{1,17},{9,25},{17,1},{25,9},{2,18},{10... | collective-permute-start | bytes 294920 | tf_op jit(solution)/shard_map/ppermute | solution.py:42
  78.0 4.2 %collective-permute-start.10 = (bf16[384,256]{1,0:T(8,128)(2,1)S(1)}, bf16[384,256]{1,0:T(8,128)(2,1)S(1)}, u32[]{:S(2)}, u32[]{:S(2)}) collective-permute-start(bf16[384,256]{1,0:T(8,128)(2,1)S(1)} %get-tuple-element.23), channel_id=1, source_target_pairs={{0,8},{8,0},{16,24},{24,16},{1,9},{9,1},{17,25},{25,17},{2,10},{10... | collective-permute-start | bytes 589832 | tf_op jit(solution)/shard_map/ppermute | solution.py:42
  80.2 2.9 %collective-permute-start.16 = (bf16[384,256]{1,0:T(8,128)(2,1)S(1)}, bf16[384,256]{1,0:T(8,128)(2,1)S(1)}, u32[]{:S(2)}, u32[]{:S(2)}) collective-permute-start(bf16[384,256]{1,0:T(8,128)(2,1)S(1)} %get-tuple-element.21), channel_id=1, source_target_pairs={{0,8},{8,0},{16,24},{24,16},{1,9},{9,1},{17,25},{25,17},{2,10},{10... | collective-permute-start | bytes 589832 | tf_op jit(solution)/shard_map/ppermute | solution.py:42

commit v14 on v11

--- a/solution.py
+++ b/solution.py
@@ -190,6 +190,15 @@
     own_gradient = gradient_wide[:, LAT_HALO : LAT_HALO + row_count, LON_HALO : LON_HALO + col_count]
     second_sum = filter_term(own_gradient, second_spread)
 
+    member_total = state_field.shape[0] * lax.axis_size("ens")
+    grad_scale = 1.0 / math.sqrt(
+        member_total * row_count * lax.axis_size("lat") * col_count * lax.axis_size("lon")
+    )
+    axes = ("ens", "lat", "lon")
+    second_grad, (second_spread, gradient_wide) = halving_sum(
+        second_sum * grad_scale, axes, hold=(second_spread, gradient_wide)
+    )
+
     if lax.axis_size("lat") == 2 and row_count == LAT_HALO:
         lower = lax.axis_index("lat") == 0
         grid_gradient = jnp.where(lower, gradient_wide[:, row_count:], gradient_wide[:, : 2 * row_count])
@@ -211,12 +220,6 @@
     own_hidden_grad = hidden_grad[:, LAT_REACH : LAT_REACH + row_count, LON_REACH : LON_REACH + col_count]
     own_first = first_near[:, LAT_REACH : LAT_REACH + row_count, :, LON_REACH : LON_REACH + col_count]
     first_sum = filter_term(own_hidden_grad, own_first)
-    member_total = state_field.shape[0] * lax.axis_size("ens")
-    grad_scale = 1.0 / math.sqrt(
-        member_total * row_count * lax.axis_size("lat") * col_count * lax.axis_size("lon")
-    )
-    axes = ("ens", "lat", "lon")
-    second_grad, second_spread = halving_sum(second_sum * grad_scale, axes, hold=second_spread)
     first_grad, hidden_grad = halving_sum(first_sum * grad_scale, axes, hold=hidden_grad)
     layer_output = mix_channels(second_weight, second_spread).astype(jnp.bfloat16)
     first_mixed = unmix(first_weight, hidden_grad)

time: 81.7 us -> 86 us (1.053)
  waiting for transfers between devices: 32.2 us -> 23.2 us
  other arithmetic: 5.01 us -> 11.9 us
  starting transfers between devices: 18.2 us -> 22.4 us
  local copies, waits for them, and re-layouts: 7.06 us -> 9.61 us
    ppermute x4, waiting for transfers between devices: 9.36 us -> 3.48 us  [halving_sum(): flat = flat + lax.ppermute(flat, axis, pairs)]
    dot_general x3, matrix products: 7.43 us -> 3.52 us  [band_of(): jnp.einsum('kiad,dpq->iapkq', stencil, lon_picker(col_count, first_source...]
    add x6, other arithmetic: 0.18 us -> 3.85 us  [halving_sum(): flat = keep + lax.ppermute(send, axis, pairs)]
    ppermute x4, starting transfers between devices: 0.88 us -> 4.07 us  [halving_sum(): flat = flat + lax.ppermute(flat, axis, pairs)]
    ppermute x6, waiting for transfers between devices: 8.21 us -> 5.68 us  [halving_sum(): flat = keep + lax.ppermute(send, axis, pairs)]
    dot_general x2, matrix products: 1.09 us -> 3.24 us  [mix_channels(): jnp.einsum('koc,cikj->oij', weight, spreaded, preferred_element_type=jnp....]
    ppermute x6, starting transfers between devices: 4.71 us -> 6.39 us  [halving_sum(): other = lax.ppermute(flat, axis, pairs)]
    ppermute x6, waiting for transfers between devices: 5.48 us -> 3.99 us  [halving_sum(): other = lax.ppermute(flat, axis, pairs)]
  transfers between devices with their start and end apart: 19 -> 19, of which waited for: 14 -> 10; matrix products, arithmetic and copies ran while one was open for 16% -> 27% of each run, Pallas kernels for 0% -> 0%
where the time goes in v14:
time: 86 us; the launch traced here: 85.5 us
  waiting for transfers between devices  23.2 us (27%)
  starting transfers between devices  22.4 us (26%)
  matrix products  17.2 us (20%)
  other arithmetic  11.9 us (14%)
  local copies, waits for them, and re-layouts  9.61 us (11%)
  between operations  1.06 us (1%)
    ppermute x1, waiting for transfers between devices, lat_halo(): other = lax.ppermute(block, 'lat', [(0, 1), (1, 0)])  6.79 us
    unnamed x26, local copies, waits for them, and re-layouts  6.42 us
    ppermute x6, starting transfers between devices, halving_sum(): other = lax.ppermute(flat, axis, pairs)  6.39 us
    ppermute x6, waiting for transfers between devices, halving_sum(): flat = keep + lax.ppermute(send, axis, pairs)  5.68 us
    ppermute x6, starting transfers between devices, halving_sum(): flat = keep + lax.ppermute(send, axis, pairs)  5.27 us
    ppermute x1, starting transfers between devices, lon_halo(): lax.ppermute(block[..., :width], 'lon', [(i, (i - 1) % count) for i in ra...  5.13 us
    ppermute x4, starting transfers between devices, halving_sum(): flat = flat + lax.ppermute(flat, axis, pairs)  4.07 us
    ppermute x6, waiting for transfers between devices, halving_sum(): other = lax.ppermute(flat, axis, pairs)  3.99 us
  transfers between devices with their start and end apart: 19, of which 10 were waited for; matrix products, arithmetic and copies ran while one was open for 27% of the time, Pallas kernels for 0%

profile of v14, /device:TPU:0, one launch (start us, length us, event | category | flops | bytes accessed | tf_op | source)
XLA Modules:
  0.0 85.5 jit_solution(4916266684836471332)
XLA Ops:
  0.6 1.1 %copy.26 = bf16[1,256,2,128]{1,3,2,0:T(8,128)(2,1)S(1)} copy(bf16[1,256,2,128]{3,2,1,0:T(2,128)(2,1)} %param.13) | data formatting | bytes 262144 | tf_op args[6]
  1.7 1.0 %copy.25 = bf16[1,256,2,128]{1,3,2,0:T(8,128)(2,1)S(1)} copy(bf16[1,256,2,128]{3,2,1,0:T(2,128)(2,1)} %param.7) | data formatting | bytes 262144 | tf_op args[0]
  2.8 5.1 %collective-permute-start.1 = (bf16[512,2,8]{0,2,1:T(8,128)(2,1)S(1)}, bf16[512,2,8]{0,2,1:T(8,128)(2,1)S(1)}, u32[]{:S(2)}, u32[]{:S(2)}) collective-permute-start(bf16[512,2,8]{0,2,1:T(8,128)(2,1)S(1)} %get-tuple-element.39), channel_id=1, source_target_pairs={{0,3},{1,0},{2,1},{3,2},{4,7},{5,4},{6,5},{7,6},{8,11},{9,8},{10,9... | collective-permute-start | bytes 49160 | tf_op jit(solution)/shard_map/ppermute | solution.py:76
  7.9 0.1 fusion.42
  8.0 0.7 broadcast_add_fusion
  8.7 0.9 %convolution_convert_fusion.2 = bf16[3,2,3,9]{3,2,1,0:T(4,128)(2,1)S(1)} fusion(s32[2,3,12]{2,0,1:T(2,128)S(1)} %get-tuple-element.42, f32[2,3,12]{2,0,1:T(2,128)} %param.10, s32[2,3,12]{2,0,1:T(2,128)S(1)} %get-tuple-element.43), kind=kOutput, calls=%fused_computation.38 | convolution fusion | flops 24570 | bytes 1188 | tf_op jit(solution)/shard_map/rks,rksa,rksd->krad/dot_general | solution.py:85
  9.6 0.1 reshape.71
  9.7 0.2 fusion.29
  10.0 0.1 copy.28
  10.1 3.3 %collective-permute-done = bf16[512,2,8]{0,2,1:T(8,128)(2,1)S(1)} collective-permute-done((bf16[512,2,8]{0,2,1:T(8,128)(2,1)S(1)}, bf16[512,2,8]{0,2,1:T(8,128)(2,1)S(1)}, u32[]{:S(2)}, u32[]{:S(2)}) %collective-permute-start) | collective-permute-done | bytes 16416 | tf_op jit(solution)/shard_map/ppermute | solution.py:75
  13.5 1.6 %collective-permute-start.2 = (bf16[513,2,144]{0,2,1:T(8,128)(2,1)S(1)}, bf16[513,2,144]{0,2,1:T(8,128)(2,1)S(1)}, u32[]{:S(2)}, u32[]{:S(2)}) collective-permute-start(bf16[513,2,144]{0,2,1:T(8,128)(2,1)S(1)} %pad_maximum_fusion.6), channel_id=1, source_target_pairs={{0,4},{4,0},{1,5},{5,1},{2,6},{6,2},{3,7},{7,3},{8,12},{12,8},{9,1... | collective-permute-start | bytes 886472 | tf_op jit(solution)/shard_map/ppermute | solution.py:55
  15.1 0.6 fusion.34
  15.6 6.8 %collective-permute-done.2 = bf16[513,2,144]{0,2,1:T(8,128)(2,1)S(1)} collective-permute-done((bf16[513,2,144]{0,2,1:T(8,128)(2,1)S(1)}, bf16[513,2,144]{0,2,1:T(8,128)(2,1)S(1)}, u32[]{:S(2)}, u32[]{:S(2)}) %collective-permute-start.2) | collective-permute-done | bytes 295520 | tf_op jit(solution)/shard_map/ppermute | solution.py:55
  22.5 0.2 maximum_reduce_fusion
  22.6 0.1 reshape_squeeze.3
  22.8 1.5 %convert_bitcast_fusion = bf16[4,3,144,3,136]{2,0,1,3,4:T(4,128)(2,1)S(1)} fusion(bf16[3,6,3,9]{3,1,2,0:T(8,128)(2,1)S(1)} %bitcast.203), kind=kOutput, calls=%fused_computation.8 | convolution fusion | flops 13747968 | bytes 1419264 | tf_op jit(solution)/shard_map/kiad,dpq->iapkq/dot_general | solution.py:104
  24.4 0.8 fusion.24
  25.1 0.6 copy-done.1
  25.8 1.3 %select_convert_fusion = (bf16[256,4,136]{0,2,1:T(8,128)(2,1)S(1)}, f32[256,4,136]{0,2,1:T(8,128)}) fusion(pred[4]{0:T(512)(128)(4,1)S(1)} %compare_and_fusion, bf16[256,4,3,136]{0,3,2,1:T(8,128)(2,1)S(1)} %fusion.24, bf16[3,256,256]{2,1,0:T(8,128)(2,1)S(1)} %copy-done), kind=kOutput, calls=%fused_computation.68 | convolution fusion | flops 215302144 | bytes 2064388 | tf_op jit(solution)/shard_map/koc,cikj->oij/dot_general | solution.py:146
  27.1 0.4 fusion.31
  27.5 0.3 fusion.27
  27.9 0.4 copy-done.3
  28.3 0.8 pad_maximum_fusion
  29.1 1.4 %fusion.10 = bf16[136,144,3,4,3]{1,3,4,2,0:T(4,128)(2,1)S(1)} fusion(pred[9,136,144,1,1]{2,1,0,3,4:T(8,128)(4,1)S(1)} %fusion.29, bf16[3,6,3,9]{3,1,2,0:T(8,128)(2,1)S(1)} %bitcast.204, pred[]{:T(512)S(6)} %eq.72), kind=kOutput, calls=%fused_computation.12 | convolution fusion | flops 12690756 | bytes 1587277 | tf_op jit(solution)/shard_map/kiad,dpq->iapkq/dot_general | solution.py:104
  30.6 3.4 %fusion.19 = f32[256,4,3,136]{0,3,1,2:T(8,128)} fusion(bf16[3,256,256]{2,1,0:T(8,128)(2,1)} %param.9, bf16[256,6,144]{0,2,1:T(8,128)(2,1)} %pad_maximum_fusion, pred[]{:T(512)S(6)} %eq.72, bf16[136,144,3,4,3]{1,3,4,2,0:T(4,128)(2,1)S(1)} %fusion.10), kind=kOutput, calls=%fused_computation.16 | convolution fusion | flops 588054528 | bytes 4064257 | tf_op jit(solution)/shard_map/cikq,iapkq->ciap/dot_general | solution.py:137
  34.1 1.3 %slice_bitcast_fusion.2 = (f32[256,3,136]{0,2,1:T(8,128)S(1)}, f32[256,3,136]{0,2,1:T(8,128)S(1)}) fusion(f32[256,4,3,136]{0,3,1,2:T(8,128)} %fusion.19), kind=kLoop, calls=%fused_computation.76 | loop fusion | bytes 1671168 | tf_op jit(solution)/shard_map/squeeze | solution.py:140
  35.3 1.2 %fusion.56 = bf16[256,4,136]{0,2,1:T(8,128)(2,1)S(1)} fusion(f32[256,4,3,136]{0,3,1,2:T(8,128)} %fusion.19, f32[256,3,136]{0,2,1:T(8,128)S(1)} %get-tuple-element.27, f32[256,3,136]{0,2,1:T(8,128)S(1)} %get-tuple-element.26), kind=kLoop, calls=%fused_computation.67 | loop fusion | flops 417792 | bytes 1671168 | tf_op jit(solution)/shard_map/convert_element_type | solution.py:208
  36.6 1.6 %collective-permute-start.12 = (f32[192,256]{1,0:T(8,128)S(1)}, f32[192,256]{1,0:T(8,128)}, u32[]{:S(2)}, u32[]{:S(2)}) collective-permute-start(f32[192,256]{1,0:T(8,128)S(1)} %constant_dynamic-slice_fusion.1), channel_id=1, source_target_pairs={{0,16},{8,24},{16,0},{24,8},{1,17},{9,25},{17,1},{25,9},{2,18},{10... | collective-permute-start | bytes 589832 | tf_op jit(solution)/shard_map/ppermute | solution.py:31
  38.1 0.4 fusion.46
  38.6 1.4 %fusion.28 = f32[256,3,256]{0,2,1:T(8,128)S(1)} fusion(bf16[256,4,3,136]{0,3,2,1:T(8,128)(2,1)} %copy-done.10, bf16[256,4,136]{0,2,1:T(8,128)(2,1)S(1)} %fusion.46), kind=kOutput, calls=%fused_computation.26 | convolution fusion | flops 100859904 | bytes 1310720 | tf_op jit(solution)/shard_map/oij,cikj->koc/dot_general | solution.py:156
  40.1 0.9 %copy-done.6 = f32[256,3,256]{0,2,1:T(8,128)} copy-done((f32[256,3,256]{0,2,1:T(8,128)}, f32[256,3,256]{0,2,1:T(8,128)S(1)}, u32[]{:S(2)}) %copy-start.6) | copy-done | bytes 786456
  40.9 0.8 constant_dynamic-slice_fusion.4
  41.7 2.0 %collective-permute-done.12 = f32[192,256]{1,0:T(8,128)} collective-permute-done((f32[192,256]{1,0:T(8,128)S(1)}, f32[192,256]{1,0:T(8,128)}, u32[]{:S(2)}, u32[]{:S(2)}) %collective-permute-start.12) | collective-permute-done | bytes 196640 | tf_op jit(solution)/shard_map/ppermute | solution.py:31
  43.7 1.0 %dynamic-slice_add_fusion.2 = f32[192,256]{1,0:T(8,128)S(1)} fusion(f32[192,256]{1,0:T(8,128)} %collective-permute-done.12, f32[384,256]{1,0:T(8,128)} %copy-done.5, s32[]{:T(128)S(6)} %select_n.179), kind=kLoop, calls=%fused_computation.113 | loop fusion | flops 49152 | bytes 589828 | tf_op jit(solution)/shard_map/add | solution.py:31
  44.8 1.6 %collective-permute-start.13 = (f32[96,256]{1,0:T(8,128)S(1)}, f32[96,256]{1,0:T(8,128)S(1)}, u32[]{:S(2)}, u32[]{:S(2)}) collective-permute-start(f32[96,256]{1,0:T(8,128)S(1)} %constant_dynamic-slice_fusion), channel_id=1, source_target_pairs={{0,4},{4,0},{1,5},{5,1},{2,6},{6,2},{3,7},{7,3},{8,12},{12,8},{9,1... | collective-permute-start | bytes 294920 | tf_op jit(solution)/shard_map/ppermute | solution.py:31
  46.4 1.2 %dynamic-slice_add_fusion = f32[384,256]{1,0:T(8,128)S(1)} fusion(f32[384,256]{1,0:T(8,128)} %collective-permute-done.4, f32[768,256]{1,0:T(8,128)} %bitcast.202, s32[]{:T(128)S(6)} %select_n.164), kind=kLoop, calls=%fused_computation.84 | loop fusion | flops 98304 | bytes 1179652 | tf_op jit(solution)/shard_map/add | solution.py:31
  47.6 1.6 %collective-permute-start.5 = (f32[192,256]{1,0:T(8,128)S(1)}, f32[192,256]{1,0:T(8,128)S(1)}, u32[]{:S(2)}, u32[]{:S(2)}) collective-permute-start(f32[192,256]{1,0:T(8,128)S(1)} %constant_dynamic-slice_fusion.3), channel_id=1, source_target_pairs={{0,16},{8,24},{16,0},{24,8},{1,17},{9,25},{17,1},{25,9},{2,18},{10... | collective-permute-start | bytes 589832 | tf_op jit(solution)/shard_map/ppermute | solution.py:31
  49.1 0.3 collective-permute-done.13
  49.5 0.7 dynamic-slice_add_fusion.4
  50.1 3.3 %collective-permute-done.5 = f32[192,256]{1,0:T(8,128)S(1)} collective-permute-done((f32[192,256]{1,0:T(8,128)S(1)}, f32[192,256]{1,0:T(8,128)S(1)}, u32[]{:S(2)}, u32[]{:S(2)}) %collective-permute-start.5) | collective-permute-done | bytes 196640 | tf_op jit(solution)/shard_map/ppermute | solution.py:31
  53.5 0.7 constant_dynamic-slice_fusion.2
  54.1 0.5 collective-permute-start.6
  54.6 2.0 %fusion.33 = bf16[1,256,2,128]{1,3,2,0:T(8,128)(2,1)} fusion(bf16[256,2,3,128]{0,3,2,1:T(8,128)(2,1)S(1)} %copy-done.4, bf16[3,256,256]{2,1,0:T(8,128)(2,1)} %param.9), kind=kOutput, calls=%fused_computation.35 | convolution fusion | flops 100728832 | bytes 917504 | tf_op jit(solution)/shard_map/koc,cikj->oij/dot_general | solution.py:146
  56.6 1.7 %copy.40 = bf16[1,256,2,128]{3,2,1,0:T(2,128)(2,1)} copy(bf16[1,256,2,128]{1,3,2,0:T(8,128)(2,1)} %fusion.33) | data formatting | bytes 262144
  58.3 1.0 %add.186 = f32[96,256]{1,0:T(8,128)S(1)} add(f32[96,256]{1,0:T(8,128)} %dynamic-slice_add_fusion.4, f32[96,256]{1,0:T(8,128)} %collective-permute-done.14) | non-fusion elementwise | flops 24576 | bytes 294912 | tf_op jit(solution)/shard_map/add | solution.py:37
  59.3 0.9 %dynamic-slice_add_fusion.5 = f32[96,256]{1,0:T(8,128)S(1)} fusion(f32[96,256]{1,0:T(8,128)} %collective-permute-done.6, f32[192,256]{1,0:T(8,128)S(1)} %dynamic-slice_add_fusion.3, s32[]{:T(128)S(6)} %select_n.181), kind=kLoop, calls=%fused_computation.128 | loop fusion | flops 24576 | bytes 294916 | tf_op jit(solution)/shard_map/add | solution.py:31
  60.2 2.0 %collective-permute-start.7 = (f32[96,256]{1,0:T(8,128)S(1)}, f32[96,256]{1,0:T(8,128)S(1)}, u32[]{:S(2)}, u32[]{:S(2)}) collective-permute-start(f32[96,256]{1,0:T(8,128)S(1)} %dynamic-slice_add_fusion.5), channel_id=1, source_target_pairs={{0,1},{1,0},{2,3},{3,2},{4,5},{5,4},{6,7},{7,6},{8,9},{9,8},{10,11... | collective-permute-start | bytes 294920 | tf_op jit(solution)/shard_map/ppermute | solution.py:37
  62.3 3.2 %fusion.14 = f32[256,4,3,144]{0,3,2,1:T(8,128)} fusion(bf16[4,3,144,3,136]{2,0,1,3,4:T(4,128)(2,1)S(1)} %copy-done.2, bf16[3,256,256]{2,1,0:T(8,128)(2,1)S(1)} %copy-done, bf16[256,4,136]{0,2,1:T(8,128)(2,1)} %copy-done.9), kind=kOutput, calls=%fused_computation.15 | convolution fusion | flops 575299584 | bytes 3851264 | tf_op jit(solution)/shard_map/cikq,iapkq->ciap/dot_general | solution.py:124
  65.5 0.4 collective-permute-done.7
  65.9 2.0 %collective-permute-start.8 = (f32[96,256]{1,0:T(8,128)S(1)}, f32[96,256]{1,0:T(8,128)S(1)}, u32[]{:S(2)}, u32[]{:S(2)}) collective-permute-start(f32[96,256]{1,0:T(8,128)S(1)} %add.182), channel_id=1, source_target_pairs={{0,2},{1,3},{2,0},{3,1},{4,6},{5,7},{6,4},{7,5},{8,10},{9,11},{10,... | collective-permute-start | bytes 294920 | tf_op jit(solution)/shard_map/ppermute | solution.py:37
  67.9 1.6 %collective-permute-start.16 = (bf16[96,256]{1,0:T(8,128)(2,1)S(1)}, bf16[96,256]{1,0:T(8,128)(2,1)S(1)}, u32[]{:S(2)}, u32[]{:S(2)}) collective-permute-start(bf16[96,256]{1,0:T(8,128)(2,1)S(1)} %add_convert_fusion), channel_id=1, source_target_pairs={{0,4},{4,0},{1,5},{5,1},{2,6},{6,2},{3,7},{7,3},{8,12},{12,8},{9,1... | collective-permute-start | bytes 147464 | tf_op jit(solution)/shard_map/ppermute | solution.py:42
  69.5 3.1 %collective-permute-done.8 = f32[96,256]{1,0:T(8,128)S(1)} collective-permute-done((f32[96,256]{1,0:T(8,128)S(1)}, f32[96,256]{1,0:T(8,128)S(1)}, u32[]{:S(2)}, u32[]{:S(2)}) %collective-permute-start.8) | collective-permute-done | bytes 98336 | tf_op jit(solution)/shard_map/ppermute | solution.py:37
  72.6 1.5 %collective-permute-start.9 = (bf16[96,256]{1,0:T(8,128)(2,1)S(1)}, bf16[96,256]{1,0:T(8,128)(2,1)S(1)}, u32[]{:S(2)}, u32[]{:S(2)}) collective-permute-start(bf16[96,256]{1,0:T(8,128)(2,1)S(1)} %add_convert_fusion.1), channel_id=1, source_target_pairs={{0,4},{4,0},{1,5},{5,1},{2,6},{6,2},{3,7},{7,3},{8,12},{12,8},{9,1... | collective-permute-start | bytes 147464 | tf_op jit(solution)/shard_map/ppermute | solution.py:42
  74.2 1.6 %collective-permute-start.17 = (bf16[192,256]{1,0:T(8,128)(2,1)S(1)}, bf16[192,256]{1,0:T(8,128)(2,1)S(1)}, u32[]{:S(2)}, u32[]{:S(2)}) collective-permute-start(bf16[192,256]{1,0:T(8,128)(2,1)S(1)} %maximum_select_fusion.5), channel_id=1, source_target_pairs={{0,16},{8,24},{16,0},{24,8},{1,17},{9,25},{17,1},{25,9},{2,18},{10... | collective-permute-start | bytes 294920 | tf_op jit(solution)/shard_map/ppermute | solution.py:42
  75.7 1.0 %collective-permute-done.9 = bf16[96,256]{1,0:T(8,128)(2,1)S(1)} collective-permute-done((bf16[96,256]{1,0:T(8,128)(2,1)S(1)}, bf16[96,256]{1,0:T(8,128)(2,1)S(1)}, u32[]{:S(2)}, u32[]{:S(2)}) %collective-permute-start.9) | collective-permute-done | bytes 49184 | tf_op jit(solution)/shard_map/ppermute | solution.py:42
  76.8 1.6 %collective-permute-start.10 = (bf16[192,256]{1,0:T(8,128)(2,1)S(1)}, bf16[192,256]{1,0:T(8,128)(2,1)S(1)}, u32[]{:S(2)}, u32[]{:S(2)}) collective-permute-start(bf16[192,256]{1,0:T(8,128)(2,1)S(1)} %maximum_select_fusion.4), channel_id=1, source_target_pairs={{0,16},{8,24},{16,0},{24,8},{1,17},{9,25},{17,1},{25,9},{2,18},{10... | collective-permute-start | bytes 294920 | tf_op jit(solution)/shard_map/ppermute | solution.py:42
  78.3 0.5 collective-permute-done.17
  78.8 0.1 fusion.95
  79.0 2.4 %collective-permute-done.10 = bf16[192,256]{1,0:T(8,128)(2,1)S(1)} collective-permute-done((bf16[192,256]{1,0:T(8,128)(2,1)S(1)}, bf16[192,256]{1,0:T(8,128)(2,1)S(1)}, u32[]{:S(2)}, u32[]{:S(2)}) %collective-permute-start.10) | collective-permute-done | bytes 98336 | tf_op jit(solution)/shard_map/ppermute | solution.py:42
  81.4 0.1 fusion.96
  81.6 1.2 %fusion.80 = bf16[1,256,2,128]{1,3,2,0:T(8,128)(2,1)S(1)} fusion(f32[256,4,3,144]{0,3,2,1:T(8,128)} %fusion.14), kind=kLoop, calls=%fused_computation.119 | loop fusion | flops 196608 | bytes 917504 | tf_op jit(solution)/shard_map/convert_element_type | solution.py:226
  82.8 0.8 copy.41
  83.6 0.9 %maximum_select_fusion.1 = f32[768,256]{1,0:T(8,128)} fusion(f32[384,256]{1,0:T(8,128)S(1)} %get-tuple-element.22, f32[384,256]{1,0:T(8,128)S(1)} %convert_element_type.137, pred[]{:T(512)S(6)} %eq.74), kind=kLoop, calls=%fused_computation.47 | loop fusion | flops 589824 | bytes 1572865 | tf_op jit(solution)/shard_map/jit(_where)/select_n | solution.py:45
  84.6 0.9 %maximum_select_fusion = f32[768,256]{1,0:T(8,128)} fusion(f32[384,256]{1,0:T(8,128)S(1)} %get-tuple-element.24, f32[384,256]{1,0:T(8,128)S(1)} %convert_element_type.134, pred[]{:T(512)S(6)} %eq.74), kind=kLoop, calls=%fused_computation.46 | loop fusion | flops 589824 | bytes 1572865 | tf_op jit(solution)/shard_map/jit(_where)/select_n | solution.py:45
  (59 shorter events, 0.9 us)
Async XLA Ops:
  0.6 25.1 %copy-start = (bf16[3,256,256]{2,1,0:T(8,128)(2,1)S(1)}, bf16[3,256,256]{2,1,0:T(8,128)(2,1)}, u32[]{:S(2)}) copy-start(bf16[3,256,256]{2,1,0:T(8,128)(2,1)} %param.8) | copy-start | bytes 1179652
  2.8 7.4 %collective-permute-start.1 = (bf16[512,2,8]{0,2,1:T(8,128)(2,1)S(1)}, bf16[512,2,8]{0,2,1:T(8,128)(2,1)S(1)}, u32[]{:S(2)}, u32[]{:S(2)}) collective-permute-start(bf16[512,2,8]{0,2,1:T(8,128)(2,1)S(1)} %get-tuple-element.39), channel_id=1, source_target_pairs={{0,3},{1,0},{2,1},{3,2},{4,7},{5,4},{6,5},{7,6},{8,11},{9,8},{10,9... | collective-permute-start | bytes 49160 | tf_op jit(solution)/shard_map/ppermute | solution.py:76
  7.9 5.5 %collective-permute-start = (bf16[512,2,8]{0,2,1:T(8,128)(2,1)S(1)}, bf16[512,2,8]{0,2,1:T(8,128)(2,1)S(1)}, u32[]{:S(2)}, u32[]{:S(2)}) collective-permute-start(bf16[512,2,8]{0,2,1:T(8,128)(2,1)S(1)} %get-tuple-element.38), channel_id=1, source_target_pairs={{0,1},{1,2},{2,3},{3,0},{4,5},{5,6},{6,7},{7,4},{8,9},{9,10},{10,1... | collective-permute-start | bytes 49160 | tf_op jit(solution)/shard_map/ppermute | solution.py:75
  13.5 9.0 %collective-permute-start.2 = (bf16[513,2,144]{0,2,1:T(8,128)(2,1)S(1)}, bf16[513,2,144]{0,2,1:T(8,128)(2,1)S(1)}, u32[]{:S(2)}, u32[]{:S(2)}) collective-permute-start(bf16[513,2,144]{0,2,1:T(8,128)(2,1)S(1)} %pad_maximum_fusion.6), channel_id=1, source_target_pairs={{0,4},{4,0},{1,5},{5,1},{2,6},{6,2},{3,7},{7,3},{8,12},{12,8},{9,1... | collective-permute-start | bytes 886472 | tf_op jit(solution)/shard_map/ppermute | solution.py:55
  24.3 1.5 %copy-start.1 = (bf16[4,3,144,3,136]{2,0,1,3,4:T(4,128)(2,1)}, bf16[4,3,144,3,136]{2,0,1,3,4:T(4,128)(2,1)S(1)}, u32[]{:S(2)}) copy-start(bf16[4,3,144,3,136]{2,0,1,3,4:T(4,128)(2,1)S(1)} %convert_bitcast_fusion) | copy-start | bytes 4230148
  25.8 1.8 %copy-start.10 = (bf16[256,4,3,136]{0,3,2,1:T(8,128)(2,1)}, bf16[256,4,3,136]{0,3,2,1:T(8,128)(2,1)S(1)}, u32[]{:S(2)}) copy-start(bf16[256,4,3,136]{0,3,2,1:T(8,128)(2,1)S(1)} %fusion.24) | copy-start | bytes 2506756
  25.8 1.8 %copy-start.8 = (bf16[1,256,2,128]{3,2,1,0:T(2,128)(2,1)S(1)}, bf16[1,256,2,128]{3,2,1,0:T(2,128)(2,1)}, u32[]{:S(2)}) copy-start(bf16[1,256,2,128]{3,2,1,0:T(2,128)(2,1)} %param.13) | copy-start | bytes 393220
  27.5 0.8 copy-start.3
  27.9 2.7 %collective-permute-start.3 = (f32[384,256]{1,0:T(8,128)S(1)}, f32[384,256]{1,0:T(8,128)S(1)}, u32[]{:S(2)}, u32[]{:S(2)}) collective-permute-start(f32[384,256]{1,0:T(8,128)S(1)} %constant_dynamic-slice_fusion.5), channel_id=1, source_target_pairs={{0,8},{8,0},{16,24},{24,16},{1,9},{9,1},{17,25},{25,17},{2,10},{10... | collective-permute-start | bytes 1179656 | tf_op jit(solution)/shard_map/ppermute | solution.py:31
  30.6 5.9 %copy-start.5 = (f32[384,256]{1,0:T(8,128)}, f32[384,256]{1,0:T(8,128)S(1)}, u32[]{:S(2)}) copy-start(f32[384,256]{1,0:T(8,128)S(1)} %dynamic-slice_add_fusion.1) | copy-start | bytes 1179652
  34.1 4.1 %copy-start.7 = (f32[256,4,136]{0,2,1:T(8,128)S(1)}, f32[256,4,136]{0,2,1:T(8,128)}, u32[]{:S(2)}) copy-start(f32[256,4,136]{0,2,1:T(8,128)} %get-tuple-element.41) | copy-start | bytes 1671172
  36.6 7.1 %collective-permute-start.12 = (f32[192,256]{1,0:T(8,128)S(1)}, f32[192,256]{1,0:T(8,128)}, u32[]{:S(2)}, u32[]{:S(2)}) collective-permute-start(f32[192,256]{1,0:T(8,128)S(1)} %constant_dynamic-slice_fusion.1), channel_id=1, source_target_pairs={{0,16},{8,24},{16,0},{24,8},{1,17},{9,25},{17,1},{25,9},{2,18},{10... | collective-permute-start | bytes 589832 | tf_op jit(solution)/shard_map/ppermute | solution.py:31
  38.6 3.1 %copy-start.9 = (bf16[256,4,136]{0,2,1:T(8,128)(2,1)}, bf16[256,4,136]{0,2,1:T(8,128)(2,1)S(1)}, u32[]{:S(2)}) copy-start(bf16[256,4,136]{0,2,1:T(8,128)(2,1)S(1)} %fusion.46) | copy-start | bytes 835588
  40.0 0.9 %copy-start.6 = (f32[256,3,256]{0,2,1:T(8,128)}, f32[256,3,256]{0,2,1:T(8,128)S(1)}, u32[]{:S(2)}) copy-start(f32[256,3,256]{0,2,1:T(8,128)S(1)} %fusion.28) | copy-start | bytes 2359300
  40.0 14.6 %copy-start.4 = (bf16[256,2,3,128]{0,3,2,1:T(8,128)(2,1)S(1)}, bf16[256,2,3,128]{0,3,2,1:T(8,128)(2,1)}, u32[]{:S(2)}) copy-start(bf16[256,2,3,128]{0,3,2,1:T(8,128)(2,1)} %copy-done.3) | copy-start | bytes 1179652
  41.7 4.7 %collective-permute-start.4 = (f32[384,256]{1,0:T(8,128)}, f32[384,256]{1,0:T(8,128)}, u32[]{:S(2)}, u32[]{:S(2)}) collective-permute-start(f32[384,256]{1,0:T(8,128)} %constant_dynamic-slice_fusion.4), channel_id=1, source_target_pairs={{0,8},{8,0},{16,24},{24,16},{1,9},{9,1},{17,25},{25,17},{2,10},{10... | collective-permute-start | bytes 1179656 | tf_op jit(solution)/shard_map/ppermute | solution.py:31
  41.7 20.6 %copy-start.2 = (bf16[4,3,144,3,136]{2,0,1,3,4:T(4,128)(2,1)S(1)}, bf16[4,3,144,3,136]{2,0,1,3,4:T(4,128)(2,1)}, u32[]{:S(2)}) copy-start(bf16[4,3,144,3,136]{2,0,1,3,4:T(4,128)(2,1)} %copy-done.1) | copy-start | bytes 4230148
  44.8 4.7 %collective-permute-start.13 = (f32[96,256]{1,0:T(8,128)S(1)}, f32[96,256]{1,0:T(8,128)S(1)}, u32[]{:S(2)}, u32[]{:S(2)}) collective-permute-start(f32[96,256]{1,0:T(8,128)S(1)} %constant_dynamic-slice_fusion), channel_id=1, source_target_pairs={{0,4},{4,0},{1,5},{5,1},{2,6},{6,2},{3,7},{7,3},{8,12},{12,8},{9,1... | collective-permute-start | bytes 294920 | tf_op jit(solution)/shard_map/ppermute | solution.py:31
  47.6 5.9 %collective-permute-start.5 = (f32[192,256]{1,0:T(8,128)S(1)}, f32[192,256]{1,0:T(8,128)S(1)}, u32[]{:S(2)}, u32[]{:S(2)}) collective-permute-start(f32[192,256]{1,0:T(8,128)S(1)} %constant_dynamic-slice_fusion.3), channel_id=1, source_target_pairs={{0,16},{8,24},{16,0},{24,8},{1,17},{9,25},{17,1},{25,9},{2,18},{10... | collective-permute-start | bytes 589832 | tf_op jit(solution)/shard_map/ppermute | solution.py:31
  50.1 8.2 %collective-permute-start.14 = (f32[96,256]{1,0:T(8,128)}, f32[96,256]{1,0:T(8,128)}, u32[]{:S(2)}, u32[]{:S(2)}) collective-permute-start(f32[96,256]{1,0:T(8,128)} %dynamic-slice_add_fusion.4), channel_id=1, source_target_pairs={{0,1},{1,0},{2,3},{3,2},{4,5},{5,4},{6,7},{7,6},{8,9},{9,8},{10,11... | collective-permute-start | bytes 294920 | tf_op jit(solution)/shard_map/ppermute | solution.py:37
  54.1 5.2 %collective-permute-start.6 = (f32[96,256]{1,0:T(8,128)}, f32[96,256]{1,0:T(8,128)}, u32[]{:S(2)}, u32[]{:S(2)}) collective-permute-start(f32[96,256]{1,0:T(8,128)} %constant_dynamic-slice_fusion.2), channel_id=1, source_target_pairs={{0,4},{4,0},{1,5},{5,1},{2,6},{6,2},{3,7},{7,3},{8,12},{12,8},{9,1... | collective-permute-start | bytes 294920 | tf_op jit(solution)/shard_map/ppermute | solution.py:31
  59.2 8.7 %collective-permute-start.15 = (f32[96,256]{1,0:T(8,128)S(1)}, f32[96,256]{1,0:T(8,128)S(1)}, u32[]{:S(2)}, u32[]{:S(2)}) collective-permute-start(f32[96,256]{1,0:T(8,128)S(1)} %add.186), channel_id=1, source_target_pairs={{0,2},{1,3},{2,0},{3,1},{4,6},{5,7},{6,4},{7,5},{8,10},{9,11},{10,... | collective-permute-start | bytes 294920 | tf_op jit(solution)/shard_map/ppermute | solution.py:37
  60.2 5.7 %collective-permute-start.7 = (f32[96,256]{1,0:T(8,128)S(1)}, f32[96,256]{1,0:T(8,128)S(1)}, u32[]{:S(2)}, u32[]{:S(2)}) collective-permute-start(f32[96,256]{1,0:T(8,128)S(1)} %dynamic-slice_add_fusion.5), channel_id=1, source_target_pairs={{0,1},{1,0},{2,3},{3,2},{4,5},{5,4},{6,7},{7,6},{8,9},{9,8},{10,11... | collective-permute-start | bytes 294920 | tf_op jit(solution)/shard_map/ppermute | solution.py:37
  65.9 6.6 %collective-permute-start.8 = (f32[96,256]{1,0:T(8,128)S(1)}, f32[96,256]{1,0:T(8,128)S(1)}, u32[]{:S(2)}, u32[]{:S(2)}) collective-permute-start(f32[96,256]{1,0:T(8,128)S(1)} %add.182), channel_id=1, source_target_pairs={{0,2},{1,3},{2,0},{3,1},{4,6},{5,7},{6,4},{7,5},{8,10},{9,11},{10,... | collective-permute-start | bytes 294920 | tf_op jit(solution)/shard_map/ppermute | solution.py:37
  67.9 6.2 %collective-permute-start.16 = (bf16[96,256]{1,0:T(8,128)(2,1)S(1)}, bf16[96,256]{1,0:T(8,128)(2,1)S(1)}, u32[]{:S(2)}, u32[]{:S(2)}) collective-permute-start(bf16[96,256]{1,0:T(8,128)(2,1)S(1)} %add_convert_fusion), channel_id=1, source_target_pairs={{0,4},{4,0},{1,5},{5,1},{2,6},{6,2},{3,7},{7,3},{8,12},{12,8},{9,1... | collective-permute-start | bytes 147464 | tf_op jit(solution)/shard_map/ppermute | solution.py:42
  72.6 4.2 %collective-permute-start.9 = (bf16[96,256]{1,0:T(8,128)(2,1)S(1)}, bf16[96,256]{1,0:T(8,128)(2,1)S(1)}, u32[]{:S(2)}, u32[]{:S(2)}) collective-permute-start(bf16[96,256]{1,0:T(8,128)(2,1)S(1)} %add_convert_fusion.1), channel_id=1, source_target_pairs={{0,4},{4,0},{1,5},{5,1},{2,6},{6,2},{3,7},{7,3},{8,12},{12,8},{9,1... | collective-permute-start | bytes 147464 | tf_op jit(solution)/shard_map/ppermute | solution.py:42
  74.2 4.7 %collective-permute-start.17 = (bf16[192,256]{1,0:T(8,128)(2,1)S(1)}, bf16[192,256]{1,0:T(8,128)(2,1)S(1)}, u32[]{:S(2)}, u32[]{:S(2)}) collective-permute-start(bf16[192,256]{1,0:T(8,128)(2,1)S(1)} %maximum_select_fusion.5), channel_id=1, source_target_pairs={{0,16},{8,24},{16,0},{24,8},{1,17},{9,25},{17,1},{25,9},{2,18},{10... | collective-permute-start | bytes 294920 | tf_op jit(solution)/shard_map/ppermute | solution.py:42
  76.8 4.7 %collective-permute-start.10 = (bf16[192,256]{1,0:T(8,128)(2,1)S(1)}, bf16[192,256]{1,0:T(8,128)(2,1)S(1)}, u32[]{:S(2)}, u32[]{:S(2)}) collective-permute-start(bf16[192,256]{1,0:T(8,128)(2,1)S(1)} %maximum_select_fusion.4), channel_id=1, source_target_pairs={{0,16},{8,24},{16,0},{24,8},{1,17},{9,25},{17,1},{25,9},{2,18},{10... | collective-permute-start | bytes 294920 | tf_op jit(solution)/shard_map/ppermute | solution.py:42
  78.9 4.6 %collective-permute-start.18 = (bf16[384,256]{1,0:T(8,128)(2,1)S(1)}, bf16[384,256]{1,0:T(8,128)(2,1)S(1)}, u32[]{:S(2)}, u32[]{:S(2)}) collective-permute-start(bf16[384,256]{1,0:T(8,128)(2,1)S(1)} %get-tuple-element.23), channel_id=1, source_target_pairs={{0,8},{8,0},{16,24},{24,16},{1,9},{9,1},{17,25},{25,17},{2,10},{10... | collective-permute-start | bytes 589832 | tf_op jit(solution)/shard_map/ppermute | solution.py:42
  81.5 3.0 %collective-permute-start.11 = (bf16[384,256]{1,0:T(8,128)(2,1)S(1)}, bf16[384,256]{1,0:T(8,128)(2,1)S(1)}, u32[]{:S(2)}, u32[]{:S(2)}) collective-permute-start(bf16[384,256]{1,0:T(8,128)(2,1)S(1)} %get-tuple-element.25), channel_id=1, source_target_pairs={{0,8},{8,0},{16,24},{24,16},{1,9},{9,1},{17,25},{25,17},{2,10},{10... | collective-permute-start | bytes 589832 | tf_op jit(solution)/shard_map/ppermute | solution.py:42

commit v15 on v13

--- a/solution.py
+++ b/solution.py
@@ -11,7 +11,7 @@
 LON_HALO = 2 * LON_REACH
 
 
-def halving_sum(value, axes, exchanged=3, hold=None):
+def halving_sum(value, axes, exchanged=2, hold=None, late=None):
     stages = []
     for axis in axes:
         bit = 1
@@ -32,9 +32,13 @@
         if hold is not None:
             flat, hold = lax.optimization_barrier((flat, hold))
             held, hold = hold, None
+            if late is not None:
+                held = late(held)
     for axis, bit in stages[len(halved) :]:
         pairs = [(i, i ^ bit) for i in range(lax.axis_size(axis))]
         flat = flat + lax.ppermute(flat, axis, pairs)
+    if late is not None:
+        flat, held = lax.optimization_barrier((flat, held))
     flat = flat.astype(jnp.bfloat16)
     for step, (axis, bit) in enumerate(reversed(halved)):
         pairs = [(i, i ^ bit) for i in range(lax.axis_size(axis))]
@@ -216,12 +220,21 @@
         member_total * row_count * lax.axis_size("lat") * col_count * lax.axis_size("lon")
     )
     axes = ("ens", "lat", "lon")
-    second_grad, second_spread = halving_sum(second_sum * grad_scale, axes, hold=second_spread)
-    first_grad, hidden_grad = halving_sum(first_sum * grad_scale, axes, hold=hidden_grad)
-    layer_output = mix_channels(second_weight, second_spread).astype(jnp.bfloat16)
-    first_mixed = unmix(first_weight, hidden_grad)
-    state_grad = spread_adjoint(first_mixed, near_band).astype(jnp.bfloat16)
-    return (layer_output[None], state_grad[None], first_grad, second_grad)
+
+    def layer_output_of(spreaded):
+        return mix_channels(second_weight, spreaded).astype(jnp.bfloat16)[None]
+
+    def state_grad_of(grad_rows):
+        first_mixed = unmix(first_weight, grad_rows)
+        return spread_adjoint(first_mixed, near_band).astype(jnp.bfloat16)[None]
+
+    second_grad, layer_output = halving_sum(
+        second_sum * grad_scale, axes, hold=second_spread, late=layer_output_of
+    )
+    first_grad, state_grad = halving_sum(
+        first_sum * grad_scale, axes, hold=hidden_grad, late=state_grad_of
+    )
+    return (layer_output, state_grad, first_grad, second_grad)
 
 
 def solution(mesh):

time: 84.5 us -> 84 us (level)
  waiting for transfers between devices: 37.4 us -> 32.2 us
  other arithmetic: 3.95 us -> 6.94 us
  matrix products: 16.6 us -> 17.9 us
    ppermute x6 -> x4, waiting for transfers between devices: 18.6 us -> 8.02 us  [halving_sum(): flat = flat + lax.ppermute(flat, axis, pairs)]
    ppermute x4 -> x6, waiting for transfers between devices: 6.72 us -> 10.1 us  [halving_sum(): flat = keep + lax.ppermute(send, axis, pairs)]
    ppermute x6 -> x4, starting transfers between devices: 4.75 us -> 2.48 us  [halving_sum(): flat = flat + lax.ppermute(flat, axis, pairs)]
    ppermute x4 -> x6, waiting for transfers between devices: 2.96 us -> 4.97 us  [halving_sum(): other = lax.ppermute(flat, axis, pairs)]
    add x4 -> x6, other arithmetic: 0.16 us -> 2.1 us  [halving_sum(): flat = keep + lax.ppermute(send, axis, pairs)]
    ppermute x4 -> x6, starting transfers between devices: 3.25 us -> 4.88 us  [halving_sum(): flat = keep + lax.ppermute(send, axis, pairs)]
    dot_general x1, matrix products: 2.74 us -> 3.98 us  [spread_adjoint(): jnp.einsum('cikq,iapkq->ciap', mixed, band, preferred_element_type=jnp.fl...]
    ppermute x4 -> x6, starting transfers between devices: 3.27 us -> 4.4 us  [halving_sum(): other = lax.ppermute(flat, axis, pairs)]
  transfers between devices with their start and end apart: 17 -> 19, of which waited for: 13 -> 14; matrix products, arithmetic and copies ran while one was open for 13% -> 18% of each run, Pallas kernels for 0% -> 0%
where the time goes in v15:
time: 84 us; the launch traced here: 83.6 us
  waiting for transfers between devices  32.2 us (38%)
  starting transfers between devices  18.5 us (22%)
  matrix products  17.9 us (21%)
  local copies, waits for them, and re-layouts  7 us (8%)
  other arithmetic  6.94 us (8%)
  between operations  1.04 us (1%)
    ppermute x6, waiting for transfers between devices, halving_sum(): flat = keep + lax.ppermute(send, axis, pairs)  10.1 us
    ppermute x4, waiting for transfers between devices, halving_sum(): flat = flat + lax.ppermute(flat, axis, pairs)  8.02 us
    dot_general x3, matrix products, band_of(): jnp.einsum('kiad,dpq->iapkq', stencil, lon_picker(col_count, first_source...  7.43 us
    ppermute x1, waiting for transfers between devices, lat_halo(): other = lax.ppermute(block, 'lat', [(0, 1), (1, 0)])  5.85 us
    unnamed x16, local copies, waits for them, and re-layouts  5.71 us
    ppermute x1, starting transfers between devices, lon_halo(): lax.ppermute(block[..., :width], 'lon', [(i, (i - 1) % count) for i in ra...  5.13 us
    ppermute x6, waiting for transfers between devices, halving_sum(): other = lax.ppermute(flat, axis, pairs)  4.97 us
    ppermute x6, starting transfers between devices, halving_sum(): flat = keep + lax.ppermute(send, axis, pairs)  4.88 us
  transfers between devices with their start and end apart: 19, of which 14 were waited for; matrix products, arithmetic and copies ran while one was open for 18% of the time, Pallas kernels for 0%

profile of v15, /device:TPU:0, one launch (start us, length us, event | category | flops | bytes accessed | tf_op | source)
XLA Modules:
  0.0 83.6 jit_solution(17256389261388056696)
XLA Ops:
  0.6 1.1 %copy.26 = bf16[1,256,2,128]{1,3,2,0:T(8,128)(2,1)S(1)} copy(bf16[1,256,2,128]{3,2,1,0:T(2,128)(2,1)} %param.13) | data formatting | bytes 262144 | tf_op args[6]
  1.7 1.0 %copy.25 = bf16[1,256,2,128]{1,3,2,0:T(8,128)(2,1)S(1)} copy(bf16[1,256,2,128]{3,2,1,0:T(2,128)(2,1)} %param.7) | data formatting | bytes 262144 | tf_op args[0]
  2.8 5.1 %collective-permute-start.1 = (bf16[512,2,8]{0,2,1:T(8,128)(2,1)S(1)}, bf16[512,2,8]{0,2,1:T(8,128)(2,1)S(1)}, u32[]{:S(2)}, u32[]{:S(2)}) collective-permute-start(bf16[512,2,8]{0,2,1:T(8,128)(2,1)S(1)} %get-tuple-element.47), channel_id=1, source_target_pairs={{0,3},{1,0},{2,1},{3,2},{4,7},{5,4},{6,5},{7,6},{8,11},{9,8},{10,9... | collective-permute-start | bytes 49160 | tf_op jit(solution)/shard_map/ppermute | solution.py:80
  7.9 0.1 fusion.42
  8.0 0.7 broadcast_add_fusion
  8.7 0.9 %convolution_convert_fusion.2 = bf16[3,2,3,9]{3,2,1,0:T(4,128)(2,1)S(1)} fusion(s32[2,3,12]{2,0,1:T(2,128)S(1)} %get-tuple-element.48, f32[2,3,12]{2,0,1:T(2,128)} %param.10, s32[2,3,12]{2,0,1:T(2,128)S(1)} %get-tuple-element.49), kind=kOutput, calls=%fused_computation.38 | convolution fusion | flops 24570 | bytes 1188 | tf_op jit(solution)/shard_map/rks,rksa,rksd->krad/dot_general | solution.py:89
  9.6 0.1 reshape.71
  9.7 0.2 fusion.29
  10.0 0.1 copy.28
  10.1 3.3 %collective-permute-done = bf16[512,2,8]{0,2,1:T(8,128)(2,1)S(1)} collective-permute-done((bf16[512,2,8]{0,2,1:T(8,128)(2,1)S(1)}, bf16[512,2,8]{0,2,1:T(8,128)(2,1)S(1)}, u32[]{:S(2)}, u32[]{:S(2)}) %collective-permute-start) | collective-permute-done | bytes 16416 | tf_op jit(solution)/shard_map/ppermute | solution.py:79
  13.5 1.6 %collective-permute-start.2 = (bf16[513,2,144]{0,2,1:T(8,128)(2,1)S(1)}, bf16[513,2,144]{0,2,1:T(8,128)(2,1)S(1)}, u32[]{:S(2)}, u32[]{:S(2)}) collective-permute-start(bf16[513,2,144]{0,2,1:T(8,128)(2,1)S(1)} %pad_maximum_fusion), channel_id=1, source_target_pairs={{0,4},{4,0},{1,5},{5,1},{2,6},{6,2},{3,7},{7,3},{8,12},{12,8},{9,1... | collective-permute-start | bytes 886472 | tf_op jit(solution)/shard_map/ppermute | solution.py:59
  15.1 1.5 %fusion.34 = bf16[136,128,3,2,3]{1,4,3,2,0:T(4,128)(2,1)} fusion(pred[9,136,128,1,1]{2,1,0,3,4:T(8,128)(4,1)S(1)} %fusion.42, bf16[3,2,3,9]{3,2,1,0:T(4,128)(2,1)S(1)} %convolution_convert_fusion.2), kind=kOutput, calls=%fused_computation.36 | convolution fusion | flops 5640192 | bytes 783684 | tf_op jit(solution)/shard_map/kiad,dpq->iapkq/dot_general | solution.py:108
  16.6 5.8 %collective-permute-done.2 = bf16[513,2,144]{0,2,1:T(8,128)(2,1)S(1)} collective-permute-done((bf16[513,2,144]{0,2,1:T(8,128)(2,1)S(1)}, bf16[513,2,144]{0,2,1:T(8,128)(2,1)S(1)}, u32[]{:S(2)}, u32[]{:S(2)}) %collective-permute-start.2) | collective-permute-done | bytes 295520 | tf_op jit(solution)/shard_map/ppermute | solution.py:59
  22.5 0.2 maximum_reduce_fusion
  22.6 0.1 reshape_squeeze.3
  22.8 3.0 %convert_bitcast_fusion = bf16[4,3,144,3,136]{2,0,1,3,4:T(4,128)(2,1)} fusion(bf16[3,6,3,9]{3,1,2,0:T(8,128)(2,1)S(1)} %bitcast.203), kind=kOutput, calls=%fused_computation.8 | convolution fusion | flops 13747968 | bytes 1419264 | tf_op jit(solution)/shard_map/kiad,dpq->iapkq/dot_general | solution.py:108
  25.7 2.9 %fusion.10 = bf16[136,144,3,4,3]{1,3,4,2,0:T(4,128)(2,1)} fusion(pred[9,136,144,1,1]{2,1,0,3,4:T(8,128)(4,1)S(1)} %fusion.29, bf16[3,6,3,9]{3,1,2,0:T(8,128)(2,1)S(1)} %bitcast.204, pred[]{:T(512)S(6)} %eq.72), kind=kOutput, calls=%fused_computation.12 | convolution fusion | flops 12690756 | bytes 1587277 | tf_op jit(solution)/shard_map/kiad,dpq->iapkq/dot_general | solution.py:108
  28.7 2.7 %fusion.19 = f32[256,4,3,136]{0,3,1,2:T(8,128)S(1)} fusion(bf16[3,256,256]{2,1,0:T(8,128)(2,1)} %param.9, bf16[513,2,144]{0,2,1:T(8,128)(2,1)S(1)} %get-tuple-element.39, bf16[1,2,144]{0,2,1:T(8,128)(2,1)S(1)} %copy.28, bf16[512,2,8]{0,2,1:T(8,128)(2,1)S(1)} %collective-permute-done.1, bf16[512,2,8]{0,2,1:T(8,128)(2,1)S(1)} %collective-permute-done, ...), kind=kOutput, calls=%fused_computation.16 | convolution fusion | flops 591593472 | bytes 4360897 | tf_op jit(solution)/shard_map/cikq,iapkq->ciap/dot_general | solution.py:141
  31.4 0.1 fusion.56
  31.6 0.1 maximum_bitcast_fusion.4
  31.7 1.5 %copy-done.1 = bf16[4,3,144,3,136]{2,0,1,3,4:T(4,128)(2,1)S(1)} copy-done((bf16[4,3,144,3,136]{2,0,1,3,4:T(4,128)(2,1)S(1)}, bf16[4,3,144,3,136]{2,0,1,3,4:T(4,128)(2,1)}, u32[]{:S(2)}) %copy-start.1) | copy-done | bytes 1410072
  33.1 0.8 fusion.24
  33.9 0.8 fusion.46
  34.8 0.3 copy-done.4
  35.1 0.4 fusion.31
  35.5 0.3 copy-done.2
  35.8 0.3 fusion.27
  36.1 0.1 collective-permute-start.3
  36.2 0.3 fusion.28
  36.6 0.6 collective-permute-start.8
  37.1 0.9 %collective-permute-done.3 = f32[384,256]{1,0:T(8,128)} collective-permute-done((f32[384,256]{1,0:T(8,128)S(1)}, f32[384,256]{1,0:T(8,128)}, u32[]{:S(2)}, u32[]{:S(2)}) %collective-permute-start.3) | collective-permute-done | bytes 393248 | tf_op jit(solution)/shard_map/ppermute | solution.py:31
  38.0 1.0 %dynamic-slice_add_fusion.1 = f32[384,256]{1,0:T(8,128)S(1)} fusion(f32[384,256]{1,0:T(8,128)} %collective-permute-done.3, f32[768,256]{1,0:T(8,128)S(1)} %bitcast.198, s32[]{:T(128)S(6)} %select_n.164), kind=kLoop, calls=%fused_computation.79 | loop fusion | flops 98304 | bytes 1179652 | tf_op jit(solution)/shard_map/add | solution.py:31
  39.1 0.7 constant_dynamic-slice_fusion.4
  39.8 1.5 %collective-permute-start.4 = (f32[192,256]{1,0:T(8,128)}, f32[192,256]{1,0:T(8,128)}, u32[]{:S(2)}, u32[]{:S(2)}) collective-permute-start(f32[192,256]{1,0:T(8,128)} %constant_dynamic-slice_fusion.4), channel_id=1, source_target_pairs={{0,16},{8,24},{16,0},{24,8},{1,17},{9,25},{17,1},{25,9},{2,18},{10... | collective-permute-start | bytes 589832 | tf_op jit(solution)/shard_map/ppermute | solution.py:31
  41.4 0.6 collective-permute-start.9
  42.0 4.0 %fusion.14 = f32[256,4,3,144]{0,3,2,1:T(8,128)} fusion(bf16[4,3,144,3,136]{2,0,1,3,4:T(4,128)(2,1)} %convert_bitcast_fusion, bf16[3,256,256]{2,1,0:T(8,128)(2,1)S(1)} %copy-done, bf16[256,4,136]{0,2,1:T(8,128)(2,1)} %copy-done.5), kind=kOutput, calls=%fused_computation.15 | convolution fusion | flops 575299584 | bytes 3851264 | tf_op jit(solution)/shard_map/cikq,iapkq->ciap/dot_general | solution.py:128
  46.0 5.2 %collective-permute-done.9 = f32[192,256]{1,0:T(8,128)S(1)} collective-permute-done((f32[192,256]{1,0:T(8,128)S(1)}, f32[192,256]{1,0:T(8,128)S(1)}, u32[]{:S(2)}, u32[]{:S(2)}) %collective-permute-start.9) | collective-permute-done | bytes 196640 | tf_op jit(solution)/shard_map/ppermute | solution.py:31
  51.2 1.6 %collective-permute-start.10 = (f32[96,256]{1,0:T(8,128)S(1)}, f32[96,256]{1,0:T(8,128)S(1)}, u32[]{:S(2)}, u32[]{:S(2)}) collective-permute-start(f32[96,256]{1,0:T(8,128)S(1)} %constant_dynamic-slice_fusion), channel_id=1, source_target_pairs={{0,4},{4,0},{1,5},{5,1},{2,6},{6,2},{3,7},{7,3},{8,12},{12,8},{9,1... | collective-permute-start | bytes 294920 | tf_op jit(solution)/shard_map/ppermute | solution.py:31
  52.8 1.0 %dynamic-slice_add_fusion.3 = f32[192,256]{1,0:T(8,128)S(1)} fusion(f32[192,256]{1,0:T(8,128)} %collective-permute-done.4, f32[384,256]{1,0:T(8,128)S(1)} %dynamic-slice_add_fusion.1, s32[]{:T(128)S(6)} %select_n.168), kind=kLoop, calls=%fused_computation.114 | loop fusion | flops 49152 | bytes 589828 | tf_op jit(solution)/shard_map/add | solution.py:31
  53.8 0.6 collective-permute-start.5
  54.3 2.0 %collective-permute-done.10 = f32[96,256]{1,0:T(8,128)S(1)} collective-permute-done((f32[96,256]{1,0:T(8,128)S(1)}, f32[96,256]{1,0:T(8,128)S(1)}, u32[]{:S(2)}, u32[]{:S(2)}) %collective-permute-start.10) | collective-permute-done | bytes 98336 | tf_op jit(solution)/shard_map/ppermute | solution.py:31
  56.4 0.1 collective-permute-start.11
  56.4 2.0 %collective-permute-done.5 = f32[96,256]{1,0:T(8,128)S(1)} collective-permute-done((f32[96,256]{1,0:T(8,128)S(1)}, f32[96,256]{1,0:T(8,128)S(1)}, u32[]{:S(2)}, u32[]{:S(2)}) %collective-permute-start.5) | collective-permute-done | bytes 98336 | tf_op jit(solution)/shard_map/ppermute | solution.py:31
  58.5 0.1 collective-permute-start.6
  58.6 3.3 %collective-permute-done.11 = f32[96,256]{1,0:T(8,128)S(1)} collective-permute-done((f32[96,256]{1,0:T(8,128)S(1)}, f32[96,256]{1,0:T(8,128)S(1)}, u32[]{:S(2)}, u32[]{:S(2)}) %collective-permute-start.11) | collective-permute-done | bytes 98336 | tf_op jit(solution)/shard_map/ppermute | solution.py:39
  61.9 1.2 %fusion.79 = bf16[1,256,2,128]{1,3,2,0:T(8,128)(2,1)S(1)} fusion(f32[256,4,3,144]{0,3,2,1:T(8,128)} %fusion.14), kind=kLoop, calls=%fused_computation.119 | loop fusion | flops 196608 | bytes 917504 | tf_op jit(solution)/shard_map/convert_element_type | solution.py:229
  63.1 0.7 collective-permute-done.6
  63.8 2.3 %collective-permute-start.7 = (f32[96,256]{1,0:T(8,128)S(1)}, f32[96,256]{1,0:T(8,128)S(1)}, u32[]{:S(2)}, u32[]{:S(2)}) collective-permute-start(f32[96,256]{1,0:T(8,128)S(1)} %add.175), channel_id=1, source_target_pairs={{0,2},{1,3},{2,0},{3,1},{4,6},{5,7},{6,4},{7,5},{8,10},{9,11},{10,... | collective-permute-start | bytes 294920 | tf_op jit(solution)/shard_map/ppermute | solution.py:39
  66.1 2.8 %collective-permute-done.12 = f32[96,256]{1,0:T(8,128)S(1)} collective-permute-done((f32[96,256]{1,0:T(8,128)S(1)}, f32[96,256]{1,0:T(8,128)S(1)}, u32[]{:S(2)}, u32[]{:S(2)}) %collective-permute-start.12) | collective-permute-done | bytes 98336 | tf_op jit(solution)/shard_map/ppermute | solution.py:39
  68.9 0.6 collective-permute-start.13
  69.5 0.3 fusion.33
  69.8 1.2 %collective-permute-done.7 = f32[96,256]{1,0:T(8,128)S(1)} collective-permute-done((f32[96,256]{1,0:T(8,128)S(1)}, f32[96,256]{1,0:T(8,128)S(1)}, u32[]{:S(2)}, u32[]{:S(2)}) %collective-permute-start.7) | collective-permute-done | bytes 98336 | tf_op jit(solution)/shard_map/ppermute | solution.py:39
  71.0 0.6 collective-permute-start.16
  71.6 1.5 %collective-permute-done.13 = bf16[96,256]{1,0:T(8,128)(2,1)S(1)} collective-permute-done((bf16[96,256]{1,0:T(8,128)(2,1)S(1)}, bf16[96,256]{1,0:T(8,128)(2,1)S(1)}, u32[]{:S(2)}, u32[]{:S(2)}) %collective-permute-start.13) | collective-permute-done | bytes 49184 | tf_op jit(solution)/shard_map/ppermute | solution.py:46
  73.1 1.6 %collective-permute-start.14 = (bf16[192,256]{1,0:T(8,128)(2,1)S(1)}, bf16[192,256]{1,0:T(8,128)(2,1)S(1)}, u32[]{:S(2)}, u32[]{:S(2)}) collective-permute-start(bf16[192,256]{1,0:T(8,128)(2,1)S(1)} %maximum_select_fusion.4), channel_id=1, source_target_pairs={{0,16},{8,24},{16,0},{24,8},{1,17},{9,25},{17,1},{25,9},{2,18},{10... | collective-permute-start | bytes 294920 | tf_op jit(solution)/shard_map/ppermute | solution.py:46
  74.7 0.5 collective-permute-done.16
  75.2 1.6 %collective-permute-start.17 = (bf16[192,256]{1,0:T(8,128)(2,1)S(1)}, bf16[192,256]{1,0:T(8,128)(2,1)S(1)}, u32[]{:S(2)}, u32[]{:S(2)}) collective-permute-start(bf16[192,256]{1,0:T(8,128)(2,1)S(1)} %maximum_select_fusion.5), channel_id=1, source_target_pairs={{0,16},{8,24},{16,0},{24,8},{1,17},{9,25},{17,1},{25,9},{2,18},{10... | collective-permute-start | bytes 294920 | tf_op jit(solution)/shard_map/ppermute | solution.py:46
  76.8 1.0 %collective-permute-done.14 = bf16[192,256]{1,0:T(8,128)(2,1)S(1)} collective-permute-done((bf16[192,256]{1,0:T(8,128)(2,1)S(1)}, bf16[192,256]{1,0:T(8,128)(2,1)S(1)}, u32[]{:S(2)}, u32[]{:S(2)}) %collective-permute-start.14) | collective-permute-done | bytes 98336 | tf_op jit(solution)/shard_map/ppermute | solution.py:46
  77.8 0.1 fusion.97
  77.9 1.9 %collective-permute-done.17 = bf16[192,256]{1,0:T(8,128)(2,1)S(1)} collective-permute-done((bf16[192,256]{1,0:T(8,128)(2,1)S(1)}, bf16[192,256]{1,0:T(8,128)(2,1)S(1)}, u32[]{:S(2)}, u32[]{:S(2)}) %collective-permute-start.17) | collective-permute-done | bytes 98336 | tf_op jit(solution)/shard_map/ppermute | solution.py:46
  80.0 0.8 copy.40
  80.8 0.8 copy.41
  81.6 0.9 %maximum_select_fusion = f32[768,256]{1,0:T(8,128)} fusion(f32[384,256]{1,0:T(8,128)S(1)} %get-tuple-element.30, f32[384,256]{1,0:T(8,128)S(1)} %convert_element_type.134, pred[]{:T(512)S(6)} %eq.74), kind=kLoop, calls=%fused_computation.46 | loop fusion | flops 589824 | bytes 1572865 | tf_op jit(solution)/shard_map/jit(_where)/select_n | solution.py:49
  82.6 0.9 %maximum_select_fusion.1 = f32[768,256]{1,0:T(8,128)} fusion(f32[384,256]{1,0:T(8,128)S(1)} %get-tuple-element.28, f32[384,256]{1,0:T(8,128)S(1)} %convert_element_type.137, pred[]{:T(512)S(6)} %eq.74), kind=kLoop, calls=%fused_computation.47 | loop fusion | flops 589824 | bytes 1572865 | tf_op jit(solution)/shard_map/jit(_where)/select_n | solution.py:49
  (47 shorter events, 1.0 us)
Async XLA Ops:
  0.6 33.3 %copy-start = (bf16[3,256,256]{2,1,0:T(8,128)(2,1)S(1)}, bf16[3,256,256]{2,1,0:T(8,128)(2,1)}, u32[]{:S(2)}) copy-start(bf16[3,256,256]{2,1,0:T(8,128)(2,1)} %param.8) | copy-start | bytes 1179652
  2.8 7.4 %collective-permute-start.1 = (bf16[512,2,8]{0,2,1:T(8,128)(2,1)S(1)}, bf16[512,2,8]{0,2,1:T(8,128)(2,1)S(1)}, u32[]{:S(2)}, u32[]{:S(2)}) collective-permute-start(bf16[512,2,8]{0,2,1:T(8,128)(2,1)S(1)} %get-tuple-element.47), channel_id=1, source_target_pairs={{0,3},{1,0},{2,1},{3,2},{4,7},{5,4},{6,5},{7,6},{8,11},{9,8},{10,9... | collective-permute-start | bytes 49160 | tf_op jit(solution)/shard_map/ppermute | solution.py:80
  7.9 5.5 %collective-permute-start = (bf16[512,2,8]{0,2,1:T(8,128)(2,1)S(1)}, bf16[512,2,8]{0,2,1:T(8,128)(2,1)S(1)}, u32[]{:S(2)}, u32[]{:S(2)}) collective-permute-start(bf16[512,2,8]{0,2,1:T(8,128)(2,1)S(1)} %get-tuple-element.46), channel_id=1, source_target_pairs={{0,1},{1,2},{2,3},{3,0},{4,5},{5,6},{6,7},{7,4},{8,9},{9,10},{10,1... | collective-permute-start | bytes 49160 | tf_op jit(solution)/shard_map/ppermute | solution.py:79
  13.5 9.0 %collective-permute-start.2 = (bf16[513,2,144]{0,2,1:T(8,128)(2,1)S(1)}, bf16[513,2,144]{0,2,1:T(8,128)(2,1)S(1)}, u32[]{:S(2)}, u32[]{:S(2)}) collective-permute-start(bf16[513,2,144]{0,2,1:T(8,128)(2,1)S(1)} %pad_maximum_fusion), channel_id=1, source_target_pairs={{0,4},{4,0},{1,5},{5,1},{2,6},{6,2},{3,7},{7,3},{8,12},{12,8},{9,1... | collective-permute-start | bytes 886472 | tf_op jit(solution)/shard_map/ppermute | solution.py:59
  31.4 1.7 %copy-start.1 = (bf16[4,3,144,3,136]{2,0,1,3,4:T(4,128)(2,1)S(1)}, bf16[4,3,144,3,136]{2,0,1,3,4:T(4,128)(2,1)}, u32[]{:S(2)}) copy-start(bf16[4,3,144,3,136]{2,0,1,3,4:T(4,128)(2,1)} %convert_bitcast_fusion) | copy-start | bytes 4230148
  33.9 1.2 %copy-start.4 = (bf16[136,128,3,2,3]{1,4,3,2,0:T(4,128)(2,1)S(1)}, bf16[136,128,3,2,3]{1,4,3,2,0:T(4,128)(2,1)}, u32[]{:S(2)}) copy-start(bf16[136,128,3,2,3]{1,4,3,2,0:T(4,128)(2,1)} %fusion.34) | copy-start | bytes 1880068
  34.7 1.8 %copy-start.5 = (bf16[256,4,136]{0,2,1:T(8,128)(2,1)}, bf16[256,4,136]{0,2,1:T(8,128)(2,1)S(1)}, u32[]{:S(2)}) copy-start(bf16[256,4,136]{0,2,1:T(8,128)(2,1)S(1)} %get-tuple-element.16) | copy-start | bytes 835588
  34.7 1.1 %copy-start.2 = (bf16[1,256,2,128]{3,2,1,0:T(2,128)(2,1)S(1)}, bf16[1,256,2,128]{3,2,1,0:T(2,128)(2,1)}, u32[]{:S(2)}) copy-start(bf16[1,256,2,128]{3,2,1,0:T(2,128)(2,1)} %param.13) | copy-start | bytes 393220
  36.1 1.9 %collective-permute-start.3 = (f32[384,256]{1,0:T(8,128)S(1)}, f32[384,256]{1,0:T(8,128)}, u32[]{:S(2)}, u32[]{:S(2)}) collective-permute-start(f32[384,256]{1,0:T(8,128)S(1)} %constant_dynamic-slice_fusion.5), channel_id=1, source_target_pairs={{0,8},{8,0},{16,24},{24,16},{1,9},{9,1},{17,25},{25,17},{2,10},{10... | collective-permute-start | bytes 1179656 | tf_op jit(solution)/shard_map/ppermute | solution.py:31
  36.6 4.7 %collective-permute-start.8 = (f32[384,256]{1,0:T(8,128)S(1)}, f32[384,256]{1,0:T(8,128)S(1)}, u32[]{:S(2)}, u32[]{:S(2)}) collective-permute-start(f32[384,256]{1,0:T(8,128)S(1)} %constant_dynamic-slice_fusion.2), channel_id=1, source_target_pairs={{0,8},{8,0},{16,24},{24,16},{1,9},{9,1},{17,25},{25,17},{2,10},{10... | collective-permute-start | bytes 1179656 | tf_op jit(solution)/shard_map/ppermute | solution.py:31
  39.8 13.0 %collective-permute-start.4 = (f32[192,256]{1,0:T(8,128)}, f32[192,256]{1,0:T(8,128)}, u32[]{:S(2)}, u32[]{:S(2)}) collective-permute-start(f32[192,256]{1,0:T(8,128)} %constant_dynamic-slice_fusion.4), channel_id=1, source_target_pairs={{0,16},{8,24},{16,0},{24,8},{1,17},{9,25},{17,1},{25,9},{2,18},{10... | collective-permute-start | bytes 589832 | tf_op jit(solution)/shard_map/ppermute | solution.py:31
  41.4 9.8 %collective-permute-start.9 = (f32[192,256]{1,0:T(8,128)S(1)}, f32[192,256]{1,0:T(8,128)S(1)}, u32[]{:S(2)}, u32[]{:S(2)}) collective-permute-start(f32[192,256]{1,0:T(8,128)S(1)} %constant_dynamic-slice_fusion.1), channel_id=1, source_target_pairs={{0,16},{8,24},{16,0},{24,8},{1,17},{9,25},{17,1},{25,9},{2,18},{10... | collective-permute-start | bytes 589832 | tf_op jit(solution)/shard_map/ppermute | solution.py:31
  46.0 23.5 %copy-start.3 = (bf16[3,256,256]{2,1,0:T(8,128)(2,1)S(1)}, bf16[3,256,256]{2,1,0:T(8,128)(2,1)}, u32[]{:S(2)}) copy-start(bf16[3,256,256]{2,1,0:T(8,128)(2,1)} %param.9) | copy-start | bytes 1179652
  51.2 5.1 %collective-permute-start.10 = (f32[96,256]{1,0:T(8,128)S(1)}, f32[96,256]{1,0:T(8,128)S(1)}, u32[]{:S(2)}, u32[]{:S(2)}) collective-permute-start(f32[96,256]{1,0:T(8,128)S(1)} %constant_dynamic-slice_fusion), channel_id=1, source_target_pairs={{0,4},{4,0},{1,5},{5,1},{2,6},{6,2},{3,7},{7,3},{8,12},{12,8},{9,1... | collective-permute-start | bytes 294920 | tf_op jit(solution)/shard_map/ppermute | solution.py:31
  53.8 4.7 %collective-permute-start.5 = (f32[96,256]{1,0:T(8,128)S(1)}, f32[96,256]{1,0:T(8,128)S(1)}, u32[]{:S(2)}, u32[]{:S(2)}) collective-permute-start(f32[96,256]{1,0:T(8,128)S(1)} %constant_dynamic-slice_fusion.3), channel_id=1, source_target_pairs={{0,4},{4,0},{1,5},{5,1},{2,6},{6,2},{3,7},{7,3},{8,12},{12,8},{9,1... | collective-permute-start | bytes 294920 | tf_op jit(solution)/shard_map/ppermute | solution.py:31
  56.4 5.5 %collective-permute-start.11 = (f32[96,256]{1,0:T(8,128)S(1)}, f32[96,256]{1,0:T(8,128)S(1)}, u32[]{:S(2)}, u32[]{:S(2)}) collective-permute-start(f32[96,256]{1,0:T(8,128)S(1)} %dynamic-slice_add_fusion.4), channel_id=1, source_target_pairs={{0,1},{1,0},{2,3},{3,2},{4,5},{5,4},{6,7},{7,6},{8,9},{9,8},{10,11... | collective-permute-start | bytes 294920 | tf_op jit(solution)/shard_map/ppermute | solution.py:39
  58.5 5.3 %collective-permute-start.6 = (f32[96,256]{1,0:T(8,128)S(1)}, f32[96,256]{1,0:T(8,128)S(1)}, u32[]{:S(2)}, u32[]{:S(2)}) collective-permute-start(f32[96,256]{1,0:T(8,128)S(1)} %dynamic-slice_add_fusion.5), channel_id=1, source_target_pairs={{0,1},{1,0},{2,3},{3,2},{4,5},{5,4},{6,7},{7,6},{8,9},{9,8},{10,11... | collective-permute-start | bytes 294920 | tf_op jit(solution)/shard_map/ppermute | solution.py:39
  61.8 7.1 %collective-permute-start.12 = (f32[96,256]{1,0:T(8,128)S(1)}, f32[96,256]{1,0:T(8,128)S(1)}, u32[]{:S(2)}, u32[]{:S(2)}) collective-permute-start(f32[96,256]{1,0:T(8,128)S(1)} %add.184), channel_id=1, source_target_pairs={{0,2},{1,3},{2,0},{3,1},{4,6},{5,7},{6,4},{7,5},{8,10},{9,11},{10,... | collective-permute-start | bytes 294920 | tf_op jit(solution)/shard_map/ppermute | solution.py:39
  63.8 7.2 %collective-permute-start.7 = (f32[96,256]{1,0:T(8,128)S(1)}, f32[96,256]{1,0:T(8,128)S(1)}, u32[]{:S(2)}, u32[]{:S(2)}) collective-permute-start(f32[96,256]{1,0:T(8,128)S(1)} %add.175), channel_id=1, source_target_pairs={{0,2},{1,3},{2,0},{3,1},{4,6},{5,7},{6,4},{7,5},{8,10},{9,11},{10,... | collective-permute-start | bytes 294920 | tf_op jit(solution)/shard_map/ppermute | solution.py:39
  68.9 4.2 %collective-permute-start.13 = (bf16[96,256]{1,0:T(8,128)(2,1)S(1)}, bf16[96,256]{1,0:T(8,128)(2,1)S(1)}, u32[]{:S(2)}, u32[]{:S(2)}) collective-permute-start(bf16[96,256]{1,0:T(8,128)(2,1)S(1)} %add.185), channel_id=1, source_target_pairs={{0,4},{4,0},{1,5},{5,1},{2,6},{6,2},{3,7},{7,3},{8,12},{12,8},{9,1... | collective-permute-start | bytes 147464 | tf_op jit(solution)/shard_map/ppermute | solution.py:46
  71.0 4.2 %collective-permute-start.16 = (bf16[96,256]{1,0:T(8,128)(2,1)S(1)}, bf16[96,256]{1,0:T(8,128)(2,1)S(1)}, u32[]{:S(2)}, u32[]{:S(2)}) collective-permute-start(bf16[96,256]{1,0:T(8,128)(2,1)S(1)} %add.176), channel_id=1, source_target_pairs={{0,4},{4,0},{1,5},{5,1},{2,6},{6,2},{3,7},{7,3},{8,12},{12,8},{9,1... | collective-permute-start | bytes 147464 | tf_op jit(solution)/shard_map/ppermute | solution.py:46
  73.1 4.7 %collective-permute-start.14 = (bf16[192,256]{1,0:T(8,128)(2,1)S(1)}, bf16[192,256]{1,0:T(8,128)(2,1)S(1)}, u32[]{:S(2)}, u32[]{:S(2)}) collective-permute-start(bf16[192,256]{1,0:T(8,128)(2,1)S(1)} %maximum_select_fusion.4), channel_id=1, source_target_pairs={{0,16},{8,24},{16,0},{24,8},{1,17},{9,25},{17,1},{25,9},{2,18},{10... | collective-permute-start | bytes 294920 | tf_op jit(solution)/shard_map/ppermute | solution.py:46
  75.2 4.7 %collective-permute-start.17 = (bf16[192,256]{1,0:T(8,128)(2,1)S(1)}, bf16[192,256]{1,0:T(8,128)(2,1)S(1)}, u32[]{:S(2)}, u32[]{:S(2)}) collective-permute-start(bf16[192,256]{1,0:T(8,128)(2,1)S(1)} %maximum_select_fusion.5), channel_id=1, source_target_pairs={{0,16},{8,24},{16,0},{24,8},{1,17},{9,25},{17,1},{25,9},{2,18},{10... | collective-permute-start | bytes 294920 | tf_op jit(solution)/shard_map/ppermute | solution.py:46
  77.9 3.7 %collective-permute-start.15 = (bf16[384,256]{1,0:T(8,128)(2,1)S(1)}, bf16[384,256]{1,0:T(8,128)(2,1)S(1)}, u32[]{:S(2)}, u32[]{:S(2)}) collective-permute-start(bf16[384,256]{1,0:T(8,128)(2,1)S(1)} %get-tuple-element.31), channel_id=1, source_target_pairs={{0,8},{8,0},{16,24},{24,16},{1,9},{9,1},{17,25},{25,17},{2,10},{10... | collective-permute-start | bytes 589832 | tf_op jit(solution)/shard_map/ppermute | solution.py:46
  80.0 2.6 %collective-permute-start.18 = (bf16[384,256]{1,0:T(8,128)(2,1)S(1)}, bf16[384,256]{1,0:T(8,128)(2,1)S(1)}, u32[]{:S(2)}, u32[]{:S(2)}) collective-permute-start(bf16[384,256]{1,0:T(8,128)(2,1)S(1)} %get-tuple-element.29), channel_id=1, source_target_pairs={{0,8},{8,0},{16,24},{24,16},{1,9},{9,1},{17,25},{25,17},{2,10},{10... | collective-permute-start | bytes 589832 | tf_op jit(solution)/shard_map/ppermute | solution.py:46

commit v16 on v11

--- a/solution.py
+++ b/solution.py
@@ -163,13 +163,14 @@
     stencil = coefficients(quadrature, lat_offsets, lon_offsets)
     basis_count = stencil.shape[0]
 
-    packed = lon_halo(jnp.concatenate([source, gradient], axis=0), LON_HALO)
+    packed = jnp.concatenate([source, gradient], axis=0)
     taps_per_row = stencil.size // row_count
     stencil_rows = jnp.transpose(stencil, (1, 0, 2, 3)).reshape(row_count, taps_per_row)
-    stencil_rows = jnp.pad(stencil_rows, ((0, 0), (0, packed.shape[2] - taps_per_row)))
-    framed = lat_halo(jnp.concatenate([packed, stencil_rows[None]], axis=0), 1, LAT_HALO)
-    source_wide, gradient_wide = framed[:channels], framed[channels : 2 * channels]
-    stencil_wide = framed[2 * channels, :, :taps_per_row].reshape(
+    stencil_rows = jnp.pad(stencil_rows, ((0, 0), (0, col_count - taps_per_row)))
+    tall = lat_halo(jnp.concatenate([packed, stencil_rows[None]], axis=0), 1, LAT_HALO)
+    framed = lon_halo(tall[: 2 * channels], LON_HALO)
+    source_wide, gradient_wide = framed[:channels], framed[channels:]
+    stencil_wide = tall[2 * channels, :, :taps_per_row].reshape(
         row_count + 2 * LAT_HALO, stencil.shape[0], stencil.shape[2], stencil.shape[3]
     )
     stencil_wide = jnp.transpose(stencil_wide, (1, 0, 2, 3))

time: 81.7 us -> 81.3 us (level)
  waiting for transfers between devices: 32.2 us -> 24.2 us
  starting transfers between devices: 18.2 us -> 22.4 us
  other arithmetic: 5.01 us -> 7.15 us
  local copies, waits for them, and re-layouts: 7.06 us -> 8.18 us
    ppermute x4, starting transfers between devices: 0.88 us -> 4.54 us  [halving_sum(): flat = flat + lax.ppermute(flat, axis, pairs)]
    ppermute x1, waiting for transfers between devices: 3.28 us -> 0.01 us  [lon_halo(): lax.ppermute(block[..., cols - width:], 'lon', [(i, (i + 1) % count) for...]
    ppermute x4, waiting for transfers between devices: 9.36 us -> 6.5 us  [halving_sum(): flat = flat + lax.ppermute(flat, axis, pairs)]
    add x6, other arithmetic: 0.18 us -> 2.17 us  [halving_sum(): flat = keep + lax.ppermute(send, axis, pairs)]
    ppermute x1, starting transfers between devices: 1.58 us -> 3.06 us  [lat_halo(): other = lax.ppermute(block, 'lat', [(0, 1), (1, 0)])]
    ppermute x1, starting transfers between devices: 5.13 us -> 3.87 us  [lon_halo(): lax.ppermute(block[..., :width], 'lon', [(i, (i - 1) % count) for i in ra...]
    another operation x1 -> x2, local copies, waits for them, and re-layouts: 0.03 us -> 0.97 us  [spread(): jnp.stack([values[:, offset:offset + row_count] for offset in range(lat_t...]
    ppermute x6, waiting for transfers between devices: 5.48 us -> 4.55 us  [halving_sum(): other = lax.ppermute(flat, axis, pairs)]
  transfers between devices with their start and end apart: 19 -> 19, of which waited for: 14 -> 13; matrix products, arithmetic and copies ran while one was open for 16% -> 23% of each run, Pallas kernels for 0% -> 0%
where the time goes in v16:
time: 81.3 us; the launch traced here: 80.9 us
  waiting for transfers between devices  24.2 us (30%)
  starting transfers between devices  22.4 us (28%)
  matrix products  17.8 us (22%)
  local copies, waits for them, and re-layouts  8.18 us (10%)
  other arithmetic  7.15 us (9%)
  between operations  1.12 us (1%)
    dot_general x3, matrix products, band_of(): jnp.einsum('kiad,dpq->iapkq', stencil, lon_picker(col_count, first_source...  7.41 us
    ppermute x6, waiting for transfers between devices, halving_sum(): flat = keep + lax.ppermute(send, axis, pairs)  7.31 us
    ppermute x4, waiting for transfers between devices, halving_sum(): flat = flat + lax.ppermute(flat, axis, pairs)  6.5 us
    ppermute x6, starting transfers between devices, halving_sum(): flat = keep + lax.ppermute(send, axis, pairs)  5.88 us
    ppermute x1, waiting for transfers between devices, lat_halo(): other = lax.ppermute(block, 'lat', [(0, 1), (1, 0)])  5.82 us
    unnamed x22, local copies, waits for them, and re-layouts  5.81 us
    ppermute x6, starting transfers between devices, halving_sum(): other = lax.ppermute(flat, axis, pairs)  5.07 us
    ppermute x6, waiting for transfers between devices, halving_sum(): other = lax.ppermute(flat, axis, pairs)  4.55 us
  transfers between devices with their start and end apart: 19, of which 13 were waited for; matrix products, arithmetic and copies ran while one was open for 23% of the time, Pallas kernels for 0%

profile of v16, /device:TPU:0, one launch (start us, length us, event | category | flops | bytes accessed | tf_op | source)
XLA Modules:
  0.0 80.9 jit_solution(7003698975052157864)
XLA Ops:
  0.6 0.8 broadcast_add_fusion
  1.4 0.9 %convolution_convert_fusion.2 = bf16[3,2,3,9]{3,2,1,0:T(4,128)(2,1)S(1)} fusion(s32[2,3,12]{2,0,1:T(2,128)S(1)} %get-tuple-element.40, f32[2,3,12]{2,0,1:T(2,128)} %param.10, s32[2,3,12]{2,0,1:T(2,128)S(1)} %get-tuple-element.41), kind=kOutput, calls=%fused_computation.38 | convolution fusion | flops 24570 | bytes 1188 | tf_op jit(solution)/shard_map/rks,rksa,rksd->krad/dot_general | solution.py:85
  2.3 0.1 reshape.71
  2.4 0.1 copy.28
  2.6 1.0 %copy.26 = bf16[1,256,2,128]{1,3,2,0:T(8,128)(2,1)S(1)} copy(bf16[1,256,2,128]{3,2,1,0:T(2,128)(2,1)} %param.13) | data formatting | bytes 262144 | tf_op args[6]
  3.6 1.0 %copy.25 = bf16[1,256,2,128]{1,3,2,0:T(8,128)(2,1)S(1)} copy(bf16[1,256,2,128]{3,2,1,0:T(2,128)(2,1)} %param.7) | data formatting | bytes 262144 | tf_op args[0]
  4.7 3.1 %collective-permute-start = (bf16[513,2,128]{0,2,1:T(8,128)(2,1)S(1)}, bf16[513,2,128]{0,2,1:T(8,128)(2,1)S(1)}, u32[]{:S(2)}, u32[]{:S(2)}) collective-permute-start(bf16[513,2,128]{0,2,1:T(8,128)(2,1)S(1)} %pad_maximum_fusion.2), channel_id=1, source_target_pairs={{0,4},{4,0},{1,5},{5,1},{2,6},{6,2},{3,7},{7,3},{8,12},{12,8},{9,1... | collective-permute-start | bytes 787976 | tf_op jit(solution)/shard_map/ppermute | solution.py:55
  7.7 0.1 fusion.42
  7.8 0.2 fusion.29
  8.1 1.5 %fusion.34 = bf16[136,128,3,2,3]{1,4,3,2,0:T(4,128)(2,1)} fusion(pred[9,136,128,1,1]{2,1,0,3,4:T(8,128)(4,1)S(1)} %fusion.42, bf16[3,2,3,9]{3,2,1,0:T(4,128)(2,1)S(1)} %convolution_convert_fusion.2), kind=kOutput, calls=%fused_computation.36 | convolution fusion | flops 5640192 | bytes 783684 | tf_op jit(solution)/shard_map/kiad,dpq->iapkq/dot_general | solution.py:104
  9.6 5.8 %collective-permute-done = bf16[513,2,128]{0,2,1:T(8,128)(2,1)S(1)} collective-permute-done((bf16[513,2,128]{0,2,1:T(8,128)(2,1)S(1)}, bf16[513,2,128]{0,2,1:T(8,128)(2,1)S(1)}, u32[]{:S(2)}, u32[]{:S(2)}) %collective-permute-start) | collective-permute-done | bytes 262688 | tf_op jit(solution)/shard_map/ppermute | solution.py:55
  15.5 0.2 maximum_reduce_fusion
  15.7 3.9 %collective-permute-start.2 = (bf16[512,6,8]{0,2,1:T(8,128)(2,1)S(1)}, bf16[512,6,8]{0,2,1:T(8,128)(2,1)S(1)}, u32[]{:S(2)}, u32[]{:S(2)}) collective-permute-start(bf16[512,6,8]{0,2,1:T(8,128)(2,1)S(1)} %get-tuple-element.27), channel_id=1, source_target_pairs={{0,3},{1,0},{2,1},{3,2},{4,7},{5,4},{6,5},{7,6},{8,11},{9,8},{10,9... | collective-permute-start | bytes 147464 | tf_op jit(solution)/shard_map/ppermute | solution.py:76
  19.5 0.1 reshape_squeeze.3
  19.6 3.0 %convert_bitcast_fusion = bf16[4,3,144,3,136]{2,0,1,3,4:T(4,128)(2,1)} fusion(bf16[3,6,3,9]{3,1,2,0:T(8,128)(2,1)S(1)} %bitcast.201), kind=kOutput, calls=%fused_computation.8 | convolution fusion | flops 13747968 | bytes 1419264 | tf_op jit(solution)/shard_map/kiad,dpq->iapkq/dot_general | solution.py:104
  22.6 2.9 %fusion.10 = bf16[136,144,3,4,3]{1,3,4,2,0:T(4,128)(2,1)} fusion(pred[9,136,144,1,1]{2,1,0,3,4:T(8,128)(4,1)S(1)} %fusion.29, bf16[3,6,3,9]{3,1,2,0:T(8,128)(2,1)S(1)} %bitcast.202, pred[]{:T(512)S(6)} %eq.72), kind=kOutput, calls=%fused_computation.12 | convolution fusion | flops 12690756 | bytes 1587277 | tf_op jit(solution)/shard_map/kiad,dpq->iapkq/dot_general | solution.py:104
  25.6 0.1 pad_maximum_fusion
  25.8 0.1 pad_maximum_fusion.1
  25.8 0.9 %slice_bitcast_fusion.5 = (bf16[256,4,1,144]{0,3,2,1:T(8,128)(2,1)}, bf16[256,4,1,144]{0,3,2,1:T(8,128)(2,1)}, bf16[256,4,1,144]{0,3,2,1:T(8,128)(2,1)}) fusion(bf16[512,6,144]{0,2,1:T(8,128)(2,1)S(1)} %pad_maximum_fusion.1), kind=kLoop, calls=%fused_computation.90 | loop fusion | bytes 1769472 | tf_op jit(solution)/shard_map/stack | solution.py:115
  26.8 2.7 %fusion.19 = f32[256,4,3,136]{0,3,1,2:T(8,128)S(1)} fusion(bf16[3,256,256]{2,1,0:T(8,128)(2,1)S(1)} %copy-done.3, bf16[512,6,144]{0,2,1:T(8,128)(2,1)S(1)} %pad_maximum_fusion.1, pred[]{:T(512)S(6)} %eq.72, bf16[136,144,3,4,3]{1,3,4,2,0:T(4,128)(2,1)} %fusion.10), kind=kOutput, calls=%fused_computation.16 | convolution fusion | flops 588054528 | bytes 4064257 | tf_op jit(solution)/shard_map/cikq,iapkq->ciap/dot_general | solution.py:137
  29.6 0.1 fusion.56
  29.7 1.4 %copy-done.1 = bf16[4,3,144,3,136]{2,0,1,3,4:T(4,128)(2,1)S(1)} copy-done((bf16[4,3,144,3,136]{2,0,1,3,4:T(4,128)(2,1)S(1)}, bf16[4,3,144,3,136]{2,0,1,3,4:T(4,128)(2,1)}, u32[]{:S(2)}) %copy-start.1) | copy-done | bytes 1410072
  31.2 0.1 copy-done.5
  31.3 0.1 copy-done.6
  31.3 0.8 fusion.24
  32.1 0.8 fusion.46
  33.0 0.3 copy-done.7
  33.3 0.4 fusion.31
  33.7 0.3 copy-done.2
  34.0 0.3 fusion.27
  34.4 0.3 fusion.28
  34.7 0.8 constant_dynamic-slice_fusion.4
  35.5 0.5 collective-permute-start.4
  36.0 0.2 collective-permute-done.3
  36.2 1.0 %dynamic-slice_add_fusion.1 = f32[384,256]{1,0:T(8,128)S(1)} fusion(f32[384,256]{1,0:T(8,128)} %collective-permute-done.3, f32[768,256]{1,0:T(8,128)S(1)} %bitcast.196, s32[]{:T(128)S(6)} %select_n.164), kind=kLoop, calls=%fused_computation.81 | loop fusion | flops 98304 | bytes 1179652 | tf_op jit(solution)/shard_map/add | solution.py:31
  37.3 0.4 collective-permute-done.4
  37.7 1.0 %dynamic-slice_add_fusion = f32[384,256]{1,0:T(8,128)S(1)} fusion(f32[384,256]{1,0:T(8,128)} %collective-permute-done.4, f32[768,256]{1,0:T(8,128)S(1)} %bitcast.200, s32[]{:T(128)S(6)} %select_n.164), kind=kLoop, calls=%fused_computation.80 | loop fusion | flops 98304 | bytes 1179652 | tf_op jit(solution)/shard_map/add | solution.py:31
  38.8 1.5 %collective-permute-start.5 = (f32[192,256]{1,0:T(8,128)S(1)}, f32[192,256]{1,0:T(8,128)S(1)}, u32[]{:S(2)}, u32[]{:S(2)}) collective-permute-start(f32[192,256]{1,0:T(8,128)S(1)} %constant_dynamic-slice_fusion.3), channel_id=1, source_target_pairs={{0,16},{8,24},{16,0},{24,8},{1,17},{9,25},{17,1},{25,9},{2,18},{10... | collective-permute-start | bytes 589832 | tf_op jit(solution)/shard_map/ppermute | solution.py:31
  40.3 0.6 collective-permute-start.12
  41.0 4.0 %fusion.14 = f32[256,4,3,144]{0,3,2,1:T(8,128)} fusion(bf16[4,3,144,3,136]{2,0,1,3,4:T(4,128)(2,1)} %convert_bitcast_fusion, bf16[3,256,256]{2,1,0:T(8,128)(2,1)S(1)} %copy-done, bf16[256,4,136]{0,2,1:T(8,128)(2,1)} %copy-done.8), kind=kOutput, calls=%fused_computation.15 | convolution fusion | flops 575299584 | bytes 3851264 | tf_op jit(solution)/shard_map/cikq,iapkq->ciap/dot_general | solution.py:124
  45.0 1.7 %collective-permute-done.5 = f32[192,256]{1,0:T(8,128)S(1)} collective-permute-done((f32[192,256]{1,0:T(8,128)S(1)}, f32[192,256]{1,0:T(8,128)S(1)}, u32[]{:S(2)}, u32[]{:S(2)}) %collective-permute-start.5) | collective-permute-done | bytes 196640 | tf_op jit(solution)/shard_map/ppermute | solution.py:31
  46.7 1.6 %collective-permute-start.6 = (f32[96,256]{1,0:T(8,128)S(1)}, f32[96,256]{1,0:T(8,128)S(1)}, u32[]{:S(2)}, u32[]{:S(2)}) collective-permute-start(f32[96,256]{1,0:T(8,128)S(1)} %constant_dynamic-slice_fusion.2), channel_id=1, source_target_pairs={{0,4},{4,0},{1,5},{5,1},{2,6},{6,2},{3,7},{7,3},{8,12},{12,8},{9,1... | collective-permute-start | bytes 294920 | tf_op jit(solution)/shard_map/ppermute | solution.py:31
  48.3 2.0 %collective-permute-done.12 = f32[192,256]{1,0:T(8,128)S(1)} collective-permute-done((f32[192,256]{1,0:T(8,128)S(1)}, f32[192,256]{1,0:T(8,128)S(1)}, u32[]{:S(2)}, u32[]{:S(2)}) %collective-permute-start.12) | collective-permute-done | bytes 196640 | tf_op jit(solution)/shard_map/ppermute | solution.py:31
  50.3 1.6 %collective-permute-start.13 = (f32[96,256]{1,0:T(8,128)S(1)}, f32[96,256]{1,0:T(8,128)S(1)}, u32[]{:S(2)}, u32[]{:S(2)}) collective-permute-start(f32[96,256]{1,0:T(8,128)S(1)} %constant_dynamic-slice_fusion), channel_id=1, source_target_pairs={{0,4},{4,0},{1,5},{5,1},{2,6},{6,2},{3,7},{7,3},{8,12},{12,8},{9,1... | collective-permute-start | bytes 294920 | tf_op jit(solution)/shard_map/ppermute | solution.py:31
  52.0 3.0 %collective-permute-done.13 = f32[96,256]{1,0:T(8,128)S(1)} collective-permute-done((f32[96,256]{1,0:T(8,128)S(1)}, f32[96,256]{1,0:T(8,128)S(1)}, u32[]{:S(2)}, u32[]{:S(2)}) %collective-permute-start.13) | collective-permute-done | bytes 98336 | tf_op jit(solution)/shard_map/ppermute | solution.py:31
  55.1 2.1 %collective-permute-done.7 = f32[96,256]{1,0:T(8,128)S(1)} collective-permute-done((f32[96,256]{1,0:T(8,128)S(1)}, f32[96,256]{1,0:T(8,128)S(1)}, u32[]{:S(2)}, u32[]{:S(2)}) %collective-permute-start.7) | collective-permute-done | bytes 98336 | tf_op jit(solution)/shard_map/ppermute | solution.py:37
  57.2 2.4 %collective-permute-start.8 = (f32[96,256]{1,0:T(8,128)S(1)}, f32[96,256]{1,0:T(8,128)S(1)}, u32[]{:S(2)}, u32[]{:S(2)}) collective-permute-start(f32[96,256]{1,0:T(8,128)S(1)} %add.182), channel_id=1, source_target_pairs={{0,2},{1,3},{2,0},{3,1},{4,6},{5,7},{6,4},{7,5},{8,10},{9,11},{10,... | collective-permute-start | bytes 294920 | tf_op jit(solution)/shard_map/ppermute | solution.py:37
  59.5 1.1 %fusion.75 = bf16[1,256,2,128]{1,3,2,0:T(8,128)(2,1)S(1)} fusion(f32[256,4,3,144]{0,3,2,1:T(8,128)} %fusion.14), kind=kLoop, calls=%fused_computation.104 | loop fusion | flops 196608 | bytes 917504 | tf_op jit(solution)/shard_map/convert_element_type | solution.py:224
  60.7 2.0 %collective-permute-start.15 = (f32[96,256]{1,0:T(8,128)S(1)}, f32[96,256]{1,0:T(8,128)S(1)}, u32[]{:S(2)}, u32[]{:S(2)}) collective-permute-start(f32[96,256]{1,0:T(8,128)S(1)} %add.186), channel_id=1, source_target_pairs={{0,2},{1,3},{2,0},{3,1},{4,6},{5,7},{6,4},{7,5},{8,10},{9,11},{10,... | collective-permute-start | bytes 294920 | tf_op jit(solution)/shard_map/ppermute | solution.py:37
  62.7 2.8 %collective-permute-done.8 = f32[96,256]{1,0:T(8,128)S(1)} collective-permute-done((f32[96,256]{1,0:T(8,128)S(1)}, f32[96,256]{1,0:T(8,128)S(1)}, u32[]{:S(2)}, u32[]{:S(2)}) %collective-permute-start.8) | collective-permute-done | bytes 98336 | tf_op jit(solution)/shard_map/ppermute | solution.py:37
  65.5 0.8 collective-permute-start.9
  66.3 1.7 %collective-permute-done.15 = f32[96,256]{1,0:T(8,128)S(1)} collective-permute-done((f32[96,256]{1,0:T(8,128)S(1)}, f32[96,256]{1,0:T(8,128)S(1)}, u32[]{:S(2)}, u32[]{:S(2)}) %collective-permute-start.15) | collective-permute-done | bytes 98336 | tf_op jit(solution)/shard_map/ppermute | solution.py:37
  68.0 1.0 %collective-permute-start.16 = (bf16[96,256]{1,0:T(8,128)(2,1)S(1)}, bf16[96,256]{1,0:T(8,128)(2,1)S(1)}, u32[]{:S(2)}, u32[]{:S(2)}) collective-permute-start(bf16[96,256]{1,0:T(8,128)(2,1)S(1)} %add_convert_fusion), channel_id=1, source_target_pairs={{0,4},{4,0},{1,5},{5,1},{2,6},{6,2},{3,7},{7,3},{8,12},{12,8},{9,1... | collective-permute-start | bytes 147464 | tf_op jit(solution)/shard_map/ppermute | solution.py:42
  69.0 1.1 %collective-permute-done.9 = bf16[96,256]{1,0:T(8,128)(2,1)S(1)} collective-permute-done((bf16[96,256]{1,0:T(8,128)(2,1)S(1)}, bf16[96,256]{1,0:T(8,128)(2,1)S(1)}, u32[]{:S(2)}, u32[]{:S(2)}) %collective-permute-start.9) | collective-permute-done | bytes 49184 | tf_op jit(solution)/shard_map/ppermute | solution.py:42
  70.2 1.6 %collective-permute-start.10 = (bf16[192,256]{1,0:T(8,128)(2,1)S(1)}, bf16[192,256]{1,0:T(8,128)(2,1)S(1)}, u32[]{:S(2)}, u32[]{:S(2)}) collective-permute-start(bf16[192,256]{1,0:T(8,128)(2,1)S(1)} %maximum_select_fusion.4), channel_id=1, source_target_pairs={{0,16},{8,24},{16,0},{24,8},{1,17},{9,25},{17,1},{25,9},{2,18},{10... | collective-permute-start | bytes 294920 | tf_op jit(solution)/shard_map/ppermute | solution.py:42
  71.7 0.5 collective-permute-done.16
  72.2 1.6 %collective-permute-start.17 = (bf16[192,256]{1,0:T(8,128)(2,1)S(1)}, bf16[192,256]{1,0:T(8,128)(2,1)S(1)}, u32[]{:S(2)}, u32[]{:S(2)}) collective-permute-start(bf16[192,256]{1,0:T(8,128)(2,1)S(1)} %maximum_select_fusion.5), channel_id=1, source_target_pairs={{0,16},{8,24},{16,0},{24,8},{1,17},{9,25},{17,1},{25,9},{2,18},{10... | collective-permute-start | bytes 294920 | tf_op jit(solution)/shard_map/ppermute | solution.py:42
  73.8 1.2 %collective-permute-done.10 = bf16[192,256]{1,0:T(8,128)(2,1)S(1)} collective-permute-done((bf16[192,256]{1,0:T(8,128)(2,1)S(1)}, bf16[192,256]{1,0:T(8,128)(2,1)S(1)}, u32[]{:S(2)}, u32[]{:S(2)}) %collective-permute-start.10) | collective-permute-done | bytes 98336 | tf_op jit(solution)/shard_map/ppermute | solution.py:42
  75.1 1.8 %collective-permute-done.17 = bf16[192,256]{1,0:T(8,128)(2,1)S(1)} collective-permute-done((bf16[192,256]{1,0:T(8,128)(2,1)S(1)}, bf16[192,256]{1,0:T(8,128)(2,1)S(1)}, u32[]{:S(2)}, u32[]{:S(2)}) %collective-permute-start.17) | collective-permute-done | bytes 98336 | tf_op jit(solution)/shard_map/ppermute | solution.py:42
  77.0 0.3 fusion.33
  77.3 0.8 copy.40
  78.1 0.8 copy.41
  78.9 0.9 %maximum_select_fusion = f32[768,256]{1,0:T(8,128)} fusion(f32[384,256]{1,0:T(8,128)S(1)} %get-tuple-element.22, f32[384,256]{1,0:T(8,128)S(1)} %convert_element_type.134, pred[]{:T(512)S(6)} %eq.74), kind=kLoop, calls=%fused_computation.48 | loop fusion | flops 589824 | bytes 1572865 | tf_op jit(solution)/shard_map/jit(_where)/select_n | solution.py:45
  79.9 0.9 %maximum_select_fusion.1 = f32[768,256]{1,0:T(8,128)} fusion(f32[384,256]{1,0:T(8,128)S(1)} %get-tuple-element.20, f32[384,256]{1,0:T(8,128)S(1)} %convert_element_type.137, pred[]{:T(512)S(6)} %eq.74), kind=kLoop, calls=%fused_computation.49 | loop fusion | flops 589824 | bytes 1572865 | tf_op jit(solution)/shard_map/jit(_where)/select_n | solution.py:45
  (56 shorter events, 1.2 us)
Async XLA Ops:
  0.6 31.5 %copy-start = (bf16[3,256,256]{2,1,0:T(8,128)(2,1)S(1)}, bf16[3,256,256]{2,1,0:T(8,128)(2,1)}, u32[]{:S(2)}) copy-start(bf16[3,256,256]{2,1,0:T(8,128)(2,1)} %param.8) | copy-start | bytes 1179652
  4.7 10.8 %collective-permute-start = (bf16[513,2,128]{0,2,1:T(8,128)(2,1)S(1)}, bf16[513,2,128]{0,2,1:T(8,128)(2,1)S(1)}, u32[]{:S(2)}, u32[]{:S(2)}) collective-permute-start(bf16[513,2,128]{0,2,1:T(8,128)(2,1)S(1)} %pad_maximum_fusion.2), channel_id=1, source_target_pairs={{0,4},{4,0},{1,5},{5,1},{2,6},{6,2},{3,7},{7,3},{8,12},{12,8},{9,1... | collective-permute-start | bytes 787976 | tf_op jit(solution)/shard_map/ppermute | solution.py:55
  15.7 10.1 %collective-permute-start.2 = (bf16[512,6,8]{0,2,1:T(8,128)(2,1)S(1)}, bf16[512,6,8]{0,2,1:T(8,128)(2,1)S(1)}, u32[]{:S(2)}, u32[]{:S(2)}) collective-permute-start(bf16[512,6,8]{0,2,1:T(8,128)(2,1)S(1)} %get-tuple-element.27), channel_id=1, source_target_pairs={{0,3},{1,0},{2,1},{3,2},{4,7},{5,4},{6,5},{7,6},{8,11},{9,8},{10,9... | collective-permute-start | bytes 147464 | tf_op jit(solution)/shard_map/ppermute | solution.py:76
  19.5 6.2 %collective-permute-start.1 = (bf16[512,6,8]{0,2,1:T(8,128)(2,1)S(1)}, bf16[512,6,8]{0,2,1:T(8,128)(2,1)S(1)}, u32[]{:S(2)}, u32[]{:S(2)}) collective-permute-start(bf16[512,6,8]{0,2,1:T(8,128)(2,1)S(1)} %get-tuple-element.26), channel_id=1, source_target_pairs={{0,1},{1,2},{2,3},{3,0},{4,5},{5,6},{6,7},{7,4},{8,9},{9,10},{10,1... | collective-permute-start | bytes 147464 | tf_op jit(solution)/shard_map/ppermute | solution.py:75
  25.7 1.1 %copy-start.3 = (bf16[3,256,256]{2,1,0:T(8,128)(2,1)S(1)}, bf16[3,256,256]{2,1,0:T(8,128)(2,1)}, u32[]{:S(2)}) copy-start(bf16[3,256,256]{2,1,0:T(8,128)(2,1)} %param.9) | copy-start | bytes 1179652
  29.5 1.7 %copy-start.1 = (bf16[4,3,144,3,136]{2,0,1,3,4:T(4,128)(2,1)S(1)}, bf16[4,3,144,3,136]{2,0,1,3,4:T(4,128)(2,1)}, u32[]{:S(2)}) copy-start(bf16[4,3,144,3,136]{2,0,1,3,4:T(4,128)(2,1)} %convert_bitcast_fusion) | copy-start | bytes 4230148
  29.5 1.7 %copy-start.4 = (bf16[256,4,1,144]{0,3,2,1:T(8,128)(2,1)S(1)}, bf16[256,4,1,144]{0,3,2,1:T(8,128)(2,1)}, u32[]{:S(2)}) copy-start(bf16[256,4,1,144]{0,3,2,1:T(8,128)(2,1)} %get-tuple-element.28) | copy-start | bytes 884740
  29.5 1.8 %copy-start.5 = (bf16[256,4,1,144]{0,3,2,1:T(8,128)(2,1)S(1)}, bf16[256,4,1,144]{0,3,2,1:T(8,128)(2,1)}, u32[]{:S(2)}) copy-start(bf16[256,4,1,144]{0,3,2,1:T(8,128)(2,1)} %get-tuple-element.29) | copy-start | bytes 884740
  29.5 1.9 %copy-start.6 = (bf16[256,4,1,144]{0,3,2,1:T(8,128)(2,1)S(1)}, bf16[256,4,1,144]{0,3,2,1:T(8,128)(2,1)}, u32[]{:S(2)}) copy-start(bf16[256,4,1,144]{0,3,2,1:T(8,128)(2,1)} %get-tuple-element.30) | copy-start | bytes 884740
  32.1 1.2 %copy-start.7 = (bf16[136,128,3,2,3]{1,4,3,2,0:T(4,128)(2,1)S(1)}, bf16[136,128,3,2,3]{1,4,3,2,0:T(4,128)(2,1)}, u32[]{:S(2)}) copy-start(bf16[136,128,3,2,3]{1,4,3,2,0:T(4,128)(2,1)} %fusion.34) | copy-start | bytes 1880068
  32.9 1.8 %copy-start.8 = (bf16[256,4,136]{0,2,1:T(8,128)(2,1)}, bf16[256,4,136]{0,2,1:T(8,128)(2,1)S(1)}, u32[]{:S(2)}) copy-start(bf16[256,4,136]{0,2,1:T(8,128)(2,1)S(1)} %get-tuple-element.9) | copy-start | bytes 835588
  32.9 1.1 %copy-start.2 = (bf16[1,256,2,128]{3,2,1,0:T(2,128)(2,1)S(1)}, bf16[1,256,2,128]{3,2,1,0:T(2,128)(2,1)}, u32[]{:S(2)}) copy-start(bf16[1,256,2,128]{3,2,1,0:T(2,128)(2,1)} %param.13) | copy-start | bytes 393220
  34.3 1.9 %collective-permute-start.3 = (f32[384,256]{1,0:T(8,128)S(1)}, f32[384,256]{1,0:T(8,128)}, u32[]{:S(2)}, u32[]{:S(2)}) collective-permute-start(f32[384,256]{1,0:T(8,128)S(1)} %constant_dynamic-slice_fusion.5), channel_id=1, source_target_pairs={{0,8},{8,0},{16,24},{24,16},{1,9},{9,1},{17,25},{25,17},{2,10},{10... | collective-permute-start | bytes 1179656 | tf_op jit(solution)/shard_map/ppermute | solution.py:31
  35.5 2.2 %collective-permute-start.4 = (f32[384,256]{1,0:T(8,128)}, f32[384,256]{1,0:T(8,128)}, u32[]{:S(2)}, u32[]{:S(2)}) collective-permute-start(f32[384,256]{1,0:T(8,128)} %constant_dynamic-slice_fusion.4), channel_id=1, source_target_pairs={{0,8},{8,0},{16,24},{24,16},{1,9},{9,1},{17,25},{25,17},{2,10},{10... | collective-permute-start | bytes 1179656 | tf_op jit(solution)/shard_map/ppermute | solution.py:31
  38.8 7.8 %collective-permute-start.5 = (f32[192,256]{1,0:T(8,128)S(1)}, f32[192,256]{1,0:T(8,128)S(1)}, u32[]{:S(2)}, u32[]{:S(2)}) collective-permute-start(f32[192,256]{1,0:T(8,128)S(1)} %constant_dynamic-slice_fusion.3), channel_id=1, source_target_pairs={{0,16},{8,24},{16,0},{24,8},{1,17},{9,25},{17,1},{25,9},{2,18},{10... | collective-permute-start | bytes 589832 | tf_op jit(solution)/shard_map/ppermute | solution.py:31
  40.3 9.9 %collective-permute-start.12 = (f32[192,256]{1,0:T(8,128)S(1)}, f32[192,256]{1,0:T(8,128)S(1)}, u32[]{:S(2)}, u32[]{:S(2)}) collective-permute-start(f32[192,256]{1,0:T(8,128)S(1)} %constant_dynamic-slice_fusion.1), channel_id=1, source_target_pairs={{0,16},{8,24},{16,0},{24,8},{1,17},{9,25},{17,1},{25,9},{2,18},{10... | collective-permute-start | bytes 589832 | tf_op jit(solution)/shard_map/ppermute | solution.py:31
  46.7 5.2 %collective-permute-start.6 = (f32[96,256]{1,0:T(8,128)S(1)}, f32[96,256]{1,0:T(8,128)S(1)}, u32[]{:S(2)}, u32[]{:S(2)}) collective-permute-start(f32[96,256]{1,0:T(8,128)S(1)} %constant_dynamic-slice_fusion.2), channel_id=1, source_target_pairs={{0,4},{4,0},{1,5},{5,1},{2,6},{6,2},{3,7},{7,3},{8,12},{12,8},{9,1... | collective-permute-start | bytes 294920 | tf_op jit(solution)/shard_map/ppermute | solution.py:31
  50.3 4.7 %collective-permute-start.13 = (f32[96,256]{1,0:T(8,128)S(1)}, f32[96,256]{1,0:T(8,128)S(1)}, u32[]{:S(2)}, u32[]{:S(2)}) collective-permute-start(f32[96,256]{1,0:T(8,128)S(1)} %constant_dynamic-slice_fusion), channel_id=1, source_target_pairs={{0,4},{4,0},{1,5},{5,1},{2,6},{6,2},{3,7},{7,3},{8,12},{12,8},{9,1... | collective-permute-start | bytes 294920 | tf_op jit(solution)/shard_map/ppermute | solution.py:31
  51.9 5.2 %collective-permute-start.7 = (f32[96,256]{1,0:T(8,128)S(1)}, f32[96,256]{1,0:T(8,128)S(1)}, u32[]{:S(2)}, u32[]{:S(2)}) collective-permute-start(f32[96,256]{1,0:T(8,128)S(1)} %dynamic-slice_add_fusion.5), channel_id=1, source_target_pairs={{0,1},{1,0},{2,3},{3,2},{4,5},{5,4},{6,7},{7,6},{8,9},{9,8},{10,11... | collective-permute-start | bytes 294920 | tf_op jit(solution)/shard_map/ppermute | solution.py:37
  55.0 5.7 %collective-permute-start.14 = (f32[96,256]{1,0:T(8,128)S(1)}, f32[96,256]{1,0:T(8,128)S(1)}, u32[]{:S(2)}, u32[]{:S(2)}) collective-permute-start(f32[96,256]{1,0:T(8,128)S(1)} %dynamic-slice_add_fusion.4), channel_id=1, source_target_pairs={{0,1},{1,0},{2,3},{3,2},{4,5},{5,4},{6,7},{7,6},{8,9},{9,8},{10,11... | collective-permute-start | bytes 294920 | tf_op jit(solution)/shard_map/ppermute | solution.py:37
  57.2 8.3 %collective-permute-start.8 = (f32[96,256]{1,0:T(8,128)S(1)}, f32[96,256]{1,0:T(8,128)S(1)}, u32[]{:S(2)}, u32[]{:S(2)}) collective-permute-start(f32[96,256]{1,0:T(8,128)S(1)} %add.182), channel_id=1, source_target_pairs={{0,2},{1,3},{2,0},{3,1},{4,6},{5,7},{6,4},{7,5},{8,10},{9,11},{10,... | collective-permute-start | bytes 294920 | tf_op jit(solution)/shard_map/ppermute | solution.py:37
  60.7 7.3 %collective-permute-start.15 = (f32[96,256]{1,0:T(8,128)S(1)}, f32[96,256]{1,0:T(8,128)S(1)}, u32[]{:S(2)}, u32[]{:S(2)}) collective-permute-start(f32[96,256]{1,0:T(8,128)S(1)} %add.186), channel_id=1, source_target_pairs={{0,2},{1,3},{2,0},{3,1},{4,6},{5,7},{6,4},{7,5},{8,10},{9,11},{10,... | collective-permute-start | bytes 294920 | tf_op jit(solution)/shard_map/ppermute | solution.py:37
  65.5 4.6 %collective-permute-start.9 = (bf16[96,256]{1,0:T(8,128)(2,1)S(1)}, bf16[96,256]{1,0:T(8,128)(2,1)S(1)}, u32[]{:S(2)}, u32[]{:S(2)}) collective-permute-start(bf16[96,256]{1,0:T(8,128)(2,1)S(1)} %add_convert_fusion.1), channel_id=1, source_target_pairs={{0,4},{4,0},{1,5},{5,1},{2,6},{6,2},{3,7},{7,3},{8,12},{12,8},{9,1... | collective-permute-start | bytes 147464 | tf_op jit(solution)/shard_map/ppermute | solution.py:42
  68.0 4.2 %collective-permute-start.16 = (bf16[96,256]{1,0:T(8,128)(2,1)S(1)}, bf16[96,256]{1,0:T(8,128)(2,1)S(1)}, u32[]{:S(2)}, u32[]{:S(2)}) collective-permute-start(bf16[96,256]{1,0:T(8,128)(2,1)S(1)} %add_convert_fusion), channel_id=1, source_target_pairs={{0,4},{4,0},{1,5},{5,1},{2,6},{6,2},{3,7},{7,3},{8,12},{12,8},{9,1... | collective-permute-start | bytes 147464 | tf_op jit(solution)/shard_map/ppermute | solution.py:42
  70.2 4.8 %collective-permute-start.10 = (bf16[192,256]{1,0:T(8,128)(2,1)S(1)}, bf16[192,256]{1,0:T(8,128)(2,1)S(1)}, u32[]{:S(2)}, u32[]{:S(2)}) collective-permute-start(bf16[192,256]{1,0:T(8,128)(2,1)S(1)} %maximum_select_fusion.4), channel_id=1, source_target_pairs={{0,16},{8,24},{16,0},{24,8},{1,17},{9,25},{17,1},{25,9},{2,18},{10... | collective-permute-start | bytes 294920 | tf_op jit(solution)/shard_map/ppermute | solution.py:42
  72.2 4.7 %collective-permute-start.17 = (bf16[192,256]{1,0:T(8,128)(2,1)S(1)}, bf16[192,256]{1,0:T(8,128)(2,1)S(1)}, u32[]{:S(2)}, u32[]{:S(2)}) collective-permute-start(bf16[192,256]{1,0:T(8,128)(2,1)S(1)} %maximum_select_fusion.5), channel_id=1, source_target_pairs={{0,16},{8,24},{16,0},{24,8},{1,17},{9,25},{17,1},{25,9},{2,18},{10... | collective-permute-start | bytes 294920 | tf_op jit(solution)/shard_map/ppermute | solution.py:42
  75.0 3.9 %collective-permute-start.11 = (bf16[384,256]{1,0:T(8,128)(2,1)S(1)}, bf16[384,256]{1,0:T(8,128)(2,1)S(1)}, u32[]{:S(2)}, u32[]{:S(2)}) collective-permute-start(bf16[384,256]{1,0:T(8,128)(2,1)S(1)} %get-tuple-element.23), channel_id=1, source_target_pairs={{0,8},{8,0},{16,24},{24,16},{1,9},{9,1},{17,25},{25,17},{2,10},{10... | collective-permute-start | bytes 589832 | tf_op jit(solution)/shard_map/ppermute | solution.py:42
  77.0 2.9 %collective-permute-start.18 = (bf16[384,256]{1,0:T(8,128)(2,1)S(1)}, bf16[384,256]{1,0:T(8,128)(2,1)S(1)}, u32[]{:S(2)}, u32[]{:S(2)}) collective-permute-start(bf16[384,256]{1,0:T(8,128)(2,1)S(1)} %get-tuple-element.21), channel_id=1, source_target_pairs={{0,8},{8,0},{16,24},{24,16},{1,9},{9,1},{17,25},{25,17},{2,10},{10... | collective-permute-start | bytes 589832 | tf_op jit(solution)/shard_map/ppermute | solution.py:42

commit v17 on v16

--- a/solution.py
+++ b/solution.py
@@ -11,7 +11,7 @@
 LON_HALO = 2 * LON_REACH
 
 
-def halving_sum(value, axes, exchanged=2, hold=None):
+def halving_sum(value, axes, exchanged=2, hold=None, lead=None):
     stages = []
     for axis in axes:
         bit = 1
@@ -20,6 +20,8 @@
             bit *= 2
     exchanged = min(exchanged, len(stages))
     halved = stages[: len(stages) - exchanged]
+    if lead is not None:
+        halved = [s for s in halved if s[0] == lead] + [s for s in halved if s[0] != lead]
     flat = value.reshape(-1, value.shape[-1])
     held = hold
     for axis, bit in halved:
@@ -217,7 +219,9 @@
         member_total * row_count * lax.axis_size("lat") * col_count * lax.axis_size("lon")
     )
     axes = ("ens", "lat", "lon")
-    second_grad, second_spread = halving_sum(second_sum * grad_scale, axes, hold=second_spread)
+    second_grad, second_spread = halving_sum(
+        second_sum * grad_scale, axes, hold=second_spread, lead="lat"
+    )
     first_grad, hidden_grad = halving_sum(first_sum * grad_scale, axes, hold=hidden_grad)
     layer_output = mix_channels(second_weight, second_spread).astype(jnp.bfloat16)
     first_mixed = unmix(first_weight, hidden_grad)

time: 81.3 us -> 89.1 us (1.096)
  waiting for transfers between devices: 24.2 us -> 33.7 us
  starting transfers between devices: 22.4 us -> 20.9 us
    ppermute x6, waiting for transfers between devices: 4.55 us -> 9.24 us  [halving_sum(): other = lax.ppermute(flat, axis, pairs)]
    ppermute x6, waiting for transfers between devices: 7.31 us -> 10.5 us  [halving_sum(): flat = keep + lax.ppermute(send, axis, pairs)]
    ppermute x4, waiting for transfers between devices: 6.5 us -> 8.14 us  [halving_sum(): flat = flat + lax.ppermute(flat, axis, pairs)]
    ppermute x6, starting transfers between devices: 5.07 us -> 3.52 us  [halving_sum(): other = lax.ppermute(flat, axis, pairs)]
    unnamed x22 -> x20, local copies, waits for them, and re-layouts: 5.81 us -> 5.74 us
  transfers between devices with their start and end apart: 19 -> 19, of which waited for: 13 -> 12; matrix products, arithmetic and copies ran while one was open for 23% -> 21% of each run, Pallas kernels for 0% -> 0%
where the time goes in v17:
time: 89.1 us; the launch traced here: 88.7 us
  waiting for transfers between devices  33.7 us (38%)
  starting transfers between devices  20.9 us (23%)
  matrix products  17.8 us (20%)
  local copies, waits for them, and re-layouts  8.09 us (9%)
  other arithmetic  7.11 us (8%)
  between operations  1.13 us (1%)
    ppermute x6, waiting for transfers between devices, halving_sum(): flat = keep + lax.ppermute(send, axis, pairs)  10.5 us
    ppermute x6, waiting for transfers between devices, halving_sum(): other = lax.ppermute(flat, axis, pairs)  9.24 us
    ppermute x4, waiting for transfers between devices, halving_sum(): flat = flat + lax.ppermute(flat, axis, pairs)  8.14 us
    dot_general x3, matrix products, band_of(): jnp.einsum('kiad,dpq->iapkq', stencil, lon_picker(col_count, first_source...  7.41 us
    ppermute x6, starting transfers between devices, halving_sum(): flat = keep + lax.ppermute(send, axis, pairs)  6.38 us
    ppermute x1, waiting for transfers between devices, lat_halo(): other = lax.ppermute(block, 'lat', [(0, 1), (1, 0)])  5.79 us
    unnamed x20, local copies, waits for them, and re-layouts  5.74 us
    ppermute x4, starting transfers between devices, halving_sum(): flat = flat + lax.ppermute(flat, axis, pairs)  4.03 us
  transfers between devices with their start and end apart: 19, of which 12 were waited for; matrix products, arithmetic and copies ran while one was open for 21% of the time, Pallas kernels for 0%

profile of v17, /device:TPU:0, one launch (start us, length us, event | category | flops | bytes accessed | tf_op | source)
XLA Modules:
  0.0 88.7 jit_solution(7536161209454678119)
XLA Ops:
  0.6 0.8 broadcast_add_fusion
  1.4 0.9 %convolution_convert_fusion.2 = bf16[3,2,3,9]{3,2,1,0:T(4,128)(2,1)S(1)} fusion(s32[2,3,12]{2,0,1:T(2,128)S(1)} %get-tuple-element.40, f32[2,3,12]{2,0,1:T(2,128)} %param.10, s32[2,3,12]{2,0,1:T(2,128)S(1)} %get-tuple-element.41), kind=kOutput, calls=%fused_computation.38 | convolution fusion | flops 24570 | bytes 1188 | tf_op jit(solution)/shard_map/rks,rksa,rksd->krad/dot_general | solution.py:87
  2.3 0.1 reshape.71
  2.4 0.1 copy.28
  2.6 1.0 %copy.26 = bf16[1,256,2,128]{1,3,2,0:T(8,128)(2,1)S(1)} copy(bf16[1,256,2,128]{3,2,1,0:T(2,128)(2,1)} %param.13) | data formatting | bytes 262144 | tf_op args[6]
  3.6 1.0 %copy.25 = bf16[1,256,2,128]{1,3,2,0:T(8,128)(2,1)S(1)} copy(bf16[1,256,2,128]{3,2,1,0:T(2,128)(2,1)} %param.7) | data formatting | bytes 262144 | tf_op args[0]
  4.6 3.1 %collective-permute-start = (bf16[513,2,128]{0,2,1:T(8,128)(2,1)S(1)}, bf16[513,2,128]{0,2,1:T(8,128)(2,1)S(1)}, u32[]{:S(2)}, u32[]{:S(2)}) collective-permute-start(bf16[513,2,128]{0,2,1:T(8,128)(2,1)S(1)} %pad_maximum_fusion.2), channel_id=1, source_target_pairs={{0,4},{4,0},{1,5},{5,1},{2,6},{6,2},{3,7},{7,3},{8,12},{12,8},{9,1... | collective-permute-start | bytes 787976 | tf_op jit(solution)/shard_map/ppermute | solution.py:57
  7.7 0.1 fusion.42
  7.8 0.2 fusion.29
  8.1 1.5 %fusion.34 = bf16[136,128,3,2,3]{1,4,3,2,0:T(4,128)(2,1)} fusion(pred[9,136,128,1,1]{2,1,0,3,4:T(8,128)(4,1)S(1)} %fusion.42, bf16[3,2,3,9]{3,2,1,0:T(4,128)(2,1)S(1)} %convolution_convert_fusion.2), kind=kOutput, calls=%fused_computation.36 | convolution fusion | flops 5640192 | bytes 783684 | tf_op jit(solution)/shard_map/kiad,dpq->iapkq/dot_general | solution.py:106
  9.6 5.8 %collective-permute-done = bf16[513,2,128]{0,2,1:T(8,128)(2,1)S(1)} collective-permute-done((bf16[513,2,128]{0,2,1:T(8,128)(2,1)S(1)}, bf16[513,2,128]{0,2,1:T(8,128)(2,1)S(1)}, u32[]{:S(2)}, u32[]{:S(2)}) %collective-permute-start) | collective-permute-done | bytes 262688 | tf_op jit(solution)/shard_map/ppermute | solution.py:57
  15.5 0.2 maximum_reduce_fusion
  15.7 3.9 %collective-permute-start.2 = (bf16[512,6,8]{0,2,1:T(8,128)(2,1)S(1)}, bf16[512,6,8]{0,2,1:T(8,128)(2,1)S(1)}, u32[]{:S(2)}, u32[]{:S(2)}) collective-permute-start(bf16[512,6,8]{0,2,1:T(8,128)(2,1)S(1)} %get-tuple-element.27), channel_id=1, source_target_pairs={{0,3},{1,0},{2,1},{3,2},{4,7},{5,4},{6,5},{7,6},{8,11},{9,8},{10,9... | collective-permute-start | bytes 147464 | tf_op jit(solution)/shard_map/ppermute | solution.py:78
  19.5 0.1 reshape_squeeze.3
  19.6 3.0 %convert_bitcast_fusion = bf16[4,3,144,3,136]{2,0,1,3,4:T(4,128)(2,1)} fusion(bf16[3,6,3,9]{3,1,2,0:T(8,128)(2,1)S(1)} %bitcast.201), kind=kOutput, calls=%fused_computation.8 | convolution fusion | flops 13747968 | bytes 1419264 | tf_op jit(solution)/shard_map/kiad,dpq->iapkq/dot_general | solution.py:106
  22.6 2.9 %fusion.10 = bf16[136,144,3,4,3]{1,3,4,2,0:T(4,128)(2,1)} fusion(pred[9,136,144,1,1]{2,1,0,3,4:T(8,128)(4,1)S(1)} %fusion.29, bf16[3,6,3,9]{3,1,2,0:T(8,128)(2,1)S(1)} %bitcast.202, pred[]{:T(512)S(6)} %eq.72), kind=kOutput, calls=%fused_computation.12 | convolution fusion | flops 12690756 | bytes 1587277 | tf_op jit(solution)/shard_map/kiad,dpq->iapkq/dot_general | solution.py:106
  25.5 0.1 pad_maximum_fusion
  25.8 0.9 %slice_bitcast_fusion.5 = (bf16[256,4,1,144]{0,3,2,1:T(8,128)(2,1)}, bf16[256,4,1,144]{0,3,2,1:T(8,128)(2,1)}, bf16[256,4,1,144]{0,3,2,1:T(8,128)(2,1)}) fusion(bf16[512,6,144]{0,2,1:T(8,128)(2,1)S(1)} %pad_maximum_fusion.1), kind=kLoop, calls=%fused_computation.90 | loop fusion | bytes 1769472 | tf_op jit(solution)/shard_map/stack | solution.py:117
  26.8 2.7 %fusion.19 = f32[256,4,3,136]{0,3,1,2:T(8,128)S(1)} fusion(bf16[3,256,256]{2,1,0:T(8,128)(2,1)S(1)} %copy-done.3, bf16[512,6,144]{0,2,1:T(8,128)(2,1)S(1)} %pad_maximum_fusion.1, pred[]{:T(512)S(6)} %eq.72, bf16[136,144,3,4,3]{1,3,4,2,0:T(4,128)(2,1)} %fusion.10), kind=kOutput, calls=%fused_computation.16 | convolution fusion | flops 588054528 | bytes 4064257 | tf_op jit(solution)/shard_map/cikq,iapkq->ciap/dot_general | solution.py:139
  29.5 0.1 fusion.56
  29.7 1.4 %copy-done.1 = bf16[4,3,144,3,136]{2,0,1,3,4:T(4,128)(2,1)S(1)} copy-done((bf16[4,3,144,3,136]{2,0,1,3,4:T(4,128)(2,1)S(1)}, bf16[4,3,144,3,136]{2,0,1,3,4:T(4,128)(2,1)}, u32[]{:S(2)}) %copy-start.1) | copy-done | bytes 1410072
  31.1 0.1 copy-done.5
  31.2 0.1 copy-done.6
  31.3 0.8 fusion.24
  32.1 0.8 fusion.46
  33.0 0.3 copy-done.7
  33.3 0.4 fusion.31
  33.7 0.2 copy-done.2
  33.9 0.3 fusion.27
  34.2 1.6 %collective-permute-start.3 = (f32[384,256]{1,0:T(8,128)S(1)}, f32[384,256]{1,0:T(8,128)}, u32[]{:S(2)}, u32[]{:S(2)}) collective-permute-start(f32[384,256]{1,0:T(8,128)S(1)} %constant_dynamic-slice_fusion.5), channel_id=1, source_target_pairs={{0,4},{4,0},{1,5},{5,1},{2,6},{6,2},{3,7},{7,3},{8,12},{12,8},{9,1... | collective-permute-start | bytes 1179656 | tf_op jit(solution)/shard_map/ppermute | solution.py:33
  35.8 0.3 fusion.28
  36.1 0.8 constant_dynamic-slice_fusion.4
  36.9 7.2 %collective-permute-done.3 = f32[384,256]{1,0:T(8,128)} collective-permute-done((f32[384,256]{1,0:T(8,128)S(1)}, f32[384,256]{1,0:T(8,128)}, u32[]{:S(2)}, u32[]{:S(2)}) %collective-permute-start.3) | collective-permute-done | bytes 393248 | tf_op jit(solution)/shard_map/ppermute | solution.py:33
  44.1 1.0 %dynamic-slice_add_fusion.1 = f32[384,256]{1,0:T(8,128)S(1)} fusion(f32[384,256]{1,0:T(8,128)} %collective-permute-done.3, f32[768,256]{1,0:T(8,128)S(1)} %bitcast.196, s32[]{:T(128)S(6)} %select_n.182), kind=kLoop, calls=%fused_computation.81 | loop fusion | flops 98304 | bytes 1179652 | tf_op jit(solution)/shard_map/add | solution.py:33
  45.1 1.1 %dynamic-slice_add_fusion = f32[384,256]{1,0:T(8,128)S(1)} fusion(f32[384,256]{1,0:T(8,128)} %collective-permute-done.4, f32[768,256]{1,0:T(8,128)S(1)} %bitcast.200, s32[]{:T(128)S(6)} %select_n.192), kind=kLoop, calls=%fused_computation.80 | loop fusion | flops 98304 | bytes 1179652 | tf_op jit(solution)/shard_map/add | solution.py:33
  46.2 1.6 %collective-permute-start.5 = (f32[192,256]{1,0:T(8,128)S(1)}, f32[192,256]{1,0:T(8,128)S(1)}, u32[]{:S(2)}, u32[]{:S(2)}) collective-permute-start(f32[192,256]{1,0:T(8,128)S(1)} %constant_dynamic-slice_fusion.3), channel_id=1, source_target_pairs={{0,16},{8,24},{16,0},{24,8},{1,17},{9,25},{17,1},{25,9},{2,18},{10... | collective-permute-start | bytes 589832 | tf_op jit(solution)/shard_map/ppermute | solution.py:33
  47.8 0.1 collective-permute-start.12
  47.9 4.0 %fusion.14 = f32[256,4,3,144]{0,3,2,1:T(8,128)} fusion(bf16[4,3,144,3,136]{2,0,1,3,4:T(4,128)(2,1)} %convert_bitcast_fusion, bf16[3,256,256]{2,1,0:T(8,128)(2,1)S(1)} %copy-done, bf16[256,4,136]{0,2,1:T(8,128)(2,1)S(1)} %get-tuple-element.9), kind=kOutput, calls=%fused_computation.15 | convolution fusion | flops 575299584 | bytes 3851264 | tf_op jit(solution)/shard_map/cikq,iapkq->ciap/dot_general | solution.py:126
  51.9 0.1 collective-permute-done.5
  52.0 1.6 %collective-permute-start.6 = (f32[96,256]{1,0:T(8,128)S(1)}, f32[96,256]{1,0:T(8,128)S(1)}, u32[]{:S(2)}, u32[]{:S(2)}) collective-permute-start(f32[96,256]{1,0:T(8,128)S(1)} %constant_dynamic-slice_fusion.2), channel_id=1, source_target_pairs={{0,4},{4,0},{1,5},{5,1},{2,6},{6,2},{3,7},{7,3},{8,12},{12,8},{9,1... | collective-permute-start | bytes 294920 | tf_op jit(solution)/shard_map/ppermute | solution.py:33
  53.7 1.6 %collective-permute-start.13 = (f32[96,256]{1,0:T(8,128)S(1)}, f32[96,256]{1,0:T(8,128)S(1)}, u32[]{:S(2)}, u32[]{:S(2)}) collective-permute-start(f32[96,256]{1,0:T(8,128)S(1)} %constant_dynamic-slice_fusion), channel_id=1, source_target_pairs={{0,16},{8,24},{16,0},{24,8},{1,17},{9,25},{17,1},{25,9},{2,18},{10... | collective-permute-start | bytes 294920 | tf_op jit(solution)/shard_map/ppermute | solution.py:33
  55.2 2.0 %collective-permute-done.6 = f32[96,256]{1,0:T(8,128)S(1)} collective-permute-done((f32[96,256]{1,0:T(8,128)S(1)}, f32[96,256]{1,0:T(8,128)S(1)}, u32[]{:S(2)}, u32[]{:S(2)}) %collective-permute-start.6) | collective-permute-done | bytes 98336 | tf_op jit(solution)/shard_map/ppermute | solution.py:33
  57.2 0.1 collective-permute-start.7
  57.3 1.3 %collective-permute-done.13 = f32[96,256]{1,0:T(8,128)S(1)} collective-permute-done((f32[96,256]{1,0:T(8,128)S(1)}, f32[96,256]{1,0:T(8,128)S(1)}, u32[]{:S(2)}, u32[]{:S(2)}) %collective-permute-start.13) | collective-permute-done | bytes 98336 | tf_op jit(solution)/shard_map/ppermute | solution.py:33
  58.6 0.8 collective-permute-start.14
  59.4 3.2 %collective-permute-done.7 = f32[96,256]{1,0:T(8,128)S(1)} collective-permute-done((f32[96,256]{1,0:T(8,128)S(1)}, f32[96,256]{1,0:T(8,128)S(1)}, u32[]{:S(2)}, u32[]{:S(2)}) %collective-permute-start.7) | collective-permute-done | bytes 98336 | tf_op jit(solution)/shard_map/ppermute | solution.py:39
  62.6 2.1 %collective-permute-start.8 = (f32[96,256]{1,0:T(8,128)S(1)}, f32[96,256]{1,0:T(8,128)S(1)}, u32[]{:S(2)}, u32[]{:S(2)}) collective-permute-start(f32[96,256]{1,0:T(8,128)S(1)} %add.196), channel_id=1, source_target_pairs={{0,2},{1,3},{2,0},{3,1},{4,6},{5,7},{6,4},{7,5},{8,10},{9,11},{10,... | collective-permute-start | bytes 294920 | tf_op jit(solution)/shard_map/ppermute | solution.py:39
  64.7 1.1 %fusion.75 = bf16[1,256,2,128]{1,3,2,0:T(8,128)(2,1)S(1)} fusion(f32[256,4,3,144]{0,3,2,1:T(8,128)} %fusion.14), kind=kLoop, calls=%fused_computation.104 | loop fusion | flops 196608 | bytes 917504 | tf_op jit(solution)/shard_map/convert_element_type | solution.py:228
  65.9 1.0 %collective-permute-start.15 = (f32[96,256]{1,0:T(8,128)S(1)}, f32[96,256]{1,0:T(8,128)S(1)}, u32[]{:S(2)}, u32[]{:S(2)}) collective-permute-start(f32[96,256]{1,0:T(8,128)S(1)} %add.204), channel_id=1, source_target_pairs={{0,2},{1,3},{2,0},{3,1},{4,6},{5,7},{6,4},{7,5},{8,10},{9,11},{10,... | collective-permute-start | bytes 294920 | tf_op jit(solution)/shard_map/ppermute | solution.py:39
  66.9 4.3 %collective-permute-done.8 = f32[96,256]{1,0:T(8,128)S(1)} collective-permute-done((f32[96,256]{1,0:T(8,128)S(1)}, f32[96,256]{1,0:T(8,128)S(1)}, u32[]{:S(2)}, u32[]{:S(2)}) %collective-permute-start.8) | collective-permute-done | bytes 98336 | tf_op jit(solution)/shard_map/ppermute | solution.py:39
  71.3 1.6 %collective-permute-start.9 = (bf16[96,256]{1,0:T(8,128)(2,1)S(1)}, bf16[96,256]{1,0:T(8,128)(2,1)S(1)}, u32[]{:S(2)}, u32[]{:S(2)}) collective-permute-start(bf16[96,256]{1,0:T(8,128)(2,1)S(1)} %add_convert_fusion.1), channel_id=1, source_target_pairs={{0,4},{4,0},{1,5},{5,1},{2,6},{6,2},{3,7},{7,3},{8,12},{12,8},{9,1... | collective-permute-start | bytes 147464 | tf_op jit(solution)/shard_map/ppermute | solution.py:44
  72.8 0.6 collective-permute-done.15
  73.5 1.9 %collective-permute-done.9 = bf16[96,256]{1,0:T(8,128)(2,1)S(1)} collective-permute-done((bf16[96,256]{1,0:T(8,128)(2,1)S(1)}, bf16[96,256]{1,0:T(8,128)(2,1)S(1)}, u32[]{:S(2)}, u32[]{:S(2)}) %collective-permute-start.9) | collective-permute-done | bytes 49184 | tf_op jit(solution)/shard_map/ppermute | solution.py:44
  75.4 0.2 collective-permute-start.10
  75.6 2.0 %collective-permute-done.16 = bf16[96,256]{1,0:T(8,128)(2,1)S(1)} collective-permute-done((bf16[96,256]{1,0:T(8,128)(2,1)S(1)}, bf16[96,256]{1,0:T(8,128)(2,1)S(1)}, u32[]{:S(2)}, u32[]{:S(2)}) %collective-permute-start.16) | collective-permute-done | bytes 49184 | tf_op jit(solution)/shard_map/ppermute | solution.py:44
  77.7 2.4 %collective-permute-done.10 = bf16[192,256]{1,0:T(8,128)(2,1)S(1)} collective-permute-done((bf16[192,256]{1,0:T(8,128)(2,1)S(1)}, bf16[192,256]{1,0:T(8,128)(2,1)S(1)}, u32[]{:S(2)}, u32[]{:S(2)}) %collective-permute-start.10) | collective-permute-done | bytes 98336 | tf_op jit(solution)/shard_map/ppermute | solution.py:44
  80.3 0.1 fusion.90
  80.4 1.6 %collective-permute-start.18 = (bf16[384,256]{1,0:T(8,128)(2,1)S(1)}, bf16[384,256]{1,0:T(8,128)(2,1)S(1)}, u32[]{:S(2)}, u32[]{:S(2)}) collective-permute-start(bf16[384,256]{1,0:T(8,128)(2,1)S(1)} %get-tuple-element.21), channel_id=1, source_target_pairs={{0,4},{4,0},{1,5},{5,1},{2,6},{6,2},{3,7},{7,3},{8,12},{12,8},{9,1... | collective-permute-start | bytes 589832 | tf_op jit(solution)/shard_map/ppermute | solution.py:44
  81.9 0.3 fusion.33
  82.2 0.8 copy.40
  83.0 0.8 copy.41
  83.8 0.9 %maximum_select_fusion = f32[768,256]{1,0:T(8,128)} fusion(f32[384,256]{1,0:T(8,128)S(1)} %get-tuple-element.22, f32[384,256]{1,0:T(8,128)S(1)} %convert_element_type.134, pred[]{:T(512)S(6)} %eq.74), kind=kLoop, calls=%fused_computation.48 | loop fusion | flops 589824 | bytes 1572865 | tf_op jit(solution)/shard_map/jit(_where)/select_n | solution.py:47
  84.8 3.0 %collective-permute-done.18 = bf16[384,256]{1,0:T(8,128)(2,1)S(1)} collective-permute-done((bf16[384,256]{1,0:T(8,128)(2,1)S(1)}, bf16[384,256]{1,0:T(8,128)(2,1)S(1)}, u32[]{:S(2)}, u32[]{:S(2)}) %collective-permute-start.18) | collective-permute-done | bytes 196640 | tf_op jit(solution)/shard_map/ppermute | solution.py:44
  87.8 0.9 %maximum_select_fusion.1 = f32[768,256]{1,0:T(8,128)} fusion(f32[384,256]{1,0:T(8,128)S(1)} %get-tuple-element.20, f32[384,256]{1,0:T(8,128)S(1)} %convert_element_type.137, pred[]{:T(512)S(6)} %eq.76), kind=kLoop, calls=%fused_computation.49 | loop fusion | flops 589824 | bytes 1572865 | tf_op jit(solution)/shard_map/jit(_where)/select_n | solution.py:47
  (54 shorter events, 1.1 us)
Async XLA Ops:
  0.6 31.5 %copy-start = (bf16[3,256,256]{2,1,0:T(8,128)(2,1)S(1)}, bf16[3,256,256]{2,1,0:T(8,128)(2,1)}, u32[]{:S(2)}) copy-start(bf16[3,256,256]{2,1,0:T(8,128)(2,1)} %param.8) | copy-start | bytes 1179652
  4.6 10.8 %collective-permute-start = (bf16[513,2,128]{0,2,1:T(8,128)(2,1)S(1)}, bf16[513,2,128]{0,2,1:T(8,128)(2,1)S(1)}, u32[]{:S(2)}, u32[]{:S(2)}) collective-permute-start(bf16[513,2,128]{0,2,1:T(8,128)(2,1)S(1)} %pad_maximum_fusion.2), channel_id=1, source_target_pairs={{0,4},{4,0},{1,5},{5,1},{2,6},{6,2},{3,7},{7,3},{8,12},{12,8},{9,1... | collective-permute-start | bytes 787976 | tf_op jit(solution)/shard_map/ppermute | solution.py:57
  15.7 10.1 %collective-permute-start.2 = (bf16[512,6,8]{0,2,1:T(8,128)(2,1)S(1)}, bf16[512,6,8]{0,2,1:T(8,128)(2,1)S(1)}, u32[]{:S(2)}, u32[]{:S(2)}) collective-permute-start(bf16[512,6,8]{0,2,1:T(8,128)(2,1)S(1)} %get-tuple-element.27), channel_id=1, source_target_pairs={{0,3},{1,0},{2,1},{3,2},{4,7},{5,4},{6,5},{7,6},{8,11},{9,8},{10,9... | collective-permute-start | bytes 147464 | tf_op jit(solution)/shard_map/ppermute | solution.py:78
  19.5 6.2 %collective-permute-start.1 = (bf16[512,6,8]{0,2,1:T(8,128)(2,1)S(1)}, bf16[512,6,8]{0,2,1:T(8,128)(2,1)S(1)}, u32[]{:S(2)}, u32[]{:S(2)}) collective-permute-start(bf16[512,6,8]{0,2,1:T(8,128)(2,1)S(1)} %get-tuple-element.26), channel_id=1, source_target_pairs={{0,1},{1,2},{2,3},{3,0},{4,5},{5,6},{6,7},{7,4},{8,9},{9,10},{10,1... | collective-permute-start | bytes 147464 | tf_op jit(solution)/shard_map/ppermute | solution.py:77
  25.7 1.0 %copy-start.3 = (bf16[3,256,256]{2,1,0:T(8,128)(2,1)S(1)}, bf16[3,256,256]{2,1,0:T(8,128)(2,1)}, u32[]{:S(2)}) copy-start(bf16[3,256,256]{2,1,0:T(8,128)(2,1)} %param.9) | copy-start | bytes 1179652
  29.4 1.7 %copy-start.1 = (bf16[4,3,144,3,136]{2,0,1,3,4:T(4,128)(2,1)S(1)}, bf16[4,3,144,3,136]{2,0,1,3,4:T(4,128)(2,1)}, u32[]{:S(2)}) copy-start(bf16[4,3,144,3,136]{2,0,1,3,4:T(4,128)(2,1)} %convert_bitcast_fusion) | copy-start | bytes 4230148
  29.4 1.7 %copy-start.4 = (bf16[256,4,1,144]{0,3,2,1:T(8,128)(2,1)S(1)}, bf16[256,4,1,144]{0,3,2,1:T(8,128)(2,1)}, u32[]{:S(2)}) copy-start(bf16[256,4,1,144]{0,3,2,1:T(8,128)(2,1)} %get-tuple-element.28) | copy-start | bytes 884740
  29.4 1.8 %copy-start.5 = (bf16[256,4,1,144]{0,3,2,1:T(8,128)(2,1)S(1)}, bf16[256,4,1,144]{0,3,2,1:T(8,128)(2,1)}, u32[]{:S(2)}) copy-start(bf16[256,4,1,144]{0,3,2,1:T(8,128)(2,1)} %get-tuple-element.29) | copy-start | bytes 884740
  29.5 1.9 %copy-start.6 = (bf16[256,4,1,144]{0,3,2,1:T(8,128)(2,1)S(1)}, bf16[256,4,1,144]{0,3,2,1:T(8,128)(2,1)}, u32[]{:S(2)}) copy-start(bf16[256,4,1,144]{0,3,2,1:T(8,128)(2,1)} %get-tuple-element.30) | copy-start | bytes 884740
  32.1 1.2 %copy-start.7 = (bf16[136,128,3,2,3]{1,4,3,2,0:T(4,128)(2,1)S(1)}, bf16[136,128,3,2,3]{1,4,3,2,0:T(4,128)(2,1)}, u32[]{:S(2)}) copy-start(bf16[136,128,3,2,3]{1,4,3,2,0:T(4,128)(2,1)} %fusion.34) | copy-start | bytes 1880068
  32.9 1.0 %copy-start.2 = (bf16[1,256,2,128]{3,2,1,0:T(2,128)(2,1)S(1)}, bf16[1,256,2,128]{3,2,1,0:T(2,128)(2,1)}, u32[]{:S(2)}) copy-start(bf16[1,256,2,128]{3,2,1,0:T(2,128)(2,1)} %param.13) | copy-start | bytes 393220
  34.2 9.9 %collective-permute-start.3 = (f32[384,256]{1,0:T(8,128)S(1)}, f32[384,256]{1,0:T(8,128)}, u32[]{:S(2)}, u32[]{:S(2)}) collective-permute-start(f32[384,256]{1,0:T(8,128)S(1)} %constant_dynamic-slice_fusion.5), channel_id=1, source_target_pairs={{0,4},{4,0},{1,5},{5,1},{2,6},{6,2},{3,7},{7,3},{8,12},{12,8},{9,1... | collective-permute-start | bytes 1179656 | tf_op jit(solution)/shard_map/ppermute | solution.py:33
  36.9 8.2 %collective-permute-start.4 = (f32[384,256]{1,0:T(8,128)}, f32[384,256]{1,0:T(8,128)}, u32[]{:S(2)}, u32[]{:S(2)}) collective-permute-start(f32[384,256]{1,0:T(8,128)} %constant_dynamic-slice_fusion.4), channel_id=1, source_target_pairs={{0,8},{8,0},{16,24},{24,16},{1,9},{9,1},{17,25},{25,17},{2,10},{10... | collective-permute-start | bytes 1179656 | tf_op jit(solution)/shard_map/ppermute | solution.py:33
  46.2 5.7 %collective-permute-start.5 = (f32[192,256]{1,0:T(8,128)S(1)}, f32[192,256]{1,0:T(8,128)S(1)}, u32[]{:S(2)}, u32[]{:S(2)}) collective-permute-start(f32[192,256]{1,0:T(8,128)S(1)} %constant_dynamic-slice_fusion.3), channel_id=1, source_target_pairs={{0,16},{8,24},{16,0},{24,8},{1,17},{9,25},{17,1},{25,9},{2,18},{10... | collective-permute-start | bytes 589832 | tf_op jit(solution)/shard_map/ppermute | solution.py:33
  47.8 5.8 %collective-permute-start.12 = (f32[192,256]{1,0:T(8,128)S(1)}, f32[192,256]{1,0:T(8,128)S(1)}, u32[]{:S(2)}, u32[]{:S(2)}) collective-permute-start(f32[192,256]{1,0:T(8,128)S(1)} %constant_dynamic-slice_fusion.1), channel_id=1, source_target_pairs={{0,8},{8,0},{16,24},{24,16},{1,9},{9,1},{17,25},{25,17},{2,10},{10... | collective-permute-start | bytes 589832 | tf_op jit(solution)/shard_map/ppermute | solution.py:33
  52.0 5.2 %collective-permute-start.6 = (f32[96,256]{1,0:T(8,128)S(1)}, f32[96,256]{1,0:T(8,128)S(1)}, u32[]{:S(2)}, u32[]{:S(2)}) collective-permute-start(f32[96,256]{1,0:T(8,128)S(1)} %constant_dynamic-slice_fusion.2), channel_id=1, source_target_pairs={{0,4},{4,0},{1,5},{5,1},{2,6},{6,2},{3,7},{7,3},{8,12},{12,8},{9,1... | collective-permute-start | bytes 294920 | tf_op jit(solution)/shard_map/ppermute | solution.py:33
  53.7 4.9 %collective-permute-start.13 = (f32[96,256]{1,0:T(8,128)S(1)}, f32[96,256]{1,0:T(8,128)S(1)}, u32[]{:S(2)}, u32[]{:S(2)}) collective-permute-start(f32[96,256]{1,0:T(8,128)S(1)} %constant_dynamic-slice_fusion), channel_id=1, source_target_pairs={{0,16},{8,24},{16,0},{24,8},{1,17},{9,25},{17,1},{25,9},{2,18},{10... | collective-permute-start | bytes 294920 | tf_op jit(solution)/shard_map/ppermute | solution.py:33
  57.2 5.4 %collective-permute-start.7 = (f32[96,256]{1,0:T(8,128)S(1)}, f32[96,256]{1,0:T(8,128)S(1)}, u32[]{:S(2)}, u32[]{:S(2)}) collective-permute-start(f32[96,256]{1,0:T(8,128)S(1)} %dynamic-slice_add_fusion.5), channel_id=1, source_target_pairs={{0,1},{1,0},{2,3},{3,2},{4,5},{5,4},{6,7},{7,6},{8,9},{9,8},{10,11... | collective-permute-start | bytes 294920 | tf_op jit(solution)/shard_map/ppermute | solution.py:39
  58.6 7.3 %collective-permute-start.14 = (f32[96,256]{1,0:T(8,128)S(1)}, f32[96,256]{1,0:T(8,128)S(1)}, u32[]{:S(2)}, u32[]{:S(2)}) collective-permute-start(f32[96,256]{1,0:T(8,128)S(1)} %dynamic-slice_add_fusion.4), channel_id=1, source_target_pairs={{0,1},{1,0},{2,3},{3,2},{4,5},{5,4},{6,7},{7,6},{8,9},{9,8},{10,11... | collective-permute-start | bytes 294920 | tf_op jit(solution)/shard_map/ppermute | solution.py:39
  62.6 8.7 %collective-permute-start.8 = (f32[96,256]{1,0:T(8,128)S(1)}, f32[96,256]{1,0:T(8,128)S(1)}, u32[]{:S(2)}, u32[]{:S(2)}) collective-permute-start(f32[96,256]{1,0:T(8,128)S(1)} %add.196), channel_id=1, source_target_pairs={{0,2},{1,3},{2,0},{3,1},{4,6},{5,7},{6,4},{7,5},{8,10},{9,11},{10,... | collective-permute-start | bytes 294920 | tf_op jit(solution)/shard_map/ppermute | solution.py:39
  65.9 7.5 %collective-permute-start.15 = (f32[96,256]{1,0:T(8,128)S(1)}, f32[96,256]{1,0:T(8,128)S(1)}, u32[]{:S(2)}, u32[]{:S(2)}) collective-permute-start(f32[96,256]{1,0:T(8,128)S(1)} %add.204), channel_id=1, source_target_pairs={{0,2},{1,3},{2,0},{3,1},{4,6},{5,7},{6,4},{7,5},{8,10},{9,11},{10,... | collective-permute-start | bytes 294920 | tf_op jit(solution)/shard_map/ppermute | solution.py:39
  71.3 4.2 %collective-permute-start.9 = (bf16[96,256]{1,0:T(8,128)(2,1)S(1)}, bf16[96,256]{1,0:T(8,128)(2,1)S(1)}, u32[]{:S(2)}, u32[]{:S(2)}) collective-permute-start(bf16[96,256]{1,0:T(8,128)(2,1)S(1)} %add_convert_fusion.1), channel_id=1, source_target_pairs={{0,4},{4,0},{1,5},{5,1},{2,6},{6,2},{3,7},{7,3},{8,12},{12,8},{9,1... | collective-permute-start | bytes 147464 | tf_op jit(solution)/shard_map/ppermute | solution.py:44
  73.4 4.2 %collective-permute-start.16 = (bf16[96,256]{1,0:T(8,128)(2,1)S(1)}, bf16[96,256]{1,0:T(8,128)(2,1)S(1)}, u32[]{:S(2)}, u32[]{:S(2)}) collective-permute-start(bf16[96,256]{1,0:T(8,128)(2,1)S(1)} %add_convert_fusion), channel_id=1, source_target_pairs={{0,16},{8,24},{16,0},{24,8},{1,17},{9,25},{17,1},{25,9},{2,18},{10... | collective-permute-start | bytes 147464 | tf_op jit(solution)/shard_map/ppermute | solution.py:44
  75.4 4.7 %collective-permute-start.10 = (bf16[192,256]{1,0:T(8,128)(2,1)S(1)}, bf16[192,256]{1,0:T(8,128)(2,1)S(1)}, u32[]{:S(2)}, u32[]{:S(2)}) collective-permute-start(bf16[192,256]{1,0:T(8,128)(2,1)S(1)} %maximum_select_fusion.4), channel_id=1, source_target_pairs={{0,16},{8,24},{16,0},{24,8},{1,17},{9,25},{17,1},{25,9},{2,18},{10... | collective-permute-start | bytes 294920 | tf_op jit(solution)/shard_map/ppermute | solution.py:44
  77.6 2.6 %collective-permute-start.17 = (bf16[192,256]{1,0:T(8,128)(2,1)S(1)}, bf16[192,256]{1,0:T(8,128)(2,1)S(1)}, u32[]{:S(2)}, u32[]{:S(2)}) collective-permute-start(bf16[192,256]{1,0:T(8,128)(2,1)S(1)} %maximum_select_fusion.5), channel_id=1, source_target_pairs={{0,8},{8,0},{16,24},{24,16},{1,9},{9,1},{17,25},{25,17},{2,10},{10... | collective-permute-start | bytes 294920 | tf_op jit(solution)/shard_map/ppermute | solution.py:44
  80.2 3.6 %collective-permute-start.11 = (bf16[384,256]{1,0:T(8,128)(2,1)S(1)}, bf16[384,256]{1,0:T(8,128)(2,1)S(1)}, u32[]{:S(2)}, u32[]{:S(2)}) collective-permute-start(bf16[384,256]{1,0:T(8,128)(2,1)S(1)} %get-tuple-element.23), channel_id=1, source_target_pairs={{0,8},{8,0},{16,24},{24,16},{1,9},{9,1},{17,25},{25,17},{2,10},{10... | collective-permute-start | bytes 589832 | tf_op jit(solution)/shard_map/ppermute | solution.py:44
  80.4 7.4 %collective-permute-start.18 = (bf16[384,256]{1,0:T(8,128)(2,1)S(1)}, bf16[384,256]{1,0:T(8,128)(2,1)S(1)}, u32[]{:S(2)}, u32[]{:S(2)}) collective-permute-start(bf16[384,256]{1,0:T(8,128)(2,1)S(1)} %get-tuple-element.21), channel_id=1, source_target_pairs={{0,4},{4,0},{1,5},{5,1},{2,6},{6,2},{3,7},{7,3},{8,12},{12,8},{9,1... | collective-permute-start | bytes 589832 | tf_op jit(solution)/shard_map/ppermute | solution.py:44

commit v18 on v16

--- a/solution.py
+++ b/solution.py
@@ -163,14 +163,15 @@
     stencil = coefficients(quadrature, lat_offsets, lon_offsets)
     basis_count = stencil.shape[0]
 
-    packed = jnp.concatenate([source, gradient], axis=0)
     taps_per_row = stencil.size // row_count
     stencil_rows = jnp.transpose(stencil, (1, 0, 2, 3)).reshape(row_count, taps_per_row)
     stencil_rows = jnp.pad(stencil_rows, ((0, 0), (0, col_count - taps_per_row)))
-    tall = lat_halo(jnp.concatenate([packed, stencil_rows[None]], axis=0), 1, LAT_HALO)
-    framed = lon_halo(tall[: 2 * channels], LON_HALO)
-    source_wide, gradient_wide = framed[:channels], framed[channels:]
-    stencil_wide = tall[2 * channels, :, :taps_per_row].reshape(
+    tall = lat_halo(jnp.concatenate([source, stencil_rows[None]], axis=0), 1, LAT_HALO)
+    own_rows = jnp.pad(gradient, ((0, 0), (LAT_HALO, LAT_HALO), (0, 0)))
+    framed = lon_halo(jnp.concatenate([tall[:channels], own_rows], axis=0), LON_HALO)
+    source_wide = framed[:channels]
+    gradient_wide = lat_halo(framed[channels:, LAT_HALO : LAT_HALO + row_count], 1, LAT_HALO)
+    stencil_wide = tall[channels, :, :taps_per_row].reshape(
         row_count + 2 * LAT_HALO, stencil.shape[0], stencil.shape[2], stencil.shape[3]
     )
     stencil_wide = jnp.transpose(stencil_wide, (1, 0, 2, 3))
@@ -188,7 +189,7 @@
     hidden = mix_channels(first_weight, first_near)
     activation = jnp.where(near_valid, jax.nn.gelu(hidden), 0.0).astype(jnp.bfloat16)
     second_spread = spread(activation, own_band, basis_count).astype(jnp.bfloat16)
-    own_gradient = gradient_wide[:, LAT_HALO : LAT_HALO + row_count, LON_HALO : LON_HALO + col_count]
+    own_gradient = gradient
     second_sum = filter_term(own_gradient, second_spread)
 
     if lax.axis_size("lat") == 2 and row_count == LAT_HALO:

time: 81.3 us -> 81.6 us (level)
  local copies, waits for them, and re-layouts: 8.18 us -> 5.69 us
  other arithmetic: 7.15 us -> 8.84 us
    unnamed x22 -> x24, local copies, waits for them, and re-layouts: 5.81 us -> 3.03 us
    ppermute x4, starting transfers between devices: 4.54 us -> 1.97 us  [halving_sum(): flat = flat + lax.ppermute(flat, axis, pairs)]
    ppermute x1 -> x2, starting transfers between devices: 3.06 us -> 4.65 us  [lat_halo(): other = lax.ppermute(block, 'lat', [(0, 1), (1, 0)])]
    dot_general x3, matrix products: 7.41 us -> 5.97 us  [band_of(): jnp.einsum('kiad,dpq->iapkq', stencil, lon_picker(col_count, first_source...]
    ppermute x6, starting transfers between devices: 5.07 us -> 6.47 us  [halving_sum(): other = lax.ppermute(flat, axis, pairs)]
    ppermute x1, waiting for transfers between devices: 0.01 us -> 1.27 us  [lon_halo(): lax.ppermute(block[..., cols - width:], 'lon', [(i, (i + 1) % count) for...]
    ppermute x1 -> x2, waiting for transfers between devices: 5.82 us -> 4.6 us  [lat_halo(): other = lax.ppermute(block, 'lat', [(0, 1), (1, 0)])]
    squeeze x1, local copies, waits for them, and re-layouts: 0.07 us -> 1.28 us  [spread_adjoint_rows(): below = jnp.pad(partial[:, 1:, 0], ((0, 0), (0, 1), (0, 0)))]
  transfers between devices with their start and end apart: 19 -> 20, of which waited for: 13 -> 16; matrix products, arithmetic and copies ran while one was open for 23% -> 23% of each run, Pallas kernels for 0% -> 0%
where the time goes in v18:
time: 81.6 us; the launch traced here: 81.2 us
  waiting for transfers between devices  24.8 us (30%)
  starting transfers between devices  22.8 us (28%)
  matrix products  17.9 us (22%)
  other arithmetic  8.84 us (11%)
  local copies, waits for them, and re-layouts  5.69 us (7%)
  between operations  1.13 us (1%)
    ppermute x6, waiting for transfers between devices, halving_sum(): flat = keep + lax.ppermute(send, axis, pairs)  7.33 us
    ppermute x4, waiting for transfers between devices, halving_sum(): flat = flat + lax.ppermute(flat, axis, pairs)  7.22 us
    ppermute x6, starting transfers between devices, halving_sum(): other = lax.ppermute(flat, axis, pairs)  6.47 us
    dot_general x3, matrix products, band_of(): jnp.einsum('kiad,dpq->iapkq', stencil, lon_picker(col_count, first_source...  5.97 us
    ppermute x6, starting transfers between devices, halving_sum(): flat = keep + lax.ppermute(send, axis, pairs)  5.88 us
    ppermute x2, starting transfers between devices, lat_halo(): other = lax.ppermute(block, 'lat', [(0, 1), (1, 0)])  4.65 us
    ppermute x2, waiting for transfers between devices, lat_halo(): other = lax.ppermute(block, 'lat', [(0, 1), (1, 0)])  4.6 us
    ppermute x6, waiting for transfers between devices, halving_sum(): other = lax.ppermute(flat, axis, pairs)  4.39 us
  transfers between devices with their start and end apart: 20, of which 16 were waited for; matrix products, arithmetic and copies ran while one was open for 23% of the time, Pallas kernels for 0%

profile of v18, /device:TPU:0, one launch (start us, length us, event | category | flops | bytes accessed | tf_op | source)
XLA Modules:
  0.0 81.2 jit_solution(14965701516455083261)
XLA Ops:
  0.7 0.8 broadcast_add_fusion
  1.4 0.9 %convolution_convert_fusion.2 = bf16[3,2,3,9]{3,2,1,0:T(4,128)(2,1)S(1)} fusion(s32[2,3,12]{2,0,1:T(2,128)S(1)} %get-tuple-element.42, f32[2,3,12]{2,0,1:T(2,128)} %param.10, s32[2,3,12]{2,0,1:T(2,128)S(1)} %get-tuple-element.43), kind=kOutput, calls=%fused_computation.38 | convolution fusion | flops 24570 | bytes 1188 | tf_op jit(solution)/shard_map/rks,rksa,rksd->krad/dot_general | solution.py:85
  2.3 0.1 reshape.71
  2.4 0.1 copy.27
  2.6 1.0 %copy.25 = bf16[1,256,2,128]{1,3,2,0:T(8,128)(2,1)S(1)} copy(bf16[1,256,2,128]{3,2,1,0:T(2,128)(2,1)} %param.7) | data formatting | bytes 262144 | tf_op args[0]
  3.7 3.1 %collective-permute-start = (bf16[257,2,128]{0,2,1:T(8,128)(2,1)S(1)}, bf16[257,2,128]{0,2,1:T(8,128)(2,1)S(1)}, u32[]{:S(2)}, u32[]{:S(2)}) collective-permute-start(bf16[257,2,128]{0,2,1:T(8,128)(2,1)S(1)} %pad_maximum_fusion.4), channel_id=1, source_target_pairs={{0,4},{4,0},{1,5},{5,1},{2,6},{6,2},{3,7},{7,3},{8,12},{12,8},{9,1... | collective-permute-start | bytes 394760 | tf_op jit(solution)/shard_map/ppermute | solution.py:55
  6.7 0.1 fusion.42
  6.8 1.5 %fusion.34 = bf16[136,128,3,2,3]{1,4,3,2,0:T(4,128)(2,1)} fusion(pred[9,136,128,1,1]{2,1,0,3,4:T(8,128)(4,1)S(1)} %fusion.42, bf16[3,2,3,9]{3,2,1,0:T(4,128)(2,1)S(1)} %convolution_convert_fusion.2), kind=kOutput, calls=%fused_computation.36 | convolution fusion | flops 5640192 | bytes 783684 | tf_op jit(solution)/shard_map/kiad,dpq->iapkq/dot_general | solution.py:104
  8.3 0.2 fusion.29
  8.6 0.1 copy.29
  8.8 2.9 %collective-permute-done = bf16[257,2,128]{0,2,1:T(8,128)(2,1)S(1)} collective-permute-done((bf16[257,2,128]{0,2,1:T(8,128)(2,1)S(1)}, bf16[257,2,128]{0,2,1:T(8,128)(2,1)S(1)}, u32[]{:S(2)}, u32[]{:S(2)}) %collective-permute-start) | collective-permute-done | bytes 131616 | tf_op jit(solution)/shard_map/ppermute | solution.py:55
  11.7 0.2 maximum_reduce_fusion
  11.9 3.9 %collective-permute-start.2 = (bf16[512,6,8]{0,2,1:T(8,128)(2,1)S(1)}, bf16[512,6,8]{0,2,1:T(8,128)(2,1)S(1)}, u32[]{:S(2)}, u32[]{:S(2)}) collective-permute-start(bf16[512,6,8]{0,2,1:T(8,128)(2,1)S(1)} %get-tuple-element.30), channel_id=1, source_target_pairs={{0,3},{1,0},{2,1},{3,2},{4,7},{5,4},{6,5},{7,6},{8,11},{9,8},{10,9... | collective-permute-start | bytes 147464 | tf_op jit(solution)/shard_map/ppermute | solution.py:76
  15.7 0.1 reshape_squeeze.3
  15.8 3.0 %fusion.10 = bf16[136,144,3,4,3]{1,3,4,2,0:T(4,128)(2,1)} fusion(pred[9,136,144,1,1]{2,1,0,3,4:T(8,128)(4,1)S(1)} %fusion.29, bf16[3,6,3,9]{3,1,2,0:T(8,128)(2,1)S(1)} %bitcast.197, pred[]{:T(512)S(6)} %eq.73), kind=kOutput, calls=%fused_computation.12 | convolution fusion | flops 12690756 | bytes 1587277 | tf_op jit(solution)/shard_map/kiad,dpq->iapkq/dot_general | solution.py:104
  18.8 1.5 %convert_bitcast_fusion = bf16[4,3,144,3,136]{2,0,1,3,4:T(4,128)(2,1)S(1)} fusion(bf16[3,6,3,9]{3,1,2,0:T(8,128)(2,1)S(1)} %bitcast.198), kind=kOutput, calls=%fused_computation.8 | convolution fusion | flops 13747968 | bytes 1419264 | tf_op jit(solution)/shard_map/kiad,dpq->iapkq/dot_general | solution.py:104
  20.4 1.3 %collective-permute-done.1 = bf16[512,6,8]{0,2,1:T(8,128)(2,1)S(1)} collective-permute-done((bf16[512,6,8]{0,2,1:T(8,128)(2,1)S(1)}, bf16[512,6,8]{0,2,1:T(8,128)(2,1)S(1)}, u32[]{:S(2)}, u32[]{:S(2)}) %collective-permute-start.1) | collective-permute-done | bytes 49184 | tf_op jit(solution)/shard_map/ppermute | solution.py:75
  21.7 1.6 %collective-permute-start.4 = (bf16[256,2,144]{0,2,1:T(8,128)(2,1)S(1)}, bf16[256,2,144]{0,2,1:T(8,128)(2,1)S(1)}, u32[]{:S(2)}, u32[]{:S(2)}) collective-permute-start(bf16[256,2,144]{0,2,1:T(8,128)(2,1)S(1)} %pad_maximum_fusion.5), channel_id=1, source_target_pairs={{0,4},{4,0},{1,5},{5,1},{2,6},{6,2},{3,7},{7,3},{8,12},{12,8},{9,1... | collective-permute-start | bytes 442376 | tf_op jit(solution)/shard_map/ppermute | solution.py:55
  23.4 1.7 %fusion.24 = bf16[256,4,3,136]{0,3,2,1:T(8,128)(2,1)} fusion(bf16[4,3,144,3,136]{2,0,1,3,4:T(4,128)(2,1)S(1)} %convert_bitcast_fusion, bf16[256,4,1,144]{0,3,2,1:T(8,128)(2,1)S(1)} %get-tuple-element.27, bf16[256,4,1,144]{0,3,2,1:T(8,128)(2,1)S(1)} %get-tuple-element.28, bf16[256,4,1,144]{0,3,2,1:T(8,128)(2,1)S(1)} %get-tuple-element.26), kind=kOutput, calls=%fused_computation.21 | convolution fusion | flops 362274816 | bytes 3130368 | tf_op jit(solution)/shard_map/ciap,iapkq->cikq/dot_general | solution.py:118
  25.1 1.7 %collective-permute-done.4 = bf16[256,2,144]{0,2,1:T(8,128)(2,1)S(1)} collective-permute-done((bf16[256,2,144]{0,2,1:T(8,128)(2,1)S(1)}, bf16[256,2,144]{0,2,1:T(8,128)(2,1)S(1)}, u32[]{:S(2)}, u32[]{:S(2)}) %collective-permute-start.4) | collective-permute-done | bytes 147488 | tf_op jit(solution)/shard_map/ppermute | solution.py:55
  26.9 0.7 broadcast_select_fusion.2
  27.6 3.2 %fusion.19 = f32[256,4,3,136]{0,3,1,2:T(8,128)} fusion(bf16[3,256,256]{2,1,0:T(8,128)(2,1)S(1)} %copy-done.4, bf16[256,2,144]{0,2,1:T(8,128)(2,1)} %get-tuple-element.41, bf16[256,2,144]{0,2,1:T(8,128)(2,1)} %copy-done.5, bf16[256,2,144]{0,2,1:T(8,128)(2,1)} %get-tuple-element.40, pred[]{:T(512)S(6)} %eq.73, bf16[136,144,3,4,3]{1,3,4,2,0:T(4,128)(2,1)S(1)} %copy-done.2), kind=kOutput, calls=%fused_computation.16 | convolution fusion | flops 589234176 | bytes 3916801 | tf_op jit(solution)/shard_map/cikq,iapkq->ciap/dot_general | solution.py:137
  30.9 1.3 %slice_bitcast_fusion.2 = (f32[256,3,136]{0,2,1:T(8,128)S(1)}, f32[256,3,136]{0,2,1:T(8,128)S(1)}) fusion(f32[256,4,3,136]{0,3,1,2:T(8,128)} %fusion.19), kind=kLoop, calls=%fused_computation.71 | loop fusion | bytes 1671168 | tf_op jit(solution)/shard_map/squeeze | solution.py:140
  32.1 1.2 %fusion.56 = bf16[256,4,136]{0,2,1:T(8,128)(2,1)S(1)} fusion(f32[256,4,3,136]{0,3,1,2:T(8,128)} %fusion.19, f32[256,3,136]{0,2,1:T(8,128)S(1)} %get-tuple-element.25, f32[256,3,136]{0,2,1:T(8,128)S(1)} %get-tuple-element.24), kind=kLoop, calls=%fused_computation.68 | loop fusion | flops 417792 | bytes 1671168 | tf_op jit(solution)/shard_map/convert_element_type | solution.py:201
  33.4 0.8 fusion.46
  34.2 0.3 copy-done.6
  34.5 0.4 fusion.31
  34.9 0.3 fusion.27
  35.3 0.1 collective-permute-start.3
  35.3 0.3 fusion.28
  35.7 0.8 constant_dynamic-slice_fusion.4
  36.5 0.5 collective-permute-start.5
  37.0 0.2 collective-permute-done.3
  37.2 1.0 %dynamic-slice_add_fusion.1 = f32[384,256]{1,0:T(8,128)S(1)} fusion(f32[384,256]{1,0:T(8,128)} %collective-permute-done.3, f32[768,256]{1,0:T(8,128)S(1)} %bitcast.188, s32[]{:T(128)S(6)} %select_n.176), kind=kLoop, calls=%fused_computation.83 | loop fusion | flops 98304 | bytes 1179652 | tf_op jit(solution)/shard_map/add | solution.py:31
  38.2 0.4 collective-permute-done.5
  38.7 1.0 %dynamic-slice_add_fusion = f32[384,256]{1,0:T(8,128)S(1)} fusion(f32[384,256]{1,0:T(8,128)} %collective-permute-done.5, f32[768,256]{1,0:T(8,128)S(1)} %bitcast.195, s32[]{:T(128)S(6)} %select_n.176), kind=kLoop, calls=%fused_computation.82 | loop fusion | flops 98304 | bytes 1179652 | tf_op jit(solution)/shard_map/add | solution.py:31
  39.7 1.6 %collective-permute-start.6 = (f32[192,256]{1,0:T(8,128)S(1)}, f32[192,256]{1,0:T(8,128)S(1)}, u32[]{:S(2)}, u32[]{:S(2)}) collective-permute-start(f32[192,256]{1,0:T(8,128)S(1)} %constant_dynamic-slice_fusion.3), channel_id=1, source_target_pairs={{0,16},{8,24},{16,0},{24,8},{1,17},{9,25},{17,1},{25,9},{2,18},{10... | collective-permute-start | bytes 589832 | tf_op jit(solution)/shard_map/ppermute | solution.py:31
  41.3 0.6 collective-permute-start.13
  41.9 4.0 %fusion.14 = f32[256,4,3,144]{0,3,2,1:T(8,128)} fusion(bf16[4,3,144,3,136]{2,0,1,3,4:T(4,128)(2,1)} %copy-done.1, bf16[3,256,256]{2,1,0:T(8,128)(2,1)S(1)} %copy-done, bf16[256,4,136]{0,2,1:T(8,128)(2,1)S(1)} %copy-done.9), kind=kOutput, calls=%fused_computation.15 | convolution fusion | flops 575299584 | bytes 3851264 | tf_op jit(solution)/shard_map/cikq,iapkq->ciap/dot_general | solution.py:124
  45.9 1.7 %collective-permute-done.6 = f32[192,256]{1,0:T(8,128)S(1)} collective-permute-done((f32[192,256]{1,0:T(8,128)S(1)}, f32[192,256]{1,0:T(8,128)S(1)}, u32[]{:S(2)}, u32[]{:S(2)}) %collective-permute-start.6) | collective-permute-done | bytes 196640 | tf_op jit(solution)/shard_map/ppermute | solution.py:31
  47.6 1.6 %collective-permute-start.7 = (f32[96,256]{1,0:T(8,128)S(1)}, f32[96,256]{1,0:T(8,128)S(1)}, u32[]{:S(2)}, u32[]{:S(2)}) collective-permute-start(f32[96,256]{1,0:T(8,128)S(1)} %constant_dynamic-slice_fusion.2), channel_id=1, source_target_pairs={{0,4},{4,0},{1,5},{5,1},{2,6},{6,2},{3,7},{7,3},{8,12},{12,8},{9,1... | collective-permute-start | bytes 294920 | tf_op jit(solution)/shard_map/ppermute | solution.py:31
  49.2 2.0 %collective-permute-done.13 = f32[192,256]{1,0:T(8,128)S(1)} collective-permute-done((f32[192,256]{1,0:T(8,128)S(1)}, f32[192,256]{1,0:T(8,128)S(1)}, u32[]{:S(2)}, u32[]{:S(2)}) %collective-permute-start.13) | collective-permute-done | bytes 196640 | tf_op jit(solution)/shard_map/ppermute | solution.py:31
  51.2 1.6 %collective-permute-start.14 = (f32[96,256]{1,0:T(8,128)S(1)}, f32[96,256]{1,0:T(8,128)S(1)}, u32[]{:S(2)}, u32[]{:S(2)}) collective-permute-start(f32[96,256]{1,0:T(8,128)S(1)} %constant_dynamic-slice_fusion), channel_id=1, source_target_pairs={{0,4},{4,0},{1,5},{5,1},{2,6},{6,2},{3,7},{7,3},{8,12},{12,8},{9,1... | collective-permute-start | bytes 294920 | tf_op jit(solution)/shard_map/ppermute | solution.py:31
  52.8 0.1 collective-permute-start.8
  52.9 3.0 %collective-permute-done.14 = f32[96,256]{1,0:T(8,128)S(1)} collective-permute-done((f32[96,256]{1,0:T(8,128)S(1)}, f32[96,256]{1,0:T(8,128)S(1)}, u32[]{:S(2)}, u32[]{:S(2)}) %collective-permute-start.14) | collective-permute-done | bytes 98336 | tf_op jit(solution)/shard_map/ppermute | solution.py:31
  56.0 2.1 %collective-permute-done.8 = f32[96,256]{1,0:T(8,128)S(1)} collective-permute-done((f32[96,256]{1,0:T(8,128)S(1)}, f32[96,256]{1,0:T(8,128)S(1)}, u32[]{:S(2)}, u32[]{:S(2)}) %collective-permute-start.8) | collective-permute-done | bytes 98336 | tf_op jit(solution)/shard_map/ppermute | solution.py:37
  58.1 1.1 %collective-permute-start.9 = (f32[96,256]{1,0:T(8,128)S(1)}, f32[96,256]{1,0:T(8,128)S(1)}, u32[]{:S(2)}, u32[]{:S(2)}) collective-permute-start(f32[96,256]{1,0:T(8,128)S(1)} %add.184), channel_id=1, source_target_pairs={{0,2},{1,3},{2,0},{3,1},{4,6},{5,7},{6,4},{7,5},{8,10},{9,11},{10,... | collective-permute-start | bytes 294920 | tf_op jit(solution)/shard_map/ppermute | solution.py:37
  59.2 1.1 %fusion.83 = bf16[1,256,2,128]{1,3,2,0:T(8,128)(2,1)S(1)} fusion(f32[256,4,3,144]{0,3,2,1:T(8,128)} %fusion.14), kind=kLoop, calls=%fused_computation.113 | loop fusion | flops 196608 | bytes 917504 | tf_op jit(solution)/shard_map/convert_element_type | solution.py:225
  60.4 1.3 %collective-permute-done.15 = f32[96,256]{1,0:T(8,128)S(1)} collective-permute-done((f32[96,256]{1,0:T(8,128)S(1)}, f32[96,256]{1,0:T(8,128)S(1)}, u32[]{:S(2)}, u32[]{:S(2)}) %collective-permute-start.15) | collective-permute-done | bytes 98336 | tf_op jit(solution)/shard_map/ppermute | solution.py:37
  61.7 0.7 collective-permute-start.16
  62.4 3.8 %collective-permute-done.9 = f32[96,256]{1,0:T(8,128)S(1)} collective-permute-done((f32[96,256]{1,0:T(8,128)S(1)}, f32[96,256]{1,0:T(8,128)S(1)}, u32[]{:S(2)}, u32[]{:S(2)}) %collective-permute-start.9) | collective-permute-done | bytes 98336 | tf_op jit(solution)/shard_map/ppermute | solution.py:37
  66.2 2.1 %collective-permute-start.10 = (bf16[96,256]{1,0:T(8,128)(2,1)S(1)}, bf16[96,256]{1,0:T(8,128)(2,1)S(1)}, u32[]{:S(2)}, u32[]{:S(2)}) collective-permute-start(bf16[96,256]{1,0:T(8,128)(2,1)S(1)} %add_convert_fusion.1), channel_id=1, source_target_pairs={{0,4},{4,0},{1,5},{5,1},{2,6},{6,2},{3,7},{7,3},{8,12},{12,8},{9,1... | collective-permute-start | bytes 147464 | tf_op jit(solution)/shard_map/ppermute | solution.py:42
  68.3 1.2 %collective-permute-start.17 = (bf16[96,256]{1,0:T(8,128)(2,1)S(1)}, bf16[96,256]{1,0:T(8,128)(2,1)S(1)}, u32[]{:S(2)}, u32[]{:S(2)}) collective-permute-start(bf16[96,256]{1,0:T(8,128)(2,1)S(1)} %add_convert_fusion), channel_id=1, source_target_pairs={{0,4},{4,0},{1,5},{5,1},{2,6},{6,2},{3,7},{7,3},{8,12},{12,8},{9,1... | collective-permute-start | bytes 147464 | tf_op jit(solution)/shard_map/ppermute | solution.py:42
  69.5 1.1 %collective-permute-done.10 = bf16[96,256]{1,0:T(8,128)(2,1)S(1)} collective-permute-done((bf16[96,256]{1,0:T(8,128)(2,1)S(1)}, bf16[96,256]{1,0:T(8,128)(2,1)S(1)}, u32[]{:S(2)}, u32[]{:S(2)}) %collective-permute-start.10) | collective-permute-done | bytes 49184 | tf_op jit(solution)/shard_map/ppermute | solution.py:42
  70.7 1.6 %collective-permute-start.11 = (bf16[192,256]{1,0:T(8,128)(2,1)S(1)}, bf16[192,256]{1,0:T(8,128)(2,1)S(1)}, u32[]{:S(2)}, u32[]{:S(2)}) collective-permute-start(bf16[192,256]{1,0:T(8,128)(2,1)S(1)} %maximum_select_fusion.5), channel_id=1, source_target_pairs={{0,16},{8,24},{16,0},{24,8},{1,17},{9,25},{17,1},{25,9},{2,18},{10... | collective-permute-start | bytes 294920 | tf_op jit(solution)/shard_map/ppermute | solution.py:42
  72.2 0.3 collective-permute-done.17
  72.5 1.6 %collective-permute-start.18 = (bf16[192,256]{1,0:T(8,128)(2,1)S(1)}, bf16[192,256]{1,0:T(8,128)(2,1)S(1)}, u32[]{:S(2)}, u32[]{:S(2)}) collective-permute-start(bf16[192,256]{1,0:T(8,128)(2,1)S(1)} %maximum_select_fusion.6), channel_id=1, source_target_pairs={{0,16},{8,24},{16,0},{24,8},{1,17},{9,25},{17,1},{25,9},{2,18},{10... | collective-permute-start | bytes 294920 | tf_op jit(solution)/shard_map/ppermute | solution.py:42
  74.1 1.3 %collective-permute-done.11 = bf16[192,256]{1,0:T(8,128)(2,1)S(1)} collective-permute-done((bf16[192,256]{1,0:T(8,128)(2,1)S(1)}, bf16[192,256]{1,0:T(8,128)(2,1)S(1)}, u32[]{:S(2)}, u32[]{:S(2)}) %collective-permute-start.11) | collective-permute-done | bytes 98336 | tf_op jit(solution)/shard_map/ppermute | solution.py:42
  75.5 1.7 %collective-permute-done.18 = bf16[192,256]{1,0:T(8,128)(2,1)S(1)} collective-permute-done((bf16[192,256]{1,0:T(8,128)(2,1)S(1)}, bf16[192,256]{1,0:T(8,128)(2,1)S(1)}, u32[]{:S(2)}, u32[]{:S(2)}) %collective-permute-start.18) | collective-permute-done | bytes 98336 | tf_op jit(solution)/shard_map/ppermute | solution.py:42
  77.4 0.3 fusion.33
  77.7 0.8 copy.40
  78.4 0.8 copy.41
  79.2 0.9 %maximum_select_fusion = f32[768,256]{1,0:T(8,128)} fusion(f32[384,256]{1,0:T(8,128)S(1)} %get-tuple-element.22, f32[384,256]{1,0:T(8,128)S(1)} %convert_element_type.136, pred[]{:T(512)S(6)} %eq.75), kind=kLoop, calls=%fused_computation.47 | loop fusion | flops 589824 | bytes 1572865 | tf_op jit(solution)/shard_map/jit(_where)/select_n | solution.py:45
  80.2 0.9 %maximum_select_fusion.1 = f32[768,256]{1,0:T(8,128)} fusion(f32[384,256]{1,0:T(8,128)S(1)} %get-tuple-element.20, f32[384,256]{1,0:T(8,128)S(1)} %convert_element_type.139, pred[]{:T(512)S(6)} %eq.75), kind=kLoop, calls=%fused_computation.48 | loop fusion | flops 589824 | bytes 1572865 | tf_op jit(solution)/shard_map/jit(_where)/select_n | solution.py:45
  (62 shorter events, 1.2 us)
Async XLA Ops:
  0.6 32.7 %copy-start = (bf16[3,256,256]{2,1,0:T(8,128)(2,1)S(1)}, bf16[3,256,256]{2,1,0:T(8,128)(2,1)}, u32[]{:S(2)}) copy-start(bf16[3,256,256]{2,1,0:T(8,128)(2,1)} %param.8) | copy-start | bytes 1179652
  0.6 7.9 %copy-start.3 = (bf16[1,256,2,128]{3,2,1,0:T(2,128)(2,1)S(1)}, bf16[1,256,2,128]{3,2,1,0:T(2,128)(2,1)}, u32[]{:S(2)}) copy-start(bf16[1,256,2,128]{3,2,1,0:T(2,128)(2,1)} %param.13) | copy-start | bytes 393220
  3.7 8.0 %collective-permute-start = (bf16[257,2,128]{0,2,1:T(8,128)(2,1)S(1)}, bf16[257,2,128]{0,2,1:T(8,128)(2,1)S(1)}, u32[]{:S(2)}, u32[]{:S(2)}) collective-permute-start(bf16[257,2,128]{0,2,1:T(8,128)(2,1)S(1)} %pad_maximum_fusion.4), channel_id=1, source_target_pairs={{0,4},{4,0},{1,5},{5,1},{2,6},{6,2},{3,7},{7,3},{8,12},{12,8},{9,1... | collective-permute-start | bytes 394760 | tf_op jit(solution)/shard_map/ppermute | solution.py:55
  11.9 8.5 %collective-permute-start.2 = (bf16[512,6,8]{0,2,1:T(8,128)(2,1)S(1)}, bf16[512,6,8]{0,2,1:T(8,128)(2,1)S(1)}, u32[]{:S(2)}, u32[]{:S(2)}) collective-permute-start(bf16[512,6,8]{0,2,1:T(8,128)(2,1)S(1)} %get-tuple-element.30), channel_id=1, source_target_pairs={{0,3},{1,0},{2,1},{3,2},{4,7},{5,4},{6,5},{7,6},{8,11},{9,8},{10,9... | collective-permute-start | bytes 147464 | tf_op jit(solution)/shard_map/ppermute | solution.py:76
  15.7 5.9 %collective-permute-start.1 = (bf16[512,6,8]{0,2,1:T(8,128)(2,1)S(1)}, bf16[512,6,8]{0,2,1:T(8,128)(2,1)S(1)}, u32[]{:S(2)}, u32[]{:S(2)}) collective-permute-start(bf16[512,6,8]{0,2,1:T(8,128)(2,1)S(1)} %get-tuple-element.29), channel_id=1, source_target_pairs={{0,1},{1,2},{2,3},{3,0},{4,5},{5,6},{6,7},{7,4},{8,9},{9,10},{10,1... | collective-permute-start | bytes 147464 | tf_op jit(solution)/shard_map/ppermute | solution.py:75
  20.3 3.0 %copy-start.1 = (bf16[4,3,144,3,136]{2,0,1,3,4:T(4,128)(2,1)}, bf16[4,3,144,3,136]{2,0,1,3,4:T(4,128)(2,1)S(1)}, u32[]{:S(2)}) copy-start(bf16[4,3,144,3,136]{2,0,1,3,4:T(4,128)(2,1)S(1)} %convert_bitcast_fusion) | copy-start | bytes 4230148
  21.6 3.5 %copy-start.5 = (bf16[256,2,144]{0,2,1:T(8,128)(2,1)}, bf16[256,2,144]{0,2,1:T(8,128)(2,1)S(1)}, u32[]{:S(2)}) copy-start(bf16[256,2,144]{0,2,1:T(8,128)(2,1)S(1)} %pad_maximum_fusion.5) | copy-start | bytes 442372
  21.7 5.2 %collective-permute-start.4 = (bf16[256,2,144]{0,2,1:T(8,128)(2,1)S(1)}, bf16[256,2,144]{0,2,1:T(8,128)(2,1)S(1)}, u32[]{:S(2)}, u32[]{:S(2)}) collective-permute-start(bf16[256,2,144]{0,2,1:T(8,128)(2,1)S(1)} %pad_maximum_fusion.5), channel_id=1, source_target_pairs={{0,4},{4,0},{1,5},{5,1},{2,6},{6,2},{3,7},{7,3},{8,12},{12,8},{9,1... | collective-permute-start | bytes 442376 | tf_op jit(solution)/shard_map/ppermute | solution.py:55
  23.4 4.2 %copy-start.2 = (bf16[136,144,3,4,3]{1,3,4,2,0:T(4,128)(2,1)S(1)}, bf16[136,144,3,4,3]{1,3,4,2,0:T(4,128)(2,1)}, u32[]{:S(2)}) copy-start(bf16[136,144,3,4,3]{1,3,4,2,0:T(4,128)(2,1)} %fusion.10) | copy-start | bytes 4230148
  23.4 4.2 %copy-start.4 = (bf16[3,256,256]{2,1,0:T(8,128)(2,1)S(1)}, bf16[3,256,256]{2,1,0:T(8,128)(2,1)}, u32[]{:S(2)}) copy-start(bf16[3,256,256]{2,1,0:T(8,128)(2,1)} %param.9) | copy-start | bytes 1179652
  30.9 2.5 %copy-start.7 = (bf16[256,4,3,136]{0,3,2,1:T(8,128)(2,1)S(1)}, bf16[256,4,3,136]{0,3,2,1:T(8,128)(2,1)}, u32[]{:S(2)}) copy-start(bf16[256,4,3,136]{0,3,2,1:T(8,128)(2,1)} %fusion.24) | copy-start | bytes 2506756
  33.4 1.2 %copy-start.6 = (bf16[136,128,3,2,3]{1,4,3,2,0:T(4,128)(2,1)S(1)}, bf16[136,128,3,2,3]{1,4,3,2,0:T(4,128)(2,1)}, u32[]{:S(2)}) copy-start(bf16[136,128,3,2,3]{1,4,3,2,0:T(4,128)(2,1)} %fusion.34) | copy-start | bytes 1880068
  34.2 1.2 %copy-start.8 = (bf16[256,4,136]{0,2,1:T(8,128)(2,1)}, bf16[256,4,136]{0,2,1:T(8,128)(2,1)S(1)}, u32[]{:S(2)}) copy-start(bf16[256,4,136]{0,2,1:T(8,128)(2,1)S(1)} %get-tuple-element.9) | copy-start | bytes 835588
  35.3 1.9 %collective-permute-start.3 = (f32[384,256]{1,0:T(8,128)S(1)}, f32[384,256]{1,0:T(8,128)}, u32[]{:S(2)}, u32[]{:S(2)}) collective-permute-start(f32[384,256]{1,0:T(8,128)S(1)} %constant_dynamic-slice_fusion.5), channel_id=1, source_target_pairs={{0,8},{8,0},{16,24},{24,16},{1,9},{9,1},{17,25},{25,17},{2,10},{10... | collective-permute-start | bytes 1179656 | tf_op jit(solution)/shard_map/ppermute | solution.py:31
  35.7 6.2 %copy-start.9 = (bf16[256,4,136]{0,2,1:T(8,128)(2,1)S(1)}, bf16[256,4,136]{0,2,1:T(8,128)(2,1)}, u32[]{:S(2)}) copy-start(bf16[256,4,136]{0,2,1:T(8,128)(2,1)} %copy-done.8) | copy-start | bytes 835588
  36.5 2.2 %collective-permute-start.5 = (f32[384,256]{1,0:T(8,128)}, f32[384,256]{1,0:T(8,128)}, u32[]{:S(2)}, u32[]{:S(2)}) collective-permute-start(f32[384,256]{1,0:T(8,128)} %constant_dynamic-slice_fusion.4), channel_id=1, source_target_pairs={{0,8},{8,0},{16,24},{24,16},{1,9},{9,1},{17,25},{25,17},{2,10},{10... | collective-permute-start | bytes 1179656 | tf_op jit(solution)/shard_map/ppermute | solution.py:31
  39.7 7.8 %collective-permute-start.6 = (f32[192,256]{1,0:T(8,128)S(1)}, f32[192,256]{1,0:T(8,128)S(1)}, u32[]{:S(2)}, u32[]{:S(2)}) collective-permute-start(f32[192,256]{1,0:T(8,128)S(1)} %constant_dynamic-slice_fusion.3), channel_id=1, source_target_pairs={{0,16},{8,24},{16,0},{24,8},{1,17},{9,25},{17,1},{25,9},{2,18},{10... | collective-permute-start | bytes 589832 | tf_op jit(solution)/shard_map/ppermute | solution.py:31
  41.3 9.9 %collective-permute-start.13 = (f32[192,256]{1,0:T(8,128)S(1)}, f32[192,256]{1,0:T(8,128)S(1)}, u32[]{:S(2)}, u32[]{:S(2)}) collective-permute-start(f32[192,256]{1,0:T(8,128)S(1)} %constant_dynamic-slice_fusion.1), channel_id=1, source_target_pairs={{0,16},{8,24},{16,0},{24,8},{1,17},{9,25},{17,1},{25,9},{2,18},{10... | collective-permute-start | bytes 589832 | tf_op jit(solution)/shard_map/ppermute | solution.py:31
  47.6 5.2 %collective-permute-start.7 = (f32[96,256]{1,0:T(8,128)S(1)}, f32[96,256]{1,0:T(8,128)S(1)}, u32[]{:S(2)}, u32[]{:S(2)}) collective-permute-start(f32[96,256]{1,0:T(8,128)S(1)} %constant_dynamic-slice_fusion.2), channel_id=1, source_target_pairs={{0,4},{4,0},{1,5},{5,1},{2,6},{6,2},{3,7},{7,3},{8,12},{12,8},{9,1... | collective-permute-start | bytes 294920 | tf_op jit(solution)/shard_map/ppermute | solution.py:31
  51.2 4.7 %collective-permute-start.14 = (f32[96,256]{1,0:T(8,128)S(1)}, f32[96,256]{1,0:T(8,128)S(1)}, u32[]{:S(2)}, u32[]{:S(2)}) collective-permute-start(f32[96,256]{1,0:T(8,128)S(1)} %constant_dynamic-slice_fusion), channel_id=1, source_target_pairs={{0,4},{4,0},{1,5},{5,1},{2,6},{6,2},{3,7},{7,3},{8,12},{12,8},{9,1... | collective-permute-start | bytes 294920 | tf_op jit(solution)/shard_map/ppermute | solution.py:31
  52.8 5.2 %collective-permute-start.8 = (f32[96,256]{1,0:T(8,128)S(1)}, f32[96,256]{1,0:T(8,128)S(1)}, u32[]{:S(2)}, u32[]{:S(2)}) collective-permute-start(f32[96,256]{1,0:T(8,128)S(1)} %dynamic-slice_add_fusion.5), channel_id=1, source_target_pairs={{0,1},{1,0},{2,3},{3,2},{4,5},{5,4},{6,7},{7,6},{8,9},{9,8},{10,11... | collective-permute-start | bytes 294920 | tf_op jit(solution)/shard_map/ppermute | solution.py:37
  55.9 5.7 %collective-permute-start.15 = (f32[96,256]{1,0:T(8,128)S(1)}, f32[96,256]{1,0:T(8,128)S(1)}, u32[]{:S(2)}, u32[]{:S(2)}) collective-permute-start(f32[96,256]{1,0:T(8,128)S(1)} %dynamic-slice_add_fusion.4), channel_id=1, source_target_pairs={{0,1},{1,0},{2,3},{3,2},{4,5},{5,4},{6,7},{7,6},{8,9},{9,8},{10,11... | collective-permute-start | bytes 294920 | tf_op jit(solution)/shard_map/ppermute | solution.py:37
  58.1 8.1 %collective-permute-start.9 = (f32[96,256]{1,0:T(8,128)S(1)}, f32[96,256]{1,0:T(8,128)S(1)}, u32[]{:S(2)}, u32[]{:S(2)}) collective-permute-start(f32[96,256]{1,0:T(8,128)S(1)} %add.184), channel_id=1, source_target_pairs={{0,2},{1,3},{2,0},{3,1},{4,6},{5,7},{6,4},{7,5},{8,10},{9,11},{10,... | collective-permute-start | bytes 294920 | tf_op jit(solution)/shard_map/ppermute | solution.py:37
  61.7 6.6 %collective-permute-start.16 = (f32[96,256]{1,0:T(8,128)S(1)}, f32[96,256]{1,0:T(8,128)S(1)}, u32[]{:S(2)}, u32[]{:S(2)}) collective-permute-start(f32[96,256]{1,0:T(8,128)S(1)} %add.188), channel_id=1, source_target_pairs={{0,2},{1,3},{2,0},{3,1},{4,6},{5,7},{6,4},{7,5},{8,10},{9,11},{10,... | collective-permute-start | bytes 294920 | tf_op jit(solution)/shard_map/ppermute | solution.py:37
  66.2 4.4 %collective-permute-start.10 = (bf16[96,256]{1,0:T(8,128)(2,1)S(1)}, bf16[96,256]{1,0:T(8,128)(2,1)S(1)}, u32[]{:S(2)}, u32[]{:S(2)}) collective-permute-start(bf16[96,256]{1,0:T(8,128)(2,1)S(1)} %add_convert_fusion.1), channel_id=1, source_target_pairs={{0,4},{4,0},{1,5},{5,1},{2,6},{6,2},{3,7},{7,3},{8,12},{12,8},{9,1... | collective-permute-start | bytes 147464 | tf_op jit(solution)/shard_map/ppermute | solution.py:42
  68.3 4.2 %collective-permute-start.17 = (bf16[96,256]{1,0:T(8,128)(2,1)S(1)}, bf16[96,256]{1,0:T(8,128)(2,1)S(1)}, u32[]{:S(2)}, u32[]{:S(2)}) collective-permute-start(bf16[96,256]{1,0:T(8,128)(2,1)S(1)} %add_convert_fusion), channel_id=1, source_target_pairs={{0,4},{4,0},{1,5},{5,1},{2,6},{6,2},{3,7},{7,3},{8,12},{12,8},{9,1... | collective-permute-start | bytes 147464 | tf_op jit(solution)/shard_map/ppermute | solution.py:42
  70.7 4.7 %collective-permute-start.11 = (bf16[192,256]{1,0:T(8,128)(2,1)S(1)}, bf16[192,256]{1,0:T(8,128)(2,1)S(1)}, u32[]{:S(2)}, u32[]{:S(2)}) collective-permute-start(bf16[192,256]{1,0:T(8,128)(2,1)S(1)} %maximum_select_fusion.5), channel_id=1, source_target_pairs={{0,16},{8,24},{16,0},{24,8},{1,17},{9,25},{17,1},{25,9},{2,18},{10... | collective-permute-start | bytes 294920 | tf_op jit(solution)/shard_map/ppermute | solution.py:42
  72.5 4.7 %collective-permute-start.18 = (bf16[192,256]{1,0:T(8,128)(2,1)S(1)}, bf16[192,256]{1,0:T(8,128)(2,1)S(1)}, u32[]{:S(2)}, u32[]{:S(2)}) collective-permute-start(bf16[192,256]{1,0:T(8,128)(2,1)S(1)} %maximum_select_fusion.6), channel_id=1, source_target_pairs={{0,16},{8,24},{16,0},{24,8},{1,17},{9,25},{17,1},{25,9},{2,18},{10... | collective-permute-start | bytes 294920 | tf_op jit(solution)/shard_map/ppermute | solution.py:42
  75.4 3.8 %collective-permute-start.12 = (bf16[384,256]{1,0:T(8,128)(2,1)S(1)}, bf16[384,256]{1,0:T(8,128)(2,1)S(1)}, u32[]{:S(2)}, u32[]{:S(2)}) collective-permute-start(bf16[384,256]{1,0:T(8,128)(2,1)S(1)} %get-tuple-element.23), channel_id=1, source_target_pairs={{0,8},{8,0},{16,24},{24,16},{1,9},{9,1},{17,25},{25,17},{2,10},{10... | collective-permute-start | bytes 589832 | tf_op jit(solution)/shard_map/ppermute | solution.py:42
  77.3 2.9 %collective-permute-start.19 = (bf16[384,256]{1,0:T(8,128)(2,1)S(1)}, bf16[384,256]{1,0:T(8,128)(2,1)S(1)}, u32[]{:S(2)}, u32[]{:S(2)}) collective-permute-start(bf16[384,256]{1,0:T(8,128)(2,1)S(1)} %get-tuple-element.21), channel_id=1, source_target_pairs={{0,8},{8,0},{16,24},{24,16},{1,9},{9,1},{17,25},{25,17},{2,10},{10... | collective-permute-start | bytes 589832 | tf_op jit(solution)/shard_map/ppermute | solution.py:42
